TPU v7x, 128 devices: a whole 4x4x4 slice. The times are simulated.
128 devices in a mesh: req: 16 (over z, x), tp: 8 (over y, core).
Axes of the slice: x: 4, y: 4, z: 4, core: 2. Of those that a mesh axis runs over, the one named last changes fastest.
Arguments:
- tokens: bfloat16 [8192, 3072], P('req', 'tp'), may hold values from -3 to 3
- norm_gain: bfloat16 [3072], P('tp'), may hold values from 0.099609375 to 1.8984375
- w_query: bfloat16 [3072, 3072], P(None, 'tp'), may hold values from -0.3125 to 0.3125
- w_key: bfloat16 [3072, 3072], P(None, 'tp'), may hold values from -0.109375 to 0.109375
- w_value: bfloat16 [3072, 3072], P(None, 'tp'), may hold values from -0.109375 to 0.109375
- w_out: bfloat16 [3072, 3072], P('tp'), may hold values from -0.109375 to 0.109375
- prev_keys: bfloat16 [65536, 3072], P('req', 'tp'), may hold values from -300 to 300
- prev_values: bfloat16 [65536, 3072], P('req', 'tp'), may hold values from -6 to 6
- earlier_lengths: int32 [16, 4], P('req'), may hold values from 1 to 2048, 4096 in all within a row
- new_lengths: int32 [16, 4], P('req'), may hold values from 1 to 256, 512 in all within a row
- page_table: int32 [16, 36], P('req'), may hold values from 0 to 575, as said below
Outputs:
- layer_out: bfloat16 [8192, 3072], P('req', 'tp')
- decode_pool: bfloat16 [288, 8, 128, 1536], P('req', 'tp')
Inputs may be any that keep to these rules, and one draw needn't show every extreme that they name: `page_table`: every value appears exactly once. Among the pages of one index of req, at most 2 share the same value // 18, and in every draw some destination receives exactly 2 of them.
All inputs are finite; a program needn't handle non-finite values.
Results may differ from a plain program's by a relative error of at most 0.0075.
Values may be sent and summed in bfloat16 or wider, within the bound.
No kernel may reach another device: no remote copies, remote signals or barrier semaphores. Data moves between devices by JAX's collectives and lax.ppermute only.
A program may use at most 256 MiB of HBM per device.

v0:
```python
import math

import jax
import jax.numpy as jnp
from jax import lax
from jax.sharding import PartitionSpec as P

HD = 96
HG = 4
PAGE = 128


EPSILON = 1e-05
THETA = 10000.0


def from_partner(value, axis, distance):
    mask = 2**distance
    pairs = [(source, source ^ mask) for source in range(lax.axis_size(axis))]
    return lax.ppermute(value, axis, pairs)


def rotate(values, positions, head_size):
    count = values.shape[0]
    half_size = head_size // 2
    shaped = values.reshape(count, -1, head_size)
    freqs = jnp.exp(-math.log(THETA) * 2.0 * jnp.arange(half_size, dtype=jnp.float32) / head_size)
    angles = positions.astype(jnp.float32)[:, None] * freqs[None, :]
    cosine = jnp.cos(angles)[:, None, :]
    sine = jnp.sin(angles)[:, None, :]
    first = shaped[:, :, :half_size]
    second = shaped[:, :, half_size:]
    turned = jnp.concatenate(
        [first * cosine - second * sine, second * cosine + first * sine], axis=2
    )
    return turned.reshape(count, -1)


def request_ids(lengths, count):
    ends = jnp.cumsum(lengths)
    row_index = jnp.arange(count, dtype=jnp.int32)
    return jnp.sum((row_index[:, None] >= ends[None, :]).astype(jnp.int32), axis=1)


def block_layout(earlier, fresh, count):
    owners = request_ids(fresh, count)
    starts = jnp.cumsum(fresh) - fresh
    onehot = (owners[:, None] == jnp.arange(fresh.shape[0], dtype=jnp.int32)[None, :]).astype(
        jnp.int32
    )
    first_row = jnp.sum(onehot * starts[None, :], axis=1)
    before = jnp.sum(onehot * earlier[None, :], axis=1)
    row_index = jnp.arange(count, dtype=jnp.int32)
    return (owners, before + row_index - first_row)


def visible(earlier, owners, prev_count, count):
    prev_owner = request_ids(earlier, prev_count)
    row_index = jnp.arange(count, dtype=jnp.int32)
    old_part = owners[:, None] == prev_owner[None, :]
    new_part = (owners[:, None] == owners[None, :]) & (row_index[None, :] <= row_index[:, None])
    return jnp.concatenate([old_part, new_part], axis=1)


def order_pair(mine, partner, own_half):
    lower = jnp.where(own_half == 0, mine, partner)
    upper = jnp.where(own_half == 0, partner, mine)
    return jnp.stack([lower, upper], axis=1)


def join_heads(stacked, local_width):
    count, halves, rows_page = (stacked.shape[0], stacked.shape[1], stacked.shape[2])
    split_rows = stacked.reshape(count, halves, rows_page, 2, local_width)
    return split_rows.transpose(0, 2, 3, 1, 4).reshape(count, rows_page, 2 * halves * local_width)


def fill_pool(page_rows, slot_ids, slot_count):
    empty = jnp.zeros((slot_count + 1, page_rows.shape[1], page_rows.shape[2]), jnp.bfloat16)
    return empty.at[slot_ids].set(page_rows)[:slot_count][:, None]


def shards(
    tokens,
    norm_gain,
    w_query,
    w_key,
    w_value,
    w_out,
    prev_keys,
    prev_values,
    earlier_lengths,
    new_lengths,
    page_table,
):
    token_count, local_width = tokens.shape
    full_width = w_query.shape[0]
    widened = tokens.astype(jnp.float32)
    square_sums = lax.psum(jnp.sum(widened * widened, axis=1), "tp")
    scaling = lax.rsqrt(square_sums / full_width + EPSILON)
    normed = (widened * scaling[:, None] * norm_gain.astype(jnp.float32)[None, :]).astype(
        jnp.bfloat16
    )
    fragment = lax.all_gather(normed, "tp", axis=1, tiled=True)
    query_raw, key_raw, value_raw = tuple(
        (
            jnp.dot(fragment, weight, preferred_element_type=jnp.float32)
            for weight in (w_query, w_key, w_value)
        )
    )
    earlier = earlier_lengths[0]
    fresh = new_lengths[0]
    owners, positions = block_layout(earlier, fresh, token_count)
    queries = rotate(query_raw, positions, HD).astype(jnp.bfloat16)
    new_keys = rotate(key_raw, positions, HD).astype(jnp.bfloat16)
    new_values = value_raw.astype(jnp.bfloat16)
    keys_all = jnp.concatenate([prev_keys, new_keys], axis=0)
    values_all = jnp.concatenate([prev_values, new_values], axis=0)
    allowed = visible(earlier, owners, prev_keys.shape[0], token_count)
    heads_here = local_width // HD
    scores = jnp.einsum(
        "qhd,khd->hqk",
        queries.reshape(token_count, heads_here, HD),
        keys_all.reshape(-1, heads_here, HD),
        preferred_element_type=jnp.float32,
    ) * HD ** (-0.5)
    scores = jnp.where(allowed[None, :, :], scores, -1e30)
    row_peak = jnp.max(scores, axis=2, keepdims=True)
    weights = jnp.exp(scores - row_peak)
    totals = jnp.sum(weights, axis=2)
    prob_rows = weights.astype(jnp.bfloat16)
    mixture = jnp.einsum(
        "hqk,khd->qhd",
        prob_rows,
        values_all.reshape(-1, heads_here, HD),
        preferred_element_type=jnp.float32,
    )
    attended = (
        (mixture / totals.T[:, :, None]).astype(jnp.bfloat16).reshape(token_count, local_width)
    )
    projected = jnp.dot(attended, w_out, preferred_element_type=jnp.float32)
    summed = lax.psum_scatter(projected, "tp", scatter_dimension=1, tiled=True)
    layer_out = (tokens.astype(jnp.float32) + summed).astype(jnp.bfloat16)
    page_total = keys_all.shape[0] // PAGE
    page_rows = jnp.concatenate(
        [
            keys_all.reshape(page_total, PAGE, local_width),
            values_all.reshape(page_total, PAGE, local_width),
        ],
        axis=2,
    )
    req_count = lax.axis_size("req")
    halves = lax.axis_size("tp") // HG
    slot_count = page_total // halves
    dest_count = req_count * halves
    capacity = 2 * ((page_total // 2 + dest_count - 1) // dest_count)
    table = page_table[0]
    target = table // slot_count
    slot_ids = table % slot_count
    own_half = lax.axis_index("tp") % halves
    order_index = jnp.arange(page_total, dtype=jnp.int32)
    earlier_mask = order_index[:, None] > order_index[None, :]
    placing = jnp.sum(
        ((target[:, None] == target[None, :]) & earlier_mask).astype(jnp.int32), axis=1
    )
    bucket = target * capacity + placing
    send_rows = (
        jnp.zeros((dest_count * capacity, PAGE, 2 * local_width), jnp.bfloat16)
        .at[bucket]
        .set(page_rows)
    )
    send_slots = jnp.full((dest_count * capacity,), slot_count, jnp.int32).at[bucket].set(slot_ids)
    got_rows, got_slots = (
        lax.all_to_all(send_rows, "req", split_axis=0, concat_axis=0, tiled=True),
        lax.all_to_all(send_slots, "req", split_axis=0, concat_axis=0, tiled=True),
    )
    got_rows = got_rows.reshape(req_count, halves, capacity, PAGE, 2 * local_width)
    got_slots = got_slots.reshape(req_count, halves, capacity)
    mine = lax.dynamic_index_in_dim(got_rows, own_half, 1, keepdims=False).reshape(
        req_count * capacity, PAGE, 2 * local_width
    )
    final_slots = lax.dynamic_index_in_dim(got_slots, own_half, 1, keepdims=False).reshape(-1)
    other = lax.dynamic_index_in_dim(got_rows, 1 - own_half, 1, keepdims=False).reshape(
        req_count * capacity, PAGE, 2 * local_width
    )
    partner = from_partner(other, "tp", 0)
    stacked = order_pair(mine, partner, own_half)
    final_rows = join_heads(stacked, local_width)
    decode_pool = fill_pool(final_rows, final_slots, slot_count)
    return (layer_out, decode_pool)


def solution(mesh):
    placed = (
        P("req", "tp"),
        P("tp"),
        P(None, "tp"),
        P(None, "tp"),
        P(None, "tp"),
        P("tp", None),
        P("req", "tp"),
        P("req", "tp"),
        P("req", None),
        P("req", None),
        P("req", None),
    )
    return jax.shard_map(
        shards,
        mesh=mesh,
        in_specs=placed,
        out_specs=(P("req", "tp"), P("req", "tp", None, None)),
        check_vma=False,
    )
```

profile of v0, /device:TPU:0, one launch (start us, length us, event | category | flops | bytes accessed | tf_op | source)
XLA Modules:
  0.0 441.2 jit_solution(15881802135246873474)
XLA Ops:
  9.2 14.9 %psum.7 = f32[512]{0:T(512)S(1)} all-reduce(f32[512]{0:T(512)S(1)} %fusion.16), channel_id=1, replica_groups=mesh['req'=16,'tp'=8] {'tp'}, use_global_device_ids=true, to_apply=%region_1.0 | all-reduce | flops 512 | bytes 4096 | tf_op jit(solution)/shard_map/psum | solution.py:98
  35.1 18.6 %all-gather.2.cloned.1.call-done = bf16[512,3072]{1,0:T(8,128)(2,1)} async-done(((bf16[512,384]{1,0:T(8,128)(2,1)}), bf16[512,3072]{1,0:T(8,128)(2,1)}) %all-gather.2.cloned.1.call-update) | async-done | bytes 3145744 | tf_op jit(solution)/shard_map/all_gather | solution.py:103
  63.9 5.8 %copy.54 = bf16[4608,384]{0,1:T(8,128)(2,1)} copy(bf16[4608,384]{1,0:T(8,128)(2,1)} %pad_maximum_fusion.2) | data formatting | bytes 7077888 | tf_op jit(solution)/shard_map/concatenate | solution.py:116
  69.7 4.5 %convolution_convert_fusion = bf16[512,384]{1,0:T(8,128)(2,1)S(1)} fusion(bf16[512,3072]{1,0:T(8,128)(2,1)} %all-gather.2.cloned.1.call-done, bf16[3072,384]{1,0:T(8,128)(2,1)} %param.15), kind=kOutput, calls=%fused_computation.20 | convolution fusion | flops 1208156160 | bytes 5898240 | tf_op jit(solution)/shard_map/dot_general | solution.py:106
  74.6 7.1 %pad_maximum_fusion = bf16[36,128,768]{2,1,0:T(8,128)(2,1)} fusion(bf16[36,128,384]{2,1,0:T(8,128)(2,1)S(1)} %bitcast.89, bf16[36,128,384]{2,1,0:T(8,128)(2,1)} %bitcast.90), kind=kLoop, calls=%fused_computation.13 | loop fusion | flops 14155776 | bytes 14155776 | tf_op jit(solution)/shard_map/concatenate | solution.py:144
  81.7 6.0 %broadcast_in_dim.20 = bf16[64,128,768]{2,1,0:T(8,128)(2,1)} broadcast(bf16[]{:T(256)} %constant.76.clone.1), dimensions={} | broadcast | bytes 12582914 | tf_op jit(solution)/shard_map/broadcast_in_dim | solution.py:167
  87.7 22.4 %scatter_fusion = bf16[64,128,768]{2,1,0:T(8,128)(2,1)} fusion(bf16[64,128,768]{2,1,0:T(8,128)(2,1)} %broadcast_in_dim.20, s32[36]{0:T(128)S(1)} %fusion.29, bf16[36,128,768]{2,1,0:T(8,128)(2,1)} %pad_maximum_fusion), kind=kCustom, calls=%fused_computation.1 | custom fusion | bytes 21233808 | tf_op jit(solution)/shard_map/scatter | solution.py:169
  110.1 7.0 %all-to-all-start.1 = ((bf16[64,128,768]{2,1,0:T(8,128)(2,1)}), bf16[64,128,768]{2,1,0:T(8,128)(2,1)}, u32[]{:S(2)}, u32[]{:S(2)}) async-start(bf16[64,128,768]{2,1,0:T(8,128)(2,1)} %scatter_fusion), calls=%async_computation.2 | async-start | bytes 25165824 | tf_op jit(solution)/shard_map/all_to_all | solution.py:173
  117.4 18.6 %fusion = (f32[4,512]{1,0:T(4,128)S(1)}, f32[4,512,4608]{2,1,0:T(8,128)}) fusion(pred[512,4608]{1,0:T(8,128)(4,1)} %pad_add_fusion, bf16[4608,4,96]{0,2,1:T(8,128)(2,1)} %bitcast.94, bf16[512,4,48]{0,2,1:T(8,128)(2,1)S(1)} %get-tuple-element.17, bf16[512,4,48]{0,2,1:T(8,128)(2,1)S(1)} %get-tuple-element.16), kind=kOutput, calls=%fused_computation.5 | convolution fusion | flops 1841035264 | bytes 44048384 | tf_op jit(solution)/shard_map/qhd,khd->hqk/dot_general | solution.py:120
  135.9 5.7 %copy.52 = bf16[4608,384]{0,1:T(8,128)(2,1)} copy(bf16[4608,384]{1,0:T(8,128)(2,1)} %copy-done.1) | data formatting | bytes 7077888 | tf_op jit(solution)/shard_map/concatenate | solution.py:117
  141.6 18.2 %fusion.1 = f32[4,512]{1,0:T(4,128)S(1)} fusion(f32[4,512,4608]{2,1,0:T(8,128)} %get-tuple-element.26, f32[4,512]{1,0:T(4,128)S(1)} %get-tuple-element.25, pred[512,4608]{1,0:T(8,128)(4,1)} %pad_add_fusion), kind=kLoop, calls=%fused_computation.6 | loop fusion | flops 37746688 | bytes 40124416 | tf_op jit(solution)/shard_map/reduce_sum | solution.py:129
  159.9 15.3 %fusion.12 = bf16[512,4,96]{0,2,1:T(8,128)(2,1)S(1)} fusion(bf16[4608,4,96]{0,2,1:T(8,128)(2,1)S(1)} %bitcast.95, f32[4,512,4608]{2,1,0:T(8,128)} %get-tuple-element.26, f32[4,512]{1,0:T(4,128)S(1)} %get-tuple-element.25, pred[512,4608]{1,0:T(8,128)(4,1)S(1)} %copy-done.2, f32[512,4]{0,1:T(4,128)S(1)} %bitcast.100), kind=kOutput, calls=%fused_computation.25 | convolution fusion | flops 1850081280 | bytes 44056576 | tf_op jit(solution)/shard_map/hqk,khd->qhd/dot_general | solution.py:131
  175.2 4.5 %fusion.39 = f32[512,3072]{1,0:T(8,128)} fusion(bf16[512,384]{0,1:T(8,128)(2,1)S(1)} %bitcast.99, bf16[384,3072]{1,0:T(8,128)(2,1)S(1)} %copy-done), kind=kOutput, calls=%fused_computation.83 | convolution fusion | flops 1207959552 | bytes 9043968 | tf_op jit(solution)/shard_map/dot_general | solution.py:140
  179.8 126.1 %all-to-all-done.1 = bf16[64,128,768]{2,1,0:T(8,128)(2,1)} async-done(((bf16[64,128,768]{2,1,0:T(8,128)(2,1)}), bf16[64,128,768]{2,1,0:T(8,128)(2,1)}, u32[]{:S(2)}, u32[]{:S(2)}) %all-to-all-start.1) | async-done | bytes 12582944 | tf_op jit(solution)/shard_map/all_to_all | solution.py:173
  305.9 10.7 %constant_dynamic-slice_fusion = (bf16[16,1,2,128,768]{4,3,2,1,0:T(8,128)(2,1)}, bf16[16,1,2,128,768]{4,3,2,1,0:T(8,128)(2,1)}) fusion(bf16[16,2,2,128,768]{4,3,2,1,0:T(8,128)(2,1)} %bitcast.28, s32[]{:T(128)S(6)} %select_n.86, s32[]{:T(128)S(6)} %select_n.89), kind=kLoop, calls=%fused_computation.63 | loop fusion | bytes 25165832 | tf_op jit(solution)/shard_map/jit(dynamic_index_in_dim)/dynamic_slice | solution.py:178
  321.7 7.2 %all-to-all-done = s32[16,4,1]{1,2,0:T(1,128)S(1)} async-done(((s32[16,4,1]{1,2,0:T(1,128)}), s32[16,4,1]{1,2,0:T(1,128)S(1)}, u32[]{:S(2)}, u32[]{:S(2)}) %all-to-all-start) | async-done | bytes 288 | tf_op jit(solution)/shard_map/all_to_all | solution.py:174
  331.2 10.3 %bitcast_select_fusion.1 = (bf16[32,128,768]{2,1,0:T(8,128)(2,1)}, bf16[32,128,768]{2,1,0:T(8,128)(2,1)}) fusion(bf16[32,128,768]{2,1,0:T(8,128)(2,1)} %collective-permute-done, bf16[16,1,2,128,768]{4,3,2,1,0:T(8,128)(2,1)} %get-tuple-element.14, pred[]{:T(512)S(6)} %eq.75), kind=kLoop, calls=%fused_computation.15 | loop fusion | flops 6291456 | bytes 25165824 | tf_op jit(solution)/shard_map/jit(_where)/select_n | solution.py:66
  341.5 8.7 %copy.58 = bf16[32,128,768]{1,2,0:T(8,128)(2,1)} copy(bf16[32,128,768]{2,1,0:T(8,128)(2,1)} %get-tuple-element.12) | data formatting | bytes 12582912 | tf_op jit(solution)/shard_map/jit(_where)/select_n | solution.py:66
  350.2 8.6 %copy.59 = bf16[32,128,768]{1,2,0:T(8,128)(2,1)} copy(bf16[32,128,768]{2,1,0:T(8,128)(2,1)} %get-tuple-element.13) | data formatting | bytes 12582912 | tf_op jit(solution)/shard_map/jit(_where)/select_n | solution.py:67
  358.8 6.2 %maximum_bitcast_fusion = bf16[32,128,2,2,384]{1,4,2,0,3:T(8,128)(2,1)S(1)} fusion(bf16[32,1,128,2,384]{2,4,3,0,1:T(8,128)(2,1)} %bitcast.92, bf16[32,1,128,2,384]{2,4,3,0,1:T(8,128)(2,1)} %bitcast.91), kind=kLoop, calls=%fused_computation.10 | loop fusion | flops 6291456 | bytes 25165824 | tf_op jit(solution)/shard_map/transpose | solution.py:74
  365.0 5.7 %copy.60 = bf16[32,128,2,2,384]{1,4,3,2,0:T(8,128)(2,1)} copy(bf16[32,128,2,2,384]{1,4,2,0,3:T(8,128)(2,1)S(1)} %maximum_bitcast_fusion) | data formatting | bytes 25165824 | tf_op jit(solution)/shard_map/transpose | solution.py:74
  370.7 16.6 %copy.61 = bf16[32,128,1536]{2,1,0:T(8,128)(2,1)} copy(bf16[32,128,1536]{1,2,0:T(8,128)(2,1)} %bitcast.88) | data formatting | bytes 25165824 | tf_op jit(solution)/shard_map/reshape | solution.py:74
  391.0 36.8 %scatter_fusion.1 = bf16[19,128,1536]{2,1,0:T(8,128)(2,1)} fusion(bf16[19,128,1536]{2,1,0:T(8,128)(2,1)} %broadcast_in_dim.18, s32[32]{0:T(128)S(1)} %fusion.30, bf16[32,128,1536]{2,1,0:T(8,128)(2,1)} %copy.61), kind=kCustom, calls=%fused_computation.2 | custom fusion | bytes 37748864 | tf_op jit(solution)/shard_map/scatter | solution.py:79
  427.8 6.6 %slice_bitcast_fusion = bf16[18,1,128,1536]{3,2,1,0:T(8,128)(2,1)} fusion(bf16[19,128,1536]{2,1,0:T(8,128)(2,1)} %scatter_fusion.1), kind=kLoop, calls=%fused_computation.12 | loop fusion | bytes 14155776
  (60 shorter events, 34.8 us)
Async XLA Ops:
  7.2 168.1 %copy-start = (bf16[384,3072]{1,0:T(8,128)(2,1)S(1)}, bf16[384,3072]{1,0:T(8,128)(2,1)}, u32[]{:S(2)}) copy-start(bf16[384,3072]{1,0:T(8,128)(2,1)} %param.16) | copy-start | bytes 7077892
  7.2 46.6 %all-gather.2.cloned.1.call-start = ((), (), s32[]{:S(2)}) async-start(), calls=%async_computation.3 | async-start | bytes 3538944 | tf_op jit(solution)/shard_map/all_gather | solution.py:103
  53.7 4.2 copy-start.6
  53.7 4.3 copy-start.7
  69.7 4.6 %copy-start.5 = (bf16[4096,384]{1,0:T(8,128)(2,1)S(1)}, bf16[4096,384]{1,0:T(8,128)(2,1)}, u32[]{:S(2)}) copy-start(bf16[4096,384]{1,0:T(8,128)(2,1)} %param.18) | copy-start | bytes 9437188
  74.6 7.1 %copy-start.1 = (bf16[4608,384]{1,0:T(8,128)(2,1)}, bf16[4608,384]{1,0:T(8,128)(2,1)S(1)}, u32[]{:S(2)}) copy-start(bf16[4608,384]{1,0:T(8,128)(2,1)S(1)} %pad_maximum_fusion.1) | copy-start | bytes 10616836
  110.1 195.8 %all-to-all-start.1 = ((bf16[64,128,768]{2,1,0:T(8,128)(2,1)}), bf16[64,128,768]{2,1,0:T(8,128)(2,1)}, u32[]{:S(2)}, u32[]{:S(2)}) async-start(bf16[64,128,768]{2,1,0:T(8,128)(2,1)} %scatter_fusion), calls=%async_computation.2 | async-start | bytes 25165824 | tf_op jit(solution)/shard_map/all_to_all | solution.py:173
  117.1 212.1 %reduce-scatter.2.cloned.1.call-start = ((), (), s32[]{:S(2)}) async-start(), calls=%async_computation.4 | async-start | bytes 7077888 | tf_op jit(solution)/shard_map/reduce_scatter | solution.py:141
  141.6 18.2 %copy-start.2 = (pred[512,4608]{1,0:T(8,128)(4,1)S(1)}, pred[512,4608]{1,0:T(8,128)(4,1)}, u32[]{:S(2)}) copy-start(pred[512,4608]{1,0:T(8,128)(4,1)} %pad_add_fusion) | copy-start | bytes 7077892
  141.6 18.2 %copy-start.3 = (bf16[4608,384]{0,1:T(8,128)(2,1)S(1)}, bf16[4608,384]{0,1:T(8,128)(2,1)}, u32[]{:S(2)}) copy-start(bf16[4608,384]{0,1:T(8,128)(2,1)} %copy.52) | copy-start | bytes 10616836
  305.9 23.3 %copy-start.4 = (bf16[512,384]{1,0:T(8,128)(2,1)S(1)}, bf16[512,384]{1,0:T(8,128)(2,1)}, u32[]{:S(2)}) copy-start(bf16[512,384]{1,0:T(8,128)(2,1)} %param.11) | copy-start | bytes 1179652
  316.6 14.5 %collective-permute-start = (bf16[32,128,768]{2,1,0:T(8,128)(2,1)}, bf16[32,128,768]{2,1,0:T(8,128)(2,1)}, u32[]{:S(2)}, u32[]{:S(2)}) collective-permute-start(bf16[32,128,768]{2,1,0:T(8,128)(2,1)} %bitcast.93), channel_id=1, source_target_pairs={{0,1},{1,0},{2,3},{3,2},{4,5},{5,4},{6,7},{7,6},{8,9},{9,8},{10,11... | collective-permute-start | bytes 18874376 | tf_op jit(solution)/shard_map/ppermute | solution.py:20
  318.0 10.9 %all-to-all-start = ((s32[16,4,1]{1,2,0:T(1,128)}), s32[16,4,1]{1,2,0:T(1,128)S(1)}, u32[]{:S(2)}, u32[]{:S(2)}) async-start(s32[16,4,1]{1,2,0:T(1,128)} %bitcast.23), calls=%async_computation.1 | async-start | bytes 16384 | tf_op jit(solution)/shard_map/all_to_all | solution.py:174
Sparse Core Ops, SparseCore 0:
  26.2 27.4 all-gather.1
  179.9 43.1 reduce-scatter.1
where the time goes:
time: 444 us; the launch traced here: 441 us
  waiting for transfers between devices  152 us (34%)
  local copies, waits for them, and re-layouts  139 us (31%)
  other arithmetic  61.3 us (14%)
  matrix products  48.6 us (11%)
  blocking collectives  14.9 us (3%)
  between operations  14.3 us (3%)
  starting transfers between devices  10.9 us (2%)
    all_to_all x1, waiting for transfers between devices, shards(): lax.all_to_all(send_rows, 'req', split_axis=0, concat_axis=0, tiled=True)  126 us
    scatter x1, local copies, waits for them, and re-layouts, fill_pool(): return empty.at[slot_ids].set(page_rows)[:slot_count][:, None]  36.8 us
    scatter x1, local copies, waits for them, and re-layouts, shards(): send_rows = jnp.zeros((dest_count * capacity, PAGE, 2 * local_width), jnp...  22.4 us
    all_gather x1, waiting for transfers between devices, shards(): fragment = lax.all_gather(normed, 'tp', axis=1, tiled=True)  18.6 us
    dot_general x1, matrix products, shards(): jnp.einsum('qhd,khd->hqk', queries.reshape(token_count, heads_here, HD),...  18.6 us
    reduce_sum x1, other arithmetic, shards(): totals = jnp.sum(weights, axis=2)  18.2 us
    reshape x1, local copies, waits for them, and re-layouts, join_heads(): split_rows.transpose(0, 2, 3, 1, 4)  16.6 us
    dot_general x1, matrix products, shards(): jnp.einsum('hqk,khd->qhd', prob_rows, values_all.reshape(-1, heads_here,...  15.3 us
  transfers between devices with their start and end apart: 5, of which 3 were waited for; matrix products, arithmetic and copies ran while one was open for 19% of the time, Pallas kernels for 0%

commit v1 on v0

v1 whole, which is shorter than its diff:
```python
import math

import jax
import jax.numpy as jnp
from jax import lax
from jax.experimental import pallas as pl
from jax.experimental.pallas import tpu as pltpu
from jax.sharding import Mesh
from jax.sharding import PartitionSpec as P

HD = 96
HG = 4
PAGE = 128
CAPACITY = 2


EPSILON = 1e-05
THETA = 10000.0


def rotate(values, positions, head_size):
    count = values.shape[0]
    half_size = head_size // 2
    shaped = values.reshape(count, -1, head_size)
    freqs = jnp.exp(-math.log(THETA) * 2.0 * jnp.arange(half_size, dtype=jnp.float32) / head_size)
    angles = positions.astype(jnp.float32)[:, None] * freqs[None, :]
    cosine = jnp.cos(angles)[:, None, :]
    sine = jnp.sin(angles)[:, None, :]
    first = shaped[:, :, :half_size]
    second = shaped[:, :, half_size:]
    turned = jnp.concatenate(
        [first * cosine - second * sine, second * cosine + first * sine], axis=2
    )
    return turned.reshape(count, -1)


def request_ids(lengths, count):
    ends = jnp.cumsum(lengths)
    row_index = jnp.arange(count, dtype=jnp.int32)
    return jnp.sum((row_index[:, None] >= ends[None, :]).astype(jnp.int32), axis=1)


def block_layout(earlier, fresh, count):
    owners = request_ids(fresh, count)
    starts = jnp.cumsum(fresh) - fresh
    onehot = (owners[:, None] == jnp.arange(fresh.shape[0], dtype=jnp.int32)[None, :]).astype(
        jnp.int32
    )
    first_row = jnp.sum(onehot * starts[None, :], axis=1)
    before = jnp.sum(onehot * earlier[None, :], axis=1)
    row_index = jnp.arange(count, dtype=jnp.int32)
    return (owners, before + row_index - first_row)


def visible(earlier, owners, prev_count, count):
    prev_owner = request_ids(earlier, prev_count)
    row_index = jnp.arange(count, dtype=jnp.int32)
    old_part = owners[:, None] == prev_owner[None, :]
    new_part = (owners[:, None] == owners[None, :]) & (row_index[None, :] <= row_index[:, None])
    return jnp.concatenate([old_part, new_part], axis=1)


def rank_in_dest(dests):
    same = (dests[..., :, None] == dests[..., None, :]).astype(jnp.int32)
    count = dests.shape[-1]
    order_index = jnp.arange(count, dtype=jnp.int32)
    earlier_mask = (order_index[None, :] < order_index[:, None]).astype(jnp.int32)
    return jnp.sum(same * earlier_mask, axis=-1)


def pack_pages(slots, prev_keys, prev_values, new_keys, new_values, slot_total):
    prev_pages = prev_keys.shape[0] // PAGE
    new_pages = new_keys.shape[0] // PAGE
    width = prev_keys.shape[1]
    sources = ((prev_keys, prev_values, prev_pages), (new_keys, new_values, new_pages))

    def body(slot_ref, pk, pv, nk, nv, out, sems):
        refs = ((pk, pv), (nk, nv))
        copies = []
        page = 0
        for which, (_, _, pages) in enumerate(sources):
            for local in range(pages):
                for kv in range(2):
                    src = refs[which][kv].at[pl.ds(local * PAGE, PAGE), :]
                    copy = pltpu.make_async_copy(
                        src, out.at[slot_ref[page], kv], sems.at[2 * page + kv]
                    )
                    copy.start()
                    copies.append(copy)
                page += 1
        for copy in copies:
            copy.wait()

    page_total = prev_pages + new_pages
    return pl.pallas_call(
        body,
        out_shape=jax.ShapeDtypeStruct((slot_total, 2, PAGE, width), jnp.bfloat16),
        grid_spec=pltpu.PrefetchScalarGridSpec(
            num_scalar_prefetch=1,
            grid=(1,),
            in_specs=[pl.BlockSpec(memory_space=pl.ANY)] * 4,
            out_specs=pl.BlockSpec(memory_space=pl.ANY),
            scratch_shapes=[pltpu.SemaphoreType.DMA((2 * page_total,))],
        ),
    )(slots, prev_keys, prev_values, new_keys, new_values)


def place_pages(sources, ranks, received, slot_count, cores):
    width = received.shape[-1]

    def body(src_ref, rank_ref, got, out, sems):
        copies = []
        for slot in range(slot_count):
            for core in range(cores):
                for kv in range(2):
                    column = (kv * cores + core) * width
                    index = (slot * cores + core) * 2 + kv
                    copy = pltpu.make_async_copy(
                        got.at[src_ref[slot] * cores + core, rank_ref[slot], kv],
                        out.at[slot, :, pl.ds(column, width)],
                        sems.at[index],
                    )
                    copy.start()
                    copies.append(copy)
        for copy in copies:
            copy.wait()

    return pl.pallas_call(
        body,
        out_shape=jax.ShapeDtypeStruct((slot_count, PAGE, 2 * cores * width), jnp.bfloat16),
        grid_spec=pltpu.PrefetchScalarGridSpec(
            num_scalar_prefetch=2,
            grid=(1,),
            in_specs=[pl.BlockSpec(memory_space=pl.ANY)],
            out_specs=pl.BlockSpec(memory_space=pl.ANY),
            scratch_shapes=[pltpu.SemaphoreType.DMA((slot_count * cores * 2,))],
        ),
    )(sources, ranks, received)


def shards(
    tokens,
    norm_gain,
    w_query,
    w_key,
    w_value,
    w_out,
    prev_keys,
    prev_values,
    earlier_lengths,
    new_lengths,
    page_table,
):
    token_count, local_width = tokens.shape
    full_width = w_query.shape[0]
    prev_count = prev_keys.shape[0]
    req_count = lax.axis_size("req")
    cores = lax.axis_size("core")
    my_req = lax.axis_index("req")
    my_core = lax.axis_index("core")

    full_tokens = lax.all_gather(tokens, ("y", "core"), axis=1, tiled=True)
    widened = full_tokens.astype(jnp.float32)
    mean_square = jnp.mean(widened * widened, axis=1, keepdims=True)
    normed = (widened * lax.rsqrt(mean_square + EPSILON) * norm_gain.astype(jnp.float32)[None, :]).astype(
        jnp.bfloat16
    )
    query_raw, key_raw, value_raw = tuple(
        (
            jnp.dot(normed, weight, preferred_element_type=jnp.float32)
            for weight in (w_query, w_key, w_value)
        )
    )
    earlier = earlier_lengths[0]
    fresh = new_lengths[0]
    owners, positions = block_layout(earlier, fresh, token_count)
    queries = rotate(query_raw, positions, HD).astype(jnp.bfloat16)
    new_keys = rotate(key_raw, positions, HD).astype(jnp.bfloat16)
    new_values = value_raw.astype(jnp.bfloat16)

    page_total = (prev_count + token_count) // PAGE
    slot_count = page_total // cores
    dest_count = req_count * cores
    slot_total = dest_count * CAPACITY
    dest_table = page_table // slot_count
    rank_table = rank_in_dest(dest_table)
    own_dests = lax.dynamic_index_in_dim(dest_table, my_req, 0, keepdims=False)
    own_ranks = lax.dynamic_index_in_dim(rank_table, my_req, 0, keepdims=False)
    send_slots = (own_dests * CAPACITY + own_ranks).astype(jnp.int32)
    send = pack_pages(send_slots, prev_keys, prev_values, new_keys, new_values, slot_total)
    received = lax.all_to_all(send, ("req", "core"), 0, 0, tiled=True)
    received = received.reshape(dest_count, CAPACITY, 2, PAGE, local_width)
    my_dest = my_req * cores + my_core
    wanted = my_dest * slot_count + jnp.arange(slot_count, dtype=jnp.int32)
    flat_table = page_table.reshape(-1)
    found = jnp.argmax(flat_table[None, :] == wanted[:, None], axis=1).astype(jnp.int32)
    from_req = found // page_total
    from_rank = rank_table.reshape(-1)[found].astype(jnp.int32)

    keys_all = jnp.concatenate([prev_keys, new_keys], axis=0)
    values_all = jnp.concatenate([prev_values, new_values], axis=0)
    allowed = visible(earlier, owners, prev_count, token_count)
    heads_here = local_width // HD
    scores = jnp.einsum(
        "qhd,khd->hqk",
        queries.reshape(token_count, heads_here, HD),
        keys_all.reshape(-1, heads_here, HD),
        preferred_element_type=jnp.float32,
    ) * HD ** (-0.5)
    scores = jnp.where(allowed[None, :, :], scores, -1e30)
    row_peak = jnp.max(scores, axis=2, keepdims=True)
    weights = jnp.exp(scores - row_peak)
    totals = jnp.sum(weights, axis=2)
    prob_rows = weights.astype(jnp.bfloat16)
    mixture = jnp.einsum(
        "hqk,khd->qhd",
        prob_rows,
        values_all.reshape(-1, heads_here, HD),
        preferred_element_type=jnp.float32,
    )
    attended = (
        (mixture / totals.T[:, :, None]).astype(jnp.bfloat16).reshape(token_count, local_width)
    )
    projected = jnp.dot(attended, w_out, preferred_element_type=jnp.float32)
    summed = lax.psum_scatter(projected, ("y", "core"), scatter_dimension=1, tiled=True)
    layer_out = (tokens.astype(jnp.float32) + summed).astype(jnp.bfloat16)

    pool = place_pages(from_req, from_rank, received, slot_count, cores)
    return (layer_out, pool[:, None])


def solution(mesh):
    req_count, tp_count = mesh.devices.shape
    cores = tp_count // HG
    split_mesh = Mesh(mesh.devices.reshape(req_count, HG, cores), ("req", "y", "core"))
    tp = ("y", "core")
    placed = (
        P("req", tp),
        P(),
        P(None, tp),
        P(None, tp),
        P(None, tp),
        P(tp, None),
        P("req", tp),
        P("req", tp),
        P("req", None),
        P("req", None),
        P(),
    )
    return jax.shard_map(
        shards,
        mesh=split_mesh,
        in_specs=placed,
        out_specs=(P("req", tp), P("req", tp, None, None)),
        check_vma=False,
    )
```

time: 444 us -> 749 us (1.69)
  Pallas kernels: 0 us -> 434 us
  local copies, waits for them, and re-layouts: 139 us -> 14.5 us
  other arithmetic: 61.3 us -> 39.8 us
  blocking collectives: 14.9 us -> 33.9 us
    pallas_call x0 -> x2, Pallas kernels: none -> 434 us  [the longest x1 217 us: place_pages(): pl.pallas_call(body, out_shape=jax.ShapeDtypeStruct((slot_count, PAGE, 2...]
    scatter x3 -> x0, local copies, waits for them, and re-layouts: 59.9 us -> none  [the longest x1 36.8 us: fill_pool(): return empty.at[slot_ids].set(page_rows)[:slot_count][:, None]]
    unnamed x0 -> x2, blocking collectives: none -> 33.9 us
    all_to_all x2 -> x1, waiting for transfers between devices: 133 us -> 157 us  [shards(): received = lax.all_to_all(send, ('req', 'core'), 0, 0, tiled=True)]
    all_gather x1, waiting for transfers between devices: 18.6 us -> 0.01 us  [shards(): full_tokens = lax.all_gather(tokens, ('y', 'core'), axis=1, tiled=True)]
    select_n x2 -> x1, local copies, waits for them, and re-layouts: 17.3 us -> 0.09 us  [shards(): dest_table = page_table // slot_count]
    reshape x2 -> x1, local copies, waits for them, and re-layouts: 16.7 us -> 0.08 us  [shards(): from_rank = rank_table.reshape(-1)[found].astype(jnp.int32)]
    psum x1 -> x0, blocking collectives: 14.9 us -> none  [shards(): square_sums = lax.psum(jnp.sum(widened * widened, axis=1), 'tp')]
  transfers between devices with their start and end apart: 5 -> 3, of which waited for: 3 -> 1; matrix products, arithmetic and copies ran while one was open for 19% -> 2% of each run, Pallas kernels for 0% -> 58%
where the time goes in v1:
time: 749 us; the launch traced here: 748 us
  Pallas kernels  434 us (58%)
  waiting for transfers between devices  158 us (21%)
  matrix products  48.6 us (6%)
  other arithmetic  39.8 us (5%)
  blocking collectives  33.9 us (5%)
  local copies, waits for them, and re-layouts  14.5 us (2%)
  between operations  14.3 us (2%)
    pallas_call x1, Pallas kernels, place_pages(): pl.pallas_call(body, out_shape=jax.ShapeDtypeStruct((slot_count, PAGE, 2...  217 us
    pallas_call x1, Pallas kernels, pack_pages(): pl.pallas_call(body, out_shape=jax.ShapeDtypeStruct((slot_total, 2, PAGE,...  217 us
    all_to_all x1, waiting for transfers between devices, shards(): received = lax.all_to_all(send, ('req', 'core'), 0, 0, tiled=True)  157 us
    unnamed x2, blocking collectives  33.9 us
    dot_general x1, matrix products, shards(): jnp.einsum('qhd,khd->hqk', queries.reshape(token_count, heads_here, HD),...  18.2 us
    reduce_sum x1, other arithmetic, shards(): totals = jnp.sum(weights, axis=2)  17.7 us
    dot_general x1, matrix products, shards(): jnp.einsum('hqk,khd->qhd', prob_rows, values_all.reshape(-1, heads_here,...  15.3 us
  transfers between devices with their start and end apart: 3, of which 1 were waited for; matrix products, arithmetic and copies ran while one was open for 2% of the time, Pallas kernels for 58%

profile of v1, /device:TPU:0, one launch (start us, length us, event | category | flops | bytes accessed | tf_op | source)
XLA Modules:
  0.0 748.5 jit_solution(8145132581438531699)
XLA Ops:
  8.6 12.1 %all-gather.2 = bf16[8,1,384]{2,1,0:T(2,128)(2,1)S(1)} all-gather(bf16[1,1,384]{2,1,0:T(2,128)(2,1)S(1)} %reshape.183), channel_id=2, replica_groups=mesh['req'=16,'y'=4,'core'=2] {'y','core'}, dimensions={0}, use_global_device_ids=true | all-gather | bytes 6912 | tf_op args[1]
  20.7 0.8 reduce-window.13
  22.4 21.9 %all-gather.3 = s32[16,1,36]{2,1,0:T(1,128)S(1)} all-gather(s32[1,1,36]{2,1,0:T(1,128)} %bitcast.62), channel_id=3, replica_groups=mesh['req'=16,'y'=4,'core'=2] {'req'}, dimensions={0}, use_global_device_ids=true | all-gather | bytes 2448 | tf_op args[10]
  46.5 1.3 broadcast_compare_fusion
  47.8 1.8 pad_add_fusion
  49.6 2.6 fusion.6
  52.2 4.3 fusion.30
  56.6 1.6 fusion.32
  58.2 1.0 subtract_convert_fusion.1
  59.5 4.2 pad_maximum_fusion.1
  63.7 5.8 copy.57
  69.4 4.6 convolution_convert_fusion.nv
  74.1 2.1 pad_maximum_fusion
  76.2 5.8 copy.55
  82.0 18.2 %fusion = (f32[4,512]{1,0:T(4,128)S(1)}, f32[4,512,4608]{2,1,0:T(8,128)}) fusion(pred[512,4608]{1,0:T(8,128)(4,1)} %pad_add_fusion, bf16[4608,4,96]{0,2,1:T(8,128)(2,1)} %bitcast.49, bf16[512,4,48]{0,2,1:T(8,128)(2,1)} %get-tuple-element.19, bf16[512,4,48]{0,2,1:T(8,128)(2,1)} %get-tuple-element.18), kind=kOutput, calls=%fused_computation.3 | convolution fusion | flops 1841035264 | bytes 44048384 | tf_op jit(solution)/shard_map/qhd,khd->hqk/dot_general | solution.py:204
  100.2 17.7 %fusion.1 = f32[4,512]{1,0:T(4,128)S(1)} fusion(f32[4,512,4608]{2,1,0:T(8,128)} %get-tuple-element.29, f32[4,512]{1,0:T(4,128)S(1)} %get-tuple-element.28, pred[512,4608]{1,0:T(8,128)(4,1)S(1)} %copy-done.2), kind=kLoop, calls=%fused_computation.4 | loop fusion | flops 37746688 | bytes 40124416 | tf_op jit(solution)/shard_map/reduce_sum | solution.py:213
  117.9 15.3 %fusion.15 = bf16[512,4,96]{0,2,1:T(8,128)(2,1)S(1)} fusion(bf16[4608,4,96]{0,2,1:T(8,128)(2,1)S(1)} %bitcast.50, f32[4,512,4608]{2,1,0:T(8,128)} %get-tuple-element.29, f32[4,512]{1,0:T(4,128)S(1)} %get-tuple-element.28, pred[512,4608]{1,0:T(8,128)(4,1)S(1)} %copy-done.2, f32[512,4]{0,1:T(4,128)S(1)} %bitcast.59), kind=kOutput, calls=%fused_computation.20 | convolution fusion | flops 1850081280 | bytes 44056576 | tf_op jit(solution)/shard_map/hqk,khd->qhd/dot_general | solution.py:215
  133.3 4.6 fusion.35
  139.4 216.8 %shard_map.122 = bf16[64,2,128,384]{3,2,1,0:T(8,128)(2,1)} custom-call(s32[36]{0:T(128)} %add_bitcast_fusion.slot_ref, bf16[4096,384]{1,0:T(8,128)(2,1)} %pk.1, bf16[4096,384]{1,0:T(8,128)(2,1)} %pv.1, bf16[512,384]{1,0:T(8,128)(2,1)} %copy-done.4, bf16[512,384]{1,0:T(8,128)(2,1)} %copy-done.7), custom_call_target="tpu_custom_call" | custom-call | tf_op jit(solution)/shard_map/pallas_call | solution.py:95
  356.2 5.7 all-to-all-start
  364.5 1.2 gather_fusion
  365.7 157.0 %all-to-all-done = bf16[64,2,128,384]{3,2,1,0:T(8,128)(2,1)} async-done(((bf16[64,2,128,384]{3,2,1,0:T(8,128)(2,1)}), bf16[64,2,128,384]{3,2,1,0:T(8,128)(2,1)}, u32[]{:S(2)}, u32[]{:S(2)}) %all-to-all-start) | async-done | bytes 12582944 | tf_op jit(solution)/shard_map/all_to_all | solution.py:191
  522.7 217.0 %shard_map.123 = bf16[18,128,1536]{2,1,0:T(8,128)(2,1)} custom-call(s32[18]{0:T(128)} %get-tuple-element.27.src_ref, s32[18]{0:T(128)} %gather_fusion, bf16[32,2,2,128,384]{4,3,2,1,0:T(8,128)(2,1)} %bitcast.23.got), custom_call_target="tpu_custom_call" | custom-call | tf_op jit(solution)/shard_map/pallas_call | solution.py:128
  739.7 2.0 add_convert_fusion
  (52 shorter events, 8.9 us)
Async XLA Ops:
  7.2 126.1 %copy-start = (bf16[384,3072]{1,0:T(8,128)(2,1)S(1)}, bf16[384,3072]{1,0:T(8,128)(2,1)}, u32[]{:S(2)}) copy-start(bf16[384,3072]{1,0:T(8,128)(2,1)} %param.16) | copy-start | bytes 7077892
  7.2 42.5 %all-gather.6.cloned.1.call-start = ((), (), s32[]{:S(2)}) async-start(), calls=%async_computation.2 | async-start | bytes 3538944 | tf_op jit(solution)/shard_map/all_gather | solution.py:162
  7.9 731.8 %reduce-scatter.2.cloned.1.call-start = ((), (), s32[]{:S(2)}) async-start(), calls=%async_computation.3 | async-start | bytes 7077888 | tf_op jit(solution)/shard_map/reduce_scatter | solution.py:225
  52.2 4.4 copy-start.5
  52.2 4.4 copy-start.8
  59.5 4.2 copy-start.4
  69.4 4.6 copy-start.1
  74.1 2.2 copy-start.7
  82.0 18.2 %copy-start.2 = (pred[512,4608]{1,0:T(8,128)(4,1)S(1)}, pred[512,4608]{1,0:T(8,128)(4,1)}, u32[]{:S(2)}) copy-start(pred[512,4608]{1,0:T(8,128)(4,1)} %pad_add_fusion) | copy-start | bytes 7077892
  100.2 17.7 %copy-start.3 = (bf16[4608,384]{0,1:T(8,128)(2,1)S(1)}, bf16[4608,384]{0,1:T(8,128)(2,1)}, u32[]{:S(2)}) copy-start(bf16[4608,384]{0,1:T(8,128)(2,1)} %copy.55) | copy-start | bytes 10616836
  356.2 166.5 %all-to-all-start = ((bf16[64,2,128,384]{3,2,1,0:T(8,128)(2,1)}), bf16[64,2,128,384]{3,2,1,0:T(8,128)(2,1)}, u32[]{:S(2)}, u32[]{:S(2)}) async-start(bf16[64,2,128,384]{3,2,1,0:T(8,128)(2,1)} %shard_map.122), calls=%async_computation.1 | async-start | bytes 25165824 | tf_op jit(solution)/shard_map/all_to_all | solution.py:191
  522.7 217.0 %copy-start.6 = (bf16[512,384]{1,0:T(8,128)(2,1)S(1)}, bf16[512,384]{1,0:T(8,128)(2,1)}, u32[]{:S(2)}) copy-start(bf16[512,384]{1,0:T(8,128)(2,1)} %param.11) | copy-start | bytes 1179652
Sparse Core Ops, SparseCore 0:
  9.7 30.1 all-gather.5
  138.0 41.0 reduce-scatter.1

commit v2 on v1

--- a/solution.py
+++ b/solution.py
@@ -68,74 +68,56 @@
     return jnp.sum(same * earlier_mask, axis=-1)
 
 
-def pack_pages(slots, prev_keys, prev_values, new_keys, new_values, slot_total):
-    prev_pages = prev_keys.shape[0] // PAGE
-    new_pages = new_keys.shape[0] // PAGE
-    width = prev_keys.shape[1]
-    sources = ((prev_keys, prev_values, prev_pages), (new_keys, new_values, new_pages))
-
-    def body(slot_ref, pk, pv, nk, nv, out, sems):
-        refs = ((pk, pv), (nk, nv))
-        copies = []
-        page = 0
-        for which, (_, _, pages) in enumerate(sources):
-            for local in range(pages):
-                for kv in range(2):
-                    src = refs[which][kv].at[pl.ds(local * PAGE, PAGE), :]
-                    copy = pltpu.make_async_copy(
-                        src, out.at[slot_ref[page], kv], sems.at[2 * page + kv]
-                    )
-                    copy.start()
-                    copies.append(copy)
-                page += 1
-        for copy in copies:
-            copy.wait()
-
-    page_total = prev_pages + new_pages
+def pack_pages(slots, keys_all, values_all, slot_total):
+    page_total = keys_all.shape[0] // PAGE
+    width = keys_all.shape[1]
+
+    def body(slot_ref, key_block, value_block, out):
+        out[0, 0] = key_block[...]
+        out[0, 1] = value_block[...]
+
     return pl.pallas_call(
         body,
         out_shape=jax.ShapeDtypeStruct((slot_total, 2, PAGE, width), jnp.bfloat16),
         grid_spec=pltpu.PrefetchScalarGridSpec(
             num_scalar_prefetch=1,
-            grid=(1,),
-            in_specs=[pl.BlockSpec(memory_space=pl.ANY)] * 4,
-            out_specs=pl.BlockSpec(memory_space=pl.ANY),
-            scratch_shapes=[pltpu.SemaphoreType.DMA((2 * page_total,))],
+            grid=(page_total,),
+            in_specs=[
+                pl.BlockSpec((PAGE, width), lambda page, slot_ref: (page, 0)),
+                pl.BlockSpec((PAGE, width), lambda page, slot_ref: (page, 0)),
+            ],
+            out_specs=pl.BlockSpec(
+                (1, 2, PAGE, width), lambda page, slot_ref: (slot_ref[page], 0, 0, 0)
+            ),
         ),
-    )(slots, prev_keys, prev_values, new_keys, new_values)
+    )(slots, keys_all, values_all)
 
 
 def place_pages(sources, ranks, received, slot_count, cores):
     width = received.shape[-1]
-
-    def body(src_ref, rank_ref, got, out, sems):
-        copies = []
-        for slot in range(slot_count):
-            for core in range(cores):
-                for kv in range(2):
-                    column = (kv * cores + core) * width
-                    index = (slot * cores + core) * 2 + kv
-                    copy = pltpu.make_async_copy(
-                        got.at[src_ref[slot] * cores + core, rank_ref[slot], kv],
-                        out.at[slot, :, pl.ds(column, width)],
-                        sems.at[index],
-                    )
-                    copy.start()
-                    copies.append(copy)
-        for copy in copies:
-            copy.wait()
+    shaped = received.reshape(-1, cores, CAPACITY, 2, PAGE, width)
+
+    def body(src_ref, rank_ref, got, out):
+        for core in range(cores):
+            for kv in range(2):
+                column = (kv * cores + core) * width
+                out[0, :, column : column + width] = got[0, core, 0, kv]
 
     return pl.pallas_call(
         body,
         out_shape=jax.ShapeDtypeStruct((slot_count, PAGE, 2 * cores * width), jnp.bfloat16),
         grid_spec=pltpu.PrefetchScalarGridSpec(
             num_scalar_prefetch=2,
-            grid=(1,),
-            in_specs=[pl.BlockSpec(memory_space=pl.ANY)],
-            out_specs=pl.BlockSpec(memory_space=pl.ANY),
-            scratch_shapes=[pltpu.SemaphoreType.DMA((slot_count * cores * 2,))],
+            grid=(slot_count,),
+            in_specs=[
+                pl.BlockSpec(
+                    (1, cores, 1, 2, PAGE, width),
+                    lambda slot, src_ref, rank_ref: (src_ref[slot], 0, rank_ref[slot], 0, 0, 0),
+                )
+            ],
+            out_specs=pl.BlockSpec((1, PAGE, 2 * cores * width), lambda slot, src_ref, rank_ref: (slot, 0, 0)),
         ),
-    )(sources, ranks, received)
+    )(sources, ranks, shaped)
 
 
 def shards(
@@ -187,7 +169,12 @@
     own_dests = lax.dynamic_index_in_dim(dest_table, my_req, 0, keepdims=False)
     own_ranks = lax.dynamic_index_in_dim(rank_table, my_req, 0, keepdims=False)
     send_slots = (own_dests * CAPACITY + own_ranks).astype(jnp.int32)
-    send = pack_pages(send_slots, prev_keys, prev_values, new_keys, new_values, slot_total)
+    keys_all = jnp.concatenate([prev_keys, new_keys], axis=0)
+    values_all = jnp.concatenate([prev_values, new_values], axis=0)
+    send = pack_pages(send_slots, keys_all, values_all, slot_total)
+    send, queries, keys_all, values_all = lax.optimization_barrier(
+        (send, queries, keys_all, values_all)
+    )
     received = lax.all_to_all(send, ("req", "core"), 0, 0, tiled=True)
     received = received.reshape(dest_count, CAPACITY, 2, PAGE, local_width)
     my_dest = my_req * cores + my_core
@@ -197,8 +184,6 @@
     from_req = found // page_total
     from_rank = rank_table.reshape(-1)[found].astype(jnp.int32)
 
-    keys_all = jnp.concatenate([prev_keys, new_keys], axis=0)
-    values_all = jnp.concatenate([prev_values, new_values], axis=0)
     allowed = visible(earlier, owners, prev_count, token_count)
     heads_here = local_width // HD
     scores = jnp.einsum(
@@ -222,6 +207,7 @@
         (mixture / totals.T[:, :, None]).astype(jnp.bfloat16).reshape(token_count, local_width)
     )
     projected = jnp.dot(attended, w_out, preferred_element_type=jnp.float32)
+    received, projected = lax.optimization_barrier((received, projected))
     summed = lax.psum_scatter(projected, ("y", "core"), scatter_dimension=1, tiled=True)
     layer_out = (tokens.astype(jnp.float32) + summed).astype(jnp.bfloat16)
 

time: 749 us -> 302 us (0.40)
  Pallas kernels: 434 us -> 34.7 us
  waiting for transfers between devices: 158 us -> 111 us
    pallas_call x1, Pallas kernels: 217 us -> 13.1 us  [place_pages(): pl.pallas_call(body, out_shape=jax.ShapeDtypeStruct((slot_count, PAGE, 2...]
    pallas_call x1, Pallas kernels: 217 us -> 21.6 us  [pack_pages(): pl.pallas_call(body, out_shape=jax.ShapeDtypeStruct((slot_total, 2, PAGE,...]
    all_to_all x1, waiting for transfers between devices: 157 us -> 89.7 us  [shards(): received = lax.all_to_all(send, ('req', 'core'), 0, 0, tiled=True)]
    reduce_scatter x1, waiting for transfers between devices: 0.02 us -> 21.1 us  [shards(): lax.psum_scatter(projected, ('y', 'core'), scatter_dimension=1, tiled=True)]
    concatenate x2 -> x0, local copies, waits for them, and re-layouts: 11.5 us -> none  [the longest x1 5.79 us: shards(): keys_all = jnp.concatenate([prev_keys, new_keys], axis=0)]
    optimization_barrier x0 -> x2, local copies, waits for them, and re-layouts: none -> 11.5 us  [shards(): lax.optimization_barrier((send, queries, keys_all, values_all))]
  transfers between devices with their start and end apart: 3 -> 3, of which waited for: 1 -> 2; matrix products, arithmetic and copies ran while one was open for 2% -> 27% of each run, Pallas kernels for 58% -> 4%
where the time goes in v2:
time: 302 us; the launch traced here: 299 us
  waiting for transfers between devices  111 us (37%)
  matrix products  46.3 us (15%)
  other arithmetic  38 us (13%)
  Pallas kernels  34.7 us (11%)
  blocking collectives  33.9 us (11%)
  local copies, waits for them, and re-layouts  14.5 us (5%)
  between operations  14.3 us (5%)
  starting transfers between devices  6.06 us (2%)
    all_to_all x1, waiting for transfers between devices, shards(): received = lax.all_to_all(send, ('req', 'core'), 0, 0, tiled=True)  89.7 us
    unnamed x2, blocking collectives  33.9 us
    pallas_call x1, Pallas kernels, pack_pages(): pl.pallas_call(body, out_shape=jax.ShapeDtypeStruct((slot_total, 2, PAGE,...  21.6 us
    reduce_scatter x1, waiting for transfers between devices, shards(): lax.psum_scatter(projected, ('y', 'core'), scatter_dimension=1, tiled=True)  21.1 us
    dot_general x1, matrix products, shards(): jnp.einsum('qhd,khd->hqk', queries.reshape(token_count, heads_here, HD),...  18.7 us
    reduce_sum x1, other arithmetic, shards(): totals = jnp.sum(weights, axis=2)  17.5 us
    dot_general x1, matrix products, shards(): jnp.einsum('hqk,khd->qhd', prob_rows, values_all.reshape(-1, heads_here,...  15.3 us
    pallas_call x1, Pallas kernels, place_pages(): pl.pallas_call(body, out_shape=jax.ShapeDtypeStruct((slot_count, PAGE, 2...  13.1 us
  transfers between devices with their start and end apart: 3, of which 2 were waited for; matrix products, arithmetic and copies ran while one was open for 27% of the time, Pallas kernels for 4%

profile of v2, /device:TPU:0, one launch (start us, length us, event | category | flops | bytes accessed | tf_op | source)
XLA Modules:
  0.0 299.3 jit_solution(1147185552930408898)
XLA Ops:
  7.9 0.8 reduce-window.13
  9.4 12.1 %all-gather.3 = bf16[8,1,384]{2,1,0:T(2,128)(2,1)S(1)} all-gather(bf16[1,1,384]{2,1,0:T(2,128)(2,1)S(1)} %reshape.193), channel_id=2, replica_groups=mesh['req'=16,'y'=4,'core'=2] {'y','core'}, dimensions={0}, use_global_device_ids=true | all-gather | bytes 6912 | tf_op args[1]
  21.5 21.9 %all-gather.2 = s32[16,1,36]{2,1,0:T(1,128)S(1)} all-gather(s32[1,1,36]{2,1,0:T(1,128)} %bitcast.66), channel_id=3, replica_groups=mesh['req'=16,'y'=4,'core'=2] {'req'}, dimensions={0}, use_global_device_ids=true | all-gather | bytes 2448 | tf_op args[10]
  46.9 2.6 fusion.6
  49.5 4.3 %fusion.25 = f32[512,384]{0,1:T(8,128)S(1)} fusion(bf16[3072,384]{1,0:T(8,128)(2,1)} %param.13, bf16[512,3072]{1,0:T(8,128)(2,1)} %all-gather.6.cloned.1.call-done, f32[3072]{0:T(1024)S(1)} %bitcast.60, f32[512]{0:T(512)S(1)} %add_rsqrt_fusion), kind=kOutput, calls=%fused_computation.60 | convolution fusion | flops 1214251008 | bytes 6305792 | tf_op jit(solution)/shard_map/dot_general | solution.py:152
  53.9 1.6 fusion.28
  56.1 4.2 %pad_maximum_fusion.key_block = bf16[4608,384]{1,0:T(8,128)(2,1)} fusion(bf16[512,384]{1,0:T(8,128)(2,1)S(1)} %copy.60, bf16[4096,384]{1,0:T(8,128)(2,1)} %param.17), kind=kLoop, calls=%fused_computation.15 | loop fusion | flops 7077888 | bytes 7077888 | tf_op jit(solution)/shard_map/concatenate | solution.py:172
  60.2 1.8 convolution_convert_fusion
  62.1 2.1 pad_maximum_fusion.1.value_block
  64.3 21.6 %shard_map.122 = bf16[64,2,128,384]{3,2,1,0:T(8,128)(2,1)} custom-call(s32[36]{0:T(128)} %add_bitcast_fusion.slot_ref, bf16[4608,384]{1,0:T(8,128)(2,1)} %pad_maximum_fusion.key_block, bf16[4608,384]{1,0:T(8,128)(2,1)} %pad_maximum_fusion.1.value_block), custom_call_target="tpu_custom_call" | custom-call | tf_op jit(solution)/shard_map/pallas_call | solution.py:79
  85.9 5.8 %all-to-all-start = ((bf16[64,2,128,384]{3,2,1,0:T(8,128)(2,1)}), bf16[64,2,128,384]{3,2,1,0:T(8,128)(2,1)}, u32[]{:S(2)}, u32[]{:S(2)}) async-start(bf16[64,2,128,384]{3,2,1,0:T(8,128)(2,1)} %shard_map.122), calls=%async_computation | async-start | bytes 25165824 | tf_op jit(solution)/shard_map/all_to_all | solution.py:178
  92.4 1.3 broadcast_compare_fusion
  93.7 1.5 pad_add_fusion
  95.3 5.8 %copy.61 = bf16[4608,384]{0,1:T(8,128)(2,1)} copy(bf16[4608,384]{1,0:T(8,128)(2,1)} %pad_maximum_fusion.1.value_block) | data formatting | bytes 7077888 | tf_op jit(solution)/shard_map/optimization_barrier | solution.py:175
  101.0 5.7 %copy.62 = bf16[4608,384]{0,1:T(8,128)(2,1)} copy(bf16[4608,384]{1,0:T(8,128)(2,1)} %pad_maximum_fusion.key_block) | data formatting | bytes 7077888 | tf_op jit(solution)/shard_map/optimization_barrier | solution.py:175
  106.8 18.7 %fusion = (f32[4,512]{1,0:T(4,128)S(1)}, f32[4,512,4608]{2,1,0:T(8,128)}) fusion(pred[512,4608]{1,0:T(8,128)(4,1)} %pad_add_fusion, bf16[512,4,96]{0,2,1:T(8,128)(2,1)S(1)} %get-tuple-element.43, bf16[4608,4,96]{0,2,1:T(8,128)(2,1)} %bitcast.54), kind=kOutput, calls=%fused_computation.3 | convolution fusion | flops 1840248832 | bytes 44048384 | tf_op jit(solution)/shard_map/qhd,khd->hqk/dot_general | solution.py:189
  125.5 17.5 %fusion.1 = f32[4,512]{1,0:T(4,128)S(1)} fusion(f32[4,512,4608]{2,1,0:T(8,128)} %get-tuple-element.41, f32[4,512]{1,0:T(4,128)S(1)} %get-tuple-element.40, pred[512,4608]{1,0:T(8,128)(4,1)S(1)} %copy-done.1), kind=kLoop, calls=%fused_computation.4 | loop fusion | flops 37746688 | bytes 40124416 | tf_op jit(solution)/shard_map/reduce_sum | solution.py:198
  142.9 15.3 %fusion.15 = bf16[512,4,96]{0,2,1:T(8,128)(2,1)S(1)} fusion(bf16[4608,4,96]{0,2,1:T(8,128)(2,1)S(1)} %bitcast.53, f32[4,512,4608]{2,1,0:T(8,128)} %get-tuple-element.41, f32[4,512]{1,0:T(4,128)S(1)} %get-tuple-element.40, pred[512,4608]{1,0:T(8,128)(4,1)S(1)} %copy-done.1, f32[512,4]{0,1:T(4,128)S(1)} %bitcast.63), kind=kOutput, calls=%fused_computation.20 | convolution fusion | flops 1850081280 | bytes 44056576 | tf_op jit(solution)/shard_map/hqk,khd->qhd/dot_general | solution.py:200
  158.3 4.5 %fusion.30 = f32[512,3072]{1,0:T(8,128)} fusion(bf16[512,384]{0,1:T(8,128)(2,1)S(1)} %bitcast.58, bf16[384,3072]{1,0:T(8,128)(2,1)S(1)} %copy-done), kind=kOutput, calls=%fused_computation.62 | convolution fusion | flops 1207959552 | bytes 9043968 | tf_op jit(solution)/shard_map/dot_general | solution.py:209
  162.8 89.7 %all-to-all-done = bf16[64,2,128,384]{3,2,1,0:T(8,128)(2,1)} async-done(((bf16[64,2,128,384]{3,2,1,0:T(8,128)(2,1)}), bf16[64,2,128,384]{3,2,1,0:T(8,128)(2,1)}, u32[]{:S(2)}, u32[]{:S(2)}) %all-to-all-start) | async-done | bytes 12582944 | tf_op jit(solution)/shard_map/all_to_all | solution.py:178
  255.1 1.2 gather_fusion
  256.4 13.1 %shard_map.123 = bf16[18,128,1536]{2,1,0:T(8,128)(2,1)} custom-call(s32[18]{0:T(128)} %get-tuple-element.39.src_ref, s32[18]{0:T(128)} %gather_fusion, bf16[16,2,2,2,128,384]{5,4,3,2,1,0:T(8,128)(2,1)} %bitcast.26.got), custom_call_target="tpu_custom_call" | custom-call | tf_op jit(solution)/shard_map/pallas_call | solution.py:106
  269.5 21.1 %reduce-scatter.2.cloned.1.call-done = f32[512,384]{1,0:T(8,128)} async-done(((f32[512,3072]{1,0:T(8,128)}), f32[512,384]{1,0:T(8,128)}) %reduce-scatter.2.cloned.1.call-update) | async-done | bytes 786448 | tf_op jit(solution)/shard_map/reduce_scatter | solution.py:211
  290.5 1.9 add_convert_fusion
  (62 shorter events, 8.8 us)
Async XLA Ops:
  7.2 151.1 %copy-start = (bf16[384,3072]{1,0:T(8,128)(2,1)S(1)}, bf16[384,3072]{1,0:T(8,128)(2,1)}, u32[]{:S(2)}) copy-start(bf16[384,3072]{1,0:T(8,128)(2,1)} %param.16) | copy-start | bytes 7077892
  7.2 39.7 %all-gather.6.cloned.1.call-start = ((), (), s32[]{:S(2)}) async-start(), calls=%async_computation.2 | async-start | bytes 3538944 | tf_op jit(solution)/shard_map/all_gather | solution.py:144
  21.5 32.4 %copy-start.9 = (f32[8,1,384]{2,1,0:T(1,128)}, f32[8,1,384]{2,1,0:T(1,128)S(1)}, u32[]{:S(2)}) copy-start(f32[8,1,384]{2,1,0:T(1,128)S(1)} %convert_element_type.69) | copy-start | bytes 36868
  44.4 2.1 copy-start.7
  49.5 4.4 %copy-start.4 = (bf16[512,3072]{1,0:T(8,128)(2,1)S(1)}, bf16[512,3072]{1,0:T(8,128)(2,1)}, u32[]{:S(2)}) copy-start(bf16[512,3072]{1,0:T(8,128)(2,1)} %all-gather.6.cloned.1.call-done) | copy-start | bytes 9437188
  49.5 4.4 %copy-start.12 = (bf16[3072,384]{1,0:T(8,128)(2,1)S(1)}, bf16[3072,384]{1,0:T(8,128)(2,1)}, u32[]{:S(2)}) copy-start(bf16[3072,384]{1,0:T(8,128)(2,1)} %param.14) | copy-start | bytes 7077892
  56.0 4.2 %copy-start.5 = (bf16[512,3072]{1,0:T(8,128)(2,1)S(1)}, bf16[512,3072]{1,0:T(8,128)(2,1)}, u32[]{:S(2)}) copy-start(bf16[512,3072]{1,0:T(8,128)(2,1)} %all-gather.6.cloned.1.call-done) | copy-start | bytes 9437188
  56.0 4.2 %copy-start.10 = (f32[8,1,384]{2,1,0:T(1,128)S(1)}, f32[8,1,384]{2,1,0:T(1,128)}, u32[]{:S(2)}) copy-start(f32[8,1,384]{2,1,0:T(1,128)} %copy-done.9) | copy-start | bytes 36868
  56.1 4.2 %copy-start.13 = (bf16[3072,384]{1,0:T(8,128)(2,1)S(1)}, bf16[3072,384]{1,0:T(8,128)(2,1)}, u32[]{:S(2)}) copy-start(bf16[3072,384]{1,0:T(8,128)(2,1)} %param.15) | copy-start | bytes 7077892
  60.2 1.9 copy-start.3
  85.9 6.0 %copy-start.11 = (s32[1,4]{1,0:T(1,128)S(1)}, s32[1,4]{1,0:T(1,128)}, u32[]{:S(2)}) copy-start(s32[1,4]{1,0:T(1,128)} %param.19) | copy-start | bytes 52
  85.9 166.6 %all-to-all-start = ((bf16[64,2,128,384]{3,2,1,0:T(8,128)(2,1)}), bf16[64,2,128,384]{3,2,1,0:T(8,128)(2,1)}, u32[]{:S(2)}, u32[]{:S(2)}) async-start(bf16[64,2,128,384]{3,2,1,0:T(8,128)(2,1)} %shard_map.122), calls=%async_computation | async-start | bytes 25165824 | tf_op jit(solution)/shard_map/all_to_all | solution.py:178
  91.7 198.9 %reduce-scatter.2.cloned.1.call-start = ((), (), s32[]{:S(2)}) async-start(), calls=%async_computation.3 | async-start | bytes 7077888 | tf_op jit(solution)/shard_map/reduce_scatter | solution.py:211
  106.8 18.7 %copy-start.1 = (pred[512,4608]{1,0:T(8,128)(4,1)S(1)}, pred[512,4608]{1,0:T(8,128)(4,1)}, u32[]{:S(2)}) copy-start(pred[512,4608]{1,0:T(8,128)(4,1)} %pad_add_fusion) | copy-start | bytes 7077892
  125.4 17.5 %copy-start.2 = (bf16[4608,384]{0,1:T(8,128)(2,1)S(1)}, bf16[4608,384]{0,1:T(8,128)(2,1)}, u32[]{:S(2)}) copy-start(bf16[4608,384]{0,1:T(8,128)(2,1)} %copy.61) | copy-start | bytes 10616836
  162.8 89.7 %copy-start.8 = (s32[16,36]{1,0:T(8,128)S(1)}, s32[16,36]{1,0:T(8,128)}, u32[]{:S(2)}) copy-start(s32[16,36]{1,0:T(8,128)} %copy-done.7) | copy-start | bytes 6916
  256.3 34.2 %copy-start.6 = (bf16[512,384]{1,0:T(8,128)(2,1)S(1)}, bf16[512,384]{1,0:T(8,128)(2,1)}, u32[]{:S(2)}) copy-start(bf16[512,384]{1,0:T(8,128)(2,1)} %param.11) | copy-start | bytes 1179652
Sparse Core Ops, SparseCore 0:
  9.7 30.1 all-gather.5
  252.6 37.8 reduce-scatter.1

commit v3 on v2

--- a/solution.py
+++ b/solution.py
@@ -68,29 +68,38 @@
     return jnp.sum(same * earlier_mask, axis=-1)
 
 
-def pack_pages(slots, keys_all, values_all, slot_total):
-    page_total = keys_all.shape[0] // PAGE
-    width = keys_all.shape[1]
-
-    def body(slot_ref, key_block, value_block, out):
+def pack_pages(slots, keys, values, slot_total, into=None):
+    page_total = keys.shape[0] // PAGE
+    width = keys.shape[1]
+
+    def body(slot_ref, key_block, value_block, *rest):
+        out = rest[-1]
         out[0, 0] = key_block[...]
         out[0, 1] = value_block[...]
 
+    in_specs = [
+        pl.BlockSpec((PAGE, width), lambda page, slot_ref: (page, 0)),
+        pl.BlockSpec((PAGE, width), lambda page, slot_ref: (page, 0)),
+    ]
+    operands = [slots, keys, values]
+    aliases = {}
+    if into is not None:
+        in_specs.append(pl.BlockSpec(memory_space=pl.ANY))
+        operands.append(into)
+        aliases = {3: 0}
     return pl.pallas_call(
         body,
         out_shape=jax.ShapeDtypeStruct((slot_total, 2, PAGE, width), jnp.bfloat16),
         grid_spec=pltpu.PrefetchScalarGridSpec(
             num_scalar_prefetch=1,
             grid=(page_total,),
-            in_specs=[
-                pl.BlockSpec((PAGE, width), lambda page, slot_ref: (page, 0)),
-                pl.BlockSpec((PAGE, width), lambda page, slot_ref: (page, 0)),
-            ],
+            in_specs=in_specs,
             out_specs=pl.BlockSpec(
                 (1, 2, PAGE, width), lambda page, slot_ref: (slot_ref[page], 0, 0, 0)
             ),
         ),
-    )(slots, keys_all, values_all)
+        input_output_aliases=aliases,
+    )(*operands)
 
 
 def place_pages(sources, ranks, received, slot_count, cores):
@@ -141,10 +150,16 @@
     my_req = lax.axis_index("req")
     my_core = lax.axis_index("core")
 
-    full_tokens = lax.all_gather(tokens, ("y", "core"), axis=1, tiled=True)
+    spare = 16
+    riders = jnp.zeros((spare, local_width), tokens.dtype).at[0].set(norm_gain)
+    gathered = lax.all_gather(
+        jnp.concatenate([tokens, riders], axis=0), ("y", "core"), axis=1, tiled=True
+    )
+    full_tokens = gathered[:token_count]
+    full_gain = gathered[token_count]
     widened = full_tokens.astype(jnp.float32)
     mean_square = jnp.mean(widened * widened, axis=1, keepdims=True)
-    normed = (widened * lax.rsqrt(mean_square + EPSILON) * norm_gain.astype(jnp.float32)[None, :]).astype(
+    normed = (widened * lax.rsqrt(mean_square + EPSILON) * full_gain.astype(jnp.float32)[None, :]).astype(
         jnp.bfloat16
     )
     query_raw, key_raw, value_raw = tuple(
@@ -164,25 +179,28 @@
     slot_count = page_total // cores
     dest_count = req_count * cores
     slot_total = dest_count * CAPACITY
-    dest_table = page_table // slot_count
-    rank_table = rank_in_dest(dest_table)
-    own_dests = lax.dynamic_index_in_dim(dest_table, my_req, 0, keepdims=False)
-    own_ranks = lax.dynamic_index_in_dim(rank_table, my_req, 0, keepdims=False)
+    own_dests = page_table[0] // slot_count
+    own_ranks = rank_in_dest(own_dests)
     send_slots = (own_dests * CAPACITY + own_ranks).astype(jnp.int32)
+    prev_pages = prev_count // PAGE
+    send = pack_pages(send_slots[:prev_pages], prev_keys, prev_values, slot_total)
+    send = pack_pages(send_slots[prev_pages:], new_keys, new_values, slot_total, into=send)
     keys_all = jnp.concatenate([prev_keys, new_keys], axis=0)
     values_all = jnp.concatenate([prev_values, new_values], axis=0)
-    send = pack_pages(send_slots, keys_all, values_all, slot_total)
-    send, queries, keys_all, values_all = lax.optimization_barrier(
-        (send, queries, keys_all, values_all)
-    )
-    received = lax.all_to_all(send, ("req", "core"), 0, 0, tiled=True)
-    received = received.reshape(dest_count, CAPACITY, 2, PAGE, local_width)
+    whole_table = lax.all_gather(page_table, "req", axis=0, tiled=True)
+    dest_table = whole_table // slot_count
+    rank_table = rank_in_dest(dest_table)
     my_dest = my_req * cores + my_core
     wanted = my_dest * slot_count + jnp.arange(slot_count, dtype=jnp.int32)
-    flat_table = page_table.reshape(-1)
+    flat_table = whole_table.reshape(-1)
     found = jnp.argmax(flat_table[None, :] == wanted[:, None], axis=1).astype(jnp.int32)
     from_req = found // page_total
     from_rank = rank_table.reshape(-1)[found].astype(jnp.int32)
+    send, queries, keys_all, values_all, from_req, from_rank = lax.optimization_barrier(
+        (send, queries, keys_all, values_all, from_req, from_rank)
+    )
+    received = lax.all_to_all(send, ("req", "core"), 0, 0, tiled=True)
+    received = received.reshape(dest_count, CAPACITY, 2, PAGE, local_width)
 
     allowed = visible(earlier, owners, prev_count, token_count)
     heads_here = local_width // HD
@@ -222,7 +240,7 @@
     tp = ("y", "core")
     placed = (
         P("req", tp),
-        P(),
+        P(tp),
         P(None, tp),
         P(None, tp),
         P(None, tp),
@@ -231,7 +249,7 @@
         P("req", tp),
         P("req", None),
         P("req", None),
-        P(),
+        P("req", None),
     )
     return jax.shard_map(
         shards,

time: 302 us -> 311 us (1.030)
  waiting for transfers between devices: 111 us -> 129 us
  blocking collectives: 33.9 us -> 22 us
    unnamed x2 -> x0, blocking collectives: 33.9 us -> none
    all_gather x0 -> x1, blocking collectives: none -> 22 us  [shards(): whole_table = lax.all_gather(page_table, 'req', axis=0, tiled=True)]
    all_to_all x1, waiting for transfers between devices: 89.7 us -> 103 us  [shards(): received = lax.all_to_all(send, ('req', 'core'), 0, 0, tiled=True)]
    optimization_barrier x2 -> x0, local copies, waits for them, and re-layouts: 11.5 us -> none  [shards(): lax.optimization_barrier((send, queries, keys_all, values_all))]
    unnamed x30 -> x22, local copies, waits for them, and re-layouts: 1.29 us -> 9.43 us
    reduce_scatter x1, waiting for transfers between devices: 21.1 us -> 26 us  [shards(): lax.psum_scatter(projected, ('y', 'core'), scatter_dimension=1, tiled=True)]
    pallas_call x1 -> x2, Pallas kernels: 21.6 us -> 23.5 us  [pack_pages(): pl.pallas_call(body, out_shape=jax.ShapeDtypeStruct((slot_total, 2, PAGE,...]
  transfers between devices with their start and end apart: 3 -> 3, of which waited for: 2 -> 2; matrix products, arithmetic and copies ran while one was open for 27% -> 24% of each run, Pallas kernels for 4% -> 11%
where the time goes in v3:
time: 311 us; the launch traced here: 309 us
  waiting for transfers between devices  129 us (41%)
  matrix products  48.4 us (16%)
  other arithmetic  38.7 us (12%)
  Pallas kernels  36.7 us (12%)
  blocking collectives  22 us (7%)
  between operations  14.3 us (5%)
  local copies, waits for them, and re-layouts  14.1 us (5%)
  starting transfers between devices  5.88 us (2%)
    all_to_all x1, waiting for transfers between devices, shards(): received = lax.all_to_all(send, ('req', 'core'), 0, 0, tiled=True)  103 us
    reduce_scatter x1, waiting for transfers between devices, shards(): lax.psum_scatter(projected, ('y', 'core'), scatter_dimension=1, tiled=True)  26 us
    pallas_call x2, Pallas kernels, pack_pages(): pl.pallas_call(body, out_shape=jax.ShapeDtypeStruct((slot_total, 2, PAGE,...  23.5 us
    all_gather x1, blocking collectives, shards(): whole_table = lax.all_gather(page_table, 'req', axis=0, tiled=True)  22 us
    dot_general x1, matrix products, shards(): jnp.einsum('qhd,khd->hqk', queries.reshape(token_count, heads_here, HD),...  18.2 us
    reduce_sum x1, other arithmetic, shards(): totals = jnp.sum(weights, axis=2)  17.5 us
    dot_general x1, matrix products, shards(): jnp.einsum('hqk,khd->qhd', prob_rows, values_all.reshape(-1, heads_here,...  15.3 us
    pallas_call x1, Pallas kernels, place_pages(): pl.pallas_call(body, out_shape=jax.ShapeDtypeStruct((slot_count, PAGE, 2...  13.2 us
  transfers between devices with their start and end apart: 3, of which 2 were waited for; matrix products, arithmetic and copies ran while one was open for 24% of the time, Pallas kernels for 11%

profile of v3, /device:TPU:0, one launch (start us, length us, event | category | flops | bytes accessed | tf_op | source)
XLA Modules:
  0.0 309.0 jit_solution(5882150718924089663)
XLA Ops:
  8.1 1.8 fusion.20
  12.9 22.0 %all-gather = s32[16,1,36]{2,1,0:T(1,128)S(1)} all-gather(s32[1,1,36]{2,1,0:T(1,128)} %bitcast.73), channel_id=1, replica_groups=mesh['req'=16,'y'=4,'core'=2] {'req'}, dimensions={0}, use_global_device_ids=true | all-gather | bytes 2448 | tf_op jit(solution)/shard_map/all_gather | solution.py:190
  37.2 4.7 %copy.47 = bf16[4096,384]{0,1:T(8,128)(2,1)} copy(bf16[4096,384]{1,0:T(8,128)(2,1)} %key_block.1) | data formatting | bytes 6291456 | tf_op args[6]
  41.9 4.6 %copy.48 = bf16[4096,384]{0,1:T(8,128)(2,1)} copy(bf16[4096,384]{1,0:T(8,128)(2,1)} %value_block.1) | data formatting | bytes 6291456 | tf_op args[7]
  46.6 19.5 %shard_map.122.rest_0_ = bf16[64,2,128,384]{3,2,1,0:T(8,128)(2,1)} custom-call(s32[32]{0:T(128)} %bitcast.70, bf16[4096,384]{1,0:T(8,128)(2,1)} %key_block.1, bf16[4096,384]{1,0:T(8,128)(2,1)} %value_block.1), custom_call_target="tpu_custom_call" | custom-call | tf_op jit(solution)/shard_map/pallas_call | solution.py:90
  67.4 1.2 gather_fusion
  69.2 2.6 fusion.6
  72.6 4.4 %convolution_convert_fusion.value_block = bf16[512,384]{1,0:T(8,128)(2,1)S(1)} fusion(bf16[3072,384]{1,0:T(8,128)(2,1)} %param.17, f32[3072]{0:T(1024)S(1)} %bitcast.66, f32[512]{0:T(512)S(1)} %add_rsqrt_fusion, bf16[528,3072]{1,0:T(8,128)(2,1)} %all-gather.3.cloned.1.call-done), kind=kOutput, calls=%fused_computation.18 | convolution fusion | flops 1214447616 | bytes 5912576 | tf_op jit(solution)/shard_map/dot_general | solution.py:167
  77.3 4.3 %fusion.28 = f32[512,384]{0,1:T(8,128)S(1)} fusion(bf16[3072,384]{1,0:T(8,128)(2,1)} %param.15, f32[3072]{0:T(1024)S(1)} %bitcast.67, f32[512]{0:T(512)S(1)} %add_rsqrt_fusion, bf16[528,3072]{1,0:T(8,128)(2,1)} %all-gather.3.cloned.1.call-done), kind=kOutput, calls=%fused_computation.70 | convolution fusion | flops 1214251008 | bytes 6305792 | tf_op jit(solution)/shard_map/dot_general | solution.py:167
  81.7 1.6 fusion.31
  83.6 0.9 copy.46.key_block
  84.5 4.1 %pad_maximum_fusion = bf16[4608,384]{0,1:T(8,128)(2,1)} fusion(bf16[512,384]{0,1:T(8,128)(2,1)S(1)} %bitcast.61, bf16[4096,384]{0,1:T(8,128)(2,1)} %copy.47), kind=kLoop, calls=%fused_computation.15 | loop fusion | flops 7077888 | bytes 7077888 | tf_op jit(solution)/shard_map/concatenate | solution.py:188
  88.6 2.1 pad_maximum_fusion.1
  90.6 4.0 %shard_map.123 = bf16[64,2,128,384]{3,2,1,0:T(8,128)(2,1)} custom-call(s32[4]{0:T(128)} %slice.38.slot_ref, bf16[512,384]{1,0:T(8,128)(2,1)} %copy.46.key_block, bf16[512,384]{1,0:T(8,128)(2,1)} %copy-done.5, bf16[64,2,128,384]{3,2,1,0:T(8,128)(2,1)} %shard_map.122.rest_0_), custom_call_target="tpu_custom_call", output_to_operand_aliasing={{}: (3, {})} | custom-call | tf_op jit(solution)/shard_map/pallas_call | solution.py:90
  94.6 5.6 %all-to-all-start = ((bf16[64,2,128,384]{3,2,1,0:T(8,128)(2,1)}), bf16[64,2,128,384]{3,2,1,0:T(8,128)(2,1)}, u32[]{:S(2)}, u32[]{:S(2)}) async-start(bf16[64,2,128,384]{3,2,1,0:T(8,128)(2,1)} %shard_map.123), calls=%async_computation | async-start | bytes 25165824 | tf_op jit(solution)/shard_map/all_to_all | solution.py:202
  101.0 1.3 broadcast_compare_fusion
  102.5 18.2 %fusion = (f32[4,512]{1,0:T(4,128)S(1)}, f32[4,512,4608]{2,1,0:T(8,128)}) fusion(pred[512,4608]{1,0:T(8,128)(4,1)S(1)} %pad_add_fusion, bf16[512,4,96]{0,2,1:T(8,128)(2,1)S(1)} %get-tuple-element.59, bf16[4608,4,96]{0,2,1:T(8,128)(2,1)} %bitcast.59), kind=kOutput, calls=%fused_computation.3 | convolution fusion | flops 1840248832 | bytes 44048384 | tf_op jit(solution)/shard_map/qhd,khd->hqk/dot_general | solution.py:207
  120.7 17.5 %fusion.1 = f32[4,512]{1,0:T(4,128)S(1)} fusion(f32[4,512,4608]{2,1,0:T(8,128)} %get-tuple-element.57, f32[4,512]{1,0:T(4,128)S(1)} %get-tuple-element.56, pred[512,4608]{1,0:T(8,128)(4,1)S(1)} %pad_add_fusion), kind=kLoop, calls=%fused_computation.4 | loop fusion | flops 37746688 | bytes 40124416 | tf_op jit(solution)/shard_map/reduce_sum | solution.py:216
  138.2 15.3 %fusion.15 = bf16[512,4,96]{0,2,1:T(8,128)(2,1)S(1)} fusion(bf16[4608,4,96]{0,2,1:T(8,128)(2,1)S(1)} %bitcast.58, f32[4,512,4608]{2,1,0:T(8,128)} %get-tuple-element.57, f32[4,512]{1,0:T(4,128)S(1)} %get-tuple-element.56, pred[512,4608]{1,0:T(8,128)(4,1)S(1)} %pad_add_fusion, f32[512,4]{0,1:T(4,128)S(1)} %bitcast.69), kind=kOutput, calls=%fused_computation.20 | convolution fusion | flops 1850081280 | bytes 44056576 | tf_op jit(solution)/shard_map/hqk,khd->qhd/dot_general | solution.py:218
  153.6 4.5 %fusion.33 = f32[512,3072]{1,0:T(8,128)} fusion(bf16[512,384]{0,1:T(8,128)(2,1)S(1)} %bitcast.64, bf16[384,3072]{1,0:T(8,128)(2,1)S(1)} %copy-done), kind=kOutput, calls=%fused_computation.72 | convolution fusion | flops 1207959552 | bytes 9043968 | tf_op jit(solution)/shard_map/dot_general | solution.py:227
  158.1 103.0 %all-to-all-done = bf16[64,2,128,384]{3,2,1,0:T(8,128)(2,1)} async-done(((bf16[64,2,128,384]{3,2,1,0:T(8,128)(2,1)}), bf16[64,2,128,384]{3,2,1,0:T(8,128)(2,1)}, u32[]{:S(2)}, u32[]{:S(2)}) %all-to-all-start) | async-done | bytes 12582944 | tf_op jit(solution)/shard_map/all_to_all | solution.py:202
  261.1 13.2 %shard_map.124 = bf16[18,128,1536]{2,1,0:T(8,128)(2,1)} custom-call(s32[18]{0:T(128)} %get-tuple-element.29.src_ref, s32[18]{0:T(128)} %gather_fusion, bf16[16,2,2,2,128,384]{5,4,3,2,1,0:T(8,128)(2,1)} %bitcast.28.got), custom_call_target="tpu_custom_call" | custom-call | tf_op jit(solution)/shard_map/pallas_call | solution.py:115
  274.3 26.0 %reduce-scatter.2.cloned.1.call-done = f32[512,384]{1,0:T(8,128)} async-done(((f32[512,3072]{1,0:T(8,128)}), f32[512,384]{1,0:T(8,128)}) %reduce-scatter.2.cloned.1.call-update) | async-done | bytes 786448 | tf_op jit(solution)/shard_map/reduce_scatter | solution.py:229
  300.3 1.9 add_convert_fusion
  (60 shorter events, 10.4 us)
Async XLA Ops:
  7.2 146.4 %copy-start = (bf16[384,3072]{1,0:T(8,128)(2,1)S(1)}, bf16[384,3072]{1,0:T(8,128)(2,1)}, u32[]{:S(2)}) copy-start(bf16[384,3072]{1,0:T(8,128)(2,1)} %param.18) | copy-start | bytes 7077892
  7.2 62.0 %all-gather.3.cloned.1.call-start = ((), (), s32[]{:S(2)}) async-start(), calls=%async_computation.2 | async-start | bytes 3649536 | tf_op jit(solution)/shard_map/all_gather | solution.py:155
  11.4 35.2 %copy-start.6 = (s32[36]{0:T(128)}, s32[36]{0:T(128)S(1)}, u32[]{:S(2)}) copy-start(s32[36]{0:T(128)S(1)} %multiply_add_fusion) | copy-start | bytes 436
  46.6 22.1 %copy-start.9 = (s32[1,4]{1,0:T(1,128)S(1)}, s32[1,4]{1,0:T(1,128)}, u32[]{:S(2)}) copy-start(s32[1,4]{1,0:T(1,128)} %param.22) | copy-start | bytes 52
  46.6 22.1 %copy-start.7 = (s32[1,4]{1,0:T(1,128)S(1)}, s32[1,4]{1,0:T(1,128)}, u32[]{:S(2)}) copy-start(s32[1,4]{1,0:T(1,128)} %param.21) | copy-start | bytes 52
  77.1 4.6 %copy-start.5 = (bf16[512,384]{1,0:T(8,128)(2,1)}, bf16[512,384]{1,0:T(8,128)(2,1)S(1)}, u32[]{:S(2)}) copy-start(bf16[512,384]{1,0:T(8,128)(2,1)S(1)} %convolution_convert_fusion.value_block) | copy-start | bytes 1179652
  77.3 4.4 %copy-start.3 = (bf16[528,3072]{1,0:T(8,128)(2,1)S(1)}, bf16[528,3072]{1,0:T(8,128)(2,1)}, u32[]{:S(2)}) copy-start(bf16[528,3072]{1,0:T(8,128)(2,1)} %all-gather.3.cloned.1.call-done) | copy-start | bytes 9732100
  77.3 4.4 %copy-start.8 = (bf16[3072,384]{1,0:T(8,128)(2,1)S(1)}, bf16[3072,384]{1,0:T(8,128)(2,1)}, u32[]{:S(2)}) copy-start(bf16[3072,384]{1,0:T(8,128)(2,1)} %param.16) | copy-start | bytes 7077892
  84.5 4.1 %copy-start.1 = (bf16[4096,384]{0,1:T(8,128)(2,1)S(1)}, bf16[4096,384]{0,1:T(8,128)(2,1)}, u32[]{:S(2)}) copy-start(bf16[4096,384]{0,1:T(8,128)(2,1)} %copy.48) | copy-start | bytes 9437188
  94.6 166.5 %all-to-all-start = ((bf16[64,2,128,384]{3,2,1,0:T(8,128)(2,1)}), bf16[64,2,128,384]{3,2,1,0:T(8,128)(2,1)}, u32[]{:S(2)}, u32[]{:S(2)}) async-start(bf16[64,2,128,384]{3,2,1,0:T(8,128)(2,1)} %shard_map.123), calls=%async_computation | async-start | bytes 25165824 | tf_op jit(solution)/shard_map/all_to_all | solution.py:202
  100.2 200.0 %reduce-scatter.2.cloned.1.call-start = ((), (), s32[]{:S(2)}) async-start(), calls=%async_computation.3 | async-start | bytes 7077888 | tf_op jit(solution)/shard_map/reduce_scatter | solution.py:229
  120.7 17.5 %copy-start.2 = (bf16[4608,384]{0,1:T(8,128)(2,1)S(1)}, bf16[4608,384]{0,1:T(8,128)(2,1)}, u32[]{:S(2)}) copy-start(bf16[4608,384]{0,1:T(8,128)(2,1)} %pad_maximum_fusion.1) | copy-start | bytes 10616836
  261.1 39.2 %copy-start.4 = (bf16[512,384]{1,0:T(8,128)(2,1)S(1)}, bf16[512,384]{1,0:T(8,128)(2,1)}, u32[]{:S(2)}) copy-start(bf16[512,384]{1,0:T(8,128)(2,1)} %param.13) | copy-start | bytes 1179652
Sparse Core Ops, SparseCore 0:
  10.0 30.5 all-gather.2
  261.2 38.9 reduce-scatter.1

commit v4 on v3

--- a/solution.py
+++ b/solution.py
@@ -187,15 +187,17 @@
     send = pack_pages(send_slots[prev_pages:], new_keys, new_values, slot_total, into=send)
     keys_all = jnp.concatenate([prev_keys, new_keys], axis=0)
     values_all = jnp.concatenate([prev_values, new_values], axis=0)
-    whole_table = lax.all_gather(page_table, "req", axis=0, tiled=True)
-    dest_table = whole_table // slot_count
-    rank_table = rank_in_dest(dest_table)
-    my_dest = my_req * cores + my_core
-    wanted = my_dest * slot_count + jnp.arange(slot_count, dtype=jnp.int32)
-    flat_table = whole_table.reshape(-1)
-    found = jnp.argmax(flat_table[None, :] == wanted[:, None], axis=1).astype(jnp.int32)
-    from_req = found // page_total
-    from_rank = rank_table.reshape(-1)[found].astype(jnp.int32)
+    carried = (
+        jnp.full((slot_total,), slot_count, jnp.int32)
+        .at[send_slots]
+        .set((page_table[0] % slot_count).astype(jnp.int32))
+    )
+    carried = lax.all_to_all(carried, ("req", "core"), 0, 0, tiled=True)
+    carried = carried.reshape(req_count, cores, CAPACITY)[:, 0, :].reshape(-1)
+    wanted = jnp.arange(slot_count, dtype=jnp.int32)
+    found = jnp.argmax(carried[None, :] == wanted[:, None], axis=1).astype(jnp.int32)
+    from_req = found // CAPACITY
+    from_rank = found % CAPACITY
     send, queries, keys_all, values_all, from_req, from_rank = lax.optimization_barrier(
         (send, queries, keys_all, values_all, from_req, from_rank)
     )

time: 311 us -> 299 us (0.961)
  blocking collectives: 22 us -> 0 us
  starting transfers between devices: 5.88 us -> 16.3 us
    all_gather x1 -> x0, blocking collectives: 22 us -> none  [shards(): whole_table = lax.all_gather(page_table, 'req', axis=0, tiled=True)]
    all_to_all x0 -> x1, starting transfers between devices: none -> 8.25 us  [shards(): carried = lax.all_to_all(carried, ('req', 'core'), 0, 0, tiled=True)]
    unnamed x22 -> x20, local copies, waits for them, and re-layouts: 9.43 us -> 9.45 us
  transfers between devices with their start and end apart: 3 -> 4, of which waited for: 2 -> 2; matrix products, arithmetic and copies ran while one was open for 24% -> 25% of each run, Pallas kernels for 11% -> 11%
where the time goes in v4:
time: 299 us; the launch traced here: 297 us
  waiting for transfers between devices  129 us (43%)
  matrix products  48.4 us (16%)
  other arithmetic  39.2 us (13%)
  Pallas kernels  36.6 us (12%)
  starting transfers between devices  16.3 us (5%)
  between operations  14.3 us (5%)
  local copies, waits for them, and re-layouts  13.5 us (5%)
    all_to_all x1, waiting for transfers between devices, shards(): received = lax.all_to_all(send, ('req', 'core'), 0, 0, tiled=True)  103 us
    reduce_scatter x1, waiting for transfers between devices, shards(): lax.psum_scatter(projected, ('y', 'core'), scatter_dimension=1, tiled=True)  25.9 us
    pallas_call x2, Pallas kernels, pack_pages(): pl.pallas_call(body, out_shape=jax.ShapeDtypeStruct((slot_total, 2, PAGE,...  23.4 us
    dot_general x1, matrix products, shards(): jnp.einsum('qhd,khd->hqk', queries.reshape(token_count, heads_here, HD),...  18.2 us
    reduce_sum x1, other arithmetic, shards(): totals = jnp.sum(weights, axis=2)  17.5 us
    dot_general x1, matrix products, shards(): jnp.einsum('hqk,khd->qhd', prob_rows, values_all.reshape(-1, heads_here,...  15.3 us
    pallas_call x1, Pallas kernels, place_pages(): pl.pallas_call(body, out_shape=jax.ShapeDtypeStruct((slot_count, PAGE, 2...  13.2 us
    dot_general x3, matrix products, shards(): jnp.dot(normed, weight, preferred_element_type=jnp.float32)  10.4 us
  transfers between devices with their start and end apart: 4, of which 2 were waited for; matrix products, arithmetic and copies ran while one was open for 25% of the time, Pallas kernels for 11%

profile of v4, /device:TPU:0, one launch (start us, length us, event | category | flops | bytes accessed | tf_op | source)
XLA Modules:
  0.0 297.1 jit_solution(3579419826148484087)
XLA Ops:
  8.1 1.8 fusion.20
  13.5 8.2 %all-to-all-start = ((s32[32,2,1]{1,2,0:T(1,128)}), s32[32,2,1]{1,2,0:T(1,128)S(1)}, u32[]{:S(2)}, u32[]{:S(2)}) async-start(s32[32,2,1]{1,2,0:T(1,128)} %bitcast.18), calls=%async_computation | async-start | bytes 32768 | tf_op jit(solution)/shard_map/all_to_all | solution.py:195
  22.4 0.8 reduce-window.13
  25.2 4.7 %copy.40 = bf16[4096,384]{0,1:T(8,128)(2,1)} copy(bf16[4096,384]{1,0:T(8,128)(2,1)} %key_block.1) | data formatting | bytes 6291456 | tf_op args[6]
  29.9 4.7 %copy.41 = bf16[4096,384]{0,1:T(8,128)(2,1)} copy(bf16[4096,384]{1,0:T(8,128)(2,1)} %value_block.1) | data formatting | bytes 6291456 | tf_op args[7]
  34.6 19.4 %shard_map.122.rest_0_ = bf16[64,2,128,384]{3,2,1,0:T(8,128)(2,1)} custom-call(s32[32]{0:T(128)} %bitcast.86, bf16[4096,384]{1,0:T(8,128)(2,1)} %key_block.1, bf16[4096,384]{1,0:T(8,128)(2,1)} %value_block.1), custom_call_target="tpu_custom_call" | custom-call | tf_op jit(solution)/shard_map/pallas_call | solution.py:90
  55.3 2.6 fusion.6
  58.7 4.4 %convolution_convert_fusion.value_block = bf16[512,384]{1,0:T(8,128)(2,1)S(1)} fusion(bf16[3072,384]{1,0:T(8,128)(2,1)} %param.17, f32[3072]{0:T(1024)S(1)} %bitcast.82, f32[512]{0:T(512)S(1)} %add_rsqrt_fusion, bf16[528,3072]{1,0:T(8,128)(2,1)} %all-gather.2.cloned.1.call-done), kind=kOutput, calls=%fused_computation.18 | convolution fusion | flops 1214447616 | bytes 5912576 | tf_op jit(solution)/shard_map/dot_general | solution.py:167
  63.3 4.3 %fusion.31 = f32[512,384]{0,1:T(8,128)S(1)} fusion(bf16[3072,384]{1,0:T(8,128)(2,1)} %param.15, f32[3072]{0:T(1024)S(1)} %bitcast.83, f32[512]{0:T(512)S(1)} %add_rsqrt_fusion, bf16[528,3072]{1,0:T(8,128)(2,1)} %all-gather.2.cloned.1.call-done), kind=kOutput, calls=%fused_computation.76 | convolution fusion | flops 1214251008 | bytes 6305792 | tf_op jit(solution)/shard_map/dot_general | solution.py:167
  67.7 1.6 fusion.34
  69.6 0.9 copy.39.key_block
  70.6 4.1 %pad_maximum_fusion = bf16[4608,384]{0,1:T(8,128)(2,1)} fusion(bf16[512,384]{0,1:T(8,128)(2,1)S(1)} %bitcast.77, bf16[4096,384]{0,1:T(8,128)(2,1)} %copy.40), kind=kLoop, calls=%fused_computation.15 | loop fusion | flops 7077888 | bytes 7077888 | tf_op jit(solution)/shard_map/concatenate | solution.py:188
  74.6 2.1 pad_maximum_fusion.1
  76.7 4.0 %shard_map.123 = bf16[64,2,128,384]{3,2,1,0:T(8,128)(2,1)} custom-call(s32[4]{0:T(128)} %slice.41.slot_ref, bf16[512,384]{1,0:T(8,128)(2,1)} %copy.39.key_block, bf16[512,384]{1,0:T(8,128)(2,1)} %copy-done.5, bf16[64,2,128,384]{3,2,1,0:T(8,128)(2,1)} %shard_map.122.rest_0_), custom_call_target="tpu_custom_call", output_to_operand_aliasing={{}: (3, {})} | custom-call | tf_op jit(solution)/shard_map/pallas_call | solution.py:90
  80.6 7.7 %all-to-all-start.1 = ((bf16[64,2,128,384]{3,2,1,0:T(8,128)(2,1)}), bf16[64,2,128,384]{3,2,1,0:T(8,128)(2,1)}, u32[]{:S(2)}, u32[]{:S(2)}) async-start(bf16[64,2,128,384]{3,2,1,0:T(8,128)(2,1)} %shard_map.123), calls=%async_computation.1 | async-start | bytes 25165824 | tf_op jit(solution)/shard_map/all_to_all | solution.py:204
  89.1 1.3 broadcast_compare_fusion
  90.7 18.2 %fusion = (f32[4,512]{1,0:T(4,128)S(1)}, f32[4,512,4608]{2,1,0:T(8,128)}) fusion(pred[512,4608]{1,0:T(8,128)(4,1)S(1)} %pad_add_fusion, bf16[512,4,96]{0,2,1:T(8,128)(2,1)S(1)} %get-tuple-element.58, bf16[4608,4,96]{0,2,1:T(8,128)(2,1)} %bitcast.75), kind=kOutput, calls=%fused_computation.3 | convolution fusion | flops 1840248832 | bytes 44048384 | tf_op jit(solution)/shard_map/qhd,khd->hqk/dot_general | solution.py:209
  108.9 17.5 %fusion.1 = f32[4,512]{1,0:T(4,128)S(1)} fusion(f32[4,512,4608]{2,1,0:T(8,128)} %get-tuple-element.56, f32[4,512]{1,0:T(4,128)S(1)} %get-tuple-element.55, pred[512,4608]{1,0:T(8,128)(4,1)S(1)} %pad_add_fusion), kind=kLoop, calls=%fused_computation.4 | loop fusion | flops 37746688 | bytes 40124416 | tf_op jit(solution)/shard_map/reduce_sum | solution.py:218
  126.4 15.3 %fusion.15 = bf16[512,4,96]{0,2,1:T(8,128)(2,1)S(1)} fusion(bf16[4608,4,96]{0,2,1:T(8,128)(2,1)S(1)} %bitcast.74, f32[4,512,4608]{2,1,0:T(8,128)} %get-tuple-element.56, f32[4,512]{1,0:T(4,128)S(1)} %get-tuple-element.55, pred[512,4608]{1,0:T(8,128)(4,1)S(1)} %pad_add_fusion, f32[512,4]{0,1:T(4,128)S(1)} %bitcast.85), kind=kOutput, calls=%fused_computation.20 | convolution fusion | flops 1850081280 | bytes 44056576 | tf_op jit(solution)/shard_map/hqk,khd->qhd/dot_general | solution.py:220
  141.7 4.5 %fusion.36 = f32[512,3072]{1,0:T(8,128)} fusion(bf16[512,384]{0,1:T(8,128)(2,1)S(1)} %bitcast.80, bf16[384,3072]{1,0:T(8,128)(2,1)S(1)} %copy-done), kind=kOutput, calls=%fused_computation.78 | convolution fusion | flops 1207959552 | bytes 9043968 | tf_op jit(solution)/shard_map/dot_general | solution.py:229
  146.2 103.0 %all-to-all-done.1 = bf16[64,2,128,384]{3,2,1,0:T(8,128)(2,1)} async-done(((bf16[64,2,128,384]{3,2,1,0:T(8,128)(2,1)}), bf16[64,2,128,384]{3,2,1,0:T(8,128)(2,1)}, u32[]{:S(2)}, u32[]{:S(2)}) %all-to-all-start.1) | async-done | bytes 12582944 | tf_op jit(solution)/shard_map/all_to_all | solution.py:204
  249.3 13.2 %shard_map.124 = bf16[18,128,1536]{2,1,0:T(8,128)(2,1)} custom-call(s32[18]{0:T(128)} %get-tuple-element.29.src_ref, s32[18]{0:T(128)} %get-tuple-element.30.rank_ref, bf16[16,2,2,2,128,384]{5,4,3,2,1,0:T(8,128)(2,1)} %bitcast.29.got), custom_call_target="tpu_custom_call" | custom-call | tf_op jit(solution)/shard_map/pallas_call | solution.py:115
  262.4 25.9 %reduce-scatter.2.cloned.1.call-done = f32[512,384]{1,0:T(8,128)} async-done(((f32[512,3072]{1,0:T(8,128)}), f32[512,384]{1,0:T(8,128)}) %reduce-scatter.2.cloned.1.call-update) | async-done | bytes 786448 | tf_op jit(solution)/shard_map/reduce_scatter | solution.py:231
  288.4 1.9 add_convert_fusion
  (52 shorter events, 10.6 us)
Async XLA Ops:
  7.2 134.6 %copy-start = (bf16[384,3072]{1,0:T(8,128)(2,1)S(1)}, bf16[384,3072]{1,0:T(8,128)(2,1)}, u32[]{:S(2)}) copy-start(bf16[384,3072]{1,0:T(8,128)(2,1)} %param.18) | copy-start | bytes 7077892
  7.2 48.1 %all-gather.2.cloned.1.call-start = ((), (), s32[]{:S(2)}) async-start(), calls=%async_computation.3 | async-start | bytes 3649536 | tf_op jit(solution)/shard_map/all_gather | solution.py:155
  13.5 40.5 %all-to-all-start = ((s32[32,2,1]{1,2,0:T(1,128)}), s32[32,2,1]{1,2,0:T(1,128)S(1)}, u32[]{:S(2)}, u32[]{:S(2)}) async-start(s32[32,2,1]{1,2,0:T(1,128)} %bitcast.18), calls=%async_computation | async-start | bytes 32768 | tf_op jit(solution)/shard_map/all_to_all | solution.py:195
  21.7 12.8 %copy-start.6 = (s32[36]{0:T(128)}, s32[36]{0:T(128)S(1)}, u32[]{:S(2)}) copy-start(s32[36]{0:T(128)S(1)} %multiply_add_fusion) | copy-start | bytes 436
  63.1 4.6 %copy-start.5 = (bf16[512,384]{1,0:T(8,128)(2,1)}, bf16[512,384]{1,0:T(8,128)(2,1)S(1)}, u32[]{:S(2)}) copy-start(bf16[512,384]{1,0:T(8,128)(2,1)S(1)} %convolution_convert_fusion.value_block) | copy-start | bytes 1179652
  63.3 4.4 %copy-start.3 = (bf16[528,3072]{1,0:T(8,128)(2,1)S(1)}, bf16[528,3072]{1,0:T(8,128)(2,1)}, u32[]{:S(2)}) copy-start(bf16[528,3072]{1,0:T(8,128)(2,1)} %all-gather.2.cloned.1.call-done) | copy-start | bytes 9732100
  63.3 4.4 %copy-start.8 = (bf16[3072,384]{1,0:T(8,128)(2,1)S(1)}, bf16[3072,384]{1,0:T(8,128)(2,1)}, u32[]{:S(2)}) copy-start(bf16[3072,384]{1,0:T(8,128)(2,1)} %param.16) | copy-start | bytes 7077892
  70.6 4.1 %copy-start.1 = (bf16[4096,384]{0,1:T(8,128)(2,1)S(1)}, bf16[4096,384]{0,1:T(8,128)(2,1)}, u32[]{:S(2)}) copy-start(bf16[4096,384]{0,1:T(8,128)(2,1)} %copy.41) | copy-start | bytes 9437188
  80.6 8.0 %copy-start.7 = (s32[1,4]{1,0:T(1,128)S(1)}, s32[1,4]{1,0:T(1,128)}, u32[]{:S(2)}) copy-start(s32[1,4]{1,0:T(1,128)} %param.21) | copy-start | bytes 52
  80.6 168.6 %all-to-all-start.1 = ((bf16[64,2,128,384]{3,2,1,0:T(8,128)(2,1)}), bf16[64,2,128,384]{3,2,1,0:T(8,128)(2,1)}, u32[]{:S(2)}, u32[]{:S(2)}) async-start(bf16[64,2,128,384]{3,2,1,0:T(8,128)(2,1)} %shard_map.123), calls=%async_computation.1 | async-start | bytes 25165824 | tf_op jit(solution)/shard_map/all_to_all | solution.py:204
  88.4 200.0 %reduce-scatter.2.cloned.1.call-start = ((), (), s32[]{:S(2)}) async-start(), calls=%async_computation.4 | async-start | bytes 7077888 | tf_op jit(solution)/shard_map/reduce_scatter | solution.py:231
  108.9 17.5 %copy-start.2 = (bf16[4608,384]{0,1:T(8,128)(2,1)S(1)}, bf16[4608,384]{0,1:T(8,128)(2,1)}, u32[]{:S(2)}) copy-start(bf16[4608,384]{0,1:T(8,128)(2,1)} %pad_maximum_fusion.1) | copy-start | bytes 10616836
  249.3 39.1 %copy-start.4 = (bf16[512,384]{1,0:T(8,128)(2,1)S(1)}, bf16[512,384]{1,0:T(8,128)(2,1)}, u32[]{:S(2)}) copy-start(bf16[512,384]{1,0:T(8,128)(2,1)} %param.13) | copy-start | bytes 1179652
Sparse Core Ops, SparseCore 0:
  10.0 30.5 all-gather.1
  249.4 38.9 reduce-scatter.1

commit v5 on v4

--- a/solution.py
+++ b/solution.py
@@ -162,16 +162,15 @@
     normed = (widened * lax.rsqrt(mean_square + EPSILON) * full_gain.astype(jnp.float32)[None, :]).astype(
         jnp.bfloat16
     )
-    query_raw, key_raw, value_raw = tuple(
+    key_raw, value_raw = tuple(
         (
             jnp.dot(normed, weight, preferred_element_type=jnp.float32)
-            for weight in (w_query, w_key, w_value)
+            for weight in (w_key, w_value)
         )
     )
     earlier = earlier_lengths[0]
     fresh = new_lengths[0]
     owners, positions = block_layout(earlier, fresh, token_count)
-    queries = rotate(query_raw, positions, HD).astype(jnp.bfloat16)
     new_keys = rotate(key_raw, positions, HD).astype(jnp.bfloat16)
     new_values = value_raw.astype(jnp.bfloat16)
 
@@ -198,9 +197,11 @@
     found = jnp.argmax(carried[None, :] == wanted[:, None], axis=1).astype(jnp.int32)
     from_req = found // CAPACITY
     from_rank = found % CAPACITY
-    send, queries, keys_all, values_all, from_req, from_rank = lax.optimization_barrier(
-        (send, queries, keys_all, values_all, from_req, from_rank)
-    )
+    send, normed, keys_all, values_all, from_req, from_rank = lax.optimization_barrier(
+        (send, normed, keys_all, values_all, from_req, from_rank)
+    )
+    query_raw = jnp.dot(normed, w_query, preferred_element_type=jnp.float32)
+    queries = rotate(query_raw, positions, HD).astype(jnp.bfloat16)
     received = lax.all_to_all(send, ("req", "core"), 0, 0, tiled=True)
     received = received.reshape(dest_count, CAPACITY, 2, PAGE, local_width)
 

time: 299 us -> 299 us (level)
  matrix products: 48.4 us -> 45.3 us
    dot_general x3 -> x2, matrix products: 10.4 us -> 5.83 us  [shards(): jnp.dot(normed, weight, preferred_element_type=jnp.float32)]
    convert_element_type x0 -> x1, other arithmetic: none -> 3.05 us  [shards(): (widened * lax.rsqrt(mean_square + EPSILON) * full_gain.astype(jnp.float3...]
    unnamed x20 -> x30, local copies, waits for them, and re-layouts: 9.45 us -> 12 us
  transfers between devices with their start and end apart: 4 -> 4, of which waited for: 2 -> 2; matrix products, arithmetic and copies ran while one was open for 25% -> 26% of each run, Pallas kernels for 11% -> 11%
where the time goes in v5:
time: 299 us; the launch traced here: 296 us
  waiting for transfers between devices  127 us (42%)
  matrix products  45.3 us (15%)
  other arithmetic  41.5 us (14%)
  Pallas kernels  36.5 us (12%)
  local copies, waits for them, and re-layouts  16 us (5%)
  starting transfers between devices  16 us (5%)
  between operations  14.4 us (5%)
    all_to_all x1, waiting for transfers between devices, shards(): received = lax.all_to_all(send, ('req', 'core'), 0, 0, tiled=True)  101 us
    reduce_scatter x1, waiting for transfers between devices, shards(): lax.psum_scatter(projected, ('y', 'core'), scatter_dimension=1, tiled=True)  26 us
    pallas_call x2, Pallas kernels, pack_pages(): pl.pallas_call(body, out_shape=jax.ShapeDtypeStruct((slot_total, 2, PAGE,...  23.3 us
    dot_general x1, matrix products, shards(): jnp.einsum('qhd,khd->hqk', queries.reshape(token_count, heads_here, HD),...  18.2 us
    reduce_sum x1, other arithmetic, shards(): totals = jnp.sum(weights, axis=2)  17.5 us
    dot_general x1, matrix products, shards(): jnp.einsum('hqk,khd->qhd', prob_rows, values_all.reshape(-1, heads_here,...  15.3 us
    pallas_call x1, Pallas kernels, place_pages(): pl.pallas_call(body, out_shape=jax.ShapeDtypeStruct((slot_count, PAGE, 2...  13.2 us
    unnamed x30, local copies, waits for them, and re-layouts  12 us
  transfers between devices with their start and end apart: 4, of which 2 were waited for; matrix products, arithmetic and copies ran while one was open for 26% of the time, Pallas kernels for 11%

profile of v5, /device:TPU:0, one launch (start us, length us, event | category | flops | bytes accessed | tf_op | source)
XLA Modules:
  0.0 296.4 jit_solution(1891234836211913911)
XLA Ops:
  8.1 1.8 fusion.20
  13.5 8.2 %all-to-all-start = ((s32[32,2,1]{1,2,0:T(1,128)}), s32[32,2,1]{1,2,0:T(1,128)S(1)}, u32[]{:S(2)}, u32[]{:S(2)}) async-start(s32[32,2,1]{1,2,0:T(1,128)} %bitcast.16), calls=%async_computation | async-start | bytes 32768 | tf_op jit(solution)/shard_map/all_to_all | solution.py:194
  25.1 4.8 %copy.36 = bf16[4096,384]{0,1:T(8,128)(2,1)} copy(bf16[4096,384]{1,0:T(8,128)(2,1)} %key_block.1) | data formatting | bytes 6291456 | tf_op args[6]
  29.9 4.8 %copy.37 = bf16[4096,384]{0,1:T(8,128)(2,1)} copy(bf16[4096,384]{1,0:T(8,128)(2,1)} %value_block.1) | data formatting | bytes 6291456 | tf_op args[7]
  34.8 19.4 %shard_map.122.rest_0_ = bf16[64,2,128,384]{3,2,1,0:T(8,128)(2,1)} custom-call(s32[32]{0:T(128)} %bitcast.84, bf16[4096,384]{1,0:T(8,128)(2,1)} %key_block.1, bf16[4096,384]{1,0:T(8,128)(2,1)} %value_block.1), custom_call_target="tpu_custom_call" | custom-call | tf_op jit(solution)/shard_map/pallas_call | solution.py:90
  55.4 2.6 fusion.6
  58.0 1.0 slice_convert_fusion
  59.0 3.1 %fusion.8 = bf16[512,3072]{1,0:T(8,128)(2,1)S(1)} fusion(f32[3072]{0:T(1024)S(1)} %bitcast.81, f32[512]{0:T(512)S(1)} %add_rsqrt_fusion, bf16[528,3072]{1,0:T(8,128)(2,1)} %all-gather.2.cloned.1.call-done), kind=kLoop, calls=%fused_computation.13 | loop fusion | flops 6291456 | bytes 6305792 | tf_op jit(solution)/shard_map/convert_element_type | solution.py:162
  62.1 1.7 copy-done.2
  63.7 1.8 convolution_convert_fusion.value_block
  65.7 4.0 %fusion.36 = f32[512,384]{0,1:T(8,128)S(1)} fusion(bf16[512,3072]{1,0:T(8,128)(2,1)} %copy-done.2, bf16[3072,384]{1,0:T(8,128)(2,1)} %param.16), kind=kOutput, calls=%fused_computation.80 | convolution fusion | flops 1207959552 | bytes 6291456 | tf_op jit(solution)/shard_map/dot_general | solution.py:167
  70.9 5.1 %pad_maximum_fusion = (bf16[4608,384]{0,1:T(8,128)(2,1)}, bf16[4608,384]{0,1:T(8,128)(2,1)}) fusion(bf16[512,384]{0,1:T(8,128)(2,1)S(1)} %bitcast.75, bf16[4096,384]{0,1:T(8,128)(2,1)} %copy.36, bf16[512,384]{0,1:T(8,128)(2,1)S(1)} %copy.38, bf16[4096,384]{0,1:T(8,128)(2,1)} %copy.37), kind=kLoop, calls=%fused_computation.15 | loop fusion | flops 14155776 | bytes 14155776 | tf_op jit(solution)/shard_map/concatenate | solution.py:187
  76.0 3.9 %shard_map.123 = bf16[64,2,128,384]{3,2,1,0:T(8,128)(2,1)} custom-call(s32[4]{0:T(128)} %slice.41.slot_ref, bf16[512,384]{1,0:T(8,128)(2,1)} %copy.35.key_block, bf16[512,384]{1,0:T(8,128)(2,1)} %copy-done.5, bf16[64,2,128,384]{3,2,1,0:T(8,128)(2,1)} %shard_map.122.rest_0_), custom_call_target="tpu_custom_call", output_to_operand_aliasing={{}: (3, {})} | custom-call | tf_op jit(solution)/shard_map/pallas_call | solution.py:90
  79.9 7.6 %all-to-all-start.1 = ((bf16[64,2,128,384]{3,2,1,0:T(8,128)(2,1)}), bf16[64,2,128,384]{3,2,1,0:T(8,128)(2,1)}, u32[]{:S(2)}, u32[]{:S(2)}) async-start(bf16[64,2,128,384]{3,2,1,0:T(8,128)(2,1)} %shard_map.123), calls=%async_computation.1 | async-start | bytes 25165824 | tf_op jit(solution)/shard_map/all_to_all | solution.py:205
  88.2 1.3 broadcast_compare_fusion
  90.6 1.4 fusion.37
  92.2 18.2 %fusion = (f32[4,512]{1,0:T(4,128)S(1)}, f32[4,512,4608]{2,1,0:T(8,128)}) fusion(pred[512,4608]{1,0:T(8,128)(4,1)S(1)} %pad_add_fusion, bf16[4608,4,96]{0,2,1:T(8,128)(2,1)} %bitcast.77, bf16[512,4,48]{0,2,1:T(8,128)(2,1)S(1)} %get-tuple-element.45, bf16[512,4,48]{0,2,1:T(8,128)(2,1)S(1)} %get-tuple-element.44), kind=kOutput, calls=%fused_computation.3 | convolution fusion | flops 1841035264 | bytes 44048384 | tf_op jit(solution)/shard_map/qhd,khd->hqk/dot_general | solution.py:210
  110.4 17.5 %fusion.1 = f32[4,512]{1,0:T(4,128)S(1)} fusion(f32[4,512,4608]{2,1,0:T(8,128)} %get-tuple-element.54, f32[4,512]{1,0:T(4,128)S(1)} %get-tuple-element.53, pred[512,4608]{1,0:T(8,128)(4,1)S(1)} %pad_add_fusion), kind=kLoop, calls=%fused_computation.4 | loop fusion | flops 37746688 | bytes 40124416 | tf_op jit(solution)/shard_map/reduce_sum | solution.py:219
  127.9 15.3 %fusion.15 = bf16[512,4,96]{0,2,1:T(8,128)(2,1)S(1)} fusion(bf16[4608,4,96]{0,2,1:T(8,128)(2,1)S(1)} %bitcast.76, f32[4,512,4608]{2,1,0:T(8,128)} %get-tuple-element.54, f32[4,512]{1,0:T(4,128)S(1)} %get-tuple-element.53, pred[512,4608]{1,0:T(8,128)(4,1)S(1)} %pad_add_fusion, f32[512,4]{0,1:T(4,128)S(1)} %bitcast.83), kind=kOutput, calls=%fused_computation.20 | convolution fusion | flops 1850081280 | bytes 44056576 | tf_op jit(solution)/shard_map/hqk,khd->qhd/dot_general | solution.py:221
  143.2 4.5 %fusion.38 = f32[512,3072]{1,0:T(8,128)} fusion(bf16[512,384]{0,1:T(8,128)(2,1)S(1)} %bitcast.80, bf16[384,3072]{1,0:T(8,128)(2,1)S(1)} %copy-done), kind=kOutput, calls=%fused_computation.82 | convolution fusion | flops 1207959552 | bytes 9043968 | tf_op jit(solution)/shard_map/dot_general | solution.py:230
  147.7 100.7 %all-to-all-done.1 = bf16[64,2,128,384]{3,2,1,0:T(8,128)(2,1)} async-done(((bf16[64,2,128,384]{3,2,1,0:T(8,128)(2,1)}), bf16[64,2,128,384]{3,2,1,0:T(8,128)(2,1)}, u32[]{:S(2)}, u32[]{:S(2)}) %all-to-all-start.1) | async-done | bytes 12582944 | tf_op jit(solution)/shard_map/all_to_all | solution.py:205
  248.5 13.2 %shard_map.124 = bf16[18,128,1536]{2,1,0:T(8,128)(2,1)} custom-call(s32[18]{0:T(128)} %get-tuple-element.29.src_ref, s32[18]{0:T(128)} %get-tuple-element.30.rank_ref, bf16[16,2,2,2,128,384]{5,4,3,2,1,0:T(8,128)(2,1)} %bitcast.27.got), custom_call_target="tpu_custom_call" | custom-call | tf_op jit(solution)/shard_map/pallas_call | solution.py:115
  261.6 26.0 %reduce-scatter.2.cloned.1.call-done = f32[512,384]{1,0:T(8,128)} async-done(((f32[512,3072]{1,0:T(8,128)}), f32[512,384]{1,0:T(8,128)}) %reduce-scatter.2.cloned.1.call-update) | async-done | bytes 786448 | tf_op jit(solution)/shard_map/reduce_scatter | solution.py:232
  287.6 1.9 add_convert_fusion
  (63 shorter events, 12.2 us)
Async XLA Ops:
  7.2 136.0 %copy-start = (bf16[384,3072]{1,0:T(8,128)(2,1)S(1)}, bf16[384,3072]{1,0:T(8,128)(2,1)}, u32[]{:S(2)}) copy-start(bf16[384,3072]{1,0:T(8,128)(2,1)} %param.18) | copy-start | bytes 7077892
  7.2 48.3 %all-gather.2.cloned.1.call-start = ((), (), s32[]{:S(2)}) async-start(), calls=%async_computation.3 | async-start | bytes 3649536 | tf_op jit(solution)/shard_map/all_gather | solution.py:155
  13.5 40.7 %all-to-all-start = ((s32[32,2,1]{1,2,0:T(1,128)}), s32[32,2,1]{1,2,0:T(1,128)S(1)}, u32[]{:S(2)}, u32[]{:S(2)}) async-start(s32[32,2,1]{1,2,0:T(1,128)} %bitcast.16), calls=%async_computation | async-start | bytes 32768 | tf_op jit(solution)/shard_map/all_to_all | solution.py:194
  21.7 13.0 %copy-start.10 = (s32[36]{0:T(128)}, s32[36]{0:T(128)S(1)}, u32[]{:S(2)}) copy-start(s32[36]{0:T(128)S(1)} %multiply_add_fusion) | copy-start | bytes 436
  25.1 44.7 %copy-start.6 = (f32[512,48]{0,1:T(8,128)}, f32[512,48]{0,1:T(8,128)S(1)}, u32[]{:S(2)}) copy-start(f32[512,48]{0,1:T(8,128)S(1)} %get-tuple-element.48) | copy-start | bytes 294916
  25.1 44.7 %copy-start.8 = (f32[512,48]{0,1:T(8,128)}, f32[512,48]{0,1:T(8,128)S(1)}, u32[]{:S(2)}) copy-start(f32[512,48]{0,1:T(8,128)S(1)} %get-tuple-element.49) | copy-start | bytes 294916
  58.0 5.7 %copy-start.12 = (bf16[3072,384]{1,0:T(8,128)(2,1)S(1)}, bf16[3072,384]{1,0:T(8,128)(2,1)}, u32[]{:S(2)}) copy-start(bf16[3072,384]{1,0:T(8,128)(2,1)} %param.17) | copy-start | bytes 7077892
  62.1 1.7 copy-start.2
  65.5 4.3 %copy-start.5 = (bf16[512,384]{1,0:T(8,128)(2,1)}, bf16[512,384]{1,0:T(8,128)(2,1)S(1)}, u32[]{:S(2)}) copy-start(bf16[512,384]{1,0:T(8,128)(2,1)S(1)} %convolution_convert_fusion.value_block) | copy-start | bytes 1179652
  79.9 7.7 %copy-start.11 = (s32[1,4]{1,0:T(1,128)S(1)}, s32[1,4]{1,0:T(1,128)}, u32[]{:S(2)}) copy-start(s32[1,4]{1,0:T(1,128)} %param.21) | copy-start | bytes 52
  79.9 168.5 %all-to-all-start.1 = ((bf16[64,2,128,384]{3,2,1,0:T(8,128)(2,1)}), bf16[64,2,128,384]{3,2,1,0:T(8,128)(2,1)}, u32[]{:S(2)}, u32[]{:S(2)}) async-start(bf16[64,2,128,384]{3,2,1,0:T(8,128)(2,1)} %shard_map.123), calls=%async_computation.1 | async-start | bytes 25165824 | tf_op jit(solution)/shard_map/all_to_all | solution.py:205
  87.6 200.0 %reduce-scatter.2.cloned.1.call-start = ((), (), s32[]{:S(2)}) async-start(), calls=%async_computation.4 | async-start | bytes 7077888 | tf_op jit(solution)/shard_map/reduce_scatter | solution.py:232
  88.0 2.0 copy-start.3
  88.0 2.6 copy-start.13
  90.6 1.4 copy-start.7
  90.6 1.4 copy-start.9
  110.4 17.5 %copy-start.1 = (bf16[4608,384]{0,1:T(8,128)(2,1)S(1)}, bf16[4608,384]{0,1:T(8,128)(2,1)}, u32[]{:S(2)}) copy-start(bf16[4608,384]{0,1:T(8,128)(2,1)} %get-tuple-element.25) | copy-start | bytes 10616836
  248.5 39.2 %copy-start.4 = (bf16[512,384]{1,0:T(8,128)(2,1)S(1)}, bf16[512,384]{1,0:T(8,128)(2,1)}, u32[]{:S(2)}) copy-start(bf16[512,384]{1,0:T(8,128)(2,1)} %param.13) | copy-start | bytes 1179652
Sparse Core Ops, SparseCore 0:
  10.3 30.5 all-gather.1
  248.6 38.9 reduce-scatter.1

commit v6 on v5

--- a/solution.py
+++ b/solution.py
@@ -184,8 +184,6 @@
     prev_pages = prev_count // PAGE
     send = pack_pages(send_slots[:prev_pages], prev_keys, prev_values, slot_total)
     send = pack_pages(send_slots[prev_pages:], new_keys, new_values, slot_total, into=send)
-    keys_all = jnp.concatenate([prev_keys, new_keys], axis=0)
-    values_all = jnp.concatenate([prev_values, new_values], axis=0)
     carried = (
         jnp.full((slot_total,), slot_count, jnp.int32)
         .at[send_slots]
@@ -197,9 +195,11 @@
     found = jnp.argmax(carried[None, :] == wanted[:, None], axis=1).astype(jnp.int32)
     from_req = found // CAPACITY
     from_rank = found % CAPACITY
-    send, normed, keys_all, values_all, from_req, from_rank = lax.optimization_barrier(
-        (send, normed, keys_all, values_all, from_req, from_rank)
-    )
+    send, normed, new_keys, new_values, from_req, from_rank = lax.optimization_barrier(
+        (send, normed, new_keys, new_values, from_req, from_rank)
+    )
+    keys_all = jnp.concatenate([prev_keys, new_keys], axis=0)
+    values_all = jnp.concatenate([prev_values, new_values], axis=0)
     query_raw = jnp.dot(normed, w_query, preferred_element_type=jnp.float32)
     queries = rotate(query_raw, positions, HD).astype(jnp.bfloat16)
     received = lax.all_to_all(send, ("req", "core"), 0, 0, tiled=True)
@@ -227,9 +227,11 @@
     attended = (
         (mixture / totals.T[:, :, None]).astype(jnp.bfloat16).reshape(token_count, local_width)
     )
-    projected = jnp.dot(attended, w_out, preferred_element_type=jnp.float32)
+    projected = jnp.einsum("tf,fo->to", attended, w_out, preferred_element_type=jnp.float32)
     received, projected = lax.optimization_barrier((received, projected))
-    summed = lax.psum_scatter(projected, ("y", "core"), scatter_dimension=1, tiled=True)
+    summed = lax.psum_scatter(
+        projected.T.astype(jnp.bfloat16), ("y", "core"), scatter_dimension=0, tiled=True
+    ).T.astype(jnp.float32)
     layer_out = (tokens.astype(jnp.float32) + summed).astype(jnp.bfloat16)
 
     pool = place_pages(from_req, from_rank, received, slot_count, cores)

time: 299 us -> 281 us (0.940)
  waiting for transfers between devices: 127 us -> 97.5 us
  local copies, waits for them, and re-layouts: 16 us -> 21.8 us
  other arithmetic: 41.5 us -> 45.4 us
    reduce_scatter x1 -> x0, waiting for transfers between devices: 26 us -> none  [shards(): lax.psum_scatter(projected, ('y', 'core'), scatter_dimension=1, tiled=True)]
    all_to_all x1, waiting for transfers between devices: 101 us -> 78.3 us  [shards(): received = lax.all_to_all(send, ('req', 'core'), 0, 0, tiled=True)]
    unnamed x2 -> x3, waiting for transfers between devices: 0.03 us -> 19.2 us
    concatenate x0 -> x2, local copies, waits for them, and re-layouts: none -> 11.6 us  [the longest x1 5.82 us: shards(): keys_all = jnp.concatenate([prev_keys, new_keys], axis=0)]
    unnamed x30 -> x20, local copies, waits for them, and re-layouts: 12 us -> 6.12 us
    concatenate x0 -> x1, other arithmetic: none -> 4.04 us  [shards(): values_all = jnp.concatenate([prev_values, new_values], axis=0)]
  transfers between devices with their start and end apart: 4 -> 4, of which waited for: 2 -> 2; matrix products, arithmetic and copies ran while one was open for 26% -> 32% of each run, Pallas kernels for 11% -> 12%
where the time goes in v6:
time: 281 us; the launch traced here: 279 us
  waiting for transfers between devices  97.5 us (35%)
  matrix products  47.3 us (17%)
  other arithmetic  45.4 us (16%)
  Pallas kernels  36.6 us (13%)
  local copies, waits for them, and re-layouts  21.8 us (8%)
  starting transfers between devices  16 us (6%)
  between operations  14.3 us (5%)
    all_to_all x1, waiting for transfers between devices, shards(): received = lax.all_to_all(send, ('req', 'core'), 0, 0, tiled=True)  78.3 us
    pallas_call x2, Pallas kernels, pack_pages(): pl.pallas_call(body, out_shape=jax.ShapeDtypeStruct((slot_total, 2, PAGE,...  23.4 us
    unnamed x3, waiting for transfers between devices  19.2 us
    dot_general x1, matrix products, shards(): jnp.einsum('qhd,khd->hqk', queries.reshape(token_count, heads_here, HD),...  17.7 us
    reduce_sum x1, other arithmetic, shards(): totals = jnp.sum(weights, axis=2)  17.5 us
    dot_general x1, matrix products, shards(): jnp.einsum('hqk,khd->qhd', prob_rows, values_all.reshape(-1, heads_here,...  15.3 us
    pallas_call x1, Pallas kernels, place_pages(): pl.pallas_call(body, out_shape=jax.ShapeDtypeStruct((slot_count, PAGE, 2...  13.2 us
    all_to_all x1, starting transfers between devices, shards(): carried = lax.all_to_all(carried, ('req', 'core'), 0, 0, tiled=True)  8.25 us
  transfers between devices with their start and end apart: 4, of which 2 were waited for; matrix products, arithmetic and copies ran while one was open for 32% of the time, Pallas kernels for 12%

profile of v6, /device:TPU:0, one launch (start us, length us, event | category | flops | bytes accessed | tf_op | source)
XLA Modules:
  0.0 278.8 jit_solution(18145252291768639365)
XLA Ops:
  8.1 1.8 fusion.21
  13.5 8.2 %all-to-all-start = ((s32[32,2,1]{1,2,0:T(1,128)}), s32[32,2,1]{1,2,0:T(1,128)S(1)}, u32[]{:S(2)}, u32[]{:S(2)}) async-start(s32[32,2,1]{1,2,0:T(1,128)} %bitcast.16), calls=%async_computation | async-start | bytes 32768 | tf_op jit(solution)/shard_map/all_to_all | solution.py:192
  25.1 19.4 %shard_map.122.rest_0_ = bf16[64,2,128,384]{3,2,1,0:T(8,128)(2,1)} custom-call(s32[32]{0:T(128)} %bitcast.91, bf16[4096,384]{1,0:T(8,128)(2,1)} %key_block.1, bf16[4096,384]{1,0:T(8,128)(2,1)} %value_block.1), custom_call_target="tpu_custom_call" | custom-call | tf_op jit(solution)/shard_map/pallas_call | solution.py:90
  45.9 2.6 fusion.6
  49.4 3.1 %fusion.8 = bf16[512,3072]{1,0:T(8,128)(2,1)S(1)} fusion(f32[3072]{0:T(1024)S(1)} %bitcast.88, f32[512]{0:T(512)S(1)} %add_rsqrt_fusion, bf16[528,3072]{1,0:T(8,128)(2,1)} %all-gather.2.cloned.1.call-done), kind=kLoop, calls=%fused_computation.13 | loop fusion | flops 6291456 | bytes 6305792 | tf_op jit(solution)/shard_map/convert_element_type | solution.py:162
  52.5 1.4 fusion.37
  55.3 5.2 %convolution_convert_fusion.value_block = bf16[512,384]{1,0:T(8,128)(2,1)} fusion(bf16[512,3072]{1,0:T(8,128)(2,1)} %copy-done.3, bf16[3072,384]{1,0:T(8,128)(2,1)} %param.17), kind=kOutput, calls=%fused_computation.19 | convolution fusion | flops 1208156160 | bytes 5898240 | tf_op jit(solution)/shard_map/dot_general | solution.py:167
  60.4 4.0 %shard_map.123 = bf16[64,2,128,384]{3,2,1,0:T(8,128)(2,1)} custom-call(s32[4]{0:T(128)} %slice.41.slot_ref, bf16[512,384]{1,0:T(8,128)(2,1)} %copy.35.key_block, bf16[512,384]{1,0:T(8,128)(2,1)} %convolution_convert_fusion.value_block, bf16[64,2,128,384]{3,2,1,0:T(8,128)(2,1)} %shard_map.122.rest_0_), custom_call_target="tpu_custom_call", output_to_operand_aliasing={{}: (3, {})} | custom-call | tf_op jit(solution)/shard_map/pallas_call | solution.py:90
  64.4 7.6 %all-to-all-start.1 = ((bf16[64,2,128,384]{3,2,1,0:T(8,128)(2,1)}), bf16[64,2,128,384]{3,2,1,0:T(8,128)(2,1)}, u32[]{:S(2)}, u32[]{:S(2)}) async-start(bf16[64,2,128,384]{3,2,1,0:T(8,128)(2,1)} %shard_map.123), calls=%async_computation.1 | async-start | bytes 25165824 | tf_op jit(solution)/shard_map/all_to_all | solution.py:205
  72.6 1.3 broadcast_compare_fusion
  73.9 1.7 pad_add_fusion
  75.8 4.0 %pad_maximum_fusion.1 = bf16[4608,384]{1,0:T(8,128)(2,1)} fusion(bf16[512,384]{1,0:T(8,128)(2,1)S(1)} %copy.40, bf16[4096,384]{1,0:T(8,128)(2,1)} %key_block.1), kind=kLoop, calls=%fused_computation.16 | loop fusion | flops 7077888 | bytes 7077888 | tf_op jit(solution)/shard_map/concatenate | solution.py:201
  79.9 5.8 %copy.41 = bf16[4608,384]{0,1:T(8,128)(2,1)} copy(bf16[4608,384]{1,0:T(8,128)(2,1)} %pad_maximum_fusion.1) | data formatting | bytes 7077888 | tf_op jit(solution)/shard_map/concatenate | solution.py:201
  85.7 4.0 %pad_maximum_fusion = bf16[4608,384]{1,0:T(8,128)(2,1)} fusion(bf16[512,384]{1,0:T(8,128)(2,1)S(1)} %copy-done.5, bf16[4096,384]{1,0:T(8,128)(2,1)} %value_block.1), kind=kLoop, calls=%fused_computation.15 | loop fusion | flops 7077888 | bytes 7077888 | tf_op jit(solution)/shard_map/concatenate | solution.py:202
  89.7 5.8 %copy.39 = bf16[4608,384]{0,1:T(8,128)(2,1)} copy(bf16[4608,384]{1,0:T(8,128)(2,1)} %pad_maximum_fusion) | data formatting | bytes 7077888 | tf_op jit(solution)/shard_map/concatenate | solution.py:202
  95.5 4.2 %fusion.38 = f32[512,384]{0,1:T(8,128)S(1)} fusion(bf16[512,3072]{1,0:T(8,128)(2,1)} %copy-done.3, bf16[3072,384]{1,0:T(8,128)(2,1)} %param.15), kind=kOutput, calls=%fused_computation.83 | convolution fusion | flops 1207959552 | bytes 6291456 | tf_op jit(solution)/shard_map/dot_general | solution.py:203
  100.5 17.7 %fusion = (f32[4,512]{1,0:T(4,128)S(1)}, f32[4,512,4608]{2,1,0:T(8,128)}) fusion(pred[512,4608]{1,0:T(8,128)(4,1)S(1)} %copy-done.1, bf16[4608,4,96]{0,2,1:T(8,128)(2,1)} %bitcast.82, bf16[512,4,48]{0,2,1:T(8,128)(2,1)} %get-tuple-element.45, bf16[512,4,48]{0,2,1:T(8,128)(2,1)S(1)} %get-tuple-element.44), kind=kOutput, calls=%fused_computation.3 | convolution fusion | flops 1841035264 | bytes 44048384 | tf_op jit(solution)/shard_map/qhd,khd->hqk/dot_general | solution.py:210
  118.2 17.5 %fusion.1 = f32[4,512]{1,0:T(4,128)S(1)} fusion(f32[4,512,4608]{2,1,0:T(8,128)} %get-tuple-element.54, f32[4,512]{1,0:T(4,128)S(1)} %get-tuple-element.53, pred[512,4608]{1,0:T(8,128)(4,1)S(1)} %copy-done.1), kind=kLoop, calls=%fused_computation.4 | loop fusion | flops 37746688 | bytes 40124416 | tf_op jit(solution)/shard_map/reduce_sum | solution.py:219
  135.7 15.3 %fusion.15 = bf16[512,4,96]{0,2,1:T(8,128)(2,1)S(1)} fusion(bf16[4608,4,96]{0,2,1:T(8,128)(2,1)S(1)} %bitcast.81, f32[4,512,4608]{2,1,0:T(8,128)} %get-tuple-element.54, f32[4,512]{1,0:T(4,128)S(1)} %get-tuple-element.53, pred[512,4608]{1,0:T(8,128)(4,1)S(1)} %copy-done.1, f32[512,4]{0,1:T(4,128)S(1)} %bitcast.90), kind=kOutput, calls=%fused_computation.21 | convolution fusion | flops 1850081280 | bytes 44056576 | tf_op jit(solution)/shard_map/hqk,khd->qhd/dot_general | solution.py:221
  151.0 3.5 %fusion.39 = bf16[512,3072]{1,0:T(8,128)(2,1)} fusion(bf16[512,384]{0,1:T(8,128)(2,1)S(1)} %bitcast.97, bf16[384,3072]{1,0:T(8,128)(2,1)S(1)} %copy-done), kind=kOutput, calls=%fused_computation.84 | convolution fusion | flops 1207959552 | bytes 5898240 | tf_op jit(solution)/shard_map/tf,fo->to/dot_general | solution.py:230
  154.5 78.3 %all-to-all-done.1 = bf16[64,2,128,384]{3,2,1,0:T(8,128)(2,1)} async-done(((bf16[64,2,128,384]{3,2,1,0:T(8,128)(2,1)}), bf16[64,2,128,384]{3,2,1,0:T(8,128)(2,1)}, u32[]{:S(2)}, u32[]{:S(2)}) %all-to-all-start.1) | async-done | bytes 12582944 | tf_op jit(solution)/shard_map/all_to_all | solution.py:205
  232.8 4.7 %copy.44 = bf16[3072,512]{1,0:T(8,128)(2,1)} copy(bf16[3072,512]{0,1:T(8,128)(2,1)} %bitcast.85) | data formatting | bytes 6291456
  237.5 13.2 %shard_map.124 = bf16[18,128,1536]{2,1,0:T(8,128)(2,1)} custom-call(s32[18]{0:T(128)} %get-tuple-element.29.src_ref, s32[18]{0:T(128)} %get-tuple-element.30.rank_ref, bf16[16,2,2,2,128,384]{5,4,3,2,1,0:T(8,128)(2,1)} %bitcast.29.got), custom_call_target="tpu_custom_call" | custom-call | tf_op jit(solution)/shard_map/pallas_call | solution.py:115
  250.7 19.2 %reduce-scatter.4.cloned.1.call-done = bf16[384,512]{1,0:T(8,128)(2,1)} async-done(((bf16[3072,512]{1,0:T(8,128)(2,1)}), bf16[384,512]{1,0:T(8,128)(2,1)}) %reduce-scatter.4.cloned.1.call-update) | async-done | bytes 393232
  (56 shorter events, 15.0 us)
Async XLA Ops:
  7.2 143.8 %copy-start = (bf16[384,3072]{1,0:T(8,128)(2,1)S(1)}, bf16[384,3072]{1,0:T(8,128)(2,1)}, u32[]{:S(2)}) copy-start(bf16[384,3072]{1,0:T(8,128)(2,1)} %param.18) | copy-start | bytes 7077892
  7.2 38.7 %all-gather.2.cloned.1.call-start = ((), (), s32[]{:S(2)}) async-start(), calls=%async_computation.3 | async-start | bytes 3649536 | tf_op jit(solution)/shard_map/all_gather | solution.py:155
  13.5 31.1 %all-to-all-start = ((s32[32,2,1]{1,2,0:T(1,128)}), s32[32,2,1]{1,2,0:T(1,128)S(1)}, u32[]{:S(2)}, u32[]{:S(2)}) async-start(s32[32,2,1]{1,2,0:T(1,128)} %bitcast.16), calls=%async_computation | async-start | bytes 32768 | tf_op jit(solution)/shard_map/all_to_all | solution.py:192
  24.1 1.1 copy-start.6
  48.5 4.0 %copy-start.8 = (bf16[3072,384]{1,0:T(8,128)(2,1)S(1)}, bf16[3072,384]{1,0:T(8,128)(2,1)}, u32[]{:S(2)}) copy-start(bf16[3072,384]{1,0:T(8,128)(2,1)} %param.16) | copy-start | bytes 7077892
  52.5 1.7 copy-start.3
  64.4 7.7 %copy-start.7 = (s32[1,4]{1,0:T(1,128)S(1)}, s32[1,4]{1,0:T(1,128)}, u32[]{:S(2)}) copy-start(s32[1,4]{1,0:T(1,128)} %param.21) | copy-start | bytes 52
  64.4 168.5 %all-to-all-start.1 = ((bf16[64,2,128,384]{3,2,1,0:T(8,128)(2,1)}), bf16[64,2,128,384]{3,2,1,0:T(8,128)(2,1)}, u32[]{:S(2)}, u32[]{:S(2)}) async-start(bf16[64,2,128,384]{3,2,1,0:T(8,128)(2,1)} %shard_map.123), calls=%async_computation.1 | async-start | bytes 25165824 | tf_op jit(solution)/shard_map/all_to_all | solution.py:205
  72.0 197.9 %reduce-scatter.4.cloned.1.call-start = ((), (), s32[]{:S(2)}) async-start(), calls=%async_computation.4 | async-start | bytes 3538944
  79.9 5.8 %copy-start.5 = (bf16[512,384]{1,0:T(8,128)(2,1)S(1)}, bf16[512,384]{1,0:T(8,128)(2,1)}, u32[]{:S(2)}) copy-start(bf16[512,384]{1,0:T(8,128)(2,1)} %convolution_convert_fusion.value_block) | copy-start | bytes 1179652
  95.5 5.0 %copy-start.1 = (pred[512,4608]{1,0:T(8,128)(4,1)S(1)}, pred[512,4608]{1,0:T(8,128)(4,1)}, u32[]{:S(2)}) copy-start(pred[512,4608]{1,0:T(8,128)(4,1)} %pad_add_fusion) | copy-start | bytes 7077892
  118.2 17.5 %copy-start.2 = (bf16[4608,384]{0,1:T(8,128)(2,1)S(1)}, bf16[4608,384]{0,1:T(8,128)(2,1)}, u32[]{:S(2)}) copy-start(bf16[4608,384]{0,1:T(8,128)(2,1)} %copy.39) | copy-start | bytes 10616836
  237.5 33.6 %copy-start.4 = (bf16[512,384]{1,0:T(8,128)(2,1)S(1)}, bf16[512,384]{1,0:T(8,128)(2,1)}, u32[]{:S(2)}) copy-start(bf16[512,384]{1,0:T(8,128)(2,1)} %param.13) | copy-start | bytes 1179652
Sparse Core Ops, SparseCore 0:
  10.3 30.5 all-gather.1
  237.6 32.2 reduce-scatter.3

commit v7 on v5

--- a/solution.py
+++ b/solution.py
@@ -68,65 +68,62 @@
     return jnp.sum(same * earlier_mask, axis=-1)
 
 
-def pack_pages(slots, keys, values, slot_total, into=None):
+def pack_pages(slots, keys, values, slot_total, into=()):
     page_total = keys.shape[0] // PAGE
     width = keys.shape[1]
 
     def body(slot_ref, key_block, value_block, *rest):
-        out = rest[-1]
-        out[0, 0] = key_block[...]
-        out[0, 1] = value_block[...]
+        key_out, value_out = rest[-2:]
+        key_out[0] = key_block[...]
+        value_out[0] = value_block[...]
 
     in_specs = [
         pl.BlockSpec((PAGE, width), lambda page, slot_ref: (page, 0)),
         pl.BlockSpec((PAGE, width), lambda page, slot_ref: (page, 0)),
-    ]
-    operands = [slots, keys, values]
-    aliases = {}
-    if into is not None:
-        in_specs.append(pl.BlockSpec(memory_space=pl.ANY))
-        operands.append(into)
-        aliases = {3: 0}
+    ] + [pl.BlockSpec(memory_space=pl.ANY)] * len(into)
+    half = jax.ShapeDtypeStruct((slot_total, PAGE, width), jnp.bfloat16)
+    out_spec = pl.BlockSpec((1, PAGE, width), lambda page, slot_ref: (slot_ref[page], 0, 0))
     return pl.pallas_call(
         body,
-        out_shape=jax.ShapeDtypeStruct((slot_total, 2, PAGE, width), jnp.bfloat16),
+        out_shape=(half, half),
         grid_spec=pltpu.PrefetchScalarGridSpec(
             num_scalar_prefetch=1,
             grid=(page_total,),
             in_specs=in_specs,
-            out_specs=pl.BlockSpec(
-                (1, 2, PAGE, width), lambda page, slot_ref: (slot_ref[page], 0, 0, 0)
-            ),
+            out_specs=(out_spec, out_spec),
         ),
-        input_output_aliases=aliases,
-    )(*operands)
-
-
-def place_pages(sources, ranks, received, slot_count, cores):
+        input_output_aliases={3 + i: i for i in range(len(into))},
+    )(slots, keys, values, *into)
+
+
+def place_pages(sources, ranks, received, slot_count, cores, part, into=()):
     width = received.shape[-1]
-    shaped = received.reshape(-1, cores, CAPACITY, 2, PAGE, width)
-
-    def body(src_ref, rank_ref, got, out):
+    shaped = received.reshape(-1, cores, CAPACITY, PAGE, width)
+
+    def body(src_ref, rank_ref, got, *rest):
+        out = rest[-1]
         for core in range(cores):
-            for kv in range(2):
-                column = (kv * cores + core) * width
-                out[0, :, column : column + width] = got[0, core, 0, kv]
-
+            out[0, :, core * width : (core + 1) * width] = got[0, core, 0]
+
+    in_specs = [
+        pl.BlockSpec(
+            (1, cores, 1, PAGE, width),
+            lambda slot, src_ref, rank_ref: (src_ref[slot], 0, rank_ref[slot], 0, 0),
+        )
+    ] + [pl.BlockSpec(memory_space=pl.ANY)] * len(into)
     return pl.pallas_call(
         body,
         out_shape=jax.ShapeDtypeStruct((slot_count, PAGE, 2 * cores * width), jnp.bfloat16),
         grid_spec=pltpu.PrefetchScalarGridSpec(
             num_scalar_prefetch=2,
             grid=(slot_count,),
-            in_specs=[
-                pl.BlockSpec(
-                    (1, cores, 1, 2, PAGE, width),
-                    lambda slot, src_ref, rank_ref: (src_ref[slot], 0, rank_ref[slot], 0, 0, 0),
-                )
-            ],
-            out_specs=pl.BlockSpec((1, PAGE, 2 * cores * width), lambda slot, src_ref, rank_ref: (slot, 0, 0)),
+            in_specs=in_specs,
+            out_specs=pl.BlockSpec(
+                (1, PAGE, cores * width), lambda slot, src_ref, rank_ref: (slot, 0, part)
+            ),
         ),
-    )(sources, ranks, shaped)
+        input_output_aliases={3 + i: 0 for i in range(len(into))},
+    )(sources, ranks, shaped, *into)
 
 
 def shards(
@@ -184,8 +181,7 @@
     prev_pages = prev_count // PAGE
     send = pack_pages(send_slots[:prev_pages], prev_keys, prev_values, slot_total)
     send = pack_pages(send_slots[prev_pages:], new_keys, new_values, slot_total, into=send)
-    keys_all = jnp.concatenate([prev_keys, new_keys], axis=0)
-    values_all = jnp.concatenate([prev_values, new_values], axis=0)
+    send_keys, send_values = send
     carried = (
         jnp.full((slot_total,), slot_count, jnp.int32)
         .at[send_slots]
@@ -197,13 +193,16 @@
     found = jnp.argmax(carried[None, :] == wanted[:, None], axis=1).astype(jnp.int32)
     from_req = found // CAPACITY
     from_rank = found % CAPACITY
-    send, normed, keys_all, values_all, from_req, from_rank = lax.optimization_barrier(
-        (send, normed, keys_all, values_all, from_req, from_rank)
-    )
+    send_keys, send_values, normed, new_keys, new_values, from_req, from_rank = (
+        lax.optimization_barrier(
+            (send_keys, send_values, normed, new_keys, new_values, from_req, from_rank)
+        )
+    )
+    keys_all = jnp.concatenate([prev_keys, new_keys], axis=0)
+    values_all = jnp.concatenate([prev_values, new_values], axis=0)
     query_raw = jnp.dot(normed, w_query, preferred_element_type=jnp.float32)
     queries = rotate(query_raw, positions, HD).astype(jnp.bfloat16)
-    received = lax.all_to_all(send, ("req", "core"), 0, 0, tiled=True)
-    received = received.reshape(dest_count, CAPACITY, 2, PAGE, local_width)
+    received_keys = lax.all_to_all(send_keys, ("req", "core"), 0, 0, tiled=True)
 
     allowed = visible(earlier, owners, prev_count, token_count)
     heads_here = local_width // HD
@@ -228,11 +227,14 @@
         (mixture / totals.T[:, :, None]).astype(jnp.bfloat16).reshape(token_count, local_width)
     )
     projected = jnp.dot(attended, w_out, preferred_element_type=jnp.float32)
-    received, projected = lax.optimization_barrier((received, projected))
+    received_keys, projected, send_values = lax.optimization_barrier(
+        (received_keys, projected, send_values)
+    )
     summed = lax.psum_scatter(projected, ("y", "core"), scatter_dimension=1, tiled=True)
     layer_out = (tokens.astype(jnp.float32) + summed).astype(jnp.bfloat16)
-
-    pool = place_pages(from_req, from_rank, received, slot_count, cores)
+    received_values = lax.all_to_all(send_values, ("req", "core"), 0, 0, tiled=True)
+    pool = place_pages(from_req, from_rank, received_keys, slot_count, cores, 0)
+    pool = place_pages(from_req, from_rank, received_values, slot_count, cores, 1, into=(pool,))
     return (layer_out, pool[:, None])
 
 

time: 299 us -> 274 us (0.916)
  waiting for transfers between devices: 127 us -> 77.4 us
  Pallas kernels: 36.5 us -> 46.8 us
  other arithmetic: 41.5 us -> 47 us
  starting transfers between devices: 16 us -> 20.9 us
  matrix products: 45.3 us -> 49 us
    reduce_scatter x1, waiting for transfers between devices: 26 us -> 0.01 us  [shards(): lax.psum_scatter(projected, ('y', 'core'), scatter_dimension=1, tiled=True)]
    all_to_all x1 -> x2, waiting for transfers between devices: 101 us -> 77.3 us  [the longest x1 66.2 us: shards(): lax.all_to_all(send_values, ('req', 'core'), 0, 0, tiled=True)]
    unnamed x30 -> x16, local copies, waits for them, and re-layouts: 12 us -> 0.26 us
    concatenate x0 -> x2, local copies, waits for them, and re-layouts: none -> 11.6 us  [the longest x1 5.78 us: shards(): values_all = jnp.concatenate([prev_values, new_values], axis=0)]
    pallas_call x1 -> x2, Pallas kernels: 13.2 us -> 23.5 us  [place_pages(): pl.pallas_call(body, out_shape=jax.ShapeDtypeStruct((slot_count, PAGE, 2...]
    all_to_all x1 -> x2, starting transfers between devices: 7.64 us -> 12.4 us  [the longest x1 7.53 us: shards(): received_keys = lax.all_to_all(send_keys, ('req', 'core'), 0, 0, tiled=True)]
    concatenate x0 -> x1, other arithmetic: none -> 4.01 us  [shards(): values_all = jnp.concatenate([prev_values, new_values], axis=0)]
  transfers between devices with their start and end apart: 4 -> 5, of which waited for: 2 -> 2; matrix products, arithmetic and copies ran while one was open for 26% -> 29% of each run, Pallas kernels for 11% -> 16%
where the time goes in v7:
time: 274 us; the launch traced here: 271 us
  waiting for transfers between devices  77.4 us (28%)
  matrix products  49 us (18%)
  other arithmetic  47 us (17%)
  Pallas kernels  46.8 us (17%)
  starting transfers between devices  20.9 us (8%)
  local copies, waits for them, and re-layouts  15.9 us (6%)
  between operations  14.3 us (5%)
    all_to_all x1, waiting for transfers between devices, shards(): lax.all_to_all(send_values, ('req', 'core'), 0, 0, tiled=True)  66.2 us
    pallas_call x2, Pallas kernels, place_pages(): pl.pallas_call(body, out_shape=jax.ShapeDtypeStruct((slot_count, PAGE, 2...  23.5 us
    pallas_call x2, Pallas kernels, pack_pages(): pl.pallas_call(body, out_shape=(half, half), grid_spec=pltpu.PrefetchScal...  23.3 us
    dot_general x1, matrix products, shards(): jnp.einsum('qhd,khd->hqk', queries.reshape(token_count, heads_here, HD),...  18.6 us
    reduce_sum x1, other arithmetic, shards(): totals = jnp.sum(weights, axis=2)  18.2 us
    dot_general x1, matrix products, shards(): jnp.einsum('hqk,khd->qhd', prob_rows, values_all.reshape(-1, heads_here,...  15.3 us
    all_to_all x1, waiting for transfers between devices, shards(): received_keys = lax.all_to_all(send_keys, ('req', 'core'), 0, 0, tiled=True)  11.2 us
    all_to_all x1, starting transfers between devices, shards(): carried = lax.all_to_all(carried, ('req', 'core'), 0, 0, tiled=True)  8.25 us
  transfers between devices with their start and end apart: 5, of which 2 were waited for; matrix products, arithmetic and copies ran while one was open for 29% of the time, Pallas kernels for 16%

profile of v7, /device:TPU:0, one launch (start us, length us, event | category | flops | bytes accessed | tf_op | source)
XLA Modules:
  0.0 271.4 jit_solution(464639134500030679)
XLA Ops:
  8.1 1.8 fusion.20
  13.5 8.2 %all-to-all-start = ((s32[32,2,1]{1,2,0:T(1,128)}), s32[32,2,1]{1,2,0:T(1,128)S(1)}, u32[]{:S(2)}, u32[]{:S(2)}) async-start(s32[32,2,1]{1,2,0:T(1,128)} %bitcast.16), calls=%async_computation | async-start | bytes 32768 | tf_op jit(solution)/shard_map/all_to_all | solution.py:190
  27.0 1.5 pad_add_fusion
  29.2 19.4 %shard_map.122 = (bf16[64,128,384]{2,1,0:T(8,128)(2,1)}, bf16[64,128,384]{2,1,0:T(8,128)(2,1)}) custom-call(s32[32]{0:T(128)} %bitcast.83, bf16[4096,384]{1,0:T(8,128)(2,1)} %key_block.1, bf16[4096,384]{1,0:T(8,128)(2,1)} %value_block.1), custom_call_target="tpu_custom_call" | custom-call | tf_op jit(solution)/shard_map/pallas_call | solution.py:86
  49.9 2.6 fusion.6
  53.5 3.1 %fusion.8 = bf16[512,3072]{1,0:T(8,128)(2,1)S(1)} fusion(f32[3072]{0:T(1024)S(1)} %bitcast.80, f32[512]{0:T(512)S(1)} %add_rsqrt_fusion, bf16[528,3072]{1,0:T(8,128)(2,1)} %all-gather.2.cloned.1.call-done), kind=kLoop, calls=%fused_computation.13 | loop fusion | flops 6291456 | bytes 6305792 | tf_op jit(solution)/shard_map/convert_element_type | solution.py:159
  59.3 5.2 %convolution_convert_fusion.value_block = bf16[512,384]{1,0:T(8,128)(2,1)} fusion(bf16[512,3072]{1,0:T(8,128)(2,1)} %copy-done.3, bf16[3072,384]{1,0:T(8,128)(2,1)} %param.17), kind=kOutput, calls=%fused_computation.18 | convolution fusion | flops 1208156160 | bytes 5898240 | tf_op jit(solution)/shard_map/dot_general | solution.py:164
  64.5 4.0 %shard_map.123 = (bf16[64,128,384]{2,1,0:T(8,128)(2,1)}, bf16[64,128,384]{2,1,0:T(8,128)(2,1)}) custom-call(s32[4]{0:T(128)} %slice.41.slot_ref, bf16[512,384]{1,0:T(8,128)(2,1)} %copy.37.key_block, bf16[512,384]{1,0:T(8,128)(2,1)} %convolution_convert_fusion.value_block, ...), custom_call_target="tpu_custom_call", output_to_operand_aliasing={{0}: (3, {}), {1}: (4, {})} | custom-call | tf_op jit(solution)/shard_map/pallas_call | solution.py:86
  68.6 4.0 %pad_maximum_fusion.1 = bf16[4608,384]{1,0:T(8,128)(2,1)} fusion(bf16[512,384]{1,0:T(8,128)(2,1)S(1)} %copy.42, bf16[4096,384]{1,0:T(8,128)(2,1)} %key_block.1), kind=kLoop, calls=%fused_computation.16 | loop fusion | flops 7077888 | bytes 7077888 | tf_op jit(solution)/shard_map/concatenate | solution.py:201
  72.6 5.8 %copy.43 = bf16[4608,384]{0,1:T(8,128)(2,1)} copy(bf16[4608,384]{1,0:T(8,128)(2,1)} %pad_maximum_fusion.1) | data formatting | bytes 7077888 | tf_op jit(solution)/shard_map/concatenate | solution.py:201
  78.4 4.0 %fusion.37 = f32[512,384]{0,1:T(8,128)S(1)} fusion(bf16[512,3072]{1,0:T(8,128)(2,1)} %copy-done.3, bf16[3072,384]{1,0:T(8,128)(2,1)} %param.15), kind=kOutput, calls=%fused_computation.81 | convolution fusion | flops 1207959552 | bytes 6291456 | tf_op jit(solution)/shard_map/dot_general | solution.py:203
  82.6 7.5 %all-to-all-start.1 = ((bf16[64,128,384]{2,1,0:T(8,128)(2,1)}), bf16[64,128,384]{2,1,0:T(8,128)(2,1)}, u32[]{:S(2)}, u32[]{:S(2)}) async-start(bf16[64,128,384]{2,1,0:T(8,128)(2,1)} %get-tuple-element.34), calls=%async_computation.1 | async-start | bytes 12582912 | tf_op jit(solution)/shard_map/all_to_all | solution.py:205
  90.4 18.6 %fusion = (f32[4,512]{1,0:T(4,128)S(1)}, f32[4,512,4608]{2,1,0:T(8,128)}) fusion(pred[512,4608]{1,0:T(8,128)(4,1)} %pad_add_fusion, bf16[4608,4,96]{0,2,1:T(8,128)(2,1)} %bitcast.73, bf16[512,4,48]{0,2,1:T(8,128)(2,1)S(1)} %get-tuple-element.57, bf16[512,4,48]{0,2,1:T(8,128)(2,1)S(1)} %get-tuple-element.56), kind=kOutput, calls=%fused_computation.3 | convolution fusion | flops 1841035264 | bytes 44048384 | tf_op jit(solution)/shard_map/qhd,khd->hqk/dot_general | solution.py:209
  109.0 4.0 %pad_maximum_fusion = bf16[4608,384]{1,0:T(8,128)(2,1)} fusion(bf16[512,384]{1,0:T(8,128)(2,1)S(1)} %copy-done.5, bf16[4096,384]{1,0:T(8,128)(2,1)} %value_block.1), kind=kLoop, calls=%fused_computation.15 | loop fusion | flops 7077888 | bytes 7077888 | tf_op jit(solution)/shard_map/concatenate | solution.py:202
  113.0 5.8 %copy.41 = bf16[4608,384]{0,1:T(8,128)(2,1)} copy(bf16[4608,384]{1,0:T(8,128)(2,1)} %pad_maximum_fusion) | data formatting | bytes 7077888 | tf_op jit(solution)/shard_map/concatenate | solution.py:202
  118.8 18.2 %fusion.1 = f32[4,512]{1,0:T(4,128)S(1)} fusion(f32[4,512,4608]{2,1,0:T(8,128)} %get-tuple-element.66, f32[4,512]{1,0:T(4,128)S(1)} %get-tuple-element.65, pred[512,4608]{1,0:T(8,128)(4,1)} %pad_add_fusion), kind=kLoop, calls=%fused_computation.4 | loop fusion | flops 37746688 | bytes 40124416 | tf_op jit(solution)/shard_map/reduce_sum | solution.py:218
  137.0 15.3 %fusion.15 = bf16[512,4,96]{0,2,1:T(8,128)(2,1)S(1)} fusion(bf16[4608,4,96]{0,2,1:T(8,128)(2,1)S(1)} %bitcast.74, f32[4,512,4608]{2,1,0:T(8,128)} %get-tuple-element.66, f32[4,512]{1,0:T(4,128)S(1)} %get-tuple-element.65, pred[512,4608]{1,0:T(8,128)(4,1)S(1)} %copy-done.1, f32[512,4]{0,1:T(4,128)S(1)} %bitcast.82), kind=kOutput, calls=%fused_computation.20 | convolution fusion | flops 1850081280 | bytes 44056576 | tf_op jit(solution)/shard_map/hqk,khd->qhd/dot_general | solution.py:220
  152.4 4.5 %fusion.38 = f32[512,3072]{1,0:T(8,128)} fusion(bf16[512,384]{0,1:T(8,128)(2,1)S(1)} %bitcast.79, bf16[384,3072]{1,0:T(8,128)(2,1)S(1)} %copy-done), kind=kOutput, calls=%fused_computation.82 | convolution fusion | flops 1207959552 | bytes 9043968 | tf_op jit(solution)/shard_map/dot_general | solution.py:229
  156.9 11.2 %all-to-all-done.1 = bf16[64,128,384]{2,1,0:T(8,128)(2,1)} async-done(((bf16[64,128,384]{2,1,0:T(8,128)(2,1)}), bf16[64,128,384]{2,1,0:T(8,128)(2,1)}, u32[]{:S(2)}, u32[]{:S(2)}) %all-to-all-start.1) | async-done | bytes 6291488 | tf_op jit(solution)/shard_map/all_to_all | solution.py:205
  168.0 4.9 %all-to-all-start.2 = ((bf16[64,128,384]{2,1,0:T(8,128)(2,1)}), bf16[64,128,384]{2,1,0:T(8,128)(2,1)}, u32[]{:S(2)}, u32[]{:S(2)}) async-start(bf16[64,128,384]{2,1,0:T(8,128)(2,1)} %get-tuple-element.42), calls=%async_computation.3 | async-start | bytes 12582912 | tf_op jit(solution)/shard_map/all_to_all | solution.py:235
  173.0 11.7 %shard_map.124.rest_0_ = bf16[18,128,1536]{2,1,0:T(8,128)(2,1)} custom-call(s32[18]{0:T(128)} %get-tuple-element.40.src_ref, s32[18]{0:T(128)} %get-tuple-element.41.rank_ref, bf16[16,2,2,128,384]{4,3,2,1,0:T(8,128)(2,1)} %bitcast.27.got), custom_call_target="tpu_custom_call" | custom-call | tf_op jit(solution)/shard_map/pallas_call | solution.py:114
  184.7 66.2 %all-to-all-done.2 = bf16[64,128,384]{2,1,0:T(8,128)(2,1)} async-done(((bf16[64,128,384]{2,1,0:T(8,128)(2,1)}), bf16[64,128,384]{2,1,0:T(8,128)(2,1)}, u32[]{:S(2)}, u32[]{:S(2)}) %all-to-all-start.2) | async-done | bytes 6291488 | tf_op jit(solution)/shard_map/all_to_all | solution.py:235
  250.9 11.8 %shard_map.125 = bf16[18,128,1536]{2,1,0:T(8,128)(2,1)} custom-call(s32[18]{0:T(128)} %get-tuple-element.40.src_ref, s32[18]{0:T(128)} %get-tuple-element.41.rank_ref, bf16[16,2,2,128,384]{4,3,2,1,0:T(8,128)(2,1)} %bitcast.26.got, bf16[18,128,1536]{2,1,0:T(8,128)(2,1)} %shard_map.124.rest_0_), custom_call_target="tpu_custom_call", output_to_operand_aliasing={{}: (3, {})} | custom-call | tf_op jit(solution)/shard_map/pallas_call | solution.py:114
  262.6 2.0 add_convert_fusion
  (55 shorter events, 16.0 us)
Async XLA Ops:
  7.2 145.2 %copy-start = (bf16[384,3072]{1,0:T(8,128)(2,1)S(1)}, bf16[384,3072]{1,0:T(8,128)(2,1)}, u32[]{:S(2)}) copy-start(bf16[384,3072]{1,0:T(8,128)(2,1)} %param.18) | copy-start | bytes 7077892
  7.2 42.8 %all-gather.2.cloned.1.call-start = ((), (), s32[]{:S(2)}) async-start(), calls=%async_computation.4 | async-start | bytes 3649536 | tf_op jit(solution)/shard_map/all_gather | solution.py:152
  13.5 35.1 %all-to-all-start = ((s32[32,2,1]{1,2,0:T(1,128)}), s32[32,2,1]{1,2,0:T(1,128)S(1)}, u32[]{:S(2)}, u32[]{:S(2)}) async-start(s32[32,2,1]{1,2,0:T(1,128)} %bitcast.16), calls=%async_computation | async-start | bytes 32768 | tf_op jit(solution)/shard_map/all_to_all | solution.py:190
  25.0 3.5 %copy-start.6 = (s32[36]{0:T(128)}, s32[36]{0:T(128)S(1)}, u32[]{:S(2)}) copy-start(s32[36]{0:T(128)S(1)} %multiply_add_fusion) | copy-start | bytes 436
  52.5 4.0 %copy-start.7 = (bf16[3072,384]{1,0:T(8,128)(2,1)S(1)}, bf16[3072,384]{1,0:T(8,128)(2,1)}, u32[]{:S(2)}) copy-start(bf16[3072,384]{1,0:T(8,128)(2,1)} %param.16) | copy-start | bytes 7077892
  56.6 1.7 copy-start.3
  82.6 85.4 %all-to-all-start.1 = ((bf16[64,128,384]{2,1,0:T(8,128)(2,1)}), bf16[64,128,384]{2,1,0:T(8,128)(2,1)}, u32[]{:S(2)}, u32[]{:S(2)}) async-start(bf16[64,128,384]{2,1,0:T(8,128)(2,1)} %get-tuple-element.34), calls=%async_computation.1 | async-start | bytes 12582912 | tf_op jit(solution)/shard_map/all_to_all | solution.py:205
  90.1 172.5 %reduce-scatter.2.cloned.1.call-start = ((), (), s32[]{:S(2)}) async-start(), calls=%async_computation.5 | async-start | bytes 7077888 | tf_op jit(solution)/shard_map/reduce_scatter | solution.py:233
  90.4 18.6 %copy-start.5 = (bf16[512,384]{1,0:T(8,128)(2,1)S(1)}, bf16[512,384]{1,0:T(8,128)(2,1)}, u32[]{:S(2)}) copy-start(bf16[512,384]{1,0:T(8,128)(2,1)} %convolution_convert_fusion.value_block) | copy-start | bytes 1179652
  118.8 18.2 %copy-start.1 = (pred[512,4608]{1,0:T(8,128)(4,1)S(1)}, pred[512,4608]{1,0:T(8,128)(4,1)}, u32[]{:S(2)}) copy-start(pred[512,4608]{1,0:T(8,128)(4,1)} %pad_add_fusion) | copy-start | bytes 7077892
  118.8 18.2 %copy-start.2 = (bf16[4608,384]{0,1:T(8,128)(2,1)S(1)}, bf16[4608,384]{0,1:T(8,128)(2,1)}, u32[]{:S(2)}) copy-start(bf16[4608,384]{0,1:T(8,128)(2,1)} %copy.41) | copy-start | bytes 10616836
  168.0 82.8 %all-to-all-start.2 = ((bf16[64,128,384]{2,1,0:T(8,128)(2,1)}), bf16[64,128,384]{2,1,0:T(8,128)(2,1)}, u32[]{:S(2)}, u32[]{:S(2)}) async-start(bf16[64,128,384]{2,1,0:T(8,128)(2,1)} %get-tuple-element.42), calls=%async_computation.3 | async-start | bytes 12582912 | tf_op jit(solution)/shard_map/all_to_all | solution.py:235
  250.9 11.8 %copy-start.4 = (bf16[512,384]{1,0:T(8,128)(2,1)S(1)}, bf16[512,384]{1,0:T(8,128)(2,1)}, u32[]{:S(2)}) copy-start(bf16[512,384]{1,0:T(8,128)(2,1)} %param.13) | copy-start | bytes 1179652
Sparse Core Ops, SparseCore 0:
  10.0 30.5 all-gather.1
  168.2 39.9 reduce-scatter.1

commit v8 on v7

--- a/solution.py
+++ b/solution.py
@@ -96,34 +96,41 @@
     )(slots, keys, values, *into)
 
 
-def place_pages(sources, ranks, received, slot_count, cores, part, into=()):
+def place_pages(sources, ranks, received, slot_count, cores, part, into=(), group=6):
     width = received.shape[-1]
     shaped = received.reshape(-1, cores, CAPACITY, PAGE, width)
 
-    def body(src_ref, rank_ref, got, *rest):
-        out = rest[-1]
-        for core in range(cores):
-            out[0, :, core * width : (core + 1) * width] = got[0, core, 0]
+    def body(src_ref, rank_ref, *refs):
+        out = refs[-1]
+        for member in range(group):
+            for core in range(cores):
+                out[member, :, core * width : (core + 1) * width] = refs[member][0, core, 0]
+
+    def source_map(member):
+        return lambda step, src_ref, rank_ref: (
+            src_ref[step * group + member],
+            0,
+            rank_ref[step * group + member],
+            0,
+            0,
+        )
 
     in_specs = [
-        pl.BlockSpec(
-            (1, cores, 1, PAGE, width),
-            lambda slot, src_ref, rank_ref: (src_ref[slot], 0, rank_ref[slot], 0, 0),
-        )
+        pl.BlockSpec((1, cores, 1, PAGE, width), source_map(member)) for member in range(group)
     ] + [pl.BlockSpec(memory_space=pl.ANY)] * len(into)
     return pl.pallas_call(
         body,
         out_shape=jax.ShapeDtypeStruct((slot_count, PAGE, 2 * cores * width), jnp.bfloat16),
         grid_spec=pltpu.PrefetchScalarGridSpec(
             num_scalar_prefetch=2,
-            grid=(slot_count,),
+            grid=(slot_count // group,),
             in_specs=in_specs,
             out_specs=pl.BlockSpec(
-                (1, PAGE, cores * width), lambda slot, src_ref, rank_ref: (slot, 0, part)
+                (group, PAGE, cores * width), lambda step, src_ref, rank_ref: (step, 0, part)
             ),
         ),
-        input_output_aliases={3 + i: 0 for i in range(len(into))},
-    )(sources, ranks, shaped, *into)
+        input_output_aliases={2 + group + i: 0 for i in range(len(into))},
+    )(sources, ranks, *([shaped] * group), *into)
 
 
 def shards(

time: 274 us -> 267 us (0.974)
  Pallas kernels: 46.8 us -> 34.5 us
  waiting for transfers between devices: 77.4 us -> 83.5 us
    pallas_call x2, Pallas kernels: 23.5 us -> 11.2 us  [place_pages(): pl.pallas_call(body, out_shape=jax.ShapeDtypeStruct((slot_count, PAGE, 2...]
    all_to_all x1, waiting for transfers between devices: 66.2 us -> 72.3 us  [shards(): lax.all_to_all(send_values, ('req', 'core'), 0, 0, tiled=True)]
  transfers between devices with their start and end apart: 5 -> 5, of which waited for: 2 -> 2; matrix products, arithmetic and copies ran while one was open for 29% -> 29% of each run, Pallas kernels for 16% -> 12%
where the time goes in v8:
time: 267 us; the launch traced here: 265 us
  waiting for transfers between devices  83.5 us (31%)
  matrix products  49 us (18%)
  other arithmetic  47 us (18%)
  Pallas kernels  34.5 us (13%)
  starting transfers between devices  20.9 us (8%)
  local copies, waits for them, and re-layouts  15.9 us (6%)
  between operations  14.3 us (5%)
    all_to_all x1, waiting for transfers between devices, shards(): lax.all_to_all(send_values, ('req', 'core'), 0, 0, tiled=True)  72.3 us
    pallas_call x2, Pallas kernels, pack_pages(): pl.pallas_call(body, out_shape=(half, half), grid_spec=pltpu.PrefetchScal...  23.3 us
    dot_general x1, matrix products, shards(): jnp.einsum('qhd,khd->hqk', queries.reshape(token_count, heads_here, HD),...  18.6 us
    reduce_sum x1, other arithmetic, shards(): totals = jnp.sum(weights, axis=2)  18.2 us
    dot_general x1, matrix products, shards(): jnp.einsum('hqk,khd->qhd', prob_rows, values_all.reshape(-1, heads_here,...  15.3 us
    pallas_call x2, Pallas kernels, place_pages(): pl.pallas_call(body, out_shape=jax.ShapeDtypeStruct((slot_count, PAGE, 2...  11.2 us
    all_to_all x1, waiting for transfers between devices, shards(): received_keys = lax.all_to_all(send_keys, ('req', 'core'), 0, 0, tiled=True)  11.2 us
    all_to_all x1, starting transfers between devices, shards(): carried = lax.all_to_all(carried, ('req', 'core'), 0, 0, tiled=True)  8.25 us
  transfers between devices with their start and end apart: 5, of which 2 were waited for; matrix products, arithmetic and copies ran while one was open for 29% of the time, Pallas kernels for 12%

profile of v8, /device:TPU:0, one launch (start us, length us, event | category | flops | bytes accessed | tf_op | source)
XLA Modules:
  0.0 265.2 jit_solution(17706772630935789030)
XLA Ops:
  8.1 1.8 fusion.20
  13.5 8.2 %all-to-all-start = ((s32[32,2,1]{1,2,0:T(1,128)}), s32[32,2,1]{1,2,0:T(1,128)S(1)}, u32[]{:S(2)}, u32[]{:S(2)}) async-start(s32[32,2,1]{1,2,0:T(1,128)} %bitcast.16), calls=%async_computation | async-start | bytes 32768 | tf_op jit(solution)/shard_map/all_to_all | solution.py:197
  27.0 1.5 pad_add_fusion
  29.2 19.4 %shard_map.122 = (bf16[64,128,384]{2,1,0:T(8,128)(2,1)}, bf16[64,128,384]{2,1,0:T(8,128)(2,1)}) custom-call(s32[32]{0:T(128)} %bitcast.83, bf16[4096,384]{1,0:T(8,128)(2,1)} %key_block.1, bf16[4096,384]{1,0:T(8,128)(2,1)} %value_block.1), custom_call_target="tpu_custom_call" | custom-call | tf_op jit(solution)/shard_map/pallas_call | solution.py:86
  49.9 2.6 fusion.6
  53.5 3.1 %fusion.8 = bf16[512,3072]{1,0:T(8,128)(2,1)S(1)} fusion(f32[3072]{0:T(1024)S(1)} %bitcast.80, f32[512]{0:T(512)S(1)} %add_rsqrt_fusion, bf16[528,3072]{1,0:T(8,128)(2,1)} %all-gather.2.cloned.1.call-done), kind=kLoop, calls=%fused_computation.13 | loop fusion | flops 6291456 | bytes 6305792 | tf_op jit(solution)/shard_map/convert_element_type | solution.py:166
  59.3 5.2 %convolution_convert_fusion.value_block = bf16[512,384]{1,0:T(8,128)(2,1)} fusion(bf16[512,3072]{1,0:T(8,128)(2,1)} %copy-done.3, bf16[3072,384]{1,0:T(8,128)(2,1)} %param.17), kind=kOutput, calls=%fused_computation.18 | convolution fusion | flops 1208156160 | bytes 5898240 | tf_op jit(solution)/shard_map/dot_general | solution.py:171
  64.5 4.0 %shard_map.123 = (bf16[64,128,384]{2,1,0:T(8,128)(2,1)}, bf16[64,128,384]{2,1,0:T(8,128)(2,1)}) custom-call(s32[4]{0:T(128)} %slice.41.slot_ref, bf16[512,384]{1,0:T(8,128)(2,1)} %copy.37.key_block, bf16[512,384]{1,0:T(8,128)(2,1)} %convolution_convert_fusion.value_block, ...), custom_call_target="tpu_custom_call", output_to_operand_aliasing={{0}: (3, {}), {1}: (4, {})} | custom-call | tf_op jit(solution)/shard_map/pallas_call | solution.py:86
  68.6 4.0 %pad_maximum_fusion.1 = bf16[4608,384]{1,0:T(8,128)(2,1)} fusion(bf16[512,384]{1,0:T(8,128)(2,1)S(1)} %copy.42, bf16[4096,384]{1,0:T(8,128)(2,1)} %key_block.1), kind=kLoop, calls=%fused_computation.16 | loop fusion | flops 7077888 | bytes 7077888 | tf_op jit(solution)/shard_map/concatenate | solution.py:208
  72.6 5.8 %copy.43 = bf16[4608,384]{0,1:T(8,128)(2,1)} copy(bf16[4608,384]{1,0:T(8,128)(2,1)} %pad_maximum_fusion.1) | data formatting | bytes 7077888 | tf_op jit(solution)/shard_map/concatenate | solution.py:208
  78.4 4.0 %fusion.37 = f32[512,384]{0,1:T(8,128)S(1)} fusion(bf16[512,3072]{1,0:T(8,128)(2,1)} %copy-done.3, bf16[3072,384]{1,0:T(8,128)(2,1)} %param.15), kind=kOutput, calls=%fused_computation.81 | convolution fusion | flops 1207959552 | bytes 6291456 | tf_op jit(solution)/shard_map/dot_general | solution.py:210
  82.6 7.5 %all-to-all-start.1 = ((bf16[64,128,384]{2,1,0:T(8,128)(2,1)}), bf16[64,128,384]{2,1,0:T(8,128)(2,1)}, u32[]{:S(2)}, u32[]{:S(2)}) async-start(bf16[64,128,384]{2,1,0:T(8,128)(2,1)} %get-tuple-element.34), calls=%async_computation.1 | async-start | bytes 12582912 | tf_op jit(solution)/shard_map/all_to_all | solution.py:212
  90.4 18.6 %fusion = (f32[4,512]{1,0:T(4,128)S(1)}, f32[4,512,4608]{2,1,0:T(8,128)}) fusion(pred[512,4608]{1,0:T(8,128)(4,1)} %pad_add_fusion, bf16[4608,4,96]{0,2,1:T(8,128)(2,1)} %bitcast.73, bf16[512,4,48]{0,2,1:T(8,128)(2,1)S(1)} %get-tuple-element.57, bf16[512,4,48]{0,2,1:T(8,128)(2,1)S(1)} %get-tuple-element.56), kind=kOutput, calls=%fused_computation.3 | convolution fusion | flops 1841035264 | bytes 44048384 | tf_op jit(solution)/shard_map/qhd,khd->hqk/dot_general | solution.py:216
  109.0 4.0 %pad_maximum_fusion = bf16[4608,384]{1,0:T(8,128)(2,1)} fusion(bf16[512,384]{1,0:T(8,128)(2,1)S(1)} %copy-done.5, bf16[4096,384]{1,0:T(8,128)(2,1)} %value_block.1), kind=kLoop, calls=%fused_computation.15 | loop fusion | flops 7077888 | bytes 7077888 | tf_op jit(solution)/shard_map/concatenate | solution.py:209
  113.0 5.8 %copy.41 = bf16[4608,384]{0,1:T(8,128)(2,1)} copy(bf16[4608,384]{1,0:T(8,128)(2,1)} %pad_maximum_fusion) | data formatting | bytes 7077888 | tf_op jit(solution)/shard_map/concatenate | solution.py:209
  118.8 18.2 %fusion.1 = f32[4,512]{1,0:T(4,128)S(1)} fusion(f32[4,512,4608]{2,1,0:T(8,128)} %get-tuple-element.66, f32[4,512]{1,0:T(4,128)S(1)} %get-tuple-element.65, pred[512,4608]{1,0:T(8,128)(4,1)} %pad_add_fusion), kind=kLoop, calls=%fused_computation.4 | loop fusion | flops 37746688 | bytes 40124416 | tf_op jit(solution)/shard_map/reduce_sum | solution.py:225
  137.0 15.3 %fusion.15 = bf16[512,4,96]{0,2,1:T(8,128)(2,1)S(1)} fusion(bf16[4608,4,96]{0,2,1:T(8,128)(2,1)S(1)} %bitcast.74, f32[4,512,4608]{2,1,0:T(8,128)} %get-tuple-element.66, f32[4,512]{1,0:T(4,128)S(1)} %get-tuple-element.65, pred[512,4608]{1,0:T(8,128)(4,1)S(1)} %copy-done.1, f32[512,4]{0,1:T(4,128)S(1)} %bitcast.82), kind=kOutput, calls=%fused_computation.20 | convolution fusion | flops 1850081280 | bytes 44056576 | tf_op jit(solution)/shard_map/hqk,khd->qhd/dot_general | solution.py:227
  152.4 4.5 %fusion.38 = f32[512,3072]{1,0:T(8,128)} fusion(bf16[512,384]{0,1:T(8,128)(2,1)S(1)} %bitcast.79, bf16[384,3072]{1,0:T(8,128)(2,1)S(1)} %copy-done), kind=kOutput, calls=%fused_computation.82 | convolution fusion | flops 1207959552 | bytes 9043968 | tf_op jit(solution)/shard_map/dot_general | solution.py:236
  156.9 11.2 %all-to-all-done.1 = bf16[64,128,384]{2,1,0:T(8,128)(2,1)} async-done(((bf16[64,128,384]{2,1,0:T(8,128)(2,1)}), bf16[64,128,384]{2,1,0:T(8,128)(2,1)}, u32[]{:S(2)}, u32[]{:S(2)}) %all-to-all-start.1) | async-done | bytes 6291488 | tf_op jit(solution)/shard_map/all_to_all | solution.py:212
  168.0 4.9 %all-to-all-start.2 = ((bf16[64,128,384]{2,1,0:T(8,128)(2,1)}), bf16[64,128,384]{2,1,0:T(8,128)(2,1)}, u32[]{:S(2)}, u32[]{:S(2)}) async-start(bf16[64,128,384]{2,1,0:T(8,128)(2,1)} %get-tuple-element.42), calls=%async_computation.3 | async-start | bytes 12582912 | tf_op jit(solution)/shard_map/all_to_all | solution.py:242
  173.0 5.6 %shard_map.124.refs_6_ = bf16[18,128,1536]{2,1,0:T(8,128)(2,1)} custom-call(s32[18]{0:T(128)} %get-tuple-element.40.src_ref, s32[18]{0:T(128)} %get-tuple-element.41.rank_ref, bf16[16,2,2,128,384]{4,3,2,1,0:T(8,128)(2,1)} %bitcast.27.refs_0_.refs_1_.refs_2_.refs_3_.refs_4_.refs_5_, ...), custom_call_target="tpu_custom_call" | custom-call | tf_op jit(solution)/shard_map/pallas_call | solution.py:121
  178.6 72.3 %all-to-all-done.2 = bf16[64,128,384]{2,1,0:T(8,128)(2,1)} async-done(((bf16[64,128,384]{2,1,0:T(8,128)(2,1)}), bf16[64,128,384]{2,1,0:T(8,128)(2,1)}, u32[]{:S(2)}, u32[]{:S(2)}) %all-to-all-start.2) | async-done | bytes 6291488 | tf_op jit(solution)/shard_map/all_to_all | solution.py:242
  250.9 5.6 %shard_map.125 = bf16[18,128,1536]{2,1,0:T(8,128)(2,1)} custom-call(s32[18]{0:T(128)} %get-tuple-element.40.src_ref, s32[18]{0:T(128)} %get-tuple-element.41.rank_ref, bf16[16,2,2,128,384]{4,3,2,1,0:T(8,128)(2,1)} %bitcast.26.refs_0_.refs_1_.refs_2_.refs_3_.refs_4_.refs_5_, ...), custom_call_target="tpu_custom_call", output_to_operand_aliasing={{}: (8, {})} | custom-call | tf_op jit(solution)/shard_map/pallas_call | solution.py:121
  256.5 2.0 add_convert_fusion
  (55 shorter events, 16.0 us)
Async XLA Ops:
  7.2 145.2 %copy-start = (bf16[384,3072]{1,0:T(8,128)(2,1)S(1)}, bf16[384,3072]{1,0:T(8,128)(2,1)}, u32[]{:S(2)}) copy-start(bf16[384,3072]{1,0:T(8,128)(2,1)} %param.18) | copy-start | bytes 7077892
  7.2 42.7 %all-gather.2.cloned.1.call-start = ((), (), s32[]{:S(2)}) async-start(), calls=%async_computation.4 | async-start | bytes 3649536 | tf_op jit(solution)/shard_map/all_gather | solution.py:159
  13.5 35.1 %all-to-all-start = ((s32[32,2,1]{1,2,0:T(1,128)}), s32[32,2,1]{1,2,0:T(1,128)S(1)}, u32[]{:S(2)}, u32[]{:S(2)}) async-start(s32[32,2,1]{1,2,0:T(1,128)} %bitcast.16), calls=%async_computation | async-start | bytes 32768 | tf_op jit(solution)/shard_map/all_to_all | solution.py:197
  25.0 3.5 %copy-start.6 = (s32[36]{0:T(128)}, s32[36]{0:T(128)S(1)}, u32[]{:S(2)}) copy-start(s32[36]{0:T(128)S(1)} %multiply_add_fusion) | copy-start | bytes 436
  52.5 4.0 %copy-start.7 = (bf16[3072,384]{1,0:T(8,128)(2,1)S(1)}, bf16[3072,384]{1,0:T(8,128)(2,1)}, u32[]{:S(2)}) copy-start(bf16[3072,384]{1,0:T(8,128)(2,1)} %param.16) | copy-start | bytes 7077892
  56.6 1.7 copy-start.3
  82.6 85.4 %all-to-all-start.1 = ((bf16[64,128,384]{2,1,0:T(8,128)(2,1)}), bf16[64,128,384]{2,1,0:T(8,128)(2,1)}, u32[]{:S(2)}, u32[]{:S(2)}) async-start(bf16[64,128,384]{2,1,0:T(8,128)(2,1)} %get-tuple-element.34), calls=%async_computation.1 | async-start | bytes 12582912 | tf_op jit(solution)/shard_map/all_to_all | solution.py:212
  90.1 166.3 %reduce-scatter.2.cloned.1.call-start = ((), (), s32[]{:S(2)}) async-start(), calls=%async_computation.5 | async-start | bytes 7077888 | tf_op jit(solution)/shard_map/reduce_scatter | solution.py:240
  90.4 18.6 %copy-start.5 = (bf16[512,384]{1,0:T(8,128)(2,1)S(1)}, bf16[512,384]{1,0:T(8,128)(2,1)}, u32[]{:S(2)}) copy-start(bf16[512,384]{1,0:T(8,128)(2,1)} %convolution_convert_fusion.value_block) | copy-start | bytes 1179652
  118.8 18.2 %copy-start.1 = (pred[512,4608]{1,0:T(8,128)(4,1)S(1)}, pred[512,4608]{1,0:T(8,128)(4,1)}, u32[]{:S(2)}) copy-start(pred[512,4608]{1,0:T(8,128)(4,1)} %pad_add_fusion) | copy-start | bytes 7077892
  118.8 18.2 %copy-start.2 = (bf16[4608,384]{0,1:T(8,128)(2,1)S(1)}, bf16[4608,384]{0,1:T(8,128)(2,1)}, u32[]{:S(2)}) copy-start(bf16[4608,384]{0,1:T(8,128)(2,1)} %copy.41) | copy-start | bytes 10616836
  168.0 82.8 %all-to-all-start.2 = ((bf16[64,128,384]{2,1,0:T(8,128)(2,1)}), bf16[64,128,384]{2,1,0:T(8,128)(2,1)}, u32[]{:S(2)}, u32[]{:S(2)}) async-start(bf16[64,128,384]{2,1,0:T(8,128)(2,1)} %get-tuple-element.42), calls=%async_computation.3 | async-start | bytes 12582912 | tf_op jit(solution)/shard_map/all_to_all | solution.py:242
  250.9 5.6 %copy-start.4 = (bf16[512,384]{1,0:T(8,128)(2,1)S(1)}, bf16[512,384]{1,0:T(8,128)(2,1)}, u32[]{:S(2)}) copy-start(bf16[512,384]{1,0:T(8,128)(2,1)} %param.13) | copy-start | bytes 1179652
Sparse Core Ops, SparseCore 0:
  10.0 30.5 all-gather.1
  168.2 39.8 reduce-scatter.1

commit v9 on v8

--- a/solution.py
+++ b/solution.py
@@ -71,34 +71,38 @@
 def pack_pages(slots, keys, values, slot_total, into=()):
     page_total = keys.shape[0] // PAGE
     width = keys.shape[1]
+    split = PAGE // 2
 
     def body(slot_ref, key_block, value_block, *rest):
-        key_out, value_out = rest[-2:]
+        key_out, low_out, high_out = rest[-3:]
         key_out[0] = key_block[...]
-        value_out[0] = value_block[...]
+        low_out[0] = value_block[:split]
+        high_out[0] = value_block[split:]
 
     in_specs = [
         pl.BlockSpec((PAGE, width), lambda page, slot_ref: (page, 0)),
         pl.BlockSpec((PAGE, width), lambda page, slot_ref: (page, 0)),
     ] + [pl.BlockSpec(memory_space=pl.ANY)] * len(into)
-    half = jax.ShapeDtypeStruct((slot_total, PAGE, width), jnp.bfloat16)
-    out_spec = pl.BlockSpec((1, PAGE, width), lambda page, slot_ref: (slot_ref[page], 0, 0))
+    full = jax.ShapeDtypeStruct((slot_total, PAGE, width), jnp.bfloat16)
+    part = jax.ShapeDtypeStruct((slot_total, split, width), jnp.bfloat16)
+    full_spec = pl.BlockSpec((1, PAGE, width), lambda page, slot_ref: (slot_ref[page], 0, 0))
+    part_spec = pl.BlockSpec((1, split, width), lambda page, slot_ref: (slot_ref[page], 0, 0))
     return pl.pallas_call(
         body,
-        out_shape=(half, half),
+        out_shape=(full, part, part),
         grid_spec=pltpu.PrefetchScalarGridSpec(
             num_scalar_prefetch=1,
             grid=(page_total,),
             in_specs=in_specs,
-            out_specs=(out_spec, out_spec),
+            out_specs=(full_spec, part_spec, part_spec),
         ),
         input_output_aliases={3 + i: i for i in range(len(into))},
     )(slots, keys, values, *into)
 
 
-def place_pages(sources, ranks, received, slot_count, cores, part, into=(), group=6):
-    width = received.shape[-1]
-    shaped = received.reshape(-1, cores, CAPACITY, PAGE, width)
+def place_pages(sources, ranks, received, slot_count, cores, part, row_block, into=(), group=6):
+    rows, width = received.shape[-2:]
+    shaped = received.reshape(-1, cores, CAPACITY, rows, width)
 
     def body(src_ref, rank_ref, *refs):
         out = refs[-1]
@@ -116,7 +120,7 @@
         )
 
     in_specs = [
-        pl.BlockSpec((1, cores, 1, PAGE, width), source_map(member)) for member in range(group)
+        pl.BlockSpec((1, cores, 1, rows, width), source_map(member)) for member in range(group)
     ] + [pl.BlockSpec(memory_space=pl.ANY)] * len(into)
     return pl.pallas_call(
         body,
@@ -126,7 +130,8 @@
             grid=(slot_count // group,),
             in_specs=in_specs,
             out_specs=pl.BlockSpec(
-                (group, PAGE, cores * width), lambda step, src_ref, rank_ref: (step, 0, part)
+                (group, rows, cores * width),
+                lambda step, src_ref, rank_ref: (step, row_block, part),
             ),
         ),
         input_output_aliases={2 + group + i: 0 for i in range(len(into))},
@@ -188,7 +193,7 @@
     prev_pages = prev_count // PAGE
     send = pack_pages(send_slots[:prev_pages], prev_keys, prev_values, slot_total)
     send = pack_pages(send_slots[prev_pages:], new_keys, new_values, slot_total, into=send)
-    send_keys, send_values = send
+    send_keys, send_low, send_high = send
     carried = (
         jnp.full((slot_total,), slot_count, jnp.int32)
         .at[send_slots]
@@ -200,16 +205,18 @@
     found = jnp.argmax(carried[None, :] == wanted[:, None], axis=1).astype(jnp.int32)
     from_req = found // CAPACITY
     from_rank = found % CAPACITY
-    send_keys, send_values, normed, new_keys, new_values, from_req, from_rank = (
+    send_keys, send_low, send_high, normed, new_keys, new_values, from_req, from_rank = (
         lax.optimization_barrier(
-            (send_keys, send_values, normed, new_keys, new_values, from_req, from_rank)
+            (send_keys, send_low, send_high, normed, new_keys, new_values, from_req, from_rank)
         )
     )
     keys_all = jnp.concatenate([prev_keys, new_keys], axis=0)
     values_all = jnp.concatenate([prev_values, new_values], axis=0)
     query_raw = jnp.dot(normed, w_query, preferred_element_type=jnp.float32)
     queries = rotate(query_raw, positions, HD).astype(jnp.bfloat16)
-    received_keys = lax.all_to_all(send_keys, ("req", "core"), 0, 0, tiled=True)
+    received_keys, received_low = lax.all_to_all(
+        (send_keys, send_low), ("req", "core"), 0, 0, tiled=True
+    )
 
     allowed = visible(earlier, owners, prev_count, token_count)
     heads_here = local_width // HD
@@ -234,14 +241,15 @@
         (mixture / totals.T[:, :, None]).astype(jnp.bfloat16).reshape(token_count, local_width)
     )
     projected = jnp.dot(attended, w_out, preferred_element_type=jnp.float32)
-    received_keys, projected, send_values = lax.optimization_barrier(
-        (received_keys, projected, send_values)
+    received_keys, received_low, projected, send_high = lax.optimization_barrier(
+        (received_keys, received_low, projected, send_high)
     )
     summed = lax.psum_scatter(projected, ("y", "core"), scatter_dimension=1, tiled=True)
     layer_out = (tokens.astype(jnp.float32) + summed).astype(jnp.bfloat16)
-    received_values = lax.all_to_all(send_values, ("req", "core"), 0, 0, tiled=True)
-    pool = place_pages(from_req, from_rank, received_keys, slot_count, cores, 0)
-    pool = place_pages(from_req, from_rank, received_values, slot_count, cores, 1, into=(pool,))
+    received_high = lax.all_to_all(send_high, ("req", "core"), 0, 0, tiled=True)
+    pool = place_pages(from_req, from_rank, received_keys, slot_count, cores, 0, 0)
+    pool = place_pages(from_req, from_rank, received_low, slot_count, cores, 1, 0, into=(pool,))
+    pool = place_pages(from_req, from_rank, received_high, slot_count, cores, 1, 1, into=(pool,))
     return (layer_out, pool[:, None])
 
 

time: 267 us -> 260 us (0.974)
  waiting for transfers between devices: 83.5 us -> 67.5 us
  starting transfers between devices: 20.9 us -> 25.7 us
  Pallas kernels: 34.5 us -> 37.9 us
    all_to_all x2 -> x3, waiting for transfers between devices: 83.4 us -> 67.5 us  [the longest x2 35.7 us: shards(): lax.all_to_all((send_keys, send_low), ('req', 'core'), 0, 0, tiled=True)]
    all_to_all x2 -> x3, starting transfers between devices: 12.4 us -> 17.2 us  [the longest x2 12.3 us: shards(): lax.all_to_all((send_keys, send_low), ('req', 'core'), 0, 0, tiled=True)]
    pallas_call x2 -> x3, Pallas kernels: 11.2 us -> 14.5 us  [place_pages(): pl.pallas_call(body, out_shape=jax.ShapeDtypeStruct((slot_count, PAGE, 2...]
  transfers between devices with their start and end apart: 5 -> 6, of which waited for: 2 -> 3; matrix products, arithmetic and copies ran while one was open for 29% -> 36% of each run, Pallas kernels for 12% -> 13%
where the time goes in v9:
time: 260 us; the launch traced here: 257 us
  waiting for transfers between devices  67.5 us (26%)
  matrix products  49 us (19%)
  other arithmetic  47.1 us (18%)
  Pallas kernels  37.9 us (15%)
  starting transfers between devices  25.7 us (10%)
  local copies, waits for them, and re-layouts  15.9 us (6%)
  between operations  14.3 us (6%)
    all_to_all x2, waiting for transfers between devices, shards(): lax.all_to_all((send_keys, send_low), ('req', 'core'), 0, 0, tiled=True)  35.7 us
    all_to_all x1, waiting for transfers between devices, shards(): received_high = lax.all_to_all(send_high, ('req', 'core'), 0, 0, tiled=True)  31.8 us
    pallas_call x2, Pallas kernels, pack_pages(): pl.pallas_call(body, out_shape=(full, part, part), grid_spec=pltpu.Prefet...  23.4 us
    dot_general x1, matrix products, shards(): jnp.einsum('qhd,khd->hqk', queries.reshape(token_count, heads_here, HD),...  18.6 us
    reduce_sum x1, other arithmetic, shards(): totals = jnp.sum(weights, axis=2)  18.2 us
    dot_general x1, matrix products, shards(): jnp.einsum('hqk,khd->qhd', prob_rows, values_all.reshape(-1, heads_here,...  15.3 us
    pallas_call x3, Pallas kernels, place_pages(): pl.pallas_call(body, out_shape=jax.ShapeDtypeStruct((slot_count, PAGE, 2...  14.5 us
    all_to_all x2, starting transfers between devices, shards(): lax.all_to_all((send_keys, send_low), ('req', 'core'), 0, 0, tiled=True)  12.3 us
  transfers between devices with their start and end apart: 6, of which 3 were waited for; matrix products, arithmetic and copies ran while one was open for 36% of the time, Pallas kernels for 13%

profile of v9, /device:TPU:0, one launch (start us, length us, event | category | flops | bytes accessed | tf_op | source)
XLA Modules:
  0.0 257.4 jit_solution(8809291916111582663)
XLA Ops:
  13.5 8.2 %all-to-all-start = ((s32[32,2,1]{1,2,0:T(1,128)}), s32[32,2,1]{1,2,0:T(1,128)S(1)}, u32[]{:S(2)}, u32[]{:S(2)}) async-start(s32[32,2,1]{1,2,0:T(1,128)} %bitcast.16), calls=%async_computation | async-start | bytes 32768 | tf_op jit(solution)/shard_map/all_to_all | solution.py:202
  26.2 19.4 %shard_map.122 = (bf16[64,128,384]{2,1,0:T(8,128)(2,1)}, bf16[64,64,384]{2,1,0:T(8,128)(2,1)}, bf16[64,64,384]{2,1,0:T(8,128)(2,1)}) custom-call(s32[32]{0:T(128)} %bitcast.84, bf16[4096,384]{1,0:T(8,128)(2,1)} %key_block.1, bf16[4096,384]{1,0:T(8,128)(2,1)} %value_block.1), custom_call_target="tpu_custom_call" | custom-call | tf_op jit(solution)/shard_map/pallas_call | solution.py:90
  47.0 2.6 %fusion.6 = f32[512]{0:T(512)S(1)} fusion(bf16[528,3072]{1,0:T(8,128)(2,1)} %all-gather.2.cloned.1.call-done), kind=kLoop, calls=%fused_computation.11 | loop fusion | flops 4718080 | bytes 3147776 | tf_op jit(solution)/shard_map/reduce_sum | solution.py:170
  50.6 3.1 %fusion.8 = bf16[512,3072]{1,0:T(8,128)(2,1)S(1)} fusion(f32[3072]{0:T(1024)S(1)} %bitcast.81, f32[512]{0:T(512)S(1)} %add_rsqrt_fusion, bf16[528,3072]{1,0:T(8,128)(2,1)} %all-gather.2.cloned.1.call-done), kind=kLoop, calls=%fused_computation.13 | loop fusion | flops 6291456 | bytes 6305792 | tf_op jit(solution)/shard_map/convert_element_type | solution.py:171
  56.4 5.2 %convolution_convert_fusion.value_block = bf16[512,384]{1,0:T(8,128)(2,1)} fusion(bf16[512,3072]{1,0:T(8,128)(2,1)} %copy-done.3, bf16[3072,384]{1,0:T(8,128)(2,1)} %param.17), kind=kOutput, calls=%fused_computation.18 | convolution fusion | flops 1208156160 | bytes 5898240 | tf_op jit(solution)/shard_map/dot_general | solution.py:176
  61.5 4.0 %shard_map.123 = (bf16[64,128,384]{2,1,0:T(8,128)(2,1)}, bf16[64,64,384]{2,1,0:T(8,128)(2,1)}, bf16[64,64,384]{2,1,0:T(8,128)(2,1)}) custom-call(s32[4]{0:T(128)} %slice.41.slot_ref, bf16[512,384]{1,0:T(8,128)(2,1)} %copy.39.key_block, ...), custom_call_target="tpu_custom_call", output_to_operand_aliasing={{0}: (3, {}), {1}: (4, {}), {2}: (5, {})} | custom-call | tf_op jit(solution)/shard_map/pallas_call | solution.py:90
  65.5 7.4 %all-to-all-start.2 = ((bf16[64,64,384]{2,1,0:T(8,128)(2,1)}), bf16[64,64,384]{2,1,0:T(8,128)(2,1)}, u32[]{:S(2)}, u32[]{:S(2)}) async-start(bf16[64,64,384]{2,1,0:T(8,128)(2,1)} %get-tuple-element.41), calls=%async_computation.2 | async-start | bytes 6291456 | tf_op jit(solution)/shard_map/all_to_all | solution.py:217
  76.1 4.0 %pad_maximum_fusion.1 = bf16[4608,384]{1,0:T(8,128)(2,1)} fusion(bf16[512,384]{1,0:T(8,128)(2,1)S(1)} %copy.44, bf16[4096,384]{1,0:T(8,128)(2,1)} %key_block.1), kind=kLoop, calls=%fused_computation.16 | loop fusion | flops 7077888 | bytes 7077888 | tf_op jit(solution)/shard_map/concatenate | solution.py:213
  80.1 5.8 %copy.45 = bf16[4608,384]{0,1:T(8,128)(2,1)} copy(bf16[4608,384]{1,0:T(8,128)(2,1)} %pad_maximum_fusion.1) | data formatting | bytes 7077888 | tf_op jit(solution)/shard_map/concatenate | solution.py:213
  85.9 4.0 %fusion.37 = f32[512,384]{0,1:T(8,128)S(1)} fusion(bf16[512,3072]{1,0:T(8,128)(2,1)} %copy-done.3, bf16[3072,384]{1,0:T(8,128)(2,1)} %param.15), kind=kOutput, calls=%fused_computation.81 | convolution fusion | flops 1207959552 | bytes 6291456 | tf_op jit(solution)/shard_map/dot_general | solution.py:215
  90.1 24.6 %all-to-all-done.2 = bf16[64,64,384]{2,1,0:T(8,128)(2,1)} async-done(((bf16[64,64,384]{2,1,0:T(8,128)(2,1)}), bf16[64,64,384]{2,1,0:T(8,128)(2,1)}, u32[]{:S(2)}, u32[]{:S(2)}) %all-to-all-start.2) | async-done | bytes 3145760 | tf_op jit(solution)/shard_map/all_to_all | solution.py:217
  114.6 4.9 %all-to-all-start.1 = ((bf16[64,128,384]{2,1,0:T(8,128)(2,1)}), bf16[64,128,384]{2,1,0:T(8,128)(2,1)}, u32[]{:S(2)}, u32[]{:S(2)}) async-start(bf16[64,128,384]{2,1,0:T(8,128)(2,1)} %get-tuple-element.40), calls=%async_computation.1 | async-start | bytes 12582912 | tf_op jit(solution)/shard_map/all_to_all | solution.py:217
  119.8 18.6 %fusion = (f32[4,512]{1,0:T(4,128)S(1)}, f32[4,512,4608]{2,1,0:T(8,128)}) fusion(pred[512,4608]{1,0:T(8,128)(4,1)} %pad_add_fusion, bf16[4608,4,96]{0,2,1:T(8,128)(2,1)} %bitcast.74, bf16[512,4,48]{0,2,1:T(8,128)(2,1)S(1)} %get-tuple-element.65, bf16[512,4,48]{0,2,1:T(8,128)(2,1)S(1)} %get-tuple-element.64), kind=kOutput, calls=%fused_computation.3 | convolution fusion | flops 1841035264 | bytes 44048384 | tf_op jit(solution)/shard_map/qhd,khd->hqk/dot_general | solution.py:223
  138.4 4.0 %pad_maximum_fusion = bf16[4608,384]{1,0:T(8,128)(2,1)} fusion(bf16[512,384]{1,0:T(8,128)(2,1)S(1)} %copy-done.5, bf16[4096,384]{1,0:T(8,128)(2,1)} %value_block.1), kind=kLoop, calls=%fused_computation.15 | loop fusion | flops 7077888 | bytes 7077888 | tf_op jit(solution)/shard_map/concatenate | solution.py:214
  142.4 5.8 %copy.43 = bf16[4608,384]{0,1:T(8,128)(2,1)} copy(bf16[4608,384]{1,0:T(8,128)(2,1)} %pad_maximum_fusion) | data formatting | bytes 7077888 | tf_op jit(solution)/shard_map/concatenate | solution.py:214
  148.2 18.2 %fusion.1 = f32[4,512]{1,0:T(4,128)S(1)} fusion(f32[4,512,4608]{2,1,0:T(8,128)} %get-tuple-element.74, f32[4,512]{1,0:T(4,128)S(1)} %get-tuple-element.73, pred[512,4608]{1,0:T(8,128)(4,1)} %pad_add_fusion), kind=kLoop, calls=%fused_computation.4 | loop fusion | flops 37746688 | bytes 40124416 | tf_op jit(solution)/shard_map/reduce_sum | solution.py:232
  166.5 15.3 %fusion.15 = bf16[512,4,96]{0,2,1:T(8,128)(2,1)S(1)} fusion(bf16[4608,4,96]{0,2,1:T(8,128)(2,1)S(1)} %bitcast.75, f32[4,512,4608]{2,1,0:T(8,128)} %get-tuple-element.74, f32[4,512]{1,0:T(4,128)S(1)} %get-tuple-element.73, pred[512,4608]{1,0:T(8,128)(4,1)S(1)} %copy-done.1, f32[512,4]{0,1:T(4,128)S(1)} %bitcast.83), kind=kOutput, calls=%fused_computation.20 | convolution fusion | flops 1850081280 | bytes 44056576 | tf_op jit(solution)/shard_map/hqk,khd->qhd/dot_general | solution.py:234
  181.8 4.5 %fusion.38 = f32[512,3072]{1,0:T(8,128)} fusion(bf16[512,384]{0,1:T(8,128)(2,1)S(1)} %bitcast.80, bf16[384,3072]{1,0:T(8,128)(2,1)S(1)} %copy-done), kind=kOutput, calls=%fused_computation.82 | convolution fusion | flops 1207959552 | bytes 9043968 | tf_op jit(solution)/shard_map/dot_general | solution.py:243
  186.3 11.1 %all-to-all-done.1 = bf16[64,128,384]{2,1,0:T(8,128)(2,1)} async-done(((bf16[64,128,384]{2,1,0:T(8,128)(2,1)}), bf16[64,128,384]{2,1,0:T(8,128)(2,1)}, u32[]{:S(2)}, u32[]{:S(2)}) %all-to-all-start.1) | async-done | bytes 6291488 | tf_op jit(solution)/shard_map/all_to_all | solution.py:217
  197.5 4.8 %all-to-all-start.3 = ((bf16[64,64,384]{2,1,0:T(8,128)(2,1)}), bf16[64,64,384]{2,1,0:T(8,128)(2,1)}, u32[]{:S(2)}, u32[]{:S(2)}) async-start(bf16[64,64,384]{2,1,0:T(8,128)(2,1)} %get-tuple-element.49), calls=%async_computation.4 | async-start | bytes 6291456 | tf_op jit(solution)/shard_map/all_to_all | solution.py:249
  202.3 5.6 %shard_map.124.refs_6_ = bf16[18,128,1536]{2,1,0:T(8,128)(2,1)} custom-call(s32[18]{0:T(128)} %get-tuple-element.47.src_ref, s32[18]{0:T(128)} %get-tuple-element.48.rank_ref, bf16[16,2,2,128,384]{4,3,2,1,0:T(8,128)(2,1)} %bitcast.28.refs_0_.refs_1_.refs_2_.refs_3_.refs_4_.refs_5_, ...), custom_call_target="tpu_custom_call" | custom-call | tf_op jit(solution)/shard_map/pallas_call | solution.py:125
  208.0 4.4 %shard_map.125.refs_6_ = bf16[18,128,1536]{2,1,0:T(8,128)(2,1)} custom-call(s32[18]{0:T(128)} %get-tuple-element.47.src_ref, s32[18]{0:T(128)} %get-tuple-element.48.rank_ref, bf16[16,2,2,64,384]{4,3,2,1,0:T(8,128)(2,1)} %bitcast.27.refs_0_.refs_1_.refs_2_.refs_3_.refs_4_.refs_5_, ...), custom_call_target="tpu_custom_call", output_to_operand_aliasing={{}: (8, {})} | custom-call | tf_op jit(solution)/shard_map/pallas_call | solution.py:125
  212.3 31.8 %all-to-all-done.3 = bf16[64,64,384]{2,1,0:T(8,128)(2,1)} async-done(((bf16[64,64,384]{2,1,0:T(8,128)(2,1)}), bf16[64,64,384]{2,1,0:T(8,128)(2,1)}, u32[]{:S(2)}, u32[]{:S(2)}) %all-to-all-start.3) | async-done | bytes 3145760 | tf_op jit(solution)/shard_map/all_to_all | solution.py:249
  244.1 4.5 %shard_map.126 = bf16[18,128,1536]{2,1,0:T(8,128)(2,1)} custom-call(s32[18]{0:T(128)} %get-tuple-element.47.src_ref, s32[18]{0:T(128)} %get-tuple-element.48.rank_ref, bf16[16,2,2,64,384]{4,3,2,1,0:T(8,128)(2,1)} %bitcast.26.refs_0_.refs_1_.refs_2_.refs_3_.refs_4_.refs_5_, ...), custom_call_target="tpu_custom_call", output_to_operand_aliasing={{}: (8, {})} | custom-call | tf_op jit(solution)/shard_map/pallas_call | solution.py:125
  (58 shorter events, 21.3 us)
Async XLA Ops:
  7.2 174.7 %copy-start = (bf16[384,3072]{1,0:T(8,128)(2,1)S(1)}, bf16[384,3072]{1,0:T(8,128)(2,1)}, u32[]{:S(2)}) copy-start(bf16[384,3072]{1,0:T(8,128)(2,1)} %param.18) | copy-start | bytes 7077892
  7.2 39.8 %all-gather.2.cloned.1.call-start = ((), (), s32[]{:S(2)}) async-start(), calls=%async_computation.5 | async-start | bytes 3649536 | tf_op jit(solution)/shard_map/all_gather | solution.py:164
  13.5 32.2 %all-to-all-start = ((s32[32,2,1]{1,2,0:T(1,128)}), s32[32,2,1]{1,2,0:T(1,128)S(1)}, u32[]{:S(2)}, u32[]{:S(2)}) async-start(s32[32,2,1]{1,2,0:T(1,128)} %bitcast.16), calls=%async_computation | async-start | bytes 32768 | tf_op jit(solution)/shard_map/all_to_all | solution.py:202
  21.8 4.5 %copy-start.6 = (s32[36]{0:T(128)}, s32[36]{0:T(128)S(1)}, u32[]{:S(2)}) copy-start(s32[36]{0:T(128)S(1)} %multiply_add_fusion) | copy-start | bytes 436
  49.6 4.0 %copy-start.7 = (bf16[3072,384]{1,0:T(8,128)(2,1)S(1)}, bf16[3072,384]{1,0:T(8,128)(2,1)}, u32[]{:S(2)}) copy-start(bf16[3072,384]{1,0:T(8,128)(2,1)} %param.16) | copy-start | bytes 7077892
  53.6 1.6 copy-start.3
  65.5 49.2 %all-to-all-start.2 = ((bf16[64,64,384]{2,1,0:T(8,128)(2,1)}), bf16[64,64,384]{2,1,0:T(8,128)(2,1)}, u32[]{:S(2)}, u32[]{:S(2)}) async-start(bf16[64,64,384]{2,1,0:T(8,128)(2,1)} %get-tuple-element.41), calls=%async_computation.2 | async-start | bytes 6291456 | tf_op jit(solution)/shard_map/all_to_all | solution.py:217
  114.6 82.8 %all-to-all-start.1 = ((bf16[64,128,384]{2,1,0:T(8,128)(2,1)}), bf16[64,128,384]{2,1,0:T(8,128)(2,1)}, u32[]{:S(2)}, u32[]{:S(2)}) async-start(bf16[64,128,384]{2,1,0:T(8,128)(2,1)} %get-tuple-element.40), calls=%async_computation.1 | async-start | bytes 12582912 | tf_op jit(solution)/shard_map/all_to_all | solution.py:217
  119.6 129.0 %reduce-scatter.2.cloned.1.call-start = ((), (), s32[]{:S(2)}) async-start(), calls=%async_computation.6 | async-start | bytes 7077888 | tf_op jit(solution)/shard_map/reduce_scatter | solution.py:247
  119.8 18.6 %copy-start.5 = (bf16[512,384]{1,0:T(8,128)(2,1)S(1)}, bf16[512,384]{1,0:T(8,128)(2,1)}, u32[]{:S(2)}) copy-start(bf16[512,384]{1,0:T(8,128)(2,1)} %convolution_convert_fusion.value_block) | copy-start | bytes 1179652
  148.2 18.2 %copy-start.1 = (pred[512,4608]{1,0:T(8,128)(4,1)S(1)}, pred[512,4608]{1,0:T(8,128)(4,1)}, u32[]{:S(2)}) copy-start(pred[512,4608]{1,0:T(8,128)(4,1)} %pad_add_fusion) | copy-start | bytes 7077892
  148.2 18.2 %copy-start.2 = (bf16[4608,384]{0,1:T(8,128)(2,1)S(1)}, bf16[4608,384]{0,1:T(8,128)(2,1)}, u32[]{:S(2)}) copy-start(bf16[4608,384]{0,1:T(8,128)(2,1)} %copy.43) | copy-start | bytes 10616836
  197.5 46.6 %all-to-all-start.3 = ((bf16[64,64,384]{2,1,0:T(8,128)(2,1)}), bf16[64,64,384]{2,1,0:T(8,128)(2,1)}, u32[]{:S(2)}, u32[]{:S(2)}) async-start(bf16[64,64,384]{2,1,0:T(8,128)(2,1)} %get-tuple-element.49), calls=%async_computation.4 | async-start | bytes 6291456 | tf_op jit(solution)/shard_map/all_to_all | solution.py:249
  244.1 4.5 %copy-start.4 = (bf16[512,384]{1,0:T(8,128)(2,1)S(1)}, bf16[512,384]{1,0:T(8,128)(2,1)}, u32[]{:S(2)}) copy-start(bf16[512,384]{1,0:T(8,128)(2,1)} %param.13) | copy-start | bytes 1179652
Sparse Core Ops, SparseCore 0:
  10.0 30.5 all-gather.1
  197.6 39.8 reduce-scatter.1

commit v10 on v9

--- a/solution.py
+++ b/solution.py
@@ -68,36 +68,35 @@
     return jnp.sum(same * earlier_mask, axis=-1)
 
 
-def pack_pages(slots, keys, values, slot_total, into=()):
-    page_total = keys.shape[0] // PAGE
-    width = keys.shape[1]
-    split = PAGE // 2
-
-    def body(slot_ref, key_block, value_block, *rest):
-        key_out, low_out, high_out = rest[-3:]
-        key_out[0] = key_block[...]
-        low_out[0] = value_block[:split]
-        high_out[0] = value_block[split:]
-
-    in_specs = [
-        pl.BlockSpec((PAGE, width), lambda page, slot_ref: (page, 0)),
-        pl.BlockSpec((PAGE, width), lambda page, slot_ref: (page, 0)),
-    ] + [pl.BlockSpec(memory_space=pl.ANY)] * len(into)
-    full = jax.ShapeDtypeStruct((slot_total, PAGE, width), jnp.bfloat16)
-    part = jax.ShapeDtypeStruct((slot_total, split, width), jnp.bfloat16)
-    full_spec = pl.BlockSpec((1, PAGE, width), lambda page, slot_ref: (slot_ref[page], 0, 0))
-    part_spec = pl.BlockSpec((1, split, width), lambda page, slot_ref: (slot_ref[page], 0, 0))
+def pack_pages(slots, source, parts, slot_total, into=()):
+    page_total = source.shape[0] // PAGE
+    width = source.shape[1]
+
+    def body(slot_ref, block, *rest):
+        outs = rest[len(rest) - len(parts) :]
+        for out, (start, rows) in zip(outs, parts):
+            out[0] = block[start : start + rows]
+
+    in_specs = [pl.BlockSpec((PAGE, width), lambda page, slot_ref: (page, 0))]
+    in_specs += [pl.BlockSpec(memory_space=pl.ANY)] * len(into)
+    out_shape = tuple(
+        jax.ShapeDtypeStruct((slot_total, rows, width), jnp.bfloat16) for _, rows in parts
+    )
+    out_specs = tuple(
+        pl.BlockSpec((1, rows, width), lambda page, slot_ref: (slot_ref[page], 0, 0))
+        for _, rows in parts
+    )
     return pl.pallas_call(
         body,
-        out_shape=(full, part, part),
+        out_shape=out_shape,
         grid_spec=pltpu.PrefetchScalarGridSpec(
             num_scalar_prefetch=1,
             grid=(page_total,),
             in_specs=in_specs,
-            out_specs=(full_spec, part_spec, part_spec),
+            out_specs=out_specs,
         ),
-        input_output_aliases={3 + i: i for i in range(len(into))},
-    )(slots, keys, values, *into)
+        input_output_aliases={2 + i: i for i in range(len(into))},
+    )(slots, source, *into)
 
 
 def place_pages(sources, ranks, received, slot_count, cores, part, row_block, into=(), group=6):
@@ -171,16 +170,10 @@
     normed = (widened * lax.rsqrt(mean_square + EPSILON) * full_gain.astype(jnp.float32)[None, :]).astype(
         jnp.bfloat16
     )
-    key_raw, value_raw = tuple(
-        (
-            jnp.dot(normed, weight, preferred_element_type=jnp.float32)
-            for weight in (w_key, w_value)
-        )
-    )
+    value_raw = jnp.dot(normed, w_value, preferred_element_type=jnp.float32)
     earlier = earlier_lengths[0]
     fresh = new_lengths[0]
     owners, positions = block_layout(earlier, fresh, token_count)
-    new_keys = rotate(key_raw, positions, HD).astype(jnp.bfloat16)
     new_values = value_raw.astype(jnp.bfloat16)
 
     page_total = (prev_count + token_count) // PAGE
@@ -191,9 +184,13 @@
     own_ranks = rank_in_dest(own_dests)
     send_slots = (own_dests * CAPACITY + own_ranks).astype(jnp.int32)
     prev_pages = prev_count // PAGE
-    send = pack_pages(send_slots[:prev_pages], prev_keys, prev_values, slot_total)
-    send = pack_pages(send_slots[prev_pages:], new_keys, new_values, slot_total, into=send)
-    send_keys, send_low, send_high = send
+    whole = ((0, PAGE),)
+    halves = ((0, PAGE // 2), (PAGE // 2, PAGE // 2))
+    (send_keys,) = pack_pages(send_slots[:prev_pages], prev_keys, whole, slot_total)
+    send_low, send_high = pack_pages(send_slots[:prev_pages], prev_values, halves, slot_total)
+    send_low, send_high = pack_pages(
+        send_slots[prev_pages:], new_values, halves, slot_total, into=(send_low, send_high)
+    )
     carried = (
         jnp.full((slot_total,), slot_count, jnp.int32)
         .at[send_slots]
@@ -205,18 +202,22 @@
     found = jnp.argmax(carried[None, :] == wanted[:, None], axis=1).astype(jnp.int32)
     from_req = found // CAPACITY
     from_rank = found % CAPACITY
-    send_keys, send_low, send_high, normed, new_keys, new_values, from_req, from_rank = (
+    send_keys, send_low, send_high, normed, new_values, from_req, from_rank = (
         lax.optimization_barrier(
-            (send_keys, send_low, send_high, normed, new_keys, new_values, from_req, from_rank)
+            (send_keys, send_low, send_high, normed, new_values, from_req, from_rank)
         )
+    )
+    received_low = lax.all_to_all(send_low, ("req", "core"), 0, 0, tiled=True)
+    key_raw = jnp.dot(normed, w_key, preferred_element_type=jnp.float32)
+    new_keys = rotate(key_raw, positions, HD).astype(jnp.bfloat16)
+    (send_keys,) = pack_pages(
+        send_slots[prev_pages:], new_keys, whole, slot_total, into=(send_keys,)
     )
     keys_all = jnp.concatenate([prev_keys, new_keys], axis=0)
     values_all = jnp.concatenate([prev_values, new_values], axis=0)
     query_raw = jnp.dot(normed, w_query, preferred_element_type=jnp.float32)
     queries = rotate(query_raw, positions, HD).astype(jnp.bfloat16)
-    received_keys, received_low = lax.all_to_all(
-        (send_keys, send_low), ("req", "core"), 0, 0, tiled=True
-    )
+    received_keys = lax.all_to_all(send_keys, ("req", "core"), 0, 0, tiled=True)
 
     allowed = visible(earlier, owners, prev_count, token_count)
     heads_here = local_width // HD

time: 260 us -> 274 us (1.054)
  Pallas kernels: 37.9 us -> 58.5 us
  waiting for transfers between devices: 67.5 us -> 61.4 us
  matrix products: 49 us -> 45.6 us
  other arithmetic: 47.1 us -> 49.9 us
    pallas_call x2 -> x4, Pallas kernels: 23.4 us -> 44.1 us  [pack_pages(): pl.pallas_call(body, out_shape=out_shape, grid_spec=pltpu.PrefetchScalarG...]
    all_to_all x2, waiting for transfers between devices: 35.7 us -> 29.6 us  [the longest x1 18.4 us: shards(): received_low = lax.all_to_all(send_low, ('req', 'core'), 0, 0, tiled=True)]
  transfers between devices with their start and end apart: 6 -> 6, of which waited for: 3 -> 3; matrix products, arithmetic and copies ran while one was open for 36% -> 36% of each run, Pallas kernels for 13% -> 20%
where the time goes in v10:
time: 274 us; the launch traced here: 271 us
  waiting for transfers between devices  61.4 us (22%)
  Pallas kernels  58.5 us (21%)
  other arithmetic  49.9 us (18%)
  matrix products  45.6 us (17%)
  starting transfers between devices  25.7 us (9%)
  local copies, waits for them, and re-layouts  15.5 us (6%)
  between operations  14.3 us (5%)
    pallas_call x4, Pallas kernels, pack_pages(): pl.pallas_call(body, out_shape=out_shape, grid_spec=pltpu.PrefetchScalarG...  44.1 us
    all_to_all x1, waiting for transfers between devices, shards(): received_high = lax.all_to_all(send_high, ('req', 'core'), 0, 0, tiled=True)  31.8 us
    dot_general x1, matrix products, shards(): jnp.einsum('qhd,khd->hqk', queries.reshape(token_count, heads_here, HD),...  18.6 us
    all_to_all x1, waiting for transfers between devices, shards(): received_low = lax.all_to_all(send_low, ('req', 'core'), 0, 0, tiled=True)  18.4 us
    reduce_sum x1, other arithmetic, shards(): totals = jnp.sum(weights, axis=2)  18.2 us
    dot_general x1, matrix products, shards(): jnp.einsum('hqk,khd->qhd', prob_rows, values_all.reshape(-1, heads_here,...  15.3 us
    pallas_call x3, Pallas kernels, place_pages(): pl.pallas_call(body, out_shape=jax.ShapeDtypeStruct((slot_count, PAGE, 2...  14.5 us
    all_to_all x1, waiting for transfers between devices, shards(): received_keys = lax.all_to_all(send_keys, ('req', 'core'), 0, 0, tiled=True)  11.1 us
  transfers between devices with their start and end apart: 6, of which 3 were waited for; matrix products, arithmetic and copies ran while one was open for 36% of the time, Pallas kernels for 20%

profile of v10, /device:TPU:0, one launch (start us, length us, event | category | flops | bytes accessed | tf_op | source)
XLA Modules:
  0.0 270.9 jit_solution(3052948135323184086)
XLA Ops:
  13.5 8.2 %all-to-all-start = ((s32[32,2,1]{1,2,0:T(1,128)}), s32[32,2,1]{1,2,0:T(1,128)S(1)}, u32[]{:S(2)}, u32[]{:S(2)}) async-start(s32[32,2,1]{1,2,0:T(1,128)} %bitcast.9), calls=%async_computation | async-start | bytes 32768 | tf_op jit(solution)/shard_map/all_to_all | solution.py:199
  28.3 18.2 %shard_map.122.rest_0_ = bf16[64,128,384]{2,1,0:T(8,128)(2,1)} custom-call(s32[32]{0:T(128)} %bitcast.84, bf16[4096,384]{1,0:T(8,128)(2,1)} %block.2), custom_call_target="tpu_custom_call" | custom-call | tf_op jit(solution)/shard_map/pallas_call | solution.py:89
  46.5 18.2 %shard_map.123 = (bf16[64,64,384]{2,1,0:T(8,128)(2,1)}, bf16[64,64,384]{2,1,0:T(8,128)(2,1)}) custom-call(s32[32]{0:T(128)} %bitcast.85, bf16[4096,384]{1,0:T(8,128)(2,1)} %block.3), custom_call_target="tpu_custom_call" | custom-call | tf_op jit(solution)/shard_map/pallas_call | solution.py:89
  69.6 3.1 %fusion.8 = bf16[512,3072]{1,0:T(8,128)(2,1)S(1)} fusion(f32[3072]{0:T(1024)S(1)} %bitcast.81, f32[512]{0:T(512)S(1)} %add_rsqrt_fusion, bf16[528,3072]{1,0:T(8,128)(2,1)} %all-gather.2.cloned.1.call-done), kind=kLoop, calls=%fused_computation.13 | loop fusion | flops 6291456 | bytes 6305792 | tf_op jit(solution)/shard_map/convert_element_type | solution.py:170
  75.2 3.8 %shard_map.124 = (bf16[64,64,384]{2,1,0:T(8,128)(2,1)}, bf16[64,64,384]{2,1,0:T(8,128)(2,1)}) custom-call(s32[4]{0:T(128)} %slice.43.slot_ref, bf16[512,384]{1,0:T(8,128)(2,1)} %convolution_convert_fusion.block, bf16[64,64,384]{2,1,0:T(8,128)(2,1)} %get-tuple-element.30.rest_0_, ...), custom_call_target="tpu_custom_call", output_to_operand_aliasing={{0}: (2, {}), {1}: (3, {})} | custom-call | tf_op jit(solution)/shard_map/pallas_call | solution.py:89
  79.0 7.5 %all-to-all-start.2 = ((bf16[64,64,384]{2,1,0:T(8,128)(2,1)}), bf16[64,64,384]{2,1,0:T(8,128)(2,1)}, u32[]{:S(2)}, u32[]{:S(2)}) async-start(bf16[64,64,384]{2,1,0:T(8,128)(2,1)} %get-tuple-element.37), calls=%async_computation.2 | async-start | bytes 6291456 | tf_op jit(solution)/shard_map/all_to_all | solution.py:210
  90.1 3.2 %fusion.37 = f32[512,384]{0,1:T(8,128)S(1)} fusion(bf16[512,3072]{1,0:T(8,128)(2,1)S(1)} %copy-done.5, bf16[3072,384]{1,0:T(8,128)(2,1)} %param.15), kind=kOutput, calls=%fused_computation.81 | convolution fusion | flops 1207959552 | bytes 6291456 | tf_op jit(solution)/shard_map/dot_general | solution.py:218
  96.0 3.9 %shard_map.125 = bf16[64,128,384]{2,1,0:T(8,128)(2,1)} custom-call(s32[4]{0:T(128)} %slice.43.slot_ref, bf16[512,384]{1,0:T(8,128)(2,1)} %copy.42.block, bf16[64,128,384]{2,1,0:T(8,128)(2,1)} %shard_map.122.rest_0_), custom_call_target="tpu_custom_call", output_to_operand_aliasing={{}: (2, {})} | custom-call | tf_op jit(solution)/shard_map/pallas_call | solution.py:89
  99.9 4.0 %pad_maximum_fusion.1 = bf16[4608,384]{1,0:T(8,128)(2,1)} fusion(bf16[512,384]{1,0:T(8,128)(2,1)S(1)} %copy-done.2, bf16[4096,384]{1,0:T(8,128)(2,1)} %block.2), kind=kLoop, calls=%fused_computation.16 | loop fusion | flops 7077888 | bytes 7077888 | tf_op jit(solution)/shard_map/concatenate | solution.py:216
  103.9 5.8 %copy.45 = bf16[4608,384]{0,1:T(8,128)(2,1)} copy(bf16[4608,384]{1,0:T(8,128)(2,1)} %pad_maximum_fusion.1) | data formatting | bytes 7077888 | tf_op jit(solution)/shard_map/concatenate | solution.py:216
  109.7 18.4 %all-to-all-done.2 = bf16[64,64,384]{2,1,0:T(8,128)(2,1)} async-done(((bf16[64,64,384]{2,1,0:T(8,128)(2,1)}), bf16[64,64,384]{2,1,0:T(8,128)(2,1)}, u32[]{:S(2)}, u32[]{:S(2)}) %all-to-all-start.2) | async-done | bytes 3145760 | tf_op jit(solution)/shard_map/all_to_all | solution.py:210
  128.2 4.9 %all-to-all-start.1 = ((bf16[64,128,384]{2,1,0:T(8,128)(2,1)}), bf16[64,128,384]{2,1,0:T(8,128)(2,1)}, u32[]{:S(2)}, u32[]{:S(2)}) async-start(bf16[64,128,384]{2,1,0:T(8,128)(2,1)} %shard_map.125), calls=%async_computation.1 | async-start | bytes 12582912 | tf_op jit(solution)/shard_map/all_to_all | solution.py:220
  133.3 18.6 %fusion = (f32[4,512]{1,0:T(4,128)S(1)}, f32[4,512,4608]{2,1,0:T(8,128)}) fusion(pred[512,4608]{1,0:T(8,128)(4,1)} %pad_add_fusion, bf16[4608,4,96]{0,2,1:T(8,128)(2,1)} %bitcast.75, bf16[512,4,48]{0,2,1:T(8,128)(2,1)S(1)} %get-tuple-element.59, bf16[512,4,48]{0,2,1:T(8,128)(2,1)S(1)} %get-tuple-element.58), kind=kOutput, calls=%fused_computation.3 | convolution fusion | flops 1841035264 | bytes 44048384 | tf_op jit(solution)/shard_map/qhd,khd->hqk/dot_general | solution.py:224
  151.9 4.0 %pad_maximum_fusion = bf16[4608,384]{1,0:T(8,128)(2,1)} fusion(bf16[512,384]{1,0:T(8,128)(2,1)S(1)} %copy-done.7, bf16[4096,384]{1,0:T(8,128)(2,1)} %block.3), kind=kLoop, calls=%fused_computation.15 | loop fusion | flops 7077888 | bytes 7077888 | tf_op jit(solution)/shard_map/concatenate | solution.py:217
  156.0 5.8 %copy.43 = bf16[4608,384]{0,1:T(8,128)(2,1)} copy(bf16[4608,384]{1,0:T(8,128)(2,1)} %pad_maximum_fusion) | data formatting | bytes 7077888 | tf_op jit(solution)/shard_map/concatenate | solution.py:217
  161.8 18.2 %fusion.1 = f32[4,512]{1,0:T(4,128)S(1)} fusion(f32[4,512,4608]{2,1,0:T(8,128)} %get-tuple-element.70, f32[4,512]{1,0:T(4,128)S(1)} %get-tuple-element.69, pred[512,4608]{1,0:T(8,128)(4,1)} %pad_add_fusion), kind=kLoop, calls=%fused_computation.4 | loop fusion | flops 37746688 | bytes 40124416 | tf_op jit(solution)/shard_map/reduce_sum | solution.py:233
  180.0 15.3 %fusion.15 = bf16[512,4,96]{0,2,1:T(8,128)(2,1)S(1)} fusion(bf16[4608,4,96]{0,2,1:T(8,128)(2,1)S(1)} %bitcast.76, f32[4,512,4608]{2,1,0:T(8,128)} %get-tuple-element.70, f32[4,512]{1,0:T(4,128)S(1)} %get-tuple-element.69, pred[512,4608]{1,0:T(8,128)(4,1)S(1)} %copy-done.1, f32[512,4]{0,1:T(4,128)S(1)} %bitcast.83), kind=kOutput, calls=%fused_computation.20 | convolution fusion | flops 1850081280 | bytes 44056576 | tf_op jit(solution)/shard_map/hqk,khd->qhd/dot_general | solution.py:235
  195.4 4.5 %fusion.38 = f32[512,3072]{1,0:T(8,128)} fusion(bf16[512,384]{0,1:T(8,128)(2,1)S(1)} %bitcast.80, bf16[384,3072]{1,0:T(8,128)(2,1)S(1)} %copy-done), kind=kOutput, calls=%fused_computation.82 | convolution fusion | flops 1207959552 | bytes 9043968 | tf_op jit(solution)/shard_map/dot_general | solution.py:244
  199.9 11.1 %all-to-all-done.1 = bf16[64,128,384]{2,1,0:T(8,128)(2,1)} async-done(((bf16[64,128,384]{2,1,0:T(8,128)(2,1)}), bf16[64,128,384]{2,1,0:T(8,128)(2,1)}, u32[]{:S(2)}, u32[]{:S(2)}) %all-to-all-start.1) | async-done | bytes 6291488 | tf_op jit(solution)/shard_map/all_to_all | solution.py:220
  211.0 4.8 %all-to-all-start.3 = ((bf16[64,64,384]{2,1,0:T(8,128)(2,1)}), bf16[64,64,384]{2,1,0:T(8,128)(2,1)}, u32[]{:S(2)}, u32[]{:S(2)}) async-start(bf16[64,64,384]{2,1,0:T(8,128)(2,1)} %get-tuple-element.43), calls=%async_computation.4 | async-start | bytes 6291456 | tf_op jit(solution)/shard_map/all_to_all | solution.py:250
  215.9 5.6 %shard_map.126.refs_6_ = bf16[18,128,1536]{2,1,0:T(8,128)(2,1)} custom-call(s32[18]{0:T(128)} %get-tuple-element.41.src_ref, s32[18]{0:T(128)} %get-tuple-element.42.rank_ref, bf16[16,2,2,128,384]{4,3,2,1,0:T(8,128)(2,1)} %bitcast.28.refs_0_.refs_1_.refs_2_.refs_3_.refs_4_.refs_5_, ...), custom_call_target="tpu_custom_call" | custom-call | tf_op jit(solution)/shard_map/pallas_call | solution.py:124
  221.5 4.4 %shard_map.127.refs_6_ = bf16[18,128,1536]{2,1,0:T(8,128)(2,1)} custom-call(s32[18]{0:T(128)} %get-tuple-element.41.src_ref, s32[18]{0:T(128)} %get-tuple-element.42.rank_ref, bf16[16,2,2,64,384]{4,3,2,1,0:T(8,128)(2,1)} %bitcast.27.refs_0_.refs_1_.refs_2_.refs_3_.refs_4_.refs_5_, ...), custom_call_target="tpu_custom_call", output_to_operand_aliasing={{}: (8, {})} | custom-call | tf_op jit(solution)/shard_map/pallas_call | solution.py:124
  225.9 31.8 %all-to-all-done.3 = bf16[64,64,384]{2,1,0:T(8,128)(2,1)} async-done(((bf16[64,64,384]{2,1,0:T(8,128)(2,1)}), bf16[64,64,384]{2,1,0:T(8,128)(2,1)}, u32[]{:S(2)}, u32[]{:S(2)}) %all-to-all-start.3) | async-done | bytes 3145760 | tf_op jit(solution)/shard_map/all_to_all | solution.py:250
  257.6 4.5 %shard_map.128 = bf16[18,128,1536]{2,1,0:T(8,128)(2,1)} custom-call(s32[18]{0:T(128)} %get-tuple-element.41.src_ref, s32[18]{0:T(128)} %get-tuple-element.42.rank_ref, bf16[16,2,2,64,384]{4,3,2,1,0:T(8,128)(2,1)} %bitcast.26.refs_0_.refs_1_.refs_2_.refs_3_.refs_4_.refs_5_, ...), custom_call_target="tpu_custom_call", output_to_operand_aliasing={{}: (8, {})} | custom-call | tf_op jit(solution)/shard_map/pallas_call | solution.py:124
  (64 shorter events, 28.8 us)
Async XLA Ops:
  7.2 188.2 %copy-start = (bf16[384,3072]{1,0:T(8,128)(2,1)S(1)}, bf16[384,3072]{1,0:T(8,128)(2,1)}, u32[]{:S(2)}) copy-start(bf16[384,3072]{1,0:T(8,128)(2,1)} %param.18) | copy-start | bytes 7077892
  7.2 58.8 %all-gather.2.cloned.1.call-start = ((), (), s32[]{:S(2)}) async-start(), calls=%async_computation.5 | async-start | bytes 3649536 | tf_op jit(solution)/shard_map/all_gather | solution.py:163
  13.5 51.2 %all-to-all-start = ((s32[32,2,1]{1,2,0:T(1,128)}), s32[32,2,1]{1,2,0:T(1,128)S(1)}, u32[]{:S(2)}, u32[]{:S(2)}) async-start(s32[32,2,1]{1,2,0:T(1,128)} %bitcast.9), calls=%async_computation | async-start | bytes 32768 | tf_op jit(solution)/shard_map/all_to_all | solution.py:199
  23.4 4.9 %copy-start.8 = (s32[36]{0:T(128)}, s32[36]{0:T(128)S(1)}, u32[]{:S(2)}) copy-start(s32[36]{0:T(128)S(1)} %multiply_add_fusion) | copy-start | bytes 436
  68.6 4.0 %copy-start.9 = (bf16[3072,384]{1,0:T(8,128)(2,1)S(1)}, bf16[3072,384]{1,0:T(8,128)(2,1)}, u32[]{:S(2)}) copy-start(bf16[3072,384]{1,0:T(8,128)(2,1)} %param.17) | copy-start | bytes 7077892
  72.6 2.5 copy-start.4
  79.0 49.2 %all-to-all-start.2 = ((bf16[64,64,384]{2,1,0:T(8,128)(2,1)}), bf16[64,64,384]{2,1,0:T(8,128)(2,1)}, u32[]{:S(2)}, u32[]{:S(2)}) async-start(bf16[64,64,384]{2,1,0:T(8,128)(2,1)} %get-tuple-element.37), calls=%async_computation.2 | async-start | bytes 6291456 | tf_op jit(solution)/shard_map/all_to_all | solution.py:210
  86.4 3.7 %copy-start.5 = (bf16[512,3072]{1,0:T(8,128)(2,1)S(1)}, bf16[512,3072]{1,0:T(8,128)(2,1)}, u32[]{:S(2)}) copy-start(bf16[512,3072]{1,0:T(8,128)(2,1)} %copy-done.4) | copy-start | bytes 9437188
  90.1 3.3 %copy-start.10 = (bf16[3072,384]{1,0:T(8,128)(2,1)S(1)}, bf16[3072,384]{1,0:T(8,128)(2,1)}, u32[]{:S(2)}) copy-start(bf16[3072,384]{1,0:T(8,128)(2,1)} %param.16) | copy-start | bytes 7077892
  96.0 3.9 %copy-start.2 = (bf16[512,384]{1,0:T(8,128)(2,1)S(1)}, bf16[512,384]{1,0:T(8,128)(2,1)}, u32[]{:S(2)}) copy-start(bf16[512,384]{1,0:T(8,128)(2,1)} %copy.42.block) | copy-start | bytes 1179652
  128.2 82.8 %all-to-all-start.1 = ((bf16[64,128,384]{2,1,0:T(8,128)(2,1)}), bf16[64,128,384]{2,1,0:T(8,128)(2,1)}, u32[]{:S(2)}, u32[]{:S(2)}) async-start(bf16[64,128,384]{2,1,0:T(8,128)(2,1)} %shard_map.125), calls=%async_computation.1 | async-start | bytes 12582912 | tf_op jit(solution)/shard_map/all_to_all | solution.py:220
  133.1 129.0 %reduce-scatter.2.cloned.1.call-start = ((), (), s32[]{:S(2)}) async-start(), calls=%async_computation.6 | async-start | bytes 7077888 | tf_op jit(solution)/shard_map/reduce_scatter | solution.py:248
  133.3 18.6 %copy-start.7 = (bf16[512,384]{1,0:T(8,128)(2,1)S(1)}, bf16[512,384]{1,0:T(8,128)(2,1)}, u32[]{:S(2)}) copy-start(bf16[512,384]{1,0:T(8,128)(2,1)} %convolution_convert_fusion.block) | copy-start | bytes 1179652
  161.8 18.2 %copy-start.1 = (pred[512,4608]{1,0:T(8,128)(4,1)S(1)}, pred[512,4608]{1,0:T(8,128)(4,1)}, u32[]{:S(2)}) copy-start(pred[512,4608]{1,0:T(8,128)(4,1)} %pad_add_fusion) | copy-start | bytes 7077892
  161.8 18.2 %copy-start.3 = (bf16[4608,384]{0,1:T(8,128)(2,1)S(1)}, bf16[4608,384]{0,1:T(8,128)(2,1)}, u32[]{:S(2)}) copy-start(bf16[4608,384]{0,1:T(8,128)(2,1)} %copy.43) | copy-start | bytes 10616836
  211.0 46.6 %all-to-all-start.3 = ((bf16[64,64,384]{2,1,0:T(8,128)(2,1)}), bf16[64,64,384]{2,1,0:T(8,128)(2,1)}, u32[]{:S(2)}, u32[]{:S(2)}) async-start(bf16[64,64,384]{2,1,0:T(8,128)(2,1)} %get-tuple-element.43), calls=%async_computation.4 | async-start | bytes 6291456 | tf_op jit(solution)/shard_map/all_to_all | solution.py:250
  257.6 4.5 %copy-start.6 = (bf16[512,384]{1,0:T(8,128)(2,1)S(1)}, bf16[512,384]{1,0:T(8,128)(2,1)}, u32[]{:S(2)}) copy-start(bf16[512,384]{1,0:T(8,128)(2,1)} %param.13) | copy-start | bytes 1179652
Sparse Core Ops, SparseCore 0:
  10.0 30.5 all-gather.1
  211.2 39.8 reduce-scatter.1

commit v11 on v10

--- a/solution.py
+++ b/solution.py
@@ -68,24 +68,26 @@
     return jnp.sum(same * earlier_mask, axis=-1)
 
 
-def pack_pages(slots, source, parts, slot_total, into=()):
-    page_total = source.shape[0] // PAGE
-    width = source.shape[1]
-
-    def body(slot_ref, block, *rest):
+def pack_pages(slots, sources, parts, slot_total, into=()):
+    page_total = sources[0].shape[0] // PAGE
+    width = sources[0].shape[1]
+
+    def body(slot_ref, *rest):
+        blocks = rest[: len(sources)]
         outs = rest[len(rest) - len(parts) :]
-        for out, (start, rows) in zip(outs, parts):
-            out[0] = block[start : start + rows]
-
-    in_specs = [pl.BlockSpec((PAGE, width), lambda page, slot_ref: (page, 0))]
+        for out, (which, start, rows) in zip(outs, parts):
+            out[0] = blocks[which][start : start + rows]
+
+    in_specs = [pl.BlockSpec((PAGE, width), lambda page, slot_ref: (page, 0))] * len(sources)
     in_specs += [pl.BlockSpec(memory_space=pl.ANY)] * len(into)
     out_shape = tuple(
-        jax.ShapeDtypeStruct((slot_total, rows, width), jnp.bfloat16) for _, rows in parts
+        jax.ShapeDtypeStruct((slot_total, rows, width), jnp.bfloat16) for _, _, rows in parts
     )
     out_specs = tuple(
         pl.BlockSpec((1, rows, width), lambda page, slot_ref: (slot_ref[page], 0, 0))
-        for _, rows in parts
-    )
+        for _, _, rows in parts
+    )
+    first_alias = 1 + len(sources)
     return pl.pallas_call(
         body,
         out_shape=out_shape,
@@ -95,8 +97,8 @@
             in_specs=in_specs,
             out_specs=out_specs,
         ),
-        input_output_aliases={2 + i: i for i in range(len(into))},
-    )(slots, source, *into)
+        input_output_aliases={first_alias + i: i for i in range(len(into))},
+    )(slots, *sources, *into)
 
 
 def place_pages(sources, ranks, received, slot_count, cores, part, row_block, into=(), group=6):
@@ -184,12 +186,14 @@
     own_ranks = rank_in_dest(own_dests)
     send_slots = (own_dests * CAPACITY + own_ranks).astype(jnp.int32)
     prev_pages = prev_count // PAGE
-    whole = ((0, PAGE),)
-    halves = ((0, PAGE // 2), (PAGE // 2, PAGE // 2))
-    (send_keys,) = pack_pages(send_slots[:prev_pages], prev_keys, whole, slot_total)
-    send_low, send_high = pack_pages(send_slots[:prev_pages], prev_values, halves, slot_total)
+    whole = ((0, 0, PAGE),)
+    halves = ((0, 0, PAGE // 2), (0, PAGE // 2, PAGE // 2))
+    both = ((0, 0, PAGE), (1, 0, PAGE // 2), (1, PAGE // 2, PAGE // 2))
+    send_keys, send_low, send_high = pack_pages(
+        send_slots[:prev_pages], (prev_keys, prev_values), both, slot_total
+    )
     send_low, send_high = pack_pages(
-        send_slots[prev_pages:], new_values, halves, slot_total, into=(send_low, send_high)
+        send_slots[prev_pages:], (new_values,), halves, slot_total, into=(send_low, send_high)
     )
     carried = (
         jnp.full((slot_total,), slot_count, jnp.int32)
@@ -211,7 +215,7 @@
     key_raw = jnp.dot(normed, w_key, preferred_element_type=jnp.float32)
     new_keys = rotate(key_raw, positions, HD).astype(jnp.bfloat16)
     (send_keys,) = pack_pages(
-        send_slots[prev_pages:], new_keys, whole, slot_total, into=(send_keys,)
+        send_slots[prev_pages:], (new_keys,), whole, slot_total, into=(send_keys,)
     )
     keys_all = jnp.concatenate([prev_keys, new_keys], axis=0)
     values_all = jnp.concatenate([prev_values, new_values], axis=0)

time: 274 us -> 256 us (0.934)
  Pallas kernels: 58.5 us -> 41.5 us
    pallas_call x4 -> x3, Pallas kernels: 44.1 us -> 27 us  [pack_pages(): pl.pallas_call(body, out_shape=out_shape, grid_spec=pltpu.PrefetchScalarG...]
  transfers between devices with their start and end apart: 6 -> 6, of which waited for: 3 -> 3; matrix products, arithmetic and copies ran while one was open for 36% -> 38% of each run, Pallas kernels for 20% -> 15%
where the time goes in v11:
time: 256 us; the launch traced here: 254 us
  waiting for transfers between devices  61.4 us (24%)
  other arithmetic  49.9 us (19%)
  matrix products  45.6 us (18%)
  Pallas kernels  41.5 us (16%)
  starting transfers between devices  25.8 us (10%)
  local copies, waits for them, and re-layouts  15.5 us (6%)
  between operations  14.3 us (6%)
    all_to_all x1, waiting for transfers between devices, shards(): received_high = lax.all_to_all(send_high, ('req', 'core'), 0, 0, tiled=True)  31.8 us
    pallas_call x3, Pallas kernels, pack_pages(): pl.pallas_call(body, out_shape=out_shape, grid_spec=pltpu.PrefetchScalarG...  27 us
    dot_general x1, matrix products, shards(): jnp.einsum('qhd,khd->hqk', queries.reshape(token_count, heads_here, HD),...  18.6 us
    all_to_all x1, waiting for transfers between devices, shards(): received_low = lax.all_to_all(send_low, ('req', 'core'), 0, 0, tiled=True)  18.4 us
    reduce_sum x1, other arithmetic, shards(): totals = jnp.sum(weights, axis=2)  18.2 us
    dot_general x1, matrix products, shards(): jnp.einsum('hqk,khd->qhd', prob_rows, values_all.reshape(-1, heads_here,...  15.3 us
    pallas_call x3, Pallas kernels, place_pages(): pl.pallas_call(body, out_shape=jax.ShapeDtypeStruct((slot_count, PAGE, 2...  14.5 us
    all_to_all x1, waiting for transfers between devices, shards(): received_keys = lax.all_to_all(send_keys, ('req', 'core'), 0, 0, tiled=True)  11.1 us
  transfers between devices with their start and end apart: 6, of which 3 were waited for; matrix products, arithmetic and copies ran while one was open for 38% of the time, Pallas kernels for 15%

profile of v11, /device:TPU:0, one launch (start us, length us, event | category | flops | bytes accessed | tf_op | source)
XLA Modules:
  0.0 254.0 jit_solution(3336300067016667147)
XLA Ops:
  13.5 8.2 %all-to-all-start = ((s32[32,2,1]{1,2,0:T(1,128)}), s32[32,2,1]{1,2,0:T(1,128)S(1)}, u32[]{:S(2)}, u32[]{:S(2)}) async-start(s32[32,2,1]{1,2,0:T(1,128)} %bitcast.9), calls=%async_computation | async-start | bytes 32768 | tf_op jit(solution)/shard_map/all_to_all | solution.py:203
  28.3 19.3 %shard_map.122 = (bf16[64,128,384]{2,1,0:T(8,128)(2,1)}, bf16[64,64,384]{2,1,0:T(8,128)(2,1)}, bf16[64,64,384]{2,1,0:T(8,128)(2,1)}) custom-call(s32[32]{0:T(128)} %bitcast.84, bf16[4096,384]{1,0:T(8,128)(2,1)} %rest_0_.1, bf16[4096,384]{1,0:T(8,128)(2,1)} %rest_1_.1), custom_call_target="tpu_custom_call" | custom-call | tf_op jit(solution)/shard_map/pallas_call | solution.py:91
  52.5 3.1 %fusion.8 = bf16[512,3072]{1,0:T(8,128)(2,1)S(1)} fusion(f32[3072]{0:T(1024)S(1)} %bitcast.81, f32[512]{0:T(512)S(1)} %add_rsqrt_fusion, bf16[528,3072]{1,0:T(8,128)(2,1)} %all-gather.2.cloned.1.call-done), kind=kLoop, calls=%fused_computation.13 | loop fusion | flops 6291456 | bytes 6305792 | tf_op jit(solution)/shard_map/convert_element_type | solution.py:172
  58.2 3.8 %shard_map.123 = (bf16[64,64,384]{2,1,0:T(8,128)(2,1)}, bf16[64,64,384]{2,1,0:T(8,128)(2,1)}) custom-call(s32[4]{0:T(128)} %slice.42.slot_ref, bf16[512,384]{1,0:T(8,128)(2,1)} %convolution_convert_fusion.rest_0_, bf16[64,64,384]{2,1,0:T(8,128)(2,1)} %get-tuple-element.32.rest_1_, ...), custom_call_target="tpu_custom_call", output_to_operand_aliasing={{0}: (2, {}), {1}: (3, {})} | custom-call | tf_op jit(solution)/shard_map/pallas_call | solution.py:91
  61.9 7.5 %all-to-all-start.2 = ((bf16[64,64,384]{2,1,0:T(8,128)(2,1)}), bf16[64,64,384]{2,1,0:T(8,128)(2,1)}, u32[]{:S(2)}, u32[]{:S(2)}) async-start(bf16[64,64,384]{2,1,0:T(8,128)(2,1)} %get-tuple-element.39), calls=%async_computation.2 | async-start | bytes 6291456 | tf_op jit(solution)/shard_map/all_to_all | solution.py:214
  70.1 3.1 %pad_add_fusion = pred[512,4608]{1,0:T(8,128)(4,1)} fusion(pred[512,512]{1,0:T(8,128)(4,1)S(1)} %fusion.18, pred[512,4096]{1,0:T(8,128)(4,1)} %broadcast_compare_fusion), kind=kLoop, calls=%fused_computation.8 | loop fusion | flops 2359296 | bytes 4718592 | tf_op jit(solution)/shard_map/concatenate | solution.py:60
  73.2 3.2 %fusion.37 = f32[512,384]{0,1:T(8,128)S(1)} fusion(bf16[512,3072]{1,0:T(8,128)(2,1)S(1)} %copy-done.5, bf16[3072,384]{1,0:T(8,128)(2,1)} %param.15), kind=kOutput, calls=%fused_computation.81 | convolution fusion | flops 1207959552 | bytes 6291456 | tf_op jit(solution)/shard_map/dot_general | solution.py:222
  79.1 3.9 %shard_map.124 = bf16[64,128,384]{2,1,0:T(8,128)(2,1)} custom-call(s32[4]{0:T(128)} %slice.42.slot_ref, bf16[512,384]{1,0:T(8,128)(2,1)} %copy.42.rest_0_, bf16[64,128,384]{2,1,0:T(8,128)(2,1)} %get-tuple-element.38.rest_1_), custom_call_target="tpu_custom_call", output_to_operand_aliasing={{}: (2, {})} | custom-call | tf_op jit(solution)/shard_map/pallas_call | solution.py:91
  83.0 4.0 %pad_maximum_fusion.1 = bf16[4608,384]{1,0:T(8,128)(2,1)} fusion(bf16[512,384]{1,0:T(8,128)(2,1)S(1)} %copy-done.2, bf16[4096,384]{1,0:T(8,128)(2,1)} %rest_0_.1), kind=kLoop, calls=%fused_computation.16 | loop fusion | flops 7077888 | bytes 7077888 | tf_op jit(solution)/shard_map/concatenate | solution.py:220
  87.0 5.8 %copy.45 = bf16[4608,384]{0,1:T(8,128)(2,1)} copy(bf16[4608,384]{1,0:T(8,128)(2,1)} %pad_maximum_fusion.1) | data formatting | bytes 7077888 | tf_op jit(solution)/shard_map/concatenate | solution.py:220
  92.8 18.4 %all-to-all-done.2 = bf16[64,64,384]{2,1,0:T(8,128)(2,1)} async-done(((bf16[64,64,384]{2,1,0:T(8,128)(2,1)}), bf16[64,64,384]{2,1,0:T(8,128)(2,1)}, u32[]{:S(2)}, u32[]{:S(2)}) %all-to-all-start.2) | async-done | bytes 3145760 | tf_op jit(solution)/shard_map/all_to_all | solution.py:214
  111.2 4.9 %all-to-all-start.1 = ((bf16[64,128,384]{2,1,0:T(8,128)(2,1)}), bf16[64,128,384]{2,1,0:T(8,128)(2,1)}, u32[]{:S(2)}, u32[]{:S(2)}) async-start(bf16[64,128,384]{2,1,0:T(8,128)(2,1)} %shard_map.124), calls=%async_computation.1 | async-start | bytes 12582912 | tf_op jit(solution)/shard_map/all_to_all | solution.py:224
  116.4 18.6 %fusion = (f32[4,512]{1,0:T(4,128)S(1)}, f32[4,512,4608]{2,1,0:T(8,128)}) fusion(pred[512,4608]{1,0:T(8,128)(4,1)} %pad_add_fusion, bf16[4608,4,96]{0,2,1:T(8,128)(2,1)} %bitcast.75, bf16[512,4,48]{0,2,1:T(8,128)(2,1)S(1)} %get-tuple-element.61, bf16[512,4,48]{0,2,1:T(8,128)(2,1)S(1)} %get-tuple-element.60), kind=kOutput, calls=%fused_computation.3 | convolution fusion | flops 1841035264 | bytes 44048384 | tf_op jit(solution)/shard_map/qhd,khd->hqk/dot_general | solution.py:228
  135.0 4.0 %pad_maximum_fusion = bf16[4608,384]{1,0:T(8,128)(2,1)} fusion(bf16[512,384]{1,0:T(8,128)(2,1)S(1)} %copy-done.7, bf16[4096,384]{1,0:T(8,128)(2,1)} %rest_1_.1), kind=kLoop, calls=%fused_computation.15 | loop fusion | flops 7077888 | bytes 7077888 | tf_op jit(solution)/shard_map/concatenate | solution.py:221
  139.0 5.8 %copy.43 = bf16[4608,384]{0,1:T(8,128)(2,1)} copy(bf16[4608,384]{1,0:T(8,128)(2,1)} %pad_maximum_fusion) | data formatting | bytes 7077888 | tf_op jit(solution)/shard_map/concatenate | solution.py:221
  144.8 18.2 %fusion.1 = f32[4,512]{1,0:T(4,128)S(1)} fusion(f32[4,512,4608]{2,1,0:T(8,128)} %get-tuple-element.72, f32[4,512]{1,0:T(4,128)S(1)} %get-tuple-element.71, pred[512,4608]{1,0:T(8,128)(4,1)} %pad_add_fusion), kind=kLoop, calls=%fused_computation.4 | loop fusion | flops 37746688 | bytes 40124416 | tf_op jit(solution)/shard_map/reduce_sum | solution.py:237
  163.1 15.3 %fusion.15 = bf16[512,4,96]{0,2,1:T(8,128)(2,1)S(1)} fusion(bf16[4608,4,96]{0,2,1:T(8,128)(2,1)S(1)} %bitcast.76, f32[4,512,4608]{2,1,0:T(8,128)} %get-tuple-element.72, f32[4,512]{1,0:T(4,128)S(1)} %get-tuple-element.71, pred[512,4608]{1,0:T(8,128)(4,1)S(1)} %copy-done.1, f32[512,4]{0,1:T(4,128)S(1)} %bitcast.83), kind=kOutput, calls=%fused_computation.20 | convolution fusion | flops 1850081280 | bytes 44056576 | tf_op jit(solution)/shard_map/hqk,khd->qhd/dot_general | solution.py:239
  178.4 4.5 %fusion.38 = f32[512,3072]{1,0:T(8,128)} fusion(bf16[512,384]{0,1:T(8,128)(2,1)S(1)} %bitcast.80, bf16[384,3072]{1,0:T(8,128)(2,1)S(1)} %copy-done), kind=kOutput, calls=%fused_computation.82 | convolution fusion | flops 1207959552 | bytes 9043968 | tf_op jit(solution)/shard_map/dot_general | solution.py:248
  182.9 11.1 %all-to-all-done.1 = bf16[64,128,384]{2,1,0:T(8,128)(2,1)} async-done(((bf16[64,128,384]{2,1,0:T(8,128)(2,1)}), bf16[64,128,384]{2,1,0:T(8,128)(2,1)}, u32[]{:S(2)}, u32[]{:S(2)}) %all-to-all-start.1) | async-done | bytes 6291488 | tf_op jit(solution)/shard_map/all_to_all | solution.py:224
  194.1 4.8 %all-to-all-start.3 = ((bf16[64,64,384]{2,1,0:T(8,128)(2,1)}), bf16[64,64,384]{2,1,0:T(8,128)(2,1)}, u32[]{:S(2)}, u32[]{:S(2)}) async-start(bf16[64,64,384]{2,1,0:T(8,128)(2,1)} %get-tuple-element.45), calls=%async_computation.4 | async-start | bytes 6291456 | tf_op jit(solution)/shard_map/all_to_all | solution.py:254
  198.9 5.6 %shard_map.125.refs_6_ = bf16[18,128,1536]{2,1,0:T(8,128)(2,1)} custom-call(s32[18]{0:T(128)} %get-tuple-element.43.src_ref, s32[18]{0:T(128)} %get-tuple-element.44.rank_ref, bf16[16,2,2,128,384]{4,3,2,1,0:T(8,128)(2,1)} %bitcast.28.refs_0_.refs_1_.refs_2_.refs_3_.refs_4_.refs_5_, ...), custom_call_target="tpu_custom_call" | custom-call | tf_op jit(solution)/shard_map/pallas_call | solution.py:126
  204.5 4.4 %shard_map.126.refs_6_ = bf16[18,128,1536]{2,1,0:T(8,128)(2,1)} custom-call(s32[18]{0:T(128)} %get-tuple-element.43.src_ref, s32[18]{0:T(128)} %get-tuple-element.44.rank_ref, bf16[16,2,2,64,384]{4,3,2,1,0:T(8,128)(2,1)} %bitcast.27.refs_0_.refs_1_.refs_2_.refs_3_.refs_4_.refs_5_, ...), custom_call_target="tpu_custom_call", output_to_operand_aliasing={{}: (8, {})} | custom-call | tf_op jit(solution)/shard_map/pallas_call | solution.py:126
  208.9 31.8 %all-to-all-done.3 = bf16[64,64,384]{2,1,0:T(8,128)(2,1)} async-done(((bf16[64,64,384]{2,1,0:T(8,128)(2,1)}), bf16[64,64,384]{2,1,0:T(8,128)(2,1)}, u32[]{:S(2)}, u32[]{:S(2)}) %all-to-all-start.3) | async-done | bytes 3145760 | tf_op jit(solution)/shard_map/all_to_all | solution.py:254
  240.7 4.5 %shard_map.127 = bf16[18,128,1536]{2,1,0:T(8,128)(2,1)} custom-call(s32[18]{0:T(128)} %get-tuple-element.43.src_ref, s32[18]{0:T(128)} %get-tuple-element.44.rank_ref, bf16[16,2,2,64,384]{4,3,2,1,0:T(8,128)(2,1)} %bitcast.26.refs_0_.refs_1_.refs_2_.refs_3_.refs_4_.refs_5_, ...), custom_call_target="tpu_custom_call", output_to_operand_aliasing={{}: (8, {})} | custom-call | tf_op jit(solution)/shard_map/pallas_call | solution.py:126
  (63 shorter events, 25.7 us)
Async XLA Ops:
  7.2 171.2 %copy-start = (bf16[384,3072]{1,0:T(8,128)(2,1)S(1)}, bf16[384,3072]{1,0:T(8,128)(2,1)}, u32[]{:S(2)}) copy-start(bf16[384,3072]{1,0:T(8,128)(2,1)} %param.18) | copy-start | bytes 7077892
  7.2 41.8 %all-gather.2.cloned.1.call-start = ((), (), s32[]{:S(2)}) async-start(), calls=%async_computation.5 | async-start | bytes 3649536 | tf_op jit(solution)/shard_map/all_gather | solution.py:165
  13.5 34.2 %all-to-all-start = ((s32[32,2,1]{1,2,0:T(1,128)}), s32[32,2,1]{1,2,0:T(1,128)S(1)}, u32[]{:S(2)}, u32[]{:S(2)}) async-start(s32[32,2,1]{1,2,0:T(1,128)} %bitcast.9), calls=%async_computation | async-start | bytes 32768 | tf_op jit(solution)/shard_map/all_to_all | solution.py:203
  25.0 3.3 %copy-start.8 = (s32[36]{0:T(128)}, s32[36]{0:T(128)S(1)}, u32[]{:S(2)}) copy-start(s32[36]{0:T(128)S(1)} %multiply_add_fusion) | copy-start | bytes 436
  51.6 4.0 %copy-start.9 = (bf16[3072,384]{1,0:T(8,128)(2,1)S(1)}, bf16[3072,384]{1,0:T(8,128)(2,1)}, u32[]{:S(2)}) copy-start(bf16[3072,384]{1,0:T(8,128)(2,1)} %param.17) | copy-start | bytes 7077892
  55.6 2.5 %copy-start.4 = (bf16[512,3072]{1,0:T(8,128)(2,1)}, bf16[512,3072]{1,0:T(8,128)(2,1)S(1)}, u32[]{:S(2)}) copy-start(bf16[512,3072]{1,0:T(8,128)(2,1)S(1)} %fusion.8) | copy-start | bytes 9437188
  61.9 49.3 %all-to-all-start.2 = ((bf16[64,64,384]{2,1,0:T(8,128)(2,1)}), bf16[64,64,384]{2,1,0:T(8,128)(2,1)}, u32[]{:S(2)}, u32[]{:S(2)}) async-start(bf16[64,64,384]{2,1,0:T(8,128)(2,1)} %get-tuple-element.39), calls=%async_computation.2 | async-start | bytes 6291456 | tf_op jit(solution)/shard_map/all_to_all | solution.py:214
  69.5 3.7 %copy-start.5 = (bf16[512,3072]{1,0:T(8,128)(2,1)S(1)}, bf16[512,3072]{1,0:T(8,128)(2,1)}, u32[]{:S(2)}) copy-start(bf16[512,3072]{1,0:T(8,128)(2,1)} %copy-done.4) | copy-start | bytes 9437188
  73.2 3.3 %copy-start.10 = (bf16[3072,384]{1,0:T(8,128)(2,1)S(1)}, bf16[3072,384]{1,0:T(8,128)(2,1)}, u32[]{:S(2)}) copy-start(bf16[3072,384]{1,0:T(8,128)(2,1)} %param.16) | copy-start | bytes 7077892
  79.1 3.9 %copy-start.2 = (bf16[512,384]{1,0:T(8,128)(2,1)S(1)}, bf16[512,384]{1,0:T(8,128)(2,1)}, u32[]{:S(2)}) copy-start(bf16[512,384]{1,0:T(8,128)(2,1)} %copy.42.rest_0_) | copy-start | bytes 1179652
  111.2 82.8 %all-to-all-start.1 = ((bf16[64,128,384]{2,1,0:T(8,128)(2,1)}), bf16[64,128,384]{2,1,0:T(8,128)(2,1)}, u32[]{:S(2)}, u32[]{:S(2)}) async-start(bf16[64,128,384]{2,1,0:T(8,128)(2,1)} %shard_map.124), calls=%async_computation.1 | async-start | bytes 12582912 | tf_op jit(solution)/shard_map/all_to_all | solution.py:224
  116.1 129.0 %reduce-scatter.2.cloned.1.call-start = ((), (), s32[]{:S(2)}) async-start(), calls=%async_computation.6 | async-start | bytes 7077888 | tf_op jit(solution)/shard_map/reduce_scatter | solution.py:252
  116.4 18.6 %copy-start.7 = (bf16[512,384]{1,0:T(8,128)(2,1)S(1)}, bf16[512,384]{1,0:T(8,128)(2,1)}, u32[]{:S(2)}) copy-start(bf16[512,384]{1,0:T(8,128)(2,1)} %convolution_convert_fusion.rest_0_) | copy-start | bytes 1179652
  144.8 18.2 %copy-start.1 = (pred[512,4608]{1,0:T(8,128)(4,1)S(1)}, pred[512,4608]{1,0:T(8,128)(4,1)}, u32[]{:S(2)}) copy-start(pred[512,4608]{1,0:T(8,128)(4,1)} %pad_add_fusion) | copy-start | bytes 7077892
  144.8 18.2 %copy-start.3 = (bf16[4608,384]{0,1:T(8,128)(2,1)S(1)}, bf16[4608,384]{0,1:T(8,128)(2,1)}, u32[]{:S(2)}) copy-start(bf16[4608,384]{0,1:T(8,128)(2,1)} %copy.43) | copy-start | bytes 10616836
  194.1 46.6 %all-to-all-start.3 = ((bf16[64,64,384]{2,1,0:T(8,128)(2,1)}), bf16[64,64,384]{2,1,0:T(8,128)(2,1)}, u32[]{:S(2)}, u32[]{:S(2)}) async-start(bf16[64,64,384]{2,1,0:T(8,128)(2,1)} %get-tuple-element.45), calls=%async_computation.4 | async-start | bytes 6291456 | tf_op jit(solution)/shard_map/all_to_all | solution.py:254
  240.7 4.5 %copy-start.6 = (bf16[512,384]{1,0:T(8,128)(2,1)S(1)}, bf16[512,384]{1,0:T(8,128)(2,1)}, u32[]{:S(2)}) copy-start(bf16[512,384]{1,0:T(8,128)(2,1)} %param.13) | copy-start | bytes 1179652
Sparse Core Ops, SparseCore 0:
  10.0 30.5 all-gather.1
  194.2 39.8 reduce-scatter.1

commit v12 on v11

--- a/solution.py
+++ b/solution.py
@@ -68,7 +68,7 @@
     return jnp.sum(same * earlier_mask, axis=-1)
 
 
-def pack_pages(slots, sources, parts, slot_total, into=()):
+def pack_pages(slots, sources, parts, slot_total, into=(), shapes=None):
     page_total = sources[0].shape[0] // PAGE
     width = sources[0].shape[1]
 
@@ -80,8 +80,10 @@
 
     in_specs = [pl.BlockSpec((PAGE, width), lambda page, slot_ref: (page, 0))] * len(sources)
     in_specs += [pl.BlockSpec(memory_space=pl.ANY)] * len(into)
+    if shapes is None:
+        shapes = [rows for _, _, rows in parts]
     out_shape = tuple(
-        jax.ShapeDtypeStruct((slot_total, rows, width), jnp.bfloat16) for _, _, rows in parts
+        jax.ShapeDtypeStruct((slot_total, full, width), jnp.bfloat16) for full in shapes
     )
     out_specs = tuple(
         pl.BlockSpec((1, rows, width), lambda page, slot_ref: (slot_ref[page], 0, 0))
@@ -97,13 +99,32 @@
             in_specs=in_specs,
             out_specs=out_specs,
         ),
-        input_output_aliases={first_alias + i: i for i in range(len(into))},
-    )(slots, *sources, *into)
-
-
-def place_pages(sources, ranks, received, slot_count, cores, part, row_block, into=(), group=6):
-    rows, width = received.shape[-2:]
-    shaped = received.reshape(-1, cores, CAPACITY, rows, width)
+        input_output_aliases={first_alias + i: out for i, out in enumerate(into)},
+    )(slots, *sources, *into.values())
+
+
+def stamp_tags(tags, first_row):
+    slot_total, tag_rows, width = tags.shape
+
+    def body(tag_block, out):
+        out[...] = tag_block[...]
+
+    return pl.pallas_call(
+        body,
+        out_shape=jax.ShapeDtypeStruct((slot_total, first_row + tag_rows, width), jnp.bfloat16),
+        grid=(1,),
+        in_specs=[pl.BlockSpec((slot_total, tag_rows, width), lambda step: (0, 0, 0))],
+        out_specs=pl.BlockSpec(
+            (slot_total, tag_rows, width), lambda step: (0, first_row // tag_rows, 0)
+        ),
+    )(tags)
+
+
+def place_pages(
+    sources, ranks, received, slot_count, cores, part, row_block, rows, into=(), group=6
+):
+    stored, width = received.shape[-2:]
+    shaped = received.reshape(-1, cores, CAPACITY, stored, width)
 
     def body(src_ref, rank_ref, *refs):
         out = refs[-1]
@@ -189,33 +210,46 @@
     whole = ((0, 0, PAGE),)
     halves = ((0, 0, PAGE // 2), (0, PAGE // 2, PAGE // 2))
     both = ((0, 0, PAGE), (1, 0, PAGE // 2), (1, PAGE // 2, PAGE // 2))
-    send_keys, send_low, send_high = pack_pages(
-        send_slots[:prev_pages], (prev_keys, prev_values), both, slot_total
-    )
-    send_low, send_high = pack_pages(
-        send_slots[prev_pages:], (new_values,), halves, slot_total, into=(send_low, send_high)
-    )
+    half_rows = PAGE // 2
+    tag_rows = 16
     carried = (
         jnp.full((slot_total,), slot_count, jnp.int32)
         .at[send_slots]
         .set((page_table[0] % slot_count).astype(jnp.int32))
     )
-    carried = lax.all_to_all(carried, ("req", "core"), 0, 0, tiled=True)
+    tags = jnp.zeros((slot_total, tag_rows, local_width), jnp.bfloat16)
+    tags = tags.at[:, 0, 0].set(carried.astype(jnp.bfloat16))
+    send_low = stamp_tags(tags, half_rows)
+    send_keys, send_low, send_high = pack_pages(
+        send_slots[:prev_pages],
+        (prev_keys, prev_values),
+        both,
+        slot_total,
+        into={1: send_low},
+        shapes=(PAGE, half_rows + tag_rows, half_rows),
+    )
+    send_low, send_high = pack_pages(
+        send_slots[prev_pages:],
+        (new_values,),
+        halves,
+        slot_total,
+        into={0: send_low, 1: send_high},
+        shapes=(half_rows + tag_rows, half_rows),
+    )
+    send_keys, send_low, send_high, normed, new_values = lax.optimization_barrier(
+        (send_keys, send_low, send_high, normed, new_values)
+    )
+    received_low = lax.all_to_all(send_low, ("req", "core"), 0, 0, tiled=True)
+    carried = received_low[:, half_rows, 0].astype(jnp.int32)
     carried = carried.reshape(req_count, cores, CAPACITY)[:, 0, :].reshape(-1)
     wanted = jnp.arange(slot_count, dtype=jnp.int32)
     found = jnp.argmax(carried[None, :] == wanted[:, None], axis=1).astype(jnp.int32)
     from_req = found // CAPACITY
     from_rank = found % CAPACITY
-    send_keys, send_low, send_high, normed, new_values, from_req, from_rank = (
-        lax.optimization_barrier(
-            (send_keys, send_low, send_high, normed, new_values, from_req, from_rank)
-        )
-    )
-    received_low = lax.all_to_all(send_low, ("req", "core"), 0, 0, tiled=True)
     key_raw = jnp.dot(normed, w_key, preferred_element_type=jnp.float32)
     new_keys = rotate(key_raw, positions, HD).astype(jnp.bfloat16)
     (send_keys,) = pack_pages(
-        send_slots[prev_pages:], (new_keys,), whole, slot_total, into=(send_keys,)
+        send_slots[prev_pages:], (new_keys,), whole, slot_total, into={0: send_keys}
     )
     keys_all = jnp.concatenate([prev_keys, new_keys], axis=0)
     values_all = jnp.concatenate([prev_values, new_values], axis=0)
@@ -252,9 +286,14 @@
     summed = lax.psum_scatter(projected, ("y", "core"), scatter_dimension=1, tiled=True)
     layer_out = (tokens.astype(jnp.float32) + summed).astype(jnp.bfloat16)
     received_high = lax.all_to_all(send_high, ("req", "core"), 0, 0, tiled=True)
-    pool = place_pages(from_req, from_rank, received_keys, slot_count, cores, 0, 0)
-    pool = place_pages(from_req, from_rank, received_low, slot_count, cores, 1, 0, into=(pool,))
-    pool = place_pages(from_req, from_rank, received_high, slot_count, cores, 1, 1, into=(pool,))
+    half_rows = PAGE // 2
+    pool = place_pages(from_req, from_rank, received_keys, slot_count, cores, 0, 0, PAGE)
+    pool = place_pages(
+        from_req, from_rank, received_low, slot_count, cores, 1, 0, half_rows, into=(pool,)
+    )
+    pool = place_pages(
+        from_req, from_rank, received_high, slot_count, cores, 1, 1, half_rows, into=(pool,)
+    )
     return (layer_out, pool[:, None])
 
 

time: 256 us -> 257 us (level)
  waiting for transfers between devices: 61.4 us -> 73.1 us
  starting transfers between devices: 25.8 us -> 17.3 us
  other arithmetic: 49.9 us -> 44.6 us
    all_to_all x1, waiting for transfers between devices: 18.4 us -> 29.4 us  [shards(): received_low = lax.all_to_all(send_low, ('req', 'core'), 0, 0, tiled=True)]
    all_to_all x1 -> x0, starting transfers between devices: 8.25 us -> none  [shards(): carried = lax.all_to_all(carried, ('req', 'core'), 0, 0, tiled=True)]
    all_gather x1, waiting for transfers between devices: 0.01 us -> 3.62 us  [shards(): lax.all_gather(jnp.concatenate([tokens, riders], axis=0), ('y', 'core'),...]
    all_to_all x1, waiting for transfers between devices: 31.8 us -> 28.9 us  [shards(): received_high = lax.all_to_all(send_high, ('req', 'core'), 0, 0, tiled=True)]
  transfers between devices with their start and end apart: 6 -> 5, of which waited for: 3 -> 4; matrix products, arithmetic and copies ran while one was open for 38% -> 36% of each run, Pallas kernels for 15% -> 16%
where the time goes in v12:
time: 257 us; the launch traced here: 254 us
  waiting for transfers between devices  73.1 us (28%)
  other arithmetic  44.6 us (17%)
  matrix products  43.8 us (17%)
  Pallas kernels  43.6 us (17%)
  local copies, waits for them, and re-layouts  17.6 us (7%)
  starting transfers between devices  17.3 us (7%)
  between operations  14.3 us (6%)
    all_to_all x1, waiting for transfers between devices, shards(): received_low = lax.all_to_all(send_low, ('req', 'core'), 0, 0, tiled=True)  29.4 us
    all_to_all x1, waiting for transfers between devices, shards(): received_high = lax.all_to_all(send_high, ('req', 'core'), 0, 0, tiled=True)  28.9 us
    pallas_call x3, Pallas kernels, pack_pages(): pl.pallas_call(body, out_shape=out_shape, grid_spec=pltpu.PrefetchScalarG...  27.1 us
    dot_general x1, matrix products, shards(): jnp.einsum('qhd,khd->hqk', queries.reshape(token_count, heads_here, HD),...  18.6 us
    reduce_sum x1, other arithmetic, shards(): totals = jnp.sum(weights, axis=2)  18.2 us
    dot_general x1, matrix products, shards(): jnp.einsum('hqk,khd->qhd', prob_rows, values_all.reshape(-1, heads_here,...  15.3 us
    pallas_call x3, Pallas kernels, place_pages(): pl.pallas_call(body, out_shape=jax.ShapeDtypeStruct((slot_count, PAGE, 2...  14.4 us
    all_to_all x1, waiting for transfers between devices, shards(): received_keys = lax.all_to_all(send_keys, ('req', 'core'), 0, 0, tiled=True)  11.1 us
  transfers between devices with their start and end apart: 5, of which 4 were waited for; matrix products, arithmetic and copies ran while one was open for 36% of the time, Pallas kernels for 16%

profile of v12, /device:TPU:0, one launch (start us, length us, event | category | flops | bytes accessed | tf_op | source)
XLA Modules:
  0.0 254.3 jit_solution(3267481849475026165)
XLA Ops:
  17.0 19.4 %shard_map.123 = (bf16[64,128,384]{2,1,0:T(8,128)(2,1)}, bf16[64,80,384]{2,1,0:T(8,128)(2,1)}, bf16[64,64,384]{2,1,0:T(8,128)(2,1)}) custom-call(s32[32]{0:T(128)} %bitcast.82, bf16[4096,384]{1,0:T(8,128)(2,1)} %rest_0_.1, bf16[4096,384]{1,0:T(8,128)(2,1)} %rest_1_.1, bf16[64,80,384]{2,1,0:T(8,128)(2,1)} %shard_map.122.rest_2_), custom_call_target="tpu_custom_call", output_to_operand_aliasing={{1}: (3, {})} | custom-call | tf_op jit(solution)/shard_map/pallas_call | solution.py:93
  37.0 3.6 %all-gather.2.cloned.1.call-done = bf16[528,3072]{1,0:T(8,128)(2,1)} async-done(((bf16[528,384]{1,0:T(8,128)(2,1)}), bf16[528,3072]{1,0:T(8,128)(2,1)}) %all-gather.2.cloned.1.call-update) | async-done | bytes 3244048 | tf_op jit(solution)/shard_map/all_gather | solution.py:186
  40.6 2.6 %fusion.6 = f32[512]{0:T(512)S(1)} fusion(bf16[528,3072]{1,0:T(8,128)(2,1)} %all-gather.2.cloned.1.call-done), kind=kLoop, calls=%fused_computation.11 | loop fusion | flops 4718080 | bytes 3147776 | tf_op jit(solution)/shard_map/reduce_sum | solution.py:192
  44.2 3.1 %fusion.8 = bf16[512,3072]{1,0:T(8,128)(2,1)S(1)} fusion(f32[3072]{0:T(1024)S(1)} %bitcast.80, f32[512]{0:T(512)S(1)} %add_rsqrt_fusion, bf16[528,3072]{1,0:T(8,128)(2,1)} %all-gather.2.cloned.1.call-done), kind=kLoop, calls=%fused_computation.13 | loop fusion | flops 6291456 | bytes 6305792 | tf_op jit(solution)/shard_map/convert_element_type | solution.py:193
  47.3 2.5 convolution_convert_fusion.rest_0_
  49.8 3.8 %shard_map.124 = (bf16[64,80,384]{2,1,0:T(8,128)(2,1)}, bf16[64,64,384]{2,1,0:T(8,128)(2,1)}) custom-call(s32[4]{0:T(128)} %slice.65.slot_ref, bf16[512,384]{1,0:T(8,128)(2,1)} %convolution_convert_fusion.rest_0_, bf16[64,80,384]{2,1,0:T(8,128)(2,1)} %get-tuple-element.42.rest_1_, ...), custom_call_target="tpu_custom_call", output_to_operand_aliasing={{0}: (2, {}), {1}: (3, {})} | custom-call | tf_op jit(solution)/shard_map/pallas_call | solution.py:93
  53.6 7.3 %all-to-all-start.1 = ((bf16[64,80,384]{2,1,0:T(8,128)(2,1)}), bf16[64,80,384]{2,1,0:T(8,128)(2,1)}, u32[]{:S(2)}, u32[]{:S(2)}) async-start(bf16[64,80,384]{2,1,0:T(8,128)(2,1)} %get-tuple-element.48), calls=%async_computation.1 | async-start | bytes 7864320 | tf_op jit(solution)/shard_map/all_to_all | solution.py:242
  68.5 3.9 %shard_map.125 = bf16[64,128,384]{2,1,0:T(8,128)(2,1)} custom-call(s32[4]{0:T(128)} %slice.65.slot_ref, bf16[512,384]{1,0:T(8,128)(2,1)} %copy.31.rest_0_, bf16[64,128,384]{2,1,0:T(8,128)(2,1)} %get-tuple-element.47.rest_1_), custom_call_target="tpu_custom_call", output_to_operand_aliasing={{}: (2, {})} | custom-call | tf_op jit(solution)/shard_map/pallas_call | solution.py:93
  72.4 4.0 %pad_maximum_fusion.1 = bf16[4608,384]{1,0:T(8,128)(2,1)} fusion(bf16[512,384]{1,0:T(8,128)(2,1)S(1)} %copy-done.2, bf16[4096,384]{1,0:T(8,128)(2,1)} %rest_0_.1), kind=kLoop, calls=%fused_computation.16 | loop fusion | flops 7077888 | bytes 7077888 | tf_op jit(solution)/shard_map/concatenate | solution.py:254
  76.4 5.7 %copy.34 = bf16[4608,384]{0,1:T(8,128)(2,1)} copy(bf16[4608,384]{1,0:T(8,128)(2,1)} %pad_maximum_fusion.1) | data formatting | bytes 7077888 | tf_op jit(solution)/shard_map/concatenate | solution.py:254
  82.2 29.4 %all-to-all-done.1 = bf16[64,80,384]{2,1,0:T(8,128)(2,1)} async-done(((bf16[64,80,384]{2,1,0:T(8,128)(2,1)}), bf16[64,80,384]{2,1,0:T(8,128)(2,1)}, u32[]{:S(2)}, u32[]{:S(2)}) %all-to-all-start.1) | async-done | bytes 3932192 | tf_op jit(solution)/shard_map/all_to_all | solution.py:242
  111.6 4.9 %all-to-all-start = ((bf16[64,128,384]{2,1,0:T(8,128)(2,1)}), bf16[64,128,384]{2,1,0:T(8,128)(2,1)}, u32[]{:S(2)}, u32[]{:S(2)}) async-start(bf16[64,128,384]{2,1,0:T(8,128)(2,1)} %shard_map.125), calls=%async_computation | async-start | bytes 12582912 | tf_op jit(solution)/shard_map/all_to_all | solution.py:258
  116.7 18.6 %fusion = (f32[4,512]{1,0:T(4,128)S(1)}, f32[4,512,4608]{2,1,0:T(8,128)}) fusion(pred[512,4608]{1,0:T(8,128)(4,1)} %pad_add_fusion, bf16[4608,4,96]{0,2,1:T(8,128)(2,1)} %bitcast.74, bf16[512,4,48]{0,2,1:T(8,128)(2,1)S(1)} %get-tuple-element.67, bf16[512,4,48]{0,2,1:T(8,128)(2,1)S(1)} %get-tuple-element.66), kind=kOutput, calls=%fused_computation.3 | convolution fusion | flops 1841035264 | bytes 44048384 | tf_op jit(solution)/shard_map/qhd,khd->hqk/dot_general | solution.py:262
  135.3 4.1 %pad_maximum_fusion = bf16[4608,384]{1,0:T(8,128)(2,1)} fusion(bf16[512,384]{1,0:T(8,128)(2,1)S(1)} %copy-done.7, bf16[4096,384]{1,0:T(8,128)(2,1)} %rest_1_.1), kind=kLoop, calls=%fused_computation.15 | loop fusion | flops 7077888 | bytes 7077888 | tf_op jit(solution)/shard_map/concatenate | solution.py:255
  139.4 5.7 %copy.32 = bf16[4608,384]{0,1:T(8,128)(2,1)} copy(bf16[4608,384]{1,0:T(8,128)(2,1)} %pad_maximum_fusion) | data formatting | bytes 7077888 | tf_op jit(solution)/shard_map/concatenate | solution.py:255
  145.2 18.2 %fusion.1 = f32[4,512]{1,0:T(4,128)S(1)} fusion(f32[4,512,4608]{2,1,0:T(8,128)} %get-tuple-element.78, f32[4,512]{1,0:T(4,128)S(1)} %get-tuple-element.77, pred[512,4608]{1,0:T(8,128)(4,1)} %pad_add_fusion), kind=kLoop, calls=%fused_computation.4 | loop fusion | flops 37746688 | bytes 40124416 | tf_op jit(solution)/shard_map/reduce_sum | solution.py:271
  163.4 15.3 %fusion.15 = bf16[512,4,96]{0,2,1:T(8,128)(2,1)S(1)} fusion(bf16[4608,4,96]{0,2,1:T(8,128)(2,1)S(1)} %bitcast.75, f32[4,512,4608]{2,1,0:T(8,128)} %get-tuple-element.78, f32[4,512]{1,0:T(4,128)S(1)} %get-tuple-element.77, pred[512,4608]{1,0:T(8,128)(4,1)S(1)} %copy-done.1, f32[512,4]{0,1:T(4,128)S(1)} %bitcast.81), kind=kOutput, calls=%fused_computation.20 | convolution fusion | flops 1850081280 | bytes 44056576 | tf_op jit(solution)/shard_map/hqk,khd->qhd/dot_general | solution.py:273
  178.8 4.5 %fusion.39 = f32[512,3072]{1,0:T(8,128)} fusion(bf16[512,384]{0,1:T(8,128)(2,1)S(1)} %bitcast.79, bf16[384,3072]{1,0:T(8,128)(2,1)S(1)} %copy-done), kind=kOutput, calls=%fused_computation.85 | convolution fusion | flops 1207959552 | bytes 9043968 | tf_op jit(solution)/shard_map/dot_general | solution.py:282
  183.3 11.1 %all-to-all-done = bf16[64,128,384]{2,1,0:T(8,128)(2,1)} async-done(((bf16[64,128,384]{2,1,0:T(8,128)(2,1)}), bf16[64,128,384]{2,1,0:T(8,128)(2,1)}, u32[]{:S(2)}, u32[]{:S(2)}) %all-to-all-start) | async-done | bytes 6291488 | tf_op jit(solution)/shard_map/all_to_all | solution.py:258
  194.4 4.8 %all-to-all-start.2 = ((bf16[64,64,384]{2,1,0:T(8,128)(2,1)}), bf16[64,64,384]{2,1,0:T(8,128)(2,1)}, u32[]{:S(2)}, u32[]{:S(2)}) async-start(bf16[64,64,384]{2,1,0:T(8,128)(2,1)} %get-tuple-element.53), calls=%async_computation.3 | async-start | bytes 6291456 | tf_op jit(solution)/shard_map/all_to_all | solution.py:288
  202.2 5.5 %shard_map.126.refs_6_ = bf16[18,128,1536]{2,1,0:T(8,128)(2,1)} custom-call(s32[18]{0:T(128)} %get-tuple-element.75.src_ref, s32[18]{0:T(128)} %get-tuple-element.74.rank_ref, bf16[16,2,2,128,384]{4,3,2,1,0:T(8,128)(2,1)} %bitcast.27.refs_0_.refs_1_.refs_2_.refs_3_.refs_4_.refs_5_, ...), custom_call_target="tpu_custom_call" | custom-call | tf_op jit(solution)/shard_map/pallas_call | solution.py:147
  207.7 4.4 %shard_map.127.refs_6_ = bf16[18,128,1536]{2,1,0:T(8,128)(2,1)} custom-call(s32[18]{0:T(128)} %get-tuple-element.75.src_ref, s32[18]{0:T(128)} %get-tuple-element.74.rank_ref, bf16[16,2,2,80,384]{4,3,2,1,0:T(8,128)(2,1)} %bitcast.26.refs_0_.refs_1_.refs_2_.refs_3_.refs_4_.refs_5_, ...), custom_call_target="tpu_custom_call", output_to_operand_aliasing={{}: (8, {})} | custom-call | tf_op jit(solution)/shard_map/pallas_call | solution.py:147
  212.1 28.9 %all-to-all-done.2 = bf16[64,64,384]{2,1,0:T(8,128)(2,1)} async-done(((bf16[64,64,384]{2,1,0:T(8,128)(2,1)}), bf16[64,64,384]{2,1,0:T(8,128)(2,1)}, u32[]{:S(2)}, u32[]{:S(2)}) %all-to-all-start.2) | async-done | bytes 3145760 | tf_op jit(solution)/shard_map/all_to_all | solution.py:288
  241.0 4.5 %shard_map.128 = bf16[18,128,1536]{2,1,0:T(8,128)(2,1)} custom-call(s32[18]{0:T(128)} %get-tuple-element.75.src_ref, s32[18]{0:T(128)} %get-tuple-element.74.rank_ref, bf16[16,2,2,64,384]{4,3,2,1,0:T(8,128)(2,1)} %bitcast.25.refs_0_.refs_1_.refs_2_.refs_3_.refs_4_.refs_5_, ...), custom_call_target="tpu_custom_call", output_to_operand_aliasing={{}: (8, {})} | custom-call | tf_op jit(solution)/shard_map/pallas_call | solution.py:147
  (72 shorter events, 24.0 us)
Async XLA Ops:
  7.2 171.6 %copy-start = (bf16[384,3072]{1,0:T(8,128)(2,1)S(1)}, bf16[384,3072]{1,0:T(8,128)(2,1)}, u32[]{:S(2)}) copy-start(bf16[384,3072]{1,0:T(8,128)(2,1)} %param.20) | copy-start | bytes 7077892
  7.2 9.5 %copy-start.13 = (s32[1,4]{1,0:T(1,128)S(1)}, s32[1,4]{1,0:T(1,128)}, u32[]{:S(2)}) copy-start(s32[1,4]{1,0:T(1,128)} %param.24) | copy-start | bytes 52
  7.2 9.7 %copy-start.9 = (s32[1,4]{1,0:T(1,128)S(1)}, s32[1,4]{1,0:T(1,128)}, u32[]{:S(2)}) copy-start(s32[1,4]{1,0:T(1,128)} %param.23) | copy-start | bytes 52
  7.2 33.4 %all-gather.2.cloned.1.call-start = ((), (), s32[]{:S(2)}) async-start(), calls=%async_computation.4 | async-start | bytes 3649536 | tf_op jit(solution)/shard_map/all_gather | solution.py:186
  11.4 5.6 %copy-start.8 = (s32[36]{0:T(128)}, s32[36]{0:T(128)S(1)}, u32[]{:S(2)}) copy-start(s32[36]{0:T(128)S(1)} %multiply_add_fusion) | copy-start | bytes 436
  43.2 4.0 %copy-start.10 = (bf16[3072,384]{1,0:T(8,128)(2,1)S(1)}, bf16[3072,384]{1,0:T(8,128)(2,1)}, u32[]{:S(2)}) copy-start(bf16[3072,384]{1,0:T(8,128)(2,1)} %param.19) | copy-start | bytes 7077892
  47.3 2.5 %copy-start.4 = (bf16[512,3072]{1,0:T(8,128)(2,1)}, bf16[512,3072]{1,0:T(8,128)(2,1)S(1)}, u32[]{:S(2)}) copy-start(bf16[512,3072]{1,0:T(8,128)(2,1)S(1)} %fusion.8) | copy-start | bytes 9437188
  53.6 57.9 %all-to-all-start.1 = ((bf16[64,80,384]{2,1,0:T(8,128)(2,1)}), bf16[64,80,384]{2,1,0:T(8,128)(2,1)}, u32[]{:S(2)}, u32[]{:S(2)}) async-start(bf16[64,80,384]{2,1,0:T(8,128)(2,1)} %get-tuple-element.48), calls=%async_computation.1 | async-start | bytes 7864320 | tf_op jit(solution)/shard_map/all_to_all | solution.py:242
  61.1 3.1 %copy-start.5 = (bf16[512,3072]{1,0:T(8,128)(2,1)S(1)}, bf16[512,3072]{1,0:T(8,128)(2,1)}, u32[]{:S(2)}) copy-start(bf16[512,3072]{1,0:T(8,128)(2,1)} %copy-done.4) | copy-start | bytes 9437188
  61.1 3.1 %copy-start.11 = (bf16[3072,384]{1,0:T(8,128)(2,1)S(1)}, bf16[3072,384]{1,0:T(8,128)(2,1)}, u32[]{:S(2)}) copy-start(bf16[3072,384]{1,0:T(8,128)(2,1)} %param.17) | copy-start | bytes 7077892
  64.2 1.7 copy-start.12
  68.5 3.9 %copy-start.2 = (bf16[512,384]{1,0:T(8,128)(2,1)S(1)}, bf16[512,384]{1,0:T(8,128)(2,1)}, u32[]{:S(2)}) copy-start(bf16[512,384]{1,0:T(8,128)(2,1)} %copy.31.rest_0_) | copy-start | bytes 1179652
  111.6 82.8 %all-to-all-start = ((bf16[64,128,384]{2,1,0:T(8,128)(2,1)}), bf16[64,128,384]{2,1,0:T(8,128)(2,1)}, u32[]{:S(2)}, u32[]{:S(2)}) async-start(bf16[64,128,384]{2,1,0:T(8,128)(2,1)} %shard_map.125), calls=%async_computation | async-start | bytes 12582912 | tf_op jit(solution)/shard_map/all_to_all | solution.py:258
  116.5 129.0 %reduce-scatter.2.cloned.1.call-start = ((), (), s32[]{:S(2)}) async-start(), calls=%async_computation.5 | async-start | bytes 7077888 | tf_op jit(solution)/shard_map/reduce_scatter | solution.py:286
  116.7 18.6 %copy-start.7 = (bf16[512,384]{1,0:T(8,128)(2,1)S(1)}, bf16[512,384]{1,0:T(8,128)(2,1)}, u32[]{:S(2)}) copy-start(bf16[512,384]{1,0:T(8,128)(2,1)} %convolution_convert_fusion.rest_0_) | copy-start | bytes 1179652
  145.2 18.2 %copy-start.1 = (pred[512,4608]{1,0:T(8,128)(4,1)S(1)}, pred[512,4608]{1,0:T(8,128)(4,1)}, u32[]{:S(2)}) copy-start(pred[512,4608]{1,0:T(8,128)(4,1)} %pad_add_fusion) | copy-start | bytes 7077892
  145.2 18.2 %copy-start.3 = (bf16[4608,384]{0,1:T(8,128)(2,1)S(1)}, bf16[4608,384]{0,1:T(8,128)(2,1)}, u32[]{:S(2)}) copy-start(bf16[4608,384]{0,1:T(8,128)(2,1)} %copy.32) | copy-start | bytes 10616836
  194.4 46.6 %all-to-all-start.2 = ((bf16[64,64,384]{2,1,0:T(8,128)(2,1)}), bf16[64,64,384]{2,1,0:T(8,128)(2,1)}, u32[]{:S(2)}, u32[]{:S(2)}) async-start(bf16[64,64,384]{2,1,0:T(8,128)(2,1)} %get-tuple-element.53), calls=%async_computation.3 | async-start | bytes 6291456 | tf_op jit(solution)/shard_map/all_to_all | solution.py:288
  241.0 4.5 %copy-start.6 = (bf16[512,384]{1,0:T(8,128)(2,1)S(1)}, bf16[512,384]{1,0:T(8,128)(2,1)}, u32[]{:S(2)}) copy-start(bf16[512,384]{1,0:T(8,128)(2,1)} %param.15) | copy-start | bytes 1179652
Sparse Core Ops, SparseCore 0:
  10.0 30.5 all-gather.1
  194.5 38.2 reduce-scatter.1

commit v13 on v12

--- a/solution.py
+++ b/solution.py
@@ -68,7 +68,7 @@
     return jnp.sum(same * earlier_mask, axis=-1)
 
 
-def pack_pages(slots, sources, parts, slot_total, into=(), shapes=None):
+def pack_pages(slots, sources, parts, slot_total, into=(), shapes=None, paired=()):
     page_total = sources[0].shape[0] // PAGE
     width = sources[0].shape[1]
 
@@ -83,11 +83,24 @@
     if shapes is None:
         shapes = [rows for _, _, rows in parts]
     out_shape = tuple(
-        jax.ShapeDtypeStruct((slot_total, full, width), jnp.bfloat16) for full in shapes
-    )
+        jax.ShapeDtypeStruct(
+            (slot_total // CAPACITY if index in paired else slot_total, full, width),
+            jnp.bfloat16,
+        )
+        for index, full in enumerate(shapes)
+    )
+
+    def out_map(index):
+        if index in paired:
+            return lambda page, slot_ref: (
+                slot_ref[page] // CAPACITY,
+                slot_ref[page] % CAPACITY,
+                0,
+            )
+        return lambda page, slot_ref: (slot_ref[page], 0, 0)
+
     out_specs = tuple(
-        pl.BlockSpec((1, rows, width), lambda page, slot_ref: (slot_ref[page], 0, 0))
-        for _, _, rows in parts
+        pl.BlockSpec((1, rows, width), out_map(index)) for index, (_, _, rows) in enumerate(parts)
     )
     first_alias = 1 + len(sources)
     return pl.pallas_call(
@@ -104,35 +117,49 @@
 
 
 def stamp_tags(tags, first_row):
-    slot_total, tag_rows, width = tags.shape
+    dest_total, tag_rows, width = tags.shape
 
     def body(tag_block, out):
         out[...] = tag_block[...]
 
     return pl.pallas_call(
         body,
-        out_shape=jax.ShapeDtypeStruct((slot_total, first_row + tag_rows, width), jnp.bfloat16),
+        out_shape=jax.ShapeDtypeStruct((dest_total, first_row + tag_rows, width), jnp.bfloat16),
         grid=(1,),
-        in_specs=[pl.BlockSpec((slot_total, tag_rows, width), lambda step: (0, 0, 0))],
+        in_specs=[pl.BlockSpec((dest_total, tag_rows, width), lambda step: (0, 0, 0))],
         out_specs=pl.BlockSpec(
-            (slot_total, tag_rows, width), lambda step: (0, first_row // tag_rows, 0)
+            (dest_total, tag_rows, width), lambda step: (0, first_row // tag_rows, 0)
         ),
     )(tags)
 
 
 def place_pages(
-    sources, ranks, received, slot_count, cores, part, row_block, rows, into=(), group=6
+    sources, ranks, received, slot_count, cores, part, row_block, rows, into=(), group=6,
+    paired=False,
 ):
     stored, width = received.shape[-2:]
-    shaped = received.reshape(-1, cores, CAPACITY, stored, width)
+    if paired:
+        shaped = received.reshape(-1, cores, stored, width)
+        block = (1, cores, rows, width)
+    else:
+        shaped = received.reshape(-1, cores, CAPACITY, stored, width)
+        block = (1, cores, 1, rows, width)
 
     def body(src_ref, rank_ref, *refs):
         out = refs[-1]
         for member in range(group):
             for core in range(cores):
-                out[member, :, core * width : (core + 1) * width] = refs[member][0, core, 0]
+                piece = refs[member][0, core] if paired else refs[member][0, core, 0]
+                out[member, :, core * width : (core + 1) * width] = piece
 
     def source_map(member):
+        if paired:
+            return lambda step, src_ref, rank_ref: (
+                src_ref[step * group + member],
+                0,
+                rank_ref[step * group + member],
+                0,
+            )
         return lambda step, src_ref, rank_ref: (
             src_ref[step * group + member],
             0,
@@ -142,7 +169,7 @@
         )
 
     in_specs = [
-        pl.BlockSpec((1, cores, 1, rows, width), source_map(member)) for member in range(group)
+        pl.BlockSpec(block, source_map(member)) for member in range(group)
     ] + [pl.BlockSpec(memory_space=pl.ANY)] * len(into)
     return pl.pallas_call(
         body,
@@ -217,16 +244,19 @@
         .at[send_slots]
         .set((page_table[0] % slot_count).astype(jnp.int32))
     )
-    tags = jnp.zeros((slot_total, tag_rows, local_width), jnp.bfloat16)
-    tags = tags.at[:, 0, 0].set(carried.astype(jnp.bfloat16))
-    send_low = stamp_tags(tags, half_rows)
+    tags = jnp.zeros((dest_count, tag_rows, local_width), jnp.bfloat16)
+    tags = tags.at[:, 0, :CAPACITY].set(
+        carried.reshape(dest_count, CAPACITY).astype(jnp.bfloat16)
+    )
+    send_low = stamp_tags(tags, CAPACITY * half_rows)
     send_keys, send_low, send_high = pack_pages(
         send_slots[:prev_pages],
         (prev_keys, prev_values),
         both,
         slot_total,
         into={1: send_low},
-        shapes=(PAGE, half_rows + tag_rows, half_rows),
+        shapes=(PAGE, CAPACITY * half_rows + tag_rows, half_rows),
+        paired=(1,),
     )
     send_low, send_high = pack_pages(
         send_slots[prev_pages:],
@@ -234,13 +264,14 @@
         halves,
         slot_total,
         into={0: send_low, 1: send_high},
-        shapes=(half_rows + tag_rows, half_rows),
+        shapes=(CAPACITY * half_rows + tag_rows, half_rows),
+        paired=(0,),
     )
     send_keys, send_low, send_high, normed, new_values = lax.optimization_barrier(
         (send_keys, send_low, send_high, normed, new_values)
     )
     received_low = lax.all_to_all(send_low, ("req", "core"), 0, 0, tiled=True)
-    carried = received_low[:, half_rows, 0].astype(jnp.int32)
+    carried = received_low[:, CAPACITY * half_rows, :CAPACITY].astype(jnp.int32)
     carried = carried.reshape(req_count, cores, CAPACITY)[:, 0, :].reshape(-1)
     wanted = jnp.arange(slot_count, dtype=jnp.int32)
     found = jnp.argmax(carried[None, :] == wanted[:, None], axis=1).astype(jnp.int32)
@@ -289,7 +320,8 @@
     half_rows = PAGE // 2
     pool = place_pages(from_req, from_rank, received_keys, slot_count, cores, 0, 0, PAGE)
     pool = place_pages(
-        from_req, from_rank, received_low, slot_count, cores, 1, 0, half_rows, into=(pool,)
+        from_req, from_rank, received_low, slot_count, cores, 1, 0, half_rows, into=(pool,),
+        paired=True,
     )
     pool = place_pages(
         from_req, from_rank, received_high, slot_count, cores, 1, 1, half_rows, into=(pool,)

time: 257 us -> 252 us (0.981)
  waiting for transfers between devices: 73.1 us -> 69.5 us
    all_to_all x1, waiting for transfers between devices: 29.4 us -> 25 us  [shards(): received_low = lax.all_to_all(send_low, ('req', 'core'), 0, 0, tiled=True)]
  transfers between devices with their start and end apart: 5 -> 5, of which waited for: 4 -> 4; matrix products, arithmetic and copies ran while one was open for 36% -> 37% of each run, Pallas kernels for 16% -> 16%
where the time goes in v13:
time: 252 us; the launch traced here: 250 us
  waiting for transfers between devices  69.5 us (28%)
  other arithmetic  44.5 us (18%)
  matrix products  43.8 us (17%)
  Pallas kernels  43.2 us (17%)
  starting transfers between devices  17.4 us (7%)
  local copies, waits for them, and re-layouts  17.2 us (7%)
  between operations  14.3 us (6%)
    all_to_all x1, waiting for transfers between devices, shards(): received_high = lax.all_to_all(send_high, ('req', 'core'), 0, 0, tiled=True)  29.5 us
    pallas_call x3, Pallas kernels, pack_pages(): pl.pallas_call(body, out_shape=out_shape, grid_spec=pltpu.PrefetchScalarG...  27.1 us
    all_to_all x1, waiting for transfers between devices, shards(): received_low = lax.all_to_all(send_low, ('req', 'core'), 0, 0, tiled=True)  25 us
    dot_general x1, matrix products, shards(): jnp.einsum('qhd,khd->hqk', queries.reshape(token_count, heads_here, HD),...  18.6 us
    reduce_sum x1, other arithmetic, shards(): totals = jnp.sum(weights, axis=2)  18.2 us
    dot_general x1, matrix products, shards(): jnp.einsum('hqk,khd->qhd', prob_rows, values_all.reshape(-1, heads_here,...  15.3 us
    pallas_call x3, Pallas kernels, place_pages(): pl.pallas_call(body, out_shape=jax.ShapeDtypeStruct((slot_count, PAGE, 2...  14.4 us
    all_to_all x1, waiting for transfers between devices, shards(): received_keys = lax.all_to_all(send_keys, ('req', 'core'), 0, 0, tiled=True)  11.1 us
  transfers between devices with their start and end apart: 5, of which 4 were waited for; matrix products, arithmetic and copies ran while one was open for 37% of the time, Pallas kernels for 16%

profile of v13, /device:TPU:0, one launch (start us, length us, event | category | flops | bytes accessed | tf_op | source)
XLA Modules:
  0.0 249.9 jit_solution(14780734758979077197)
XLA Ops:
  16.5 19.4 %shard_map.123 = (bf16[64,128,384]{2,1,0:T(8,128)(2,1)}, bf16[32,144,384]{2,1,0:T(8,128)(2,1)}, bf16[64,64,384]{2,1,0:T(8,128)(2,1)}) custom-call(s32[32]{0:T(128)} %bitcast.85, bf16[4096,384]{1,0:T(8,128)(2,1)} %rest_0_.1, bf16[4096,384]{1,0:T(8,128)(2,1)} %rest_1_.1, bf16[32,144,384]{2,1,0:T(8,128)(2,1)} %shard_map.122.rest_2_), custom_call_target="tpu_custom_call", output_to_operand_aliasing={{1}: (3, {})} | custom-call | tf_op jit(solution)/shard_map/pallas_call | solution.py:106
  36.8 3.8 %all-gather.2.cloned.1.call-done = bf16[528,3072]{1,0:T(8,128)(2,1)} async-done(((bf16[528,384]{1,0:T(8,128)(2,1)}), bf16[528,3072]{1,0:T(8,128)(2,1)}) %all-gather.2.cloned.1.call-update) | async-done | bytes 3244048 | tf_op jit(solution)/shard_map/all_gather | solution.py:213
  40.6 2.6 %fusion.6 = f32[512]{0:T(512)S(1)} fusion(bf16[528,3072]{1,0:T(8,128)(2,1)} %all-gather.2.cloned.1.call-done), kind=kLoop, calls=%fused_computation.11 | loop fusion | flops 4718080 | bytes 3147776 | tf_op jit(solution)/shard_map/reduce_sum | solution.py:219
  44.2 3.1 %fusion.8 = bf16[512,3072]{1,0:T(8,128)(2,1)S(1)} fusion(f32[3072]{0:T(1024)S(1)} %bitcast.82, f32[512]{0:T(512)S(1)} %add_rsqrt_fusion, bf16[528,3072]{1,0:T(8,128)(2,1)} %all-gather.2.cloned.1.call-done), kind=kLoop, calls=%fused_computation.13 | loop fusion | flops 6291456 | bytes 6305792 | tf_op jit(solution)/shard_map/convert_element_type | solution.py:220
  47.3 2.5 %convolution_convert_fusion.rest_0_ = bf16[512,384]{1,0:T(8,128)(2,1)} fusion(bf16[512,3072]{1,0:T(8,128)(2,1)S(1)} %fusion.8, bf16[3072,384]{1,0:T(8,128)(2,1)S(1)} %copy-done.10), kind=kOutput, calls=%fused_computation.18 | convolution fusion | flops 1208156160 | bytes 5898240 | tf_op jit(solution)/shard_map/dot_general | solution.py:223
  49.8 3.8 %shard_map.124 = (bf16[32,144,384]{2,1,0:T(8,128)(2,1)}, bf16[64,64,384]{2,1,0:T(8,128)(2,1)}) custom-call(s32[4]{0:T(128)} %slice.69.slot_ref, bf16[512,384]{1,0:T(8,128)(2,1)} %convolution_convert_fusion.rest_0_, bf16[32,144,384]{2,1,0:T(8,128)(2,1)} %get-tuple-element.42.rest_1_, ...), custom_call_target="tpu_custom_call", output_to_operand_aliasing={{0}: (2, {}), {1}: (3, {})} | custom-call | tf_op jit(solution)/shard_map/pallas_call | solution.py:106
  53.6 7.3 %all-to-all-start.1 = ((bf16[32,144,384]{2,1,0:T(8,128)(2,1)}), bf16[32,144,384]{2,1,0:T(8,128)(2,1)}, u32[]{:S(2)}, u32[]{:S(2)}) async-start(bf16[32,144,384]{2,1,0:T(8,128)(2,1)} %get-tuple-element.48), calls=%async_computation.1 | async-start | bytes 7077888 | tf_op jit(solution)/shard_map/all_to_all | solution.py:273
  68.4 3.9 %shard_map.125 = bf16[64,128,384]{2,1,0:T(8,128)(2,1)} custom-call(s32[4]{0:T(128)} %slice.69.slot_ref, bf16[512,384]{1,0:T(8,128)(2,1)} %copy.43.rest_0_, bf16[64,128,384]{2,1,0:T(8,128)(2,1)} %get-tuple-element.47.rest_1_), custom_call_target="tpu_custom_call", output_to_operand_aliasing={{}: (2, {})} | custom-call | tf_op jit(solution)/shard_map/pallas_call | solution.py:106
  72.3 4.1 %pad_maximum_fusion.1 = bf16[4608,384]{1,0:T(8,128)(2,1)} fusion(bf16[512,384]{1,0:T(8,128)(2,1)S(1)} %copy-done.2, bf16[4096,384]{1,0:T(8,128)(2,1)} %rest_0_.1), kind=kLoop, calls=%fused_computation.16 | loop fusion | flops 7077888 | bytes 7077888 | tf_op jit(solution)/shard_map/concatenate | solution.py:285
  76.3 5.8 %copy.46 = bf16[4608,384]{0,1:T(8,128)(2,1)} copy(bf16[4608,384]{1,0:T(8,128)(2,1)} %pad_maximum_fusion.1) | data formatting | bytes 7077888 | tf_op jit(solution)/shard_map/concatenate | solution.py:285
  82.1 25.0 %all-to-all-done.1 = bf16[32,144,384]{2,1,0:T(8,128)(2,1)} async-done(((bf16[32,144,384]{2,1,0:T(8,128)(2,1)}), bf16[32,144,384]{2,1,0:T(8,128)(2,1)}, u32[]{:S(2)}, u32[]{:S(2)}) %all-to-all-start.1) | async-done | bytes 3538976 | tf_op jit(solution)/shard_map/all_to_all | solution.py:273
  107.2 4.9 %all-to-all-start = ((bf16[64,128,384]{2,1,0:T(8,128)(2,1)}), bf16[64,128,384]{2,1,0:T(8,128)(2,1)}, u32[]{:S(2)}, u32[]{:S(2)}) async-start(bf16[64,128,384]{2,1,0:T(8,128)(2,1)} %shard_map.125), calls=%async_computation | async-start | bytes 12582912 | tf_op jit(solution)/shard_map/all_to_all | solution.py:289
  112.3 18.6 %fusion = (f32[4,512]{1,0:T(4,128)S(1)}, f32[4,512,4608]{2,1,0:T(8,128)}) fusion(pred[512,4608]{1,0:T(8,128)(4,1)} %pad_add_fusion, bf16[4608,4,96]{0,2,1:T(8,128)(2,1)} %bitcast.76, bf16[512,4,48]{0,2,1:T(8,128)(2,1)S(1)} %get-tuple-element.69, bf16[512,4,48]{0,2,1:T(8,128)(2,1)S(1)} %get-tuple-element.68), kind=kOutput, calls=%fused_computation.3 | convolution fusion | flops 1841035264 | bytes 44048384 | tf_op jit(solution)/shard_map/qhd,khd->hqk/dot_general | solution.py:293
  130.9 4.1 %pad_maximum_fusion = bf16[4608,384]{1,0:T(8,128)(2,1)} fusion(bf16[512,384]{1,0:T(8,128)(2,1)S(1)} %copy-done.6, bf16[4096,384]{1,0:T(8,128)(2,1)} %rest_1_.1), kind=kLoop, calls=%fused_computation.15 | loop fusion | flops 7077888 | bytes 7077888 | tf_op jit(solution)/shard_map/concatenate | solution.py:286
  135.0 5.8 %copy.44 = bf16[4608,384]{0,1:T(8,128)(2,1)} copy(bf16[4608,384]{1,0:T(8,128)(2,1)} %pad_maximum_fusion) | data formatting | bytes 7077888 | tf_op jit(solution)/shard_map/concatenate | solution.py:286
  140.9 18.2 %fusion.1 = f32[4,512]{1,0:T(4,128)S(1)} fusion(f32[4,512,4608]{2,1,0:T(8,128)} %get-tuple-element.80, f32[4,512]{1,0:T(4,128)S(1)} %get-tuple-element.79, pred[512,4608]{1,0:T(8,128)(4,1)} %pad_add_fusion), kind=kLoop, calls=%fused_computation.4 | loop fusion | flops 37746688 | bytes 40124416 | tf_op jit(solution)/shard_map/reduce_sum | solution.py:302
  159.1 15.3 %fusion.15 = bf16[512,4,96]{0,2,1:T(8,128)(2,1)S(1)} fusion(bf16[4608,4,96]{0,2,1:T(8,128)(2,1)S(1)} %bitcast.77, f32[4,512,4608]{2,1,0:T(8,128)} %get-tuple-element.80, f32[4,512]{1,0:T(4,128)S(1)} %get-tuple-element.79, pred[512,4608]{1,0:T(8,128)(4,1)S(1)} %copy-done.1, f32[512,4]{0,1:T(4,128)S(1)} %bitcast.84), kind=kOutput, calls=%fused_computation.20 | convolution fusion | flops 1850081280 | bytes 44056576 | tf_op jit(solution)/shard_map/hqk,khd->qhd/dot_general | solution.py:304
  174.5 4.5 %fusion.38 = f32[512,3072]{1,0:T(8,128)} fusion(bf16[512,384]{0,1:T(8,128)(2,1)S(1)} %bitcast.81, bf16[384,3072]{1,0:T(8,128)(2,1)S(1)} %copy-done), kind=kOutput, calls=%fused_computation.81 | convolution fusion | flops 1207959552 | bytes 9043968 | tf_op jit(solution)/shard_map/dot_general | solution.py:313
  179.0 11.1 %all-to-all-done = bf16[64,128,384]{2,1,0:T(8,128)(2,1)} async-done(((bf16[64,128,384]{2,1,0:T(8,128)(2,1)}), bf16[64,128,384]{2,1,0:T(8,128)(2,1)}, u32[]{:S(2)}, u32[]{:S(2)}) %all-to-all-start) | async-done | bytes 6291488 | tf_op jit(solution)/shard_map/all_to_all | solution.py:289
  190.0 4.8 %all-to-all-start.2 = ((bf16[64,64,384]{2,1,0:T(8,128)(2,1)}), bf16[64,64,384]{2,1,0:T(8,128)(2,1)}, u32[]{:S(2)}, u32[]{:S(2)}) async-start(bf16[64,64,384]{2,1,0:T(8,128)(2,1)} %get-tuple-element.53), calls=%async_computation.3 | async-start | bytes 6291456 | tf_op jit(solution)/shard_map/all_to_all | solution.py:319
  197.2 5.5 %shard_map.126.refs_6_ = bf16[18,128,1536]{2,1,0:T(8,128)(2,1)} custom-call(s32[18]{0:T(128)} %get-tuple-element.77.src_ref, s32[18]{0:T(128)} %get-tuple-element.76.rank_ref, bf16[16,2,2,128,384]{4,3,2,1,0:T(8,128)(2,1)} %bitcast.26.refs_0_.refs_1_.refs_2_.refs_3_.refs_4_.refs_5_, ...), custom_call_target="tpu_custom_call" | custom-call | tf_op jit(solution)/shard_map/pallas_call | solution.py:174
  202.7 4.4 %shard_map.127.refs_6_ = bf16[18,128,1536]{2,1,0:T(8,128)(2,1)} custom-call(s32[18]{0:T(128)} %get-tuple-element.77.src_ref, s32[18]{0:T(128)} %get-tuple-element.76.rank_ref, bf16[16,2,144,384]{3,2,1,0:T(8,128)(2,1)} %bitcast.25.refs_0_.refs_1_.refs_2_.refs_3_.refs_4_.refs_5_, ...), custom_call_target="tpu_custom_call", output_to_operand_aliasing={{}: (8, {})} | custom-call | tf_op jit(solution)/shard_map/pallas_call | solution.py:174
  207.1 29.5 %all-to-all-done.2 = bf16[64,64,384]{2,1,0:T(8,128)(2,1)} async-done(((bf16[64,64,384]{2,1,0:T(8,128)(2,1)}), bf16[64,64,384]{2,1,0:T(8,128)(2,1)}, u32[]{:S(2)}, u32[]{:S(2)}) %all-to-all-start.2) | async-done | bytes 3145760 | tf_op jit(solution)/shard_map/all_to_all | solution.py:319
  236.7 4.5 %shard_map.128 = bf16[18,128,1536]{2,1,0:T(8,128)(2,1)} custom-call(s32[18]{0:T(128)} %get-tuple-element.77.src_ref, s32[18]{0:T(128)} %get-tuple-element.76.rank_ref, bf16[16,2,2,64,384]{4,3,2,1,0:T(8,128)(2,1)} %bitcast.24.refs_0_.refs_1_.refs_2_.refs_3_.refs_4_.refs_5_, ...), custom_call_target="tpu_custom_call", output_to_operand_aliasing={{}: (8, {})} | custom-call | tf_op jit(solution)/shard_map/pallas_call | solution.py:174
  (74 shorter events, 23.0 us)
Async XLA Ops:
  7.2 167.3 %copy-start = (bf16[384,3072]{1,0:T(8,128)(2,1)S(1)}, bf16[384,3072]{1,0:T(8,128)(2,1)}, u32[]{:S(2)}) copy-start(bf16[384,3072]{1,0:T(8,128)(2,1)} %param.20) | copy-start | bytes 7077892
  7.2 9.0 %copy-start.13 = (s32[1,4]{1,0:T(1,128)S(1)}, s32[1,4]{1,0:T(1,128)}, u32[]{:S(2)}) copy-start(s32[1,4]{1,0:T(1,128)} %param.24) | copy-start | bytes 52
  7.2 9.1 %copy-start.9 = (s32[1,4]{1,0:T(1,128)S(1)}, s32[1,4]{1,0:T(1,128)}, u32[]{:S(2)}) copy-start(s32[1,4]{1,0:T(1,128)} %param.23) | copy-start | bytes 52
  7.2 33.4 %all-gather.2.cloned.1.call-start = ((), (), s32[]{:S(2)}) async-start(), calls=%async_computation.4 | async-start | bytes 3649536 | tf_op jit(solution)/shard_map/all_gather | solution.py:213
  11.4 5.1 %copy-start.8 = (s32[36]{0:T(128)}, s32[36]{0:T(128)S(1)}, u32[]{:S(2)}) copy-start(s32[36]{0:T(128)S(1)} %multiply_add_fusion) | copy-start | bytes 436
  43.2 4.0 %copy-start.10 = (bf16[3072,384]{1,0:T(8,128)(2,1)S(1)}, bf16[3072,384]{1,0:T(8,128)(2,1)}, u32[]{:S(2)}) copy-start(bf16[3072,384]{1,0:T(8,128)(2,1)} %param.19) | copy-start | bytes 7077892
  47.3 2.5 %copy-start.4 = (bf16[512,3072]{1,0:T(8,128)(2,1)}, bf16[512,3072]{1,0:T(8,128)(2,1)S(1)}, u32[]{:S(2)}) copy-start(bf16[512,3072]{1,0:T(8,128)(2,1)S(1)} %fusion.8) | copy-start | bytes 9437188
  53.6 53.6 %all-to-all-start.1 = ((bf16[32,144,384]{2,1,0:T(8,128)(2,1)}), bf16[32,144,384]{2,1,0:T(8,128)(2,1)}, u32[]{:S(2)}, u32[]{:S(2)}) async-start(bf16[32,144,384]{2,1,0:T(8,128)(2,1)} %get-tuple-element.48), calls=%async_computation.1 | async-start | bytes 7077888 | tf_op jit(solution)/shard_map/all_to_all | solution.py:273
  61.0 2.9 %copy-start.5 = (bf16[512,3072]{1,0:T(8,128)(2,1)S(1)}, bf16[512,3072]{1,0:T(8,128)(2,1)}, u32[]{:S(2)}) copy-start(bf16[512,3072]{1,0:T(8,128)(2,1)} %copy-done.4) | copy-start | bytes 9437188
  61.0 3.0 %copy-start.11 = (bf16[3072,384]{1,0:T(8,128)(2,1)S(1)}, bf16[3072,384]{1,0:T(8,128)(2,1)}, u32[]{:S(2)}) copy-start(bf16[3072,384]{1,0:T(8,128)(2,1)} %param.17) | copy-start | bytes 7077892
  64.0 1.7 copy-start.12
  68.4 3.9 %copy-start.2 = (bf16[512,384]{1,0:T(8,128)(2,1)S(1)}, bf16[512,384]{1,0:T(8,128)(2,1)}, u32[]{:S(2)}) copy-start(bf16[512,384]{1,0:T(8,128)(2,1)} %copy.43.rest_0_) | copy-start | bytes 1179652
  107.2 82.8 %all-to-all-start = ((bf16[64,128,384]{2,1,0:T(8,128)(2,1)}), bf16[64,128,384]{2,1,0:T(8,128)(2,1)}, u32[]{:S(2)}, u32[]{:S(2)}) async-start(bf16[64,128,384]{2,1,0:T(8,128)(2,1)} %shard_map.125), calls=%async_computation | async-start | bytes 12582912 | tf_op jit(solution)/shard_map/all_to_all | solution.py:289
  112.1 129.0 %reduce-scatter.2.cloned.1.call-start = ((), (), s32[]{:S(2)}) async-start(), calls=%async_computation.5 | async-start | bytes 7077888 | tf_op jit(solution)/shard_map/reduce_scatter | solution.py:317
  112.3 18.6 %copy-start.6 = (bf16[512,384]{1,0:T(8,128)(2,1)S(1)}, bf16[512,384]{1,0:T(8,128)(2,1)}, u32[]{:S(2)}) copy-start(bf16[512,384]{1,0:T(8,128)(2,1)} %convolution_convert_fusion.rest_0_) | copy-start | bytes 1179652
  140.9 18.2 %copy-start.1 = (pred[512,4608]{1,0:T(8,128)(4,1)S(1)}, pred[512,4608]{1,0:T(8,128)(4,1)}, u32[]{:S(2)}) copy-start(pred[512,4608]{1,0:T(8,128)(4,1)} %pad_add_fusion) | copy-start | bytes 7077892
  140.9 18.2 %copy-start.3 = (bf16[4608,384]{0,1:T(8,128)(2,1)S(1)}, bf16[4608,384]{0,1:T(8,128)(2,1)}, u32[]{:S(2)}) copy-start(bf16[4608,384]{0,1:T(8,128)(2,1)} %copy.44) | copy-start | bytes 10616836
  190.0 46.6 %all-to-all-start.2 = ((bf16[64,64,384]{2,1,0:T(8,128)(2,1)}), bf16[64,64,384]{2,1,0:T(8,128)(2,1)}, u32[]{:S(2)}, u32[]{:S(2)}) async-start(bf16[64,64,384]{2,1,0:T(8,128)(2,1)} %get-tuple-element.53), calls=%async_computation.3 | async-start | bytes 6291456 | tf_op jit(solution)/shard_map/all_to_all | solution.py:319
  236.7 4.5 %copy-start.7 = (bf16[512,384]{1,0:T(8,128)(2,1)S(1)}, bf16[512,384]{1,0:T(8,128)(2,1)}, u32[]{:S(2)}) copy-start(bf16[512,384]{1,0:T(8,128)(2,1)} %param.15) | copy-start | bytes 1179652
Sparse Core Ops, SparseCore 0:
  10.0 30.5 all-gather.1
  190.2 38.2 reduce-scatter.1

commit v14 on v13

--- a/solution.py
+++ b/solution.py
@@ -134,7 +134,7 @@
 
 
 def place_pages(
-    sources, ranks, received, slot_count, cores, part, row_block, rows, into=(), group=6,
+    sources, ranks, received, slot_count, cores, part, row_block, rows, into=(), group=9,
     paired=False,
 ):
     stored, width = received.shape[-2:]

time: 252 us -> 251 us (level)
  Pallas kernels: 43.2 us -> 40 us
    pallas_call x3, Pallas kernels: 14.4 us -> 11.2 us  [place_pages(): pl.pallas_call(body, out_shape=jax.ShapeDtypeStruct((slot_count, PAGE, 2...]
  transfers between devices with their start and end apart: 5 -> 5, of which waited for: 4 -> 4; matrix products, arithmetic and copies ran while one was open for 37% -> 37% of each run, Pallas kernels for 16% -> 15%
where the time goes in v14:
time: 251 us; the launch traced here: 249 us
  waiting for transfers between devices  71.7 us (29%)
  other arithmetic  44.5 us (18%)
  matrix products  43.8 us (17%)
  Pallas kernels  40 us (16%)
  starting transfers between devices  17.4 us (7%)
  local copies, waits for them, and re-layouts  17.2 us (7%)
  between operations  14.3 us (6%)
    all_to_all x1, waiting for transfers between devices, shards(): received_high = lax.all_to_all(send_high, ('req', 'core'), 0, 0, tiled=True)  31.7 us
    pallas_call x3, Pallas kernels, pack_pages(): pl.pallas_call(body, out_shape=out_shape, grid_spec=pltpu.PrefetchScalarG...  27.1 us
    all_to_all x1, waiting for transfers between devices, shards(): received_low = lax.all_to_all(send_low, ('req', 'core'), 0, 0, tiled=True)  25 us
    dot_general x1, matrix products, shards(): jnp.einsum('qhd,khd->hqk', queries.reshape(token_count, heads_here, HD),...  18.6 us
    reduce_sum x1, other arithmetic, shards(): totals = jnp.sum(weights, axis=2)  18.2 us
    dot_general x1, matrix products, shards(): jnp.einsum('hqk,khd->qhd', prob_rows, values_all.reshape(-1, heads_here,...  15.3 us
    pallas_call x3, Pallas kernels, place_pages(): pl.pallas_call(body, out_shape=jax.ShapeDtypeStruct((slot_count, PAGE, 2...  11.2 us
    all_to_all x1, waiting for transfers between devices, shards(): received_keys = lax.all_to_all(send_keys, ('req', 'core'), 0, 0, tiled=True)  11.1 us
  transfers between devices with their start and end apart: 5, of which 4 were waited for; matrix products, arithmetic and copies ran while one was open for 37% of the time, Pallas kernels for 15%

profile of v14, /device:TPU:0, one launch (start us, length us, event | category | flops | bytes accessed | tf_op | source)
XLA Modules:
  0.0 248.9 jit_solution(13946289216234793934)
XLA Ops:
  16.5 19.4 %shard_map.123 = (bf16[64,128,384]{2,1,0:T(8,128)(2,1)}, bf16[32,144,384]{2,1,0:T(8,128)(2,1)}, bf16[64,64,384]{2,1,0:T(8,128)(2,1)}) custom-call(s32[32]{0:T(128)} %bitcast.85, bf16[4096,384]{1,0:T(8,128)(2,1)} %rest_0_.1, bf16[4096,384]{1,0:T(8,128)(2,1)} %rest_1_.1, bf16[32,144,384]{2,1,0:T(8,128)(2,1)} %shard_map.122.rest_2_), custom_call_target="tpu_custom_call", output_to_operand_aliasing={{1}: (3, {})} | custom-call | tf_op jit(solution)/shard_map/pallas_call | solution.py:106
  36.8 3.8 %all-gather.2.cloned.1.call-done = bf16[528,3072]{1,0:T(8,128)(2,1)} async-done(((bf16[528,384]{1,0:T(8,128)(2,1)}), bf16[528,3072]{1,0:T(8,128)(2,1)}) %all-gather.2.cloned.1.call-update) | async-done | bytes 3244048 | tf_op jit(solution)/shard_map/all_gather | solution.py:213
  40.6 2.6 %fusion.6 = f32[512]{0:T(512)S(1)} fusion(bf16[528,3072]{1,0:T(8,128)(2,1)} %all-gather.2.cloned.1.call-done), kind=kLoop, calls=%fused_computation.11 | loop fusion | flops 4718080 | bytes 3147776 | tf_op jit(solution)/shard_map/reduce_sum | solution.py:219
  44.2 3.1 %fusion.8 = bf16[512,3072]{1,0:T(8,128)(2,1)S(1)} fusion(f32[3072]{0:T(1024)S(1)} %bitcast.82, f32[512]{0:T(512)S(1)} %add_rsqrt_fusion, bf16[528,3072]{1,0:T(8,128)(2,1)} %all-gather.2.cloned.1.call-done), kind=kLoop, calls=%fused_computation.13 | loop fusion | flops 6291456 | bytes 6305792 | tf_op jit(solution)/shard_map/convert_element_type | solution.py:220
  47.3 2.5 %convolution_convert_fusion.rest_0_ = bf16[512,384]{1,0:T(8,128)(2,1)} fusion(bf16[512,3072]{1,0:T(8,128)(2,1)S(1)} %fusion.8, bf16[3072,384]{1,0:T(8,128)(2,1)S(1)} %copy-done.10), kind=kOutput, calls=%fused_computation.18 | convolution fusion | flops 1208156160 | bytes 5898240 | tf_op jit(solution)/shard_map/dot_general | solution.py:223
  49.8 3.8 %shard_map.124 = (bf16[32,144,384]{2,1,0:T(8,128)(2,1)}, bf16[64,64,384]{2,1,0:T(8,128)(2,1)}) custom-call(s32[4]{0:T(128)} %slice.69.slot_ref, bf16[512,384]{1,0:T(8,128)(2,1)} %convolution_convert_fusion.rest_0_, bf16[32,144,384]{2,1,0:T(8,128)(2,1)} %get-tuple-element.42.rest_1_, ...), custom_call_target="tpu_custom_call", output_to_operand_aliasing={{0}: (2, {}), {1}: (3, {})} | custom-call | tf_op jit(solution)/shard_map/pallas_call | solution.py:106
  53.6 7.3 %all-to-all-start.1 = ((bf16[32,144,384]{2,1,0:T(8,128)(2,1)}), bf16[32,144,384]{2,1,0:T(8,128)(2,1)}, u32[]{:S(2)}, u32[]{:S(2)}) async-start(bf16[32,144,384]{2,1,0:T(8,128)(2,1)} %get-tuple-element.48), calls=%async_computation.1 | async-start | bytes 7077888 | tf_op jit(solution)/shard_map/all_to_all | solution.py:273
  68.4 3.9 %shard_map.125 = bf16[64,128,384]{2,1,0:T(8,128)(2,1)} custom-call(s32[4]{0:T(128)} %slice.69.slot_ref, bf16[512,384]{1,0:T(8,128)(2,1)} %copy.43.rest_0_, bf16[64,128,384]{2,1,0:T(8,128)(2,1)} %get-tuple-element.47.rest_1_), custom_call_target="tpu_custom_call", output_to_operand_aliasing={{}: (2, {})} | custom-call | tf_op jit(solution)/shard_map/pallas_call | solution.py:106
  72.3 4.1 %pad_maximum_fusion.1 = bf16[4608,384]{1,0:T(8,128)(2,1)} fusion(bf16[512,384]{1,0:T(8,128)(2,1)S(1)} %copy-done.2, bf16[4096,384]{1,0:T(8,128)(2,1)} %rest_0_.1), kind=kLoop, calls=%fused_computation.16 | loop fusion | flops 7077888 | bytes 7077888 | tf_op jit(solution)/shard_map/concatenate | solution.py:285
  76.3 5.8 %copy.46 = bf16[4608,384]{0,1:T(8,128)(2,1)} copy(bf16[4608,384]{1,0:T(8,128)(2,1)} %pad_maximum_fusion.1) | data formatting | bytes 7077888 | tf_op jit(solution)/shard_map/concatenate | solution.py:285
  82.1 25.0 %all-to-all-done.1 = bf16[32,144,384]{2,1,0:T(8,128)(2,1)} async-done(((bf16[32,144,384]{2,1,0:T(8,128)(2,1)}), bf16[32,144,384]{2,1,0:T(8,128)(2,1)}, u32[]{:S(2)}, u32[]{:S(2)}) %all-to-all-start.1) | async-done | bytes 3538976 | tf_op jit(solution)/shard_map/all_to_all | solution.py:273
  107.2 4.9 %all-to-all-start = ((bf16[64,128,384]{2,1,0:T(8,128)(2,1)}), bf16[64,128,384]{2,1,0:T(8,128)(2,1)}, u32[]{:S(2)}, u32[]{:S(2)}) async-start(bf16[64,128,384]{2,1,0:T(8,128)(2,1)} %shard_map.125), calls=%async_computation | async-start | bytes 12582912 | tf_op jit(solution)/shard_map/all_to_all | solution.py:289
  112.3 18.6 %fusion = (f32[4,512]{1,0:T(4,128)S(1)}, f32[4,512,4608]{2,1,0:T(8,128)}) fusion(pred[512,4608]{1,0:T(8,128)(4,1)} %pad_add_fusion, bf16[4608,4,96]{0,2,1:T(8,128)(2,1)} %bitcast.76, bf16[512,4,48]{0,2,1:T(8,128)(2,1)S(1)} %get-tuple-element.69, bf16[512,4,48]{0,2,1:T(8,128)(2,1)S(1)} %get-tuple-element.68), kind=kOutput, calls=%fused_computation.3 | convolution fusion | flops 1841035264 | bytes 44048384 | tf_op jit(solution)/shard_map/qhd,khd->hqk/dot_general | solution.py:293
  130.9 4.1 %pad_maximum_fusion = bf16[4608,384]{1,0:T(8,128)(2,1)} fusion(bf16[512,384]{1,0:T(8,128)(2,1)S(1)} %copy-done.6, bf16[4096,384]{1,0:T(8,128)(2,1)} %rest_1_.1), kind=kLoop, calls=%fused_computation.15 | loop fusion | flops 7077888 | bytes 7077888 | tf_op jit(solution)/shard_map/concatenate | solution.py:286
  135.0 5.8 %copy.44 = bf16[4608,384]{0,1:T(8,128)(2,1)} copy(bf16[4608,384]{1,0:T(8,128)(2,1)} %pad_maximum_fusion) | data formatting | bytes 7077888 | tf_op jit(solution)/shard_map/concatenate | solution.py:286
  140.9 18.2 %fusion.1 = f32[4,512]{1,0:T(4,128)S(1)} fusion(f32[4,512,4608]{2,1,0:T(8,128)} %get-tuple-element.80, f32[4,512]{1,0:T(4,128)S(1)} %get-tuple-element.79, pred[512,4608]{1,0:T(8,128)(4,1)} %pad_add_fusion), kind=kLoop, calls=%fused_computation.4 | loop fusion | flops 37746688 | bytes 40124416 | tf_op jit(solution)/shard_map/reduce_sum | solution.py:302
  159.1 15.3 %fusion.15 = bf16[512,4,96]{0,2,1:T(8,128)(2,1)S(1)} fusion(bf16[4608,4,96]{0,2,1:T(8,128)(2,1)S(1)} %bitcast.77, f32[4,512,4608]{2,1,0:T(8,128)} %get-tuple-element.80, f32[4,512]{1,0:T(4,128)S(1)} %get-tuple-element.79, pred[512,4608]{1,0:T(8,128)(4,1)S(1)} %copy-done.1, f32[512,4]{0,1:T(4,128)S(1)} %bitcast.84), kind=kOutput, calls=%fused_computation.20 | convolution fusion | flops 1850081280 | bytes 44056576 | tf_op jit(solution)/shard_map/hqk,khd->qhd/dot_general | solution.py:304
  174.4 4.5 %fusion.38 = f32[512,3072]{1,0:T(8,128)} fusion(bf16[512,384]{0,1:T(8,128)(2,1)S(1)} %bitcast.81, bf16[384,3072]{1,0:T(8,128)(2,1)S(1)} %copy-done), kind=kOutput, calls=%fused_computation.81 | convolution fusion | flops 1207959552 | bytes 9043968 | tf_op jit(solution)/shard_map/dot_general | solution.py:313
  178.9 11.1 %all-to-all-done = bf16[64,128,384]{2,1,0:T(8,128)(2,1)} async-done(((bf16[64,128,384]{2,1,0:T(8,128)(2,1)}), bf16[64,128,384]{2,1,0:T(8,128)(2,1)}, u32[]{:S(2)}, u32[]{:S(2)}) %all-to-all-start) | async-done | bytes 6291488 | tf_op jit(solution)/shard_map/all_to_all | solution.py:289
  190.0 4.8 %all-to-all-start.2 = ((bf16[64,64,384]{2,1,0:T(8,128)(2,1)}), bf16[64,64,384]{2,1,0:T(8,128)(2,1)}, u32[]{:S(2)}, u32[]{:S(2)}) async-start(bf16[64,64,384]{2,1,0:T(8,128)(2,1)} %get-tuple-element.53), calls=%async_computation.3 | async-start | bytes 6291456 | tf_op jit(solution)/shard_map/all_to_all | solution.py:319
  197.2 4.3 %shard_map.126.refs_9_ = bf16[18,128,1536]{2,1,0:T(8,128)(2,1)} custom-call(s32[18]{0:T(128)} %get-tuple-element.77.src_ref, s32[18]{0:T(128)} %get-tuple-element.76.rank_ref, bf16[16,2,2,128,384]{4,3,2,1,0:T(8,128)(2,1)} %bitcast.26.refs_0_.refs_1_.refs_2_.refs_3_.refs_4_.refs_5_.refs_6_.refs_7_.refs_8_, ...), custom_call_target="tpu_custom_call" | custom-call | tf_op jit(solution)/shard_map/pallas_call | solution.py:174
  201.5 3.4 %shard_map.127.refs_9_ = bf16[18,128,1536]{2,1,0:T(8,128)(2,1)} custom-call(s32[18]{0:T(128)} %get-tuple-element.77.src_ref, s32[18]{0:T(128)} %get-tuple-element.76.rank_ref, bf16[16,2,144,384]{3,2,1,0:T(8,128)(2,1)} %bitcast.25.refs_0_.refs_1_.refs_2_.refs_3_.refs_4_.refs_5_.refs_6_.refs_7_.refs_8_, ...), custom_call_target="tpu_custom_call", output_to_operand_aliasing={{}: (11, {})} | custom-call | tf_op jit(solution)/shard_map/pallas_call | solution.py:174
  204.9 31.7 %all-to-all-done.2 = bf16[64,64,384]{2,1,0:T(8,128)(2,1)} async-done(((bf16[64,64,384]{2,1,0:T(8,128)(2,1)}), bf16[64,64,384]{2,1,0:T(8,128)(2,1)}, u32[]{:S(2)}, u32[]{:S(2)}) %all-to-all-start.2) | async-done | bytes 3145760 | tf_op jit(solution)/shard_map/all_to_all | solution.py:319
  236.6 3.5 %shard_map.128 = bf16[18,128,1536]{2,1,0:T(8,128)(2,1)} custom-call(s32[18]{0:T(128)} %get-tuple-element.77.src_ref, s32[18]{0:T(128)} %get-tuple-element.76.rank_ref, bf16[16,2,2,64,384]{4,3,2,1,0:T(8,128)(2,1)} %bitcast.24.refs_0_.refs_1_.refs_2_.refs_3_.refs_4_.refs_5_.refs_6_.refs_7_.refs_8_, ...), custom_call_target="tpu_custom_call", output_to_operand_aliasing={{}: (11, {})} | custom-call | tf_op jit(solution)/shard_map/pallas_call | solution.py:174
  (74 shorter events, 23.0 us)
Async XLA Ops:
  7.2 167.3 %copy-start = (bf16[384,3072]{1,0:T(8,128)(2,1)S(1)}, bf16[384,3072]{1,0:T(8,128)(2,1)}, u32[]{:S(2)}) copy-start(bf16[384,3072]{1,0:T(8,128)(2,1)} %param.20) | copy-start | bytes 7077892
  7.2 9.0 %copy-start.13 = (s32[1,4]{1,0:T(1,128)S(1)}, s32[1,4]{1,0:T(1,128)}, u32[]{:S(2)}) copy-start(s32[1,4]{1,0:T(1,128)} %param.24) | copy-start | bytes 52
  7.2 9.1 %copy-start.9 = (s32[1,4]{1,0:T(1,128)S(1)}, s32[1,4]{1,0:T(1,128)}, u32[]{:S(2)}) copy-start(s32[1,4]{1,0:T(1,128)} %param.23) | copy-start | bytes 52
  7.2 33.4 %all-gather.2.cloned.1.call-start = ((), (), s32[]{:S(2)}) async-start(), calls=%async_computation.4 | async-start | bytes 3649536 | tf_op jit(solution)/shard_map/all_gather | solution.py:213
  11.4 5.1 %copy-start.8 = (s32[36]{0:T(128)}, s32[36]{0:T(128)S(1)}, u32[]{:S(2)}) copy-start(s32[36]{0:T(128)S(1)} %multiply_add_fusion) | copy-start | bytes 436
  43.2 4.0 %copy-start.10 = (bf16[3072,384]{1,0:T(8,128)(2,1)S(1)}, bf16[3072,384]{1,0:T(8,128)(2,1)}, u32[]{:S(2)}) copy-start(bf16[3072,384]{1,0:T(8,128)(2,1)} %param.19) | copy-start | bytes 7077892
  47.3 2.5 %copy-start.4 = (bf16[512,3072]{1,0:T(8,128)(2,1)}, bf16[512,3072]{1,0:T(8,128)(2,1)S(1)}, u32[]{:S(2)}) copy-start(bf16[512,3072]{1,0:T(8,128)(2,1)S(1)} %fusion.8) | copy-start | bytes 9437188
  53.6 53.6 %all-to-all-start.1 = ((bf16[32,144,384]{2,1,0:T(8,128)(2,1)}), bf16[32,144,384]{2,1,0:T(8,128)(2,1)}, u32[]{:S(2)}, u32[]{:S(2)}) async-start(bf16[32,144,384]{2,1,0:T(8,128)(2,1)} %get-tuple-element.48), calls=%async_computation.1 | async-start | bytes 7077888 | tf_op jit(solution)/shard_map/all_to_all | solution.py:273
  61.0 2.9 %copy-start.5 = (bf16[512,3072]{1,0:T(8,128)(2,1)S(1)}, bf16[512,3072]{1,0:T(8,128)(2,1)}, u32[]{:S(2)}) copy-start(bf16[512,3072]{1,0:T(8,128)(2,1)} %copy-done.4) | copy-start | bytes 9437188
  61.0 3.0 %copy-start.11 = (bf16[3072,384]{1,0:T(8,128)(2,1)S(1)}, bf16[3072,384]{1,0:T(8,128)(2,1)}, u32[]{:S(2)}) copy-start(bf16[3072,384]{1,0:T(8,128)(2,1)} %param.17) | copy-start | bytes 7077892
  64.0 1.7 copy-start.12
  68.4 3.9 %copy-start.2 = (bf16[512,384]{1,0:T(8,128)(2,1)S(1)}, bf16[512,384]{1,0:T(8,128)(2,1)}, u32[]{:S(2)}) copy-start(bf16[512,384]{1,0:T(8,128)(2,1)} %copy.43.rest_0_) | copy-start | bytes 1179652
  107.2 82.8 %all-to-all-start = ((bf16[64,128,384]{2,1,0:T(8,128)(2,1)}), bf16[64,128,384]{2,1,0:T(8,128)(2,1)}, u32[]{:S(2)}, u32[]{:S(2)}) async-start(bf16[64,128,384]{2,1,0:T(8,128)(2,1)} %shard_map.125), calls=%async_computation | async-start | bytes 12582912 | tf_op jit(solution)/shard_map/all_to_all | solution.py:289
  112.1 128.0 %reduce-scatter.2.cloned.1.call-start = ((), (), s32[]{:S(2)}) async-start(), calls=%async_computation.5 | async-start | bytes 7077888 | tf_op jit(solution)/shard_map/reduce_scatter | solution.py:317
  112.3 18.6 %copy-start.6 = (bf16[512,384]{1,0:T(8,128)(2,1)S(1)}, bf16[512,384]{1,0:T(8,128)(2,1)}, u32[]{:S(2)}) copy-start(bf16[512,384]{1,0:T(8,128)(2,1)} %convolution_convert_fusion.rest_0_) | copy-start | bytes 1179652
  140.8 18.2 %copy-start.1 = (pred[512,4608]{1,0:T(8,128)(4,1)S(1)}, pred[512,4608]{1,0:T(8,128)(4,1)}, u32[]{:S(2)}) copy-start(pred[512,4608]{1,0:T(8,128)(4,1)} %pad_add_fusion) | copy-start | bytes 7077892
  140.8 18.2 %copy-start.3 = (bf16[4608,384]{0,1:T(8,128)(2,1)S(1)}, bf16[4608,384]{0,1:T(8,128)(2,1)}, u32[]{:S(2)}) copy-start(bf16[4608,384]{0,1:T(8,128)(2,1)} %copy.44) | copy-start | bytes 10616836
  190.0 46.6 %all-to-all-start.2 = ((bf16[64,64,384]{2,1,0:T(8,128)(2,1)}), bf16[64,64,384]{2,1,0:T(8,128)(2,1)}, u32[]{:S(2)}, u32[]{:S(2)}) async-start(bf16[64,64,384]{2,1,0:T(8,128)(2,1)} %get-tuple-element.53), calls=%async_computation.3 | async-start | bytes 6291456 | tf_op jit(solution)/shard_map/all_to_all | solution.py:319
  236.6 3.5 %copy-start.7 = (bf16[512,384]{1,0:T(8,128)(2,1)S(1)}, bf16[512,384]{1,0:T(8,128)(2,1)}, u32[]{:S(2)}) copy-start(bf16[512,384]{1,0:T(8,128)(2,1)} %param.15) | copy-start | bytes 1179652
Sparse Core Ops, SparseCore 0:
  10.0 30.5 all-gather.1
  190.1 38.2 reduce-scatter.1

commit v15 on v14

--- a/solution.py
+++ b/solution.py
@@ -210,17 +210,26 @@
 
     spare = 16
     riders = jnp.zeros((spare, local_width), tokens.dtype).at[0].set(norm_gain)
-    gathered = lax.all_gather(
-        jnp.concatenate([tokens, riders], axis=0), ("y", "core"), axis=1, tiled=True
-    )
-    full_tokens = gathered[:token_count]
-    full_gain = gathered[token_count]
-    widened = full_tokens.astype(jnp.float32)
-    mean_square = jnp.mean(widened * widened, axis=1, keepdims=True)
-    normed = (widened * lax.rsqrt(mean_square + EPSILON) * full_gain.astype(jnp.float32)[None, :]).astype(
-        jnp.bfloat16
-    )
-    value_raw = jnp.dot(normed, w_value, preferred_element_type=jnp.float32)
+    half = token_count // 2
+    first = lax.all_gather(
+        jnp.concatenate([tokens[:half], riders], axis=0), ("y", "core"), axis=1, tiled=True
+    )
+    second = lax.all_gather(tokens[half:], ("y", "core"), axis=1, tiled=True)
+    full_gain = first[half].astype(jnp.float32)
+
+    def normalize(rows):
+        widened = rows.astype(jnp.float32)
+        mean_square = jnp.mean(widened * widened, axis=1, keepdims=True)
+        return (widened * lax.rsqrt(mean_square + EPSILON) * full_gain[None, :]).astype(
+            jnp.bfloat16
+        )
+
+    normed_parts = (normalize(first[:half]), normalize(second))
+    value_raw = jnp.concatenate(
+        [jnp.dot(part, w_value, preferred_element_type=jnp.float32) for part in normed_parts],
+        axis=0,
+    )
+    normed = jnp.concatenate(normed_parts, axis=0)
     earlier = earlier_lengths[0]
     fresh = new_lengths[0]
     owners, positions = block_layout(earlier, fresh, token_count)

time: 251 us -> 275 us (1.096)
  waiting for transfers between devices: 71.7 us -> 92.1 us
    all_gather x1 -> x2, waiting for transfers between devices: 3.8 us -> 24.1 us  [the longest x1 24.1 us: shards(): lax.all_gather(jnp.concatenate([tokens[:half], riders], axis=0), ('y', 'c...]
  transfers between devices with their start and end apart: 5 -> 6, of which waited for: 4 -> 4; matrix products, arithmetic and copies ran while one was open for 37% -> 35% of each run, Pallas kernels for 15% -> 13%
where the time goes in v15:
time: 275 us; the launch traced here: 273 us
  waiting for transfers between devices  92.1 us (33%)
  other arithmetic  47.1 us (17%)
  matrix products  43.3 us (16%)
  Pallas kernels  40 us (15%)
  local copies, waits for them, and re-layouts  19 us (7%)
  starting transfers between devices  17.4 us (6%)
  between operations  14 us (5%)
    all_to_all x1, waiting for transfers between devices, shards(): received_high = lax.all_to_all(send_high, ('req', 'core'), 0, 0, tiled=True)  31.7 us
    pallas_call x3, Pallas kernels, pack_pages(): pl.pallas_call(body, out_shape=out_shape, grid_spec=pltpu.PrefetchScalarG...  27 us
    all_to_all x1, waiting for transfers between devices, shards(): received_low = lax.all_to_all(send_low, ('req', 'core'), 0, 0, tiled=True)  25.1 us
    all_gather x1, waiting for transfers between devices, shards(): lax.all_gather(jnp.concatenate([tokens[:half], riders], axis=0), ('y', 'c...  24.1 us
    dot_general x1, matrix products, shards(): jnp.einsum('qhd,khd->hqk', queries.reshape(token_count, heads_here, HD),...  18.6 us
    reduce_sum x1, other arithmetic, shards(): totals = jnp.sum(weights, axis=2)  18.2 us
    dot_general x1, matrix products, shards(): jnp.einsum('hqk,khd->qhd', prob_rows, values_all.reshape(-1, heads_here,...  15.3 us
    all_to_all x1, waiting for transfers between devices, shards(): received_keys = lax.all_to_all(send_keys, ('req', 'core'), 0, 0, tiled=True)  11.2 us
  transfers between devices with their start and end apart: 6, of which 4 were waited for; matrix products, arithmetic and copies ran while one was open for 35% of the time, Pallas kernels for 13%

profile of v15, /device:TPU:0, one launch (start us, length us, event | category | flops | bytes accessed | tf_op | source)
XLA Modules:
  0.0 272.9 jit_solution(4611672629287847800)
XLA Ops:
  7.2 1.9 fusion.39
  17.2 19.3 %shard_map.123 = (bf16[64,128,384]{2,1,0:T(8,128)(2,1)}, bf16[32,144,384]{2,1,0:T(8,128)(2,1)}, bf16[64,64,384]{2,1,0:T(8,128)(2,1)}) custom-call(s32[32]{0:T(128)} %bitcast.87, bf16[4096,384]{1,0:T(8,128)(2,1)} %rest_0_.1, bf16[4096,384]{1,0:T(8,128)(2,1)} %rest_1_.1, bf16[32,144,384]{2,1,0:T(8,128)(2,1)} %shard_map.122.rest_2_), custom_call_target="tpu_custom_call", output_to_operand_aliasing={{1}: (3, {})} | custom-call | tf_op jit(solution)/shard_map/pallas_call | solution.py:106
  39.4 24.1 %all-gather.3.cloned.1.call-done = bf16[272,3072]{1,0:T(8,128)(2,1)} async-done(((bf16[272,384]{1,0:T(8,128)(2,1)}), bf16[272,3072]{1,0:T(8,128)(2,1)}) %all-gather.3.cloned.1.call-update) | async-done | bytes 1671184 | tf_op jit(solution)/shard_map/all_gather | solution.py:214
  66.1 3.2 %fusion.8 = (bf16[256,3072]{1,0:T(8,128)(2,1)S(1)}, bf16[256,3072]{1,0:T(8,128)(2,1)S(1)}) fusion(f32[3072]{0:T(1024)S(1)} %bitcast.84, f32[256]{0:T(256)S(1)} %add_rsqrt_fusion.1, bf16[272,3072]{1,0:T(8,128)(2,1)} %all-gather.3.cloned.1.call-done, f32[256]{0:T(256)S(1)} %add_rsqrt_fusion, bf16[256,3072]{1,0:T(8,128)(2,1)} %all-gather.5.cloned.1.call-done), kind=kLoop, calls=%fused_computation.18 | loop fusion | flops 6291456 | bytes 6305792 | tf_op jit(solution)/shard_map/convert_element_type | solution.py:223
  73.9 3.8 %shard_map.124 = (bf16[32,144,384]{2,1,0:T(8,128)(2,1)}, bf16[64,64,384]{2,1,0:T(8,128)(2,1)}) custom-call(s32[4]{0:T(128)} %slice.75.slot_ref, bf16[512,384]{1,0:T(8,128)(2,1)} %pad_maximum_fusion.3.rest_0_, bf16[32,144,384]{2,1,0:T(8,128)(2,1)} %get-tuple-element.42.rest_1_, ...), custom_call_target="tpu_custom_call", output_to_operand_aliasing={{0}: (2, {}), {1}: (3, {})} | custom-call | tf_op jit(solution)/shard_map/pallas_call | solution.py:106
  77.7 7.3 %all-to-all-start.1 = ((bf16[32,144,384]{2,1,0:T(8,128)(2,1)}), bf16[32,144,384]{2,1,0:T(8,128)(2,1)}, u32[]{:S(2)}, u32[]{:S(2)}) async-start(bf16[32,144,384]{2,1,0:T(8,128)(2,1)} %get-tuple-element.48), calls=%async_computation.1 | async-start | bytes 7077888 | tf_op jit(solution)/shard_map/all_to_all | solution.py:282
  92.5 3.9 %shard_map.125 = bf16[64,128,384]{2,1,0:T(8,128)(2,1)} custom-call(s32[4]{0:T(128)} %slice.75.slot_ref, bf16[512,384]{1,0:T(8,128)(2,1)} %copy.43.rest_0_, bf16[64,128,384]{2,1,0:T(8,128)(2,1)} %get-tuple-element.47.rest_1_), custom_call_target="tpu_custom_call", output_to_operand_aliasing={{}: (2, {})} | custom-call | tf_op jit(solution)/shard_map/pallas_call | solution.py:106
  96.4 4.1 %pad_maximum_fusion.1 = bf16[4608,384]{1,0:T(8,128)(2,1)} fusion(bf16[512,384]{1,0:T(8,128)(2,1)S(1)} %copy-done.3, bf16[4096,384]{1,0:T(8,128)(2,1)} %rest_0_.1), kind=kLoop, calls=%fused_computation.15 | loop fusion | flops 7077888 | bytes 7077888 | tf_op jit(solution)/shard_map/concatenate | solution.py:294
  100.4 5.8 %copy.46 = bf16[4608,384]{0,1:T(8,128)(2,1)} copy(bf16[4608,384]{1,0:T(8,128)(2,1)} %pad_maximum_fusion.1) | data formatting | bytes 7077888 | tf_op jit(solution)/shard_map/concatenate | solution.py:294
  106.2 25.1 %all-to-all-done.1 = bf16[32,144,384]{2,1,0:T(8,128)(2,1)} async-done(((bf16[32,144,384]{2,1,0:T(8,128)(2,1)}), bf16[32,144,384]{2,1,0:T(8,128)(2,1)}, u32[]{:S(2)}, u32[]{:S(2)}) %all-to-all-start.1) | async-done | bytes 3538976 | tf_op jit(solution)/shard_map/all_to_all | solution.py:282
  131.3 5.1 %all-to-all-start = ((bf16[64,128,384]{2,1,0:T(8,128)(2,1)}), bf16[64,128,384]{2,1,0:T(8,128)(2,1)}, u32[]{:S(2)}, u32[]{:S(2)}) async-start(bf16[64,128,384]{2,1,0:T(8,128)(2,1)} %shard_map.125), calls=%async_computation | async-start | bytes 12582912 | tf_op jit(solution)/shard_map/all_to_all | solution.py:298
  136.4 18.6 %fusion = (f32[4,512]{1,0:T(4,128)S(1)}, f32[4,512,4608]{2,1,0:T(8,128)}) fusion(pred[512,4608]{1,0:T(8,128)(4,1)} %pad_add_fusion, bf16[4608,4,96]{0,2,1:T(8,128)(2,1)} %bitcast.78, bf16[512,4,48]{0,2,1:T(8,128)(2,1)S(1)} %get-tuple-element.69, bf16[512,4,48]{0,2,1:T(8,128)(2,1)S(1)} %get-tuple-element.68), kind=kOutput, calls=%fused_computation.3 | convolution fusion | flops 1841035264 | bytes 44048384 | tf_op jit(solution)/shard_map/qhd,khd->hqk/dot_general | solution.py:302
  155.0 4.1 %pad_maximum_fusion = bf16[4608,384]{1,0:T(8,128)(2,1)} fusion(bf16[512,384]{1,0:T(8,128)(2,1)S(1)} %copy-done.2, bf16[4096,384]{1,0:T(8,128)(2,1)} %rest_1_.1), kind=kLoop, calls=%fused_computation.14 | loop fusion | flops 7077888 | bytes 7077888 | tf_op jit(solution)/shard_map/concatenate | solution.py:295
  159.1 5.8 %copy.44 = bf16[4608,384]{0,1:T(8,128)(2,1)} copy(bf16[4608,384]{1,0:T(8,128)(2,1)} %pad_maximum_fusion) | data formatting | bytes 7077888 | tf_op jit(solution)/shard_map/concatenate | solution.py:295
  165.0 18.2 %fusion.1 = f32[4,512]{1,0:T(4,128)S(1)} fusion(f32[4,512,4608]{2,1,0:T(8,128)} %get-tuple-element.84, f32[4,512]{1,0:T(4,128)S(1)} %get-tuple-element.83, pred[512,4608]{1,0:T(8,128)(4,1)} %pad_add_fusion), kind=kLoop, calls=%fused_computation.4 | loop fusion | flops 37746688 | bytes 40124416 | tf_op jit(solution)/shard_map/reduce_sum | solution.py:311
  183.2 15.3 %fusion.18 = bf16[512,4,96]{0,2,1:T(8,128)(2,1)S(1)} fusion(bf16[4608,4,96]{0,2,1:T(8,128)(2,1)S(1)} %bitcast.79, f32[4,512,4608]{2,1,0:T(8,128)} %get-tuple-element.84, f32[4,512]{1,0:T(4,128)S(1)} %get-tuple-element.83, pred[512,4608]{1,0:T(8,128)(4,1)S(1)} %copy-done.1, f32[512,4]{0,1:T(4,128)S(1)} %bitcast.86), kind=kOutput, calls=%fused_computation.27 | convolution fusion | flops 1850081280 | bytes 44056576 | tf_op jit(solution)/shard_map/hqk,khd->qhd/dot_general | solution.py:313
  198.6 4.5 %fusion.42 = f32[512,3072]{1,0:T(8,128)} fusion(bf16[512,384]{0,1:T(8,128)(2,1)S(1)} %bitcast.83, bf16[384,3072]{1,0:T(8,128)(2,1)S(1)} %copy-done), kind=kOutput, calls=%fused_computation.91 | convolution fusion | flops 1207959552 | bytes 9043968 | tf_op jit(solution)/shard_map/dot_general | solution.py:322
  203.1 11.2 %all-to-all-done = bf16[64,128,384]{2,1,0:T(8,128)(2,1)} async-done(((bf16[64,128,384]{2,1,0:T(8,128)(2,1)}), bf16[64,128,384]{2,1,0:T(8,128)(2,1)}, u32[]{:S(2)}, u32[]{:S(2)}) %all-to-all-start) | async-done | bytes 6291488 | tf_op jit(solution)/shard_map/all_to_all | solution.py:298
  214.3 4.8 %all-to-all-start.2 = ((bf16[64,64,384]{2,1,0:T(8,128)(2,1)}), bf16[64,64,384]{2,1,0:T(8,128)(2,1)}, u32[]{:S(2)}, u32[]{:S(2)}) async-start(bf16[64,64,384]{2,1,0:T(8,128)(2,1)} %get-tuple-element.53), calls=%async_computation.3 | async-start | bytes 6291456 | tf_op jit(solution)/shard_map/all_to_all | solution.py:328
  221.5 4.3 %shard_map.126.refs_9_ = bf16[18,128,1536]{2,1,0:T(8,128)(2,1)} custom-call(s32[18]{0:T(128)} %get-tuple-element.81.src_ref, s32[18]{0:T(128)} %get-tuple-element.80.rank_ref, bf16[16,2,2,128,384]{4,3,2,1,0:T(8,128)(2,1)} %bitcast.26.refs_0_.refs_1_.refs_2_.refs_3_.refs_4_.refs_5_.refs_6_.refs_7_.refs_8_, ...), custom_call_target="tpu_custom_call" | custom-call | tf_op jit(solution)/shard_map/pallas_call | solution.py:174
  225.8 3.4 %shard_map.127.refs_9_ = bf16[18,128,1536]{2,1,0:T(8,128)(2,1)} custom-call(s32[18]{0:T(128)} %get-tuple-element.81.src_ref, s32[18]{0:T(128)} %get-tuple-element.80.rank_ref, bf16[16,2,144,384]{3,2,1,0:T(8,128)(2,1)} %bitcast.25.refs_0_.refs_1_.refs_2_.refs_3_.refs_4_.refs_5_.refs_6_.refs_7_.refs_8_, ...), custom_call_target="tpu_custom_call", output_to_operand_aliasing={{}: (11, {})} | custom-call | tf_op jit(solution)/shard_map/pallas_call | solution.py:174
  229.2 31.7 %all-to-all-done.2 = bf16[64,64,384]{2,1,0:T(8,128)(2,1)} async-done(((bf16[64,64,384]{2,1,0:T(8,128)(2,1)}), bf16[64,64,384]{2,1,0:T(8,128)(2,1)}, u32[]{:S(2)}, u32[]{:S(2)}) %all-to-all-start.2) | async-done | bytes 3145760 | tf_op jit(solution)/shard_map/all_to_all | solution.py:328
  260.9 3.5 %shard_map.128 = bf16[18,128,1536]{2,1,0:T(8,128)(2,1)} custom-call(s32[18]{0:T(128)} %get-tuple-element.81.src_ref, s32[18]{0:T(128)} %get-tuple-element.80.rank_ref, bf16[16,2,2,64,384]{4,3,2,1,0:T(8,128)(2,1)} %bitcast.24.refs_0_.refs_1_.refs_2_.refs_3_.refs_4_.refs_5_.refs_6_.refs_7_.refs_8_, ...), custom_call_target="tpu_custom_call", output_to_operand_aliasing={{}: (11, {})} | custom-call | tf_op jit(solution)/shard_map/pallas_call | solution.py:174
  264.4 2.0 add_convert_fusion
  (81 shorter events, 27.8 us)
Async XLA Ops:
  7.2 191.4 %copy-start = (bf16[384,3072]{1,0:T(8,128)(2,1)S(1)}, bf16[384,3072]{1,0:T(8,128)(2,1)}, u32[]{:S(2)}) copy-start(bf16[384,3072]{1,0:T(8,128)(2,1)} %param.20) | copy-start | bytes 7077892
  7.2 9.7 %copy-start.12 = (s32[1,4]{1,0:T(1,128)S(1)}, s32[1,4]{1,0:T(1,128)}, u32[]{:S(2)}) copy-start(s32[1,4]{1,0:T(1,128)} %param.24) | copy-start | bytes 52
  7.2 9.9 %copy-start.8 = (s32[1,4]{1,0:T(1,128)S(1)}, s32[1,4]{1,0:T(1,128)}, u32[]{:S(2)}) copy-start(s32[1,4]{1,0:T(1,128)} %param.23) | copy-start | bytes 52
  7.2 30.4 %all-gather.5.cloned.1.call-start = ((), (), s32[]{:S(2)}) async-start(), calls=%async_computation.5 | async-start | bytes 1769472 | tf_op jit(solution)/shard_map/all_gather | solution.py:217
  9.1 54.3 %all-gather.3.cloned.1.call-start = ((), (), s32[]{:S(2)}) async-start(), calls=%async_computation.4 | async-start | bytes 1880064 | tf_op jit(solution)/shard_map/all_gather | solution.py:214
  12.1 5.1 %copy-start.7 = (s32[36]{0:T(128)}, s32[36]{0:T(128)S(1)}, u32[]{:S(2)}) copy-start(s32[36]{0:T(128)S(1)} %multiply_add_fusion) | copy-start | bytes 436
  66.1 3.2 %copy-start.9 = (bf16[3072,384]{1,0:T(8,128)(2,1)S(1)}, bf16[3072,384]{1,0:T(8,128)(2,1)}, u32[]{:S(2)}) copy-start(bf16[3072,384]{1,0:T(8,128)(2,1)} %param.19) | copy-start | bytes 7077892
  77.7 53.5 %all-to-all-start.1 = ((bf16[32,144,384]{2,1,0:T(8,128)(2,1)}), bf16[32,144,384]{2,1,0:T(8,128)(2,1)}, u32[]{:S(2)}, u32[]{:S(2)}) async-start(bf16[32,144,384]{2,1,0:T(8,128)(2,1)} %get-tuple-element.48), calls=%async_computation.1 | async-start | bytes 7077888 | tf_op jit(solution)/shard_map/all_to_all | solution.py:282
  85.1 2.9 %copy-start.5 = (bf16[512,3072]{1,0:T(8,128)(2,1)S(1)}, bf16[512,3072]{1,0:T(8,128)(2,1)}, u32[]{:S(2)}) copy-start(bf16[512,3072]{1,0:T(8,128)(2,1)} %pad_maximum_fusion.2) | copy-start | bytes 9437188
  85.1 3.0 %copy-start.10 = (bf16[3072,384]{1,0:T(8,128)(2,1)S(1)}, bf16[3072,384]{1,0:T(8,128)(2,1)}, u32[]{:S(2)}) copy-start(bf16[3072,384]{1,0:T(8,128)(2,1)} %param.17) | copy-start | bytes 7077892
  88.1 1.7 copy-start.11
  92.5 3.9 %copy-start.3 = (bf16[512,384]{1,0:T(8,128)(2,1)S(1)}, bf16[512,384]{1,0:T(8,128)(2,1)}, u32[]{:S(2)}) copy-start(bf16[512,384]{1,0:T(8,128)(2,1)} %copy.43.rest_0_) | copy-start | bytes 1179652
  131.3 83.0 %all-to-all-start = ((bf16[64,128,384]{2,1,0:T(8,128)(2,1)}), bf16[64,128,384]{2,1,0:T(8,128)(2,1)}, u32[]{:S(2)}, u32[]{:S(2)}) async-start(bf16[64,128,384]{2,1,0:T(8,128)(2,1)} %shard_map.125), calls=%async_computation | async-start | bytes 12582912 | tf_op jit(solution)/shard_map/all_to_all | solution.py:298
  136.4 128.0 %reduce-scatter.2.cloned.1.call-start = ((), (), s32[]{:S(2)}) async-start(), calls=%async_computation.6 | async-start | bytes 7077888 | tf_op jit(solution)/shard_map/reduce_scatter | solution.py:326
  136.4 18.6 %copy-start.2 = (bf16[512,384]{1,0:T(8,128)(2,1)S(1)}, bf16[512,384]{1,0:T(8,128)(2,1)}, u32[]{:S(2)}) copy-start(bf16[512,384]{1,0:T(8,128)(2,1)} %pad_maximum_fusion.3.rest_0_) | copy-start | bytes 1179652
  165.0 18.2 %copy-start.1 = (pred[512,4608]{1,0:T(8,128)(4,1)S(1)}, pred[512,4608]{1,0:T(8,128)(4,1)}, u32[]{:S(2)}) copy-start(pred[512,4608]{1,0:T(8,128)(4,1)} %pad_add_fusion) | copy-start | bytes 7077892
  165.0 18.2 %copy-start.4 = (bf16[4608,384]{0,1:T(8,128)(2,1)S(1)}, bf16[4608,384]{0,1:T(8,128)(2,1)}, u32[]{:S(2)}) copy-start(bf16[4608,384]{0,1:T(8,128)(2,1)} %copy.44) | copy-start | bytes 10616836
  214.3 46.6 %all-to-all-start.2 = ((bf16[64,64,384]{2,1,0:T(8,128)(2,1)}), bf16[64,64,384]{2,1,0:T(8,128)(2,1)}, u32[]{:S(2)}, u32[]{:S(2)}) async-start(bf16[64,64,384]{2,1,0:T(8,128)(2,1)} %get-tuple-element.53), calls=%async_computation.3 | async-start | bytes 6291456 | tf_op jit(solution)/shard_map/all_to_all | solution.py:328
  260.9 3.5 %copy-start.6 = (bf16[512,384]{1,0:T(8,128)(2,1)S(1)}, bf16[512,384]{1,0:T(8,128)(2,1)}, u32[]{:S(2)}) copy-start(bf16[512,384]{1,0:T(8,128)(2,1)} %param.15) | copy-start | bytes 1179652
Sparse Core Ops, SparseCore 0:
  9.7 27.1 all-gather.4
  38.6 24.8 all-gather.2
  214.4 38.2 reduce-scatter.1

commit v16 on v14

--- a/solution.py
+++ b/solution.py
@@ -317,6 +317,7 @@
     summed = lax.psum_scatter(projected, ("y", "core"), scatter_dimension=1, tiled=True)
     layer_out = (tokens.astype(jnp.float32) + summed).astype(jnp.bfloat16)
     received_high = lax.all_to_all(send_high, ("req", "core"), 0, 0, tiled=True)
+    received_high, layer_out = lax.optimization_barrier((received_high, layer_out))
     half_rows = PAGE // 2
     pool = place_pages(from_req, from_rank, received_keys, slot_count, cores, 0, 0, PAGE)
     pool = place_pages(

time: 251 us -> 249 us (level)
    all_to_all x1, waiting for transfers between devices: 31.7 us -> 6.26 us  [shards(): received_high = lax.all_to_all(send_high, ('req', 'core'), 0, 0, tiled=True)]
    reduce_scatter x1, waiting for transfers between devices: 0.01 us -> 23.4 us  [shards(): lax.psum_scatter(projected, ('y', 'core'), scatter_dimension=1, tiled=True)]
  transfers between devices with their start and end apart: 5 -> 5, of which waited for: 4 -> 5; matrix products, arithmetic and copies ran while one was open for 37% -> 38% of each run, Pallas kernels for 15% -> 13%
where the time goes in v16:
time: 249 us; the launch traced here: 247 us
  waiting for transfers between devices  69.6 us (28%)
  other arithmetic  44.5 us (18%)
  matrix products  43.8 us (18%)
  Pallas kernels  40 us (16%)
  starting transfers between devices  17.4 us (7%)
  local copies, waits for them, and re-layouts  17.2 us (7%)
  between operations  14.3 us (6%)
    pallas_call x3, Pallas kernels, pack_pages(): pl.pallas_call(body, out_shape=out_shape, grid_spec=pltpu.PrefetchScalarG...  27.1 us
    all_to_all x1, waiting for transfers between devices, shards(): received_low = lax.all_to_all(send_low, ('req', 'core'), 0, 0, tiled=True)  25 us
    reduce_scatter x1, waiting for transfers between devices, shards(): lax.psum_scatter(projected, ('y', 'core'), scatter_dimension=1, tiled=True)  23.4 us
    dot_general x1, matrix products, shards(): jnp.einsum('qhd,khd->hqk', queries.reshape(token_count, heads_here, HD),...  18.6 us
    reduce_sum x1, other arithmetic, shards(): totals = jnp.sum(weights, axis=2)  18.2 us
    dot_general x1, matrix products, shards(): jnp.einsum('hqk,khd->qhd', prob_rows, values_all.reshape(-1, heads_here,...  15.3 us
    pallas_call x3, Pallas kernels, place_pages(): pl.pallas_call(body, out_shape=jax.ShapeDtypeStruct((slot_count, PAGE, 2...  11.2 us
    all_to_all x1, waiting for transfers between devices, shards(): received_keys = lax.all_to_all(send_keys, ('req', 'core'), 0, 0, tiled=True)  11.1 us
  transfers between devices with their start and end apart: 5, of which 5 were waited for; matrix products, arithmetic and copies ran while one was open for 38% of the time, Pallas kernels for 13%

profile of v16, /device:TPU:0, one launch (start us, length us, event | category | flops | bytes accessed | tf_op | source)
XLA Modules:
  0.0 246.8 jit_solution(3899381208091711423)
XLA Ops:
  16.5 19.4 %shard_map.123 = (bf16[64,128,384]{2,1,0:T(8,128)(2,1)}, bf16[32,144,384]{2,1,0:T(8,128)(2,1)}, bf16[64,64,384]{2,1,0:T(8,128)(2,1)}) custom-call(s32[32]{0:T(128)} %bitcast.85, bf16[4096,384]{1,0:T(8,128)(2,1)} %rest_0_.1, bf16[4096,384]{1,0:T(8,128)(2,1)} %rest_1_.1, bf16[32,144,384]{2,1,0:T(8,128)(2,1)} %shard_map.122.rest_2_), custom_call_target="tpu_custom_call", output_to_operand_aliasing={{1}: (3, {})} | custom-call | tf_op jit(solution)/shard_map/pallas_call | solution.py:106
  36.8 3.8 %all-gather.2.cloned.1.call-done = bf16[528,3072]{1,0:T(8,128)(2,1)} async-done(((bf16[528,384]{1,0:T(8,128)(2,1)}), bf16[528,3072]{1,0:T(8,128)(2,1)}) %all-gather.2.cloned.1.call-update) | async-done | bytes 3244048 | tf_op jit(solution)/shard_map/all_gather | solution.py:213
  40.6 2.6 %fusion.6 = f32[512]{0:T(512)S(1)} fusion(bf16[528,3072]{1,0:T(8,128)(2,1)} %all-gather.2.cloned.1.call-done), kind=kLoop, calls=%fused_computation.11 | loop fusion | flops 4718080 | bytes 3147776 | tf_op jit(solution)/shard_map/reduce_sum | solution.py:219
  44.2 3.1 %fusion.8 = bf16[512,3072]{1,0:T(8,128)(2,1)S(1)} fusion(f32[3072]{0:T(1024)S(1)} %bitcast.82, f32[512]{0:T(512)S(1)} %add_rsqrt_fusion, bf16[528,3072]{1,0:T(8,128)(2,1)} %all-gather.2.cloned.1.call-done), kind=kLoop, calls=%fused_computation.13 | loop fusion | flops 6291456 | bytes 6305792 | tf_op jit(solution)/shard_map/convert_element_type | solution.py:220
  49.8 3.8 %shard_map.124 = (bf16[32,144,384]{2,1,0:T(8,128)(2,1)}, bf16[64,64,384]{2,1,0:T(8,128)(2,1)}) custom-call(s32[4]{0:T(128)} %slice.69.slot_ref, bf16[512,384]{1,0:T(8,128)(2,1)} %convolution_convert_fusion.rest_0_, bf16[32,144,384]{2,1,0:T(8,128)(2,1)} %get-tuple-element.44.rest_1_, ...), custom_call_target="tpu_custom_call", output_to_operand_aliasing={{0}: (2, {}), {1}: (3, {})} | custom-call | tf_op jit(solution)/shard_map/pallas_call | solution.py:106
  53.6 7.3 %all-to-all-start.1 = ((bf16[32,144,384]{2,1,0:T(8,128)(2,1)}), bf16[32,144,384]{2,1,0:T(8,128)(2,1)}, u32[]{:S(2)}, u32[]{:S(2)}) async-start(bf16[32,144,384]{2,1,0:T(8,128)(2,1)} %get-tuple-element.50), calls=%async_computation.1 | async-start | bytes 7077888 | tf_op jit(solution)/shard_map/all_to_all | solution.py:273
  68.4 3.9 %shard_map.125 = bf16[64,128,384]{2,1,0:T(8,128)(2,1)} custom-call(s32[4]{0:T(128)} %slice.69.slot_ref, bf16[512,384]{1,0:T(8,128)(2,1)} %copy.43.rest_0_, bf16[64,128,384]{2,1,0:T(8,128)(2,1)} %get-tuple-element.49.rest_1_), custom_call_target="tpu_custom_call", output_to_operand_aliasing={{}: (2, {})} | custom-call | tf_op jit(solution)/shard_map/pallas_call | solution.py:106
  72.3 4.1 %pad_maximum_fusion.1 = bf16[4608,384]{1,0:T(8,128)(2,1)} fusion(bf16[512,384]{1,0:T(8,128)(2,1)S(1)} %copy-done.2, bf16[4096,384]{1,0:T(8,128)(2,1)} %rest_0_.1), kind=kLoop, calls=%fused_computation.16 | loop fusion | flops 7077888 | bytes 7077888 | tf_op jit(solution)/shard_map/concatenate | solution.py:285
  76.3 5.8 %copy.46 = bf16[4608,384]{0,1:T(8,128)(2,1)} copy(bf16[4608,384]{1,0:T(8,128)(2,1)} %pad_maximum_fusion.1) | data formatting | bytes 7077888 | tf_op jit(solution)/shard_map/concatenate | solution.py:285
  82.1 25.0 %all-to-all-done.1 = bf16[32,144,384]{2,1,0:T(8,128)(2,1)} async-done(((bf16[32,144,384]{2,1,0:T(8,128)(2,1)}), bf16[32,144,384]{2,1,0:T(8,128)(2,1)}, u32[]{:S(2)}, u32[]{:S(2)}) %all-to-all-start.1) | async-done | bytes 3538976 | tf_op jit(solution)/shard_map/all_to_all | solution.py:273
  107.2 4.9 %all-to-all-start = ((bf16[64,128,384]{2,1,0:T(8,128)(2,1)}), bf16[64,128,384]{2,1,0:T(8,128)(2,1)}, u32[]{:S(2)}, u32[]{:S(2)}) async-start(bf16[64,128,384]{2,1,0:T(8,128)(2,1)} %shard_map.125), calls=%async_computation | async-start | bytes 12582912 | tf_op jit(solution)/shard_map/all_to_all | solution.py:289
  112.3 18.6 %fusion = (f32[4,512]{1,0:T(4,128)S(1)}, f32[4,512,4608]{2,1,0:T(8,128)}) fusion(pred[512,4608]{1,0:T(8,128)(4,1)} %pad_add_fusion, bf16[4608,4,96]{0,2,1:T(8,128)(2,1)} %bitcast.76, bf16[512,4,48]{0,2,1:T(8,128)(2,1)S(1)} %get-tuple-element.73, bf16[512,4,48]{0,2,1:T(8,128)(2,1)S(1)} %get-tuple-element.72), kind=kOutput, calls=%fused_computation.3 | convolution fusion | flops 1841035264 | bytes 44048384 | tf_op jit(solution)/shard_map/qhd,khd->hqk/dot_general | solution.py:293
  130.9 4.1 %pad_maximum_fusion = bf16[4608,384]{1,0:T(8,128)(2,1)} fusion(bf16[512,384]{1,0:T(8,128)(2,1)S(1)} %copy-done.6, bf16[4096,384]{1,0:T(8,128)(2,1)} %rest_1_.1), kind=kLoop, calls=%fused_computation.15 | loop fusion | flops 7077888 | bytes 7077888 | tf_op jit(solution)/shard_map/concatenate | solution.py:286
  135.0 5.8 %copy.44 = bf16[4608,384]{0,1:T(8,128)(2,1)} copy(bf16[4608,384]{1,0:T(8,128)(2,1)} %pad_maximum_fusion) | data formatting | bytes 7077888 | tf_op jit(solution)/shard_map/concatenate | solution.py:286
  140.9 18.2 %fusion.1 = f32[4,512]{1,0:T(4,128)S(1)} fusion(f32[4,512,4608]{2,1,0:T(8,128)} %get-tuple-element.84, f32[4,512]{1,0:T(4,128)S(1)} %get-tuple-element.83, pred[512,4608]{1,0:T(8,128)(4,1)} %pad_add_fusion), kind=kLoop, calls=%fused_computation.4 | loop fusion | flops 37746688 | bytes 40124416 | tf_op jit(solution)/shard_map/reduce_sum | solution.py:302
  159.1 15.3 %fusion.15 = bf16[512,4,96]{0,2,1:T(8,128)(2,1)S(1)} fusion(bf16[4608,4,96]{0,2,1:T(8,128)(2,1)S(1)} %bitcast.77, f32[4,512,4608]{2,1,0:T(8,128)} %get-tuple-element.84, f32[4,512]{1,0:T(4,128)S(1)} %get-tuple-element.83, pred[512,4608]{1,0:T(8,128)(4,1)S(1)} %copy-done.1, f32[512,4]{0,1:T(4,128)S(1)} %bitcast.84), kind=kOutput, calls=%fused_computation.20 | convolution fusion | flops 1850081280 | bytes 44056576 | tf_op jit(solution)/shard_map/hqk,khd->qhd/dot_general | solution.py:304
  174.5 4.5 %fusion.38 = f32[512,3072]{1,0:T(8,128)} fusion(bf16[512,384]{0,1:T(8,128)(2,1)S(1)} %bitcast.81, bf16[384,3072]{1,0:T(8,128)(2,1)S(1)} %copy-done), kind=kOutput, calls=%fused_computation.81 | convolution fusion | flops 1207959552 | bytes 9043968 | tf_op jit(solution)/shard_map/dot_general | solution.py:313
  179.0 11.1 %all-to-all-done = bf16[64,128,384]{2,1,0:T(8,128)(2,1)} async-done(((bf16[64,128,384]{2,1,0:T(8,128)(2,1)}), bf16[64,128,384]{2,1,0:T(8,128)(2,1)}, u32[]{:S(2)}, u32[]{:S(2)}) %all-to-all-start) | async-done | bytes 6291488 | tf_op jit(solution)/shard_map/all_to_all | solution.py:289
  190.0 4.8 %all-to-all-start.2 = ((bf16[64,64,384]{2,1,0:T(8,128)(2,1)}), bf16[64,64,384]{2,1,0:T(8,128)(2,1)}, u32[]{:S(2)}, u32[]{:S(2)}) async-start(bf16[64,64,384]{2,1,0:T(8,128)(2,1)} %get-tuple-element.53), calls=%async_computation.2 | async-start | bytes 6291456 | tf_op jit(solution)/shard_map/all_to_all | solution.py:319
  197.2 4.3 %shard_map.126.refs_9_ = bf16[18,128,1536]{2,1,0:T(8,128)(2,1)} custom-call(s32[18]{0:T(128)} %get-tuple-element.81.src_ref, s32[18]{0:T(128)} %get-tuple-element.80.rank_ref, bf16[16,2,2,128,384]{4,3,2,1,0:T(8,128)(2,1)} %bitcast.26.refs_0_.refs_1_.refs_2_.refs_3_.refs_4_.refs_5_.refs_6_.refs_7_.refs_8_, ...), custom_call_target="tpu_custom_call" | custom-call | tf_op jit(solution)/shard_map/pallas_call | solution.py:174
  201.5 3.6 %shard_map.127.refs_9_ = bf16[18,128,1536]{2,1,0:T(8,128)(2,1)} custom-call(s32[18]{0:T(128)} %get-tuple-element.81.src_ref, s32[18]{0:T(128)} %get-tuple-element.80.rank_ref, bf16[16,2,144,384]{3,2,1,0:T(8,128)(2,1)} %bitcast.25.refs_0_.refs_1_.refs_2_.refs_3_.refs_4_.refs_5_.refs_6_.refs_7_.refs_8_, ...), custom_call_target="tpu_custom_call", output_to_operand_aliasing={{}: (11, {})} | custom-call | tf_op jit(solution)/shard_map/pallas_call | solution.py:174
  205.1 23.4 %reduce-scatter.2.cloned.1.call-done = f32[512,384]{1,0:T(8,128)} async-done(((f32[512,3072]{1,0:T(8,128)}), f32[512,384]{1,0:T(8,128)}) %reduce-scatter.2.cloned.1.call-update) | async-done | bytes 786448 | tf_op jit(solution)/shard_map/reduce_scatter | solution.py:317
  230.4 6.3 %all-to-all-done.2 = bf16[64,64,384]{2,1,0:T(8,128)(2,1)} async-done(((bf16[64,64,384]{2,1,0:T(8,128)(2,1)}), bf16[64,64,384]{2,1,0:T(8,128)(2,1)}, u32[]{:S(2)}, u32[]{:S(2)}) %all-to-all-start.2) | async-done | bytes 3145760 | tf_op jit(solution)/shard_map/all_to_all | solution.py:319
  236.7 3.3 %shard_map.128 = bf16[18,128,1536]{2,1,0:T(8,128)(2,1)} custom-call(s32[18]{0:T(128)} %get-tuple-element.81.src_ref, s32[18]{0:T(128)} %get-tuple-element.80.rank_ref, bf16[16,2,2,64,384]{4,3,2,1,0:T(8,128)(2,1)} %bitcast.24.refs_0_.refs_1_.refs_2_.refs_3_.refs_4_.refs_5_.refs_6_.refs_7_.refs_8_, ...), custom_call_target="tpu_custom_call", output_to_operand_aliasing={{}: (11, {})} | custom-call | tf_op jit(solution)/shard_map/pallas_call | solution.py:174
  (74 shorter events, 25.6 us)
Async XLA Ops:
  7.2 167.3 %copy-start = (bf16[384,3072]{1,0:T(8,128)(2,1)S(1)}, bf16[384,3072]{1,0:T(8,128)(2,1)}, u32[]{:S(2)}) copy-start(bf16[384,3072]{1,0:T(8,128)(2,1)} %param.20) | copy-start | bytes 7077892
  7.2 9.0 %copy-start.13 = (s32[1,4]{1,0:T(1,128)S(1)}, s32[1,4]{1,0:T(1,128)}, u32[]{:S(2)}) copy-start(s32[1,4]{1,0:T(1,128)} %param.24) | copy-start | bytes 52
  7.2 9.1 %copy-start.9 = (s32[1,4]{1,0:T(1,128)S(1)}, s32[1,4]{1,0:T(1,128)}, u32[]{:S(2)}) copy-start(s32[1,4]{1,0:T(1,128)} %param.23) | copy-start | bytes 52
  7.2 33.4 %all-gather.2.cloned.1.call-start = ((), (), s32[]{:S(2)}) async-start(), calls=%async_computation.4 | async-start | bytes 3649536 | tf_op jit(solution)/shard_map/all_gather | solution.py:213
  11.4 5.1 %copy-start.8 = (s32[36]{0:T(128)}, s32[36]{0:T(128)S(1)}, u32[]{:S(2)}) copy-start(s32[36]{0:T(128)S(1)} %multiply_add_fusion) | copy-start | bytes 436
  43.2 4.0 %copy-start.10 = (bf16[3072,384]{1,0:T(8,128)(2,1)S(1)}, bf16[3072,384]{1,0:T(8,128)(2,1)}, u32[]{:S(2)}) copy-start(bf16[3072,384]{1,0:T(8,128)(2,1)} %param.19) | copy-start | bytes 7077892
  47.3 2.5 %copy-start.4 = (bf16[512,3072]{1,0:T(8,128)(2,1)}, bf16[512,3072]{1,0:T(8,128)(2,1)S(1)}, u32[]{:S(2)}) copy-start(bf16[512,3072]{1,0:T(8,128)(2,1)S(1)} %fusion.8) | copy-start | bytes 9437188
  53.6 53.6 %all-to-all-start.1 = ((bf16[32,144,384]{2,1,0:T(8,128)(2,1)}), bf16[32,144,384]{2,1,0:T(8,128)(2,1)}, u32[]{:S(2)}, u32[]{:S(2)}) async-start(bf16[32,144,384]{2,1,0:T(8,128)(2,1)} %get-tuple-element.50), calls=%async_computation.1 | async-start | bytes 7077888 | tf_op jit(solution)/shard_map/all_to_all | solution.py:273
  61.0 2.9 %copy-start.5 = (bf16[512,3072]{1,0:T(8,128)(2,1)S(1)}, bf16[512,3072]{1,0:T(8,128)(2,1)}, u32[]{:S(2)}) copy-start(bf16[512,3072]{1,0:T(8,128)(2,1)} %copy-done.4) | copy-start | bytes 9437188
  61.0 3.0 %copy-start.11 = (bf16[3072,384]{1,0:T(8,128)(2,1)S(1)}, bf16[3072,384]{1,0:T(8,128)(2,1)}, u32[]{:S(2)}) copy-start(bf16[3072,384]{1,0:T(8,128)(2,1)} %param.17) | copy-start | bytes 7077892
  64.0 1.7 copy-start.12
  68.4 3.9 %copy-start.2 = (bf16[512,384]{1,0:T(8,128)(2,1)S(1)}, bf16[512,384]{1,0:T(8,128)(2,1)}, u32[]{:S(2)}) copy-start(bf16[512,384]{1,0:T(8,128)(2,1)} %copy.43.rest_0_) | copy-start | bytes 1179652
  107.2 82.8 %all-to-all-start = ((bf16[64,128,384]{2,1,0:T(8,128)(2,1)}), bf16[64,128,384]{2,1,0:T(8,128)(2,1)}, u32[]{:S(2)}, u32[]{:S(2)}) async-start(bf16[64,128,384]{2,1,0:T(8,128)(2,1)} %shard_map.125), calls=%async_computation | async-start | bytes 12582912 | tf_op jit(solution)/shard_map/all_to_all | solution.py:289
  112.1 116.3 %reduce-scatter.2.cloned.1.call-start = ((), (), s32[]{:S(2)}) async-start(), calls=%async_computation.5 | async-start | bytes 7077888 | tf_op jit(solution)/shard_map/reduce_scatter | solution.py:317
  112.3 18.6 %copy-start.6 = (bf16[512,384]{1,0:T(8,128)(2,1)S(1)}, bf16[512,384]{1,0:T(8,128)(2,1)}, u32[]{:S(2)}) copy-start(bf16[512,384]{1,0:T(8,128)(2,1)} %convolution_convert_fusion.rest_0_) | copy-start | bytes 1179652
  140.9 18.2 %copy-start.1 = (pred[512,4608]{1,0:T(8,128)(4,1)S(1)}, pred[512,4608]{1,0:T(8,128)(4,1)}, u32[]{:S(2)}) copy-start(pred[512,4608]{1,0:T(8,128)(4,1)} %pad_add_fusion) | copy-start | bytes 7077892
  140.9 18.2 %copy-start.3 = (bf16[4608,384]{0,1:T(8,128)(2,1)S(1)}, bf16[4608,384]{0,1:T(8,128)(2,1)}, u32[]{:S(2)}) copy-start(bf16[4608,384]{0,1:T(8,128)(2,1)} %copy.44) | copy-start | bytes 10616836
  190.0 46.6 %all-to-all-start.2 = ((bf16[64,64,384]{2,1,0:T(8,128)(2,1)}), bf16[64,64,384]{2,1,0:T(8,128)(2,1)}, u32[]{:S(2)}, u32[]{:S(2)}) async-start(bf16[64,64,384]{2,1,0:T(8,128)(2,1)} %get-tuple-element.53), calls=%async_computation.2 | async-start | bytes 6291456 | tf_op jit(solution)/shard_map/all_to_all | solution.py:319
  201.5 26.9 %copy-start.7 = (bf16[512,384]{1,0:T(8,128)(2,1)S(1)}, bf16[512,384]{1,0:T(8,128)(2,1)}, u32[]{:S(2)}) copy-start(bf16[512,384]{1,0:T(8,128)(2,1)} %param.15) | copy-start | bytes 1179652
Sparse Core Ops, SparseCore 0:
  10.0 30.5 all-gather.1
  190.2 38.2 reduce-scatter.1

commit v17 on v16

--- a/solution.py
+++ b/solution.py
@@ -325,7 +325,8 @@
         paired=True,
     )
     pool = place_pages(
-        from_req, from_rank, received_high, slot_count, cores, 1, 1, half_rows, into=(pool,)
+        from_req, from_rank, received_high, slot_count, cores, 1, 1, half_rows, into=(pool,),
+        group=slot_count,
     )
     return (layer_out, pool[:, None])
 

time: 249 us -> 249 us (level)
  no operation moved by 1% of the time
where the time goes in v17:
time: 249 us; the launch traced here: 247 us
  waiting for transfers between devices  69.6 us (28%)
  other arithmetic  44.5 us (18%)
  matrix products  43.8 us (18%)
  Pallas kernels  40.3 us (16%)
  starting transfers between devices  17.4 us (7%)
  local copies, waits for them, and re-layouts  17.3 us (7%)
  between operations  14.3 us (6%)
    pallas_call x3, Pallas kernels, pack_pages(): pl.pallas_call(body, out_shape=out_shape, grid_spec=pltpu.PrefetchScalarG...  27.1 us
    all_to_all x1, waiting for transfers between devices, shards(): received_low = lax.all_to_all(send_low, ('req', 'core'), 0, 0, tiled=True)  25 us
    reduce_scatter x1, waiting for transfers between devices, shards(): lax.psum_scatter(projected, ('y', 'core'), scatter_dimension=1, tiled=True)  23.4 us
    dot_general x1, matrix products, shards(): jnp.einsum('qhd,khd->hqk', queries.reshape(token_count, heads_here, HD),...  18.6 us
    reduce_sum x1, other arithmetic, shards(): totals = jnp.sum(weights, axis=2)  18.2 us
    dot_general x1, matrix products, shards(): jnp.einsum('hqk,khd->qhd', prob_rows, values_all.reshape(-1, heads_here,...  15.3 us
    pallas_call x3, Pallas kernels, place_pages(): pl.pallas_call(body, out_shape=jax.ShapeDtypeStruct((slot_count, PAGE, 2...  11.4 us
    all_to_all x1, waiting for transfers between devices, shards(): received_keys = lax.all_to_all(send_keys, ('req', 'core'), 0, 0, tiled=True)  11.1 us
  transfers between devices with their start and end apart: 5, of which 5 were waited for; matrix products, arithmetic and copies ran while one was open for 38% of the time, Pallas kernels for 13%

profile of v17, /device:TPU:0, one launch (start us, length us, event | category | flops | bytes accessed | tf_op | source)
XLA Modules:
  0.0 247.1 jit_solution(13269496305803075686)
XLA Ops:
  16.5 19.4 %shard_map.123 = (bf16[64,128,384]{2,1,0:T(8,128)(2,1)}, bf16[32,144,384]{2,1,0:T(8,128)(2,1)}, bf16[64,64,384]{2,1,0:T(8,128)(2,1)}) custom-call(s32[32]{0:T(128)} %bitcast.85, bf16[4096,384]{1,0:T(8,128)(2,1)} %rest_0_.1, bf16[4096,384]{1,0:T(8,128)(2,1)} %rest_1_.1, bf16[32,144,384]{2,1,0:T(8,128)(2,1)} %shard_map.122.rest_2_), custom_call_target="tpu_custom_call", output_to_operand_aliasing={{1}: (3, {})} | custom-call | tf_op jit(solution)/shard_map/pallas_call | solution.py:106
  36.8 3.8 %all-gather.2.cloned.1.call-done = bf16[528,3072]{1,0:T(8,128)(2,1)} async-done(((bf16[528,384]{1,0:T(8,128)(2,1)}), bf16[528,3072]{1,0:T(8,128)(2,1)}) %all-gather.2.cloned.1.call-update) | async-done | bytes 3244048 | tf_op jit(solution)/shard_map/all_gather | solution.py:213
  40.6 2.6 %fusion.6 = f32[512]{0:T(512)S(1)} fusion(bf16[528,3072]{1,0:T(8,128)(2,1)} %all-gather.2.cloned.1.call-done), kind=kLoop, calls=%fused_computation.11 | loop fusion | flops 4718080 | bytes 3147776 | tf_op jit(solution)/shard_map/reduce_sum | solution.py:219
  44.2 3.1 %fusion.8 = bf16[512,3072]{1,0:T(8,128)(2,1)S(1)} fusion(f32[3072]{0:T(1024)S(1)} %bitcast.82, f32[512]{0:T(512)S(1)} %add_rsqrt_fusion, bf16[528,3072]{1,0:T(8,128)(2,1)} %all-gather.2.cloned.1.call-done), kind=kLoop, calls=%fused_computation.13 | loop fusion | flops 6291456 | bytes 6305792 | tf_op jit(solution)/shard_map/convert_element_type | solution.py:220
  49.8 3.8 %shard_map.124 = (bf16[32,144,384]{2,1,0:T(8,128)(2,1)}, bf16[64,64,384]{2,1,0:T(8,128)(2,1)}) custom-call(s32[4]{0:T(128)} %slice.69.slot_ref, bf16[512,384]{1,0:T(8,128)(2,1)} %convolution_convert_fusion.rest_0_, bf16[32,144,384]{2,1,0:T(8,128)(2,1)} %get-tuple-element.44.rest_1_, ...), custom_call_target="tpu_custom_call", output_to_operand_aliasing={{0}: (2, {}), {1}: (3, {})} | custom-call | tf_op jit(solution)/shard_map/pallas_call | solution.py:106
  53.6 7.3 %all-to-all-start.1 = ((bf16[32,144,384]{2,1,0:T(8,128)(2,1)}), bf16[32,144,384]{2,1,0:T(8,128)(2,1)}, u32[]{:S(2)}, u32[]{:S(2)}) async-start(bf16[32,144,384]{2,1,0:T(8,128)(2,1)} %get-tuple-element.50), calls=%async_computation.1 | async-start | bytes 7077888 | tf_op jit(solution)/shard_map/all_to_all | solution.py:273
  68.4 3.9 %shard_map.125 = bf16[64,128,384]{2,1,0:T(8,128)(2,1)} custom-call(s32[4]{0:T(128)} %slice.69.slot_ref, bf16[512,384]{1,0:T(8,128)(2,1)} %copy.43.rest_0_, bf16[64,128,384]{2,1,0:T(8,128)(2,1)} %get-tuple-element.49.rest_1_), custom_call_target="tpu_custom_call", output_to_operand_aliasing={{}: (2, {})} | custom-call | tf_op jit(solution)/shard_map/pallas_call | solution.py:106
  72.3 4.1 %pad_maximum_fusion.1 = bf16[4608,384]{1,0:T(8,128)(2,1)} fusion(bf16[512,384]{1,0:T(8,128)(2,1)S(1)} %copy-done.2, bf16[4096,384]{1,0:T(8,128)(2,1)} %rest_0_.1), kind=kLoop, calls=%fused_computation.16 | loop fusion | flops 7077888 | bytes 7077888 | tf_op jit(solution)/shard_map/concatenate | solution.py:285
  76.3 5.8 %copy.46 = bf16[4608,384]{0,1:T(8,128)(2,1)} copy(bf16[4608,384]{1,0:T(8,128)(2,1)} %pad_maximum_fusion.1) | data formatting | bytes 7077888 | tf_op jit(solution)/shard_map/concatenate | solution.py:285
  82.1 25.0 %all-to-all-done.1 = bf16[32,144,384]{2,1,0:T(8,128)(2,1)} async-done(((bf16[32,144,384]{2,1,0:T(8,128)(2,1)}), bf16[32,144,384]{2,1,0:T(8,128)(2,1)}, u32[]{:S(2)}, u32[]{:S(2)}) %all-to-all-start.1) | async-done | bytes 3538976 | tf_op jit(solution)/shard_map/all_to_all | solution.py:273
  107.2 4.9 %all-to-all-start = ((bf16[64,128,384]{2,1,0:T(8,128)(2,1)}), bf16[64,128,384]{2,1,0:T(8,128)(2,1)}, u32[]{:S(2)}, u32[]{:S(2)}) async-start(bf16[64,128,384]{2,1,0:T(8,128)(2,1)} %shard_map.125), calls=%async_computation | async-start | bytes 12582912 | tf_op jit(solution)/shard_map/all_to_all | solution.py:289
  112.3 18.6 %fusion = (f32[4,512]{1,0:T(4,128)S(1)}, f32[4,512,4608]{2,1,0:T(8,128)}) fusion(pred[512,4608]{1,0:T(8,128)(4,1)} %pad_add_fusion, bf16[4608,4,96]{0,2,1:T(8,128)(2,1)} %bitcast.76, bf16[512,4,48]{0,2,1:T(8,128)(2,1)S(1)} %get-tuple-element.73, bf16[512,4,48]{0,2,1:T(8,128)(2,1)S(1)} %get-tuple-element.72), kind=kOutput, calls=%fused_computation.3 | convolution fusion | flops 1841035264 | bytes 44048384 | tf_op jit(solution)/shard_map/qhd,khd->hqk/dot_general | solution.py:293
  130.9 4.1 %pad_maximum_fusion = bf16[4608,384]{1,0:T(8,128)(2,1)} fusion(bf16[512,384]{1,0:T(8,128)(2,1)S(1)} %copy-done.6, bf16[4096,384]{1,0:T(8,128)(2,1)} %rest_1_.1), kind=kLoop, calls=%fused_computation.15 | loop fusion | flops 7077888 | bytes 7077888 | tf_op jit(solution)/shard_map/concatenate | solution.py:286
  135.0 5.8 %copy.44 = bf16[4608,384]{0,1:T(8,128)(2,1)} copy(bf16[4608,384]{1,0:T(8,128)(2,1)} %pad_maximum_fusion) | data formatting | bytes 7077888 | tf_op jit(solution)/shard_map/concatenate | solution.py:286
  140.9 18.2 %fusion.1 = f32[4,512]{1,0:T(4,128)S(1)} fusion(f32[4,512,4608]{2,1,0:T(8,128)} %get-tuple-element.84, f32[4,512]{1,0:T(4,128)S(1)} %get-tuple-element.83, pred[512,4608]{1,0:T(8,128)(4,1)} %pad_add_fusion), kind=kLoop, calls=%fused_computation.4 | loop fusion | flops 37746688 | bytes 40124416 | tf_op jit(solution)/shard_map/reduce_sum | solution.py:302
  159.1 15.3 %fusion.15 = bf16[512,4,96]{0,2,1:T(8,128)(2,1)S(1)} fusion(bf16[4608,4,96]{0,2,1:T(8,128)(2,1)S(1)} %bitcast.77, f32[4,512,4608]{2,1,0:T(8,128)} %get-tuple-element.84, f32[4,512]{1,0:T(4,128)S(1)} %get-tuple-element.83, pred[512,4608]{1,0:T(8,128)(4,1)S(1)} %copy-done.1, f32[512,4]{0,1:T(4,128)S(1)} %bitcast.84), kind=kOutput, calls=%fused_computation.20 | convolution fusion | flops 1850081280 | bytes 44056576 | tf_op jit(solution)/shard_map/hqk,khd->qhd/dot_general | solution.py:304
  174.4 4.5 %fusion.38 = f32[512,3072]{1,0:T(8,128)} fusion(bf16[512,384]{0,1:T(8,128)(2,1)S(1)} %bitcast.81, bf16[384,3072]{1,0:T(8,128)(2,1)S(1)} %copy-done), kind=kOutput, calls=%fused_computation.81 | convolution fusion | flops 1207959552 | bytes 9043968 | tf_op jit(solution)/shard_map/dot_general | solution.py:313
  178.9 11.1 %all-to-all-done = bf16[64,128,384]{2,1,0:T(8,128)(2,1)} async-done(((bf16[64,128,384]{2,1,0:T(8,128)(2,1)}), bf16[64,128,384]{2,1,0:T(8,128)(2,1)}, u32[]{:S(2)}, u32[]{:S(2)}) %all-to-all-start) | async-done | bytes 6291488 | tf_op jit(solution)/shard_map/all_to_all | solution.py:289
  190.0 4.8 %all-to-all-start.2 = ((bf16[64,64,384]{2,1,0:T(8,128)(2,1)}), bf16[64,64,384]{2,1,0:T(8,128)(2,1)}, u32[]{:S(2)}, u32[]{:S(2)}) async-start(bf16[64,64,384]{2,1,0:T(8,128)(2,1)} %get-tuple-element.53), calls=%async_computation.2 | async-start | bytes 6291456 | tf_op jit(solution)/shard_map/all_to_all | solution.py:319
  197.2 4.3 %shard_map.126.refs_9_ = bf16[18,128,1536]{2,1,0:T(8,128)(2,1)} custom-call(s32[18]{0:T(128)} %get-tuple-element.81.src_ref, s32[18]{0:T(128)} %get-tuple-element.80.rank_ref, bf16[16,2,2,128,384]{4,3,2,1,0:T(8,128)(2,1)} %bitcast.26.refs_0_.refs_1_.refs_2_.refs_3_.refs_4_.refs_5_.refs_6_.refs_7_.refs_8_, ...), custom_call_target="tpu_custom_call" | custom-call | tf_op jit(solution)/shard_map/pallas_call | solution.py:174
  201.5 3.6 %shard_map.127.refs_18_ = bf16[18,128,1536]{2,1,0:T(8,128)(2,1)} custom-call(s32[18]{0:T(128)} %get-tuple-element.81.src_ref, s32[18]{0:T(128)} %get-tuple-element.80.rank_ref, bf16[16,2,144,384]{3,2,1,0:T(8,128)(2,1)} %bitcast.25.refs_0_.refs_1_.refs_2_.refs_3_.refs_4_.refs_5_.refs_6_.refs_7_.refs_8_, ...), custom_call_target="tpu_custom_call", output_to_operand_aliasing={{}: (11, {})} | custom-call | tf_op jit(solution)/shard_map/pallas_call | solution.py:174
  205.0 23.4 %reduce-scatter.2.cloned.1.call-done = f32[512,384]{1,0:T(8,128)} async-done(((f32[512,3072]{1,0:T(8,128)}), f32[512,384]{1,0:T(8,128)}) %reduce-scatter.2.cloned.1.call-update) | async-done | bytes 786448 | tf_op jit(solution)/shard_map/reduce_scatter | solution.py:317
  230.4 6.3 %all-to-all-done.2 = bf16[64,64,384]{2,1,0:T(8,128)(2,1)} async-done(((bf16[64,64,384]{2,1,0:T(8,128)(2,1)}), bf16[64,64,384]{2,1,0:T(8,128)(2,1)}, u32[]{:S(2)}, u32[]{:S(2)}) %all-to-all-start.2) | async-done | bytes 3145760 | tf_op jit(solution)/shard_map/all_to_all | solution.py:319
  236.6 3.6 %shard_map.128 = bf16[18,128,1536]{2,1,0:T(8,128)(2,1)} custom-call(s32[18]{0:T(128)} %get-tuple-element.81.src_ref, s32[18]{0:T(128)} %get-tuple-element.80.rank_ref, ...), custom_call_target="tpu_custom_call", output_to_operand_aliasing={{}: (20, {})} | custom-call | tf_op jit(solution)/shard_map/pallas_call | solution.py:174
  (74 shorter events, 25.6 us)
Async XLA Ops:
  7.2 167.3 %copy-start = (bf16[384,3072]{1,0:T(8,128)(2,1)S(1)}, bf16[384,3072]{1,0:T(8,128)(2,1)}, u32[]{:S(2)}) copy-start(bf16[384,3072]{1,0:T(8,128)(2,1)} %param.20) | copy-start | bytes 7077892
  7.2 9.0 %copy-start.13 = (s32[1,4]{1,0:T(1,128)S(1)}, s32[1,4]{1,0:T(1,128)}, u32[]{:S(2)}) copy-start(s32[1,4]{1,0:T(1,128)} %param.24) | copy-start | bytes 52
  7.2 9.1 %copy-start.9 = (s32[1,4]{1,0:T(1,128)S(1)}, s32[1,4]{1,0:T(1,128)}, u32[]{:S(2)}) copy-start(s32[1,4]{1,0:T(1,128)} %param.23) | copy-start | bytes 52
  7.2 33.4 %all-gather.2.cloned.1.call-start = ((), (), s32[]{:S(2)}) async-start(), calls=%async_computation.4 | async-start | bytes 3649536 | tf_op jit(solution)/shard_map/all_gather | solution.py:213
  11.4 5.1 %copy-start.8 = (s32[36]{0:T(128)}, s32[36]{0:T(128)S(1)}, u32[]{:S(2)}) copy-start(s32[36]{0:T(128)S(1)} %multiply_add_fusion) | copy-start | bytes 436
  43.2 4.0 %copy-start.10 = (bf16[3072,384]{1,0:T(8,128)(2,1)S(1)}, bf16[3072,384]{1,0:T(8,128)(2,1)}, u32[]{:S(2)}) copy-start(bf16[3072,384]{1,0:T(8,128)(2,1)} %param.19) | copy-start | bytes 7077892
  47.3 2.5 %copy-start.4 = (bf16[512,3072]{1,0:T(8,128)(2,1)}, bf16[512,3072]{1,0:T(8,128)(2,1)S(1)}, u32[]{:S(2)}) copy-start(bf16[512,3072]{1,0:T(8,128)(2,1)S(1)} %fusion.8) | copy-start | bytes 9437188
  53.6 53.6 %all-to-all-start.1 = ((bf16[32,144,384]{2,1,0:T(8,128)(2,1)}), bf16[32,144,384]{2,1,0:T(8,128)(2,1)}, u32[]{:S(2)}, u32[]{:S(2)}) async-start(bf16[32,144,384]{2,1,0:T(8,128)(2,1)} %get-tuple-element.50), calls=%async_computation.1 | async-start | bytes 7077888 | tf_op jit(solution)/shard_map/all_to_all | solution.py:273
  61.0 2.9 %copy-start.5 = (bf16[512,3072]{1,0:T(8,128)(2,1)S(1)}, bf16[512,3072]{1,0:T(8,128)(2,1)}, u32[]{:S(2)}) copy-start(bf16[512,3072]{1,0:T(8,128)(2,1)} %copy-done.4) | copy-start | bytes 9437188
  61.0 3.0 %copy-start.11 = (bf16[3072,384]{1,0:T(8,128)(2,1)S(1)}, bf16[3072,384]{1,0:T(8,128)(2,1)}, u32[]{:S(2)}) copy-start(bf16[3072,384]{1,0:T(8,128)(2,1)} %param.17) | copy-start | bytes 7077892
  64.0 1.7 copy-start.12
  68.4 3.9 %copy-start.2 = (bf16[512,384]{1,0:T(8,128)(2,1)S(1)}, bf16[512,384]{1,0:T(8,128)(2,1)}, u32[]{:S(2)}) copy-start(bf16[512,384]{1,0:T(8,128)(2,1)} %copy.43.rest_0_) | copy-start | bytes 1179652
  107.2 82.8 %all-to-all-start = ((bf16[64,128,384]{2,1,0:T(8,128)(2,1)}), bf16[64,128,384]{2,1,0:T(8,128)(2,1)}, u32[]{:S(2)}, u32[]{:S(2)}) async-start(bf16[64,128,384]{2,1,0:T(8,128)(2,1)} %shard_map.125), calls=%async_computation | async-start | bytes 12582912 | tf_op jit(solution)/shard_map/all_to_all | solution.py:289
  112.1 116.3 %reduce-scatter.2.cloned.1.call-start = ((), (), s32[]{:S(2)}) async-start(), calls=%async_computation.5 | async-start | bytes 7077888 | tf_op jit(solution)/shard_map/reduce_scatter | solution.py:317
  112.3 18.6 %copy-start.6 = (bf16[512,384]{1,0:T(8,128)(2,1)S(1)}, bf16[512,384]{1,0:T(8,128)(2,1)}, u32[]{:S(2)}) copy-start(bf16[512,384]{1,0:T(8,128)(2,1)} %convolution_convert_fusion.rest_0_) | copy-start | bytes 1179652
  140.8 18.2 %copy-start.1 = (pred[512,4608]{1,0:T(8,128)(4,1)S(1)}, pred[512,4608]{1,0:T(8,128)(4,1)}, u32[]{:S(2)}) copy-start(pred[512,4608]{1,0:T(8,128)(4,1)} %pad_add_fusion) | copy-start | bytes 7077892
  140.9 18.2 %copy-start.3 = (bf16[4608,384]{0,1:T(8,128)(2,1)S(1)}, bf16[4608,384]{0,1:T(8,128)(2,1)}, u32[]{:S(2)}) copy-start(bf16[4608,384]{0,1:T(8,128)(2,1)} %copy.44) | copy-start | bytes 10616836
  190.0 46.6 %all-to-all-start.2 = ((bf16[64,64,384]{2,1,0:T(8,128)(2,1)}), bf16[64,64,384]{2,1,0:T(8,128)(2,1)}, u32[]{:S(2)}, u32[]{:S(2)}) async-start(bf16[64,64,384]{2,1,0:T(8,128)(2,1)} %get-tuple-element.53), calls=%async_computation.2 | async-start | bytes 6291456 | tf_op jit(solution)/shard_map/all_to_all | solution.py:319
  201.5 26.9 %copy-start.7 = (bf16[512,384]{1,0:T(8,128)(2,1)S(1)}, bf16[512,384]{1,0:T(8,128)(2,1)}, u32[]{:S(2)}) copy-start(bf16[512,384]{1,0:T(8,128)(2,1)} %param.15) | copy-start | bytes 1179652
Sparse Core Ops, SparseCore 0:
  10.0 30.5 all-gather.1
  190.1 38.2 reduce-scatter.1
